TPU v7x, 32 devices: a whole 2x2x4 slice. The times are simulated.
32 devices in a mesh: vox: 16 (over z, y, core), star: 2 (over x).
Axes of the slice: x: 2, y: 2, z: 4, core: 2. Of those that a mesh axis runs over, the one named last changes fastest.
Arguments:
- mean_field: float32 [32, 128, 128], P('vox', 'star'), may hold values from -3 to 3
- deviations: float32 [4, 32, 128, 128], P(None, 'vox', 'star'), may hold values from -4 to 4
- stencil: float32 [3, 3], replicated, may hold values from -2 to 2
- vertical_mix: float32 [128, 128], replicated, may hold values from -0.5 to 0.5
- log_mean: float32 [128], replicated, may hold values from -1.6 to -0.4
- responses: bfloat16 [3072, 128, 128], P(('vox', 'star')), may hold values from 0 to 0.015625
- pair_line: int32 [3072], P(('vox', 'star')), may hold values from 0 to 127
- pair_owner: int32 [3072, 1], P(('vox', 'star')), may hold values from 0 to 15; in each aligned block of 96 rows (0 to 95, 96 to 191, ...) at most 12 rows name the same one
- pair_star: int32 [3072], P(('vox', 'star')), may hold values from 0 to 7
- observed: float32 [256, 128], P(('vox', 'star')), may hold values from 0 to 15
- inv_var: float32 [256, 128], P(('vox', 'star')), may hold values from 0.05 to 0.5
Outputs:
- gradient: float32 [32, 128, 128], P('vox', 'star')
- residual_mean: float32 [256, 128], P(('vox', 'star'))
Inputs may be any that keep to these rules, and one draw needn't show every extreme that they name: `pair_owner`: among the 96 pairs of one device at most 12 name one owner, a bound that some block reaches.
All inputs are finite; a program needn't handle non-finite values.
Results may differ from a plain program's by a relative error of at most 0.0015.
Values may be sent and summed in bfloat16 or wider, within the bound.
No kernel may reach another device: no remote copies, remote signals or barrier semaphores. Data moves between devices by JAX's collectives and lax.ppermute only.
A program may use at most 64 MiB of HBM per device.

v0:
```python
import jax
import jax.numpy as jnp
from jax import lax
from jax.sharding import PartitionSpec as P

HIGH = lax.Precision.HIGHEST


def with_halo(cells, sides, width):
    for axis, dim in sides:
        count = lax.axis_size(axis)
        ends = count - 1
        head = lax.slice_in_dim(cells, 0, width, axis=dim)
        tail = lax.slice_in_dim(cells, cells.shape[dim] - width, cells.shape[dim], axis=dim)
        cells = jnp.concatenate(
            [
                lax.ppermute(tail, axis, [(i, (i + 1) % count) for i in range(ends)]),
                cells,
                lax.ppermute(head, axis, [((i + 1) % count, i) for i in range(ends)]),
            ],
            axis=dim,
        )
    return cells


def per_device(
    mean_field,
    deviations,
    stencil,
    vertical_mix,
    log_mean,
    responses,
    pair_line,
    pair_owner,
    pair_star,
    observed,
    inv_var,
):
    samples = deviations.shape[0]
    width_x = deviations.shape[1]
    width_y = deviations.shape[2]
    length = deviations.shape[3]
    pair_count = responses.shape[0]
    block_count = observed.shape[0]
    group_size = lax.axis_size("vox")
    capacity = max(2, 2 * pair_count // group_size)
    latent = mean_field[None] + deviations
    padded = with_halo(latent, (("vox", 1), ("star", 2)), 1)
    smoothed = jnp.zeros(latent.shape, jnp.float32)
    for offset_x in range(3):
        for offset_y in range(3):
            smoothed = (
                smoothed
                + stencil[offset_x, offset_y]
                * padded[:, offset_x : offset_x + width_x, offset_y : offset_y + width_y, :]
            )
    log_density = jnp.einsum("sxyw,zw->sxyz", smoothed, vertical_mix, precision=HIGH) + log_mean
    density = jnp.exp(log_density)
    density_b = density.astype(jnp.bfloat16).reshape(samples, width_x * width_y, length)
    picked = jnp.take(density_b, pair_line, axis=1)
    contribution = jnp.einsum("pij,spj->psi", responses, picked, preferred_element_type=jnp.float32)
    owner = pair_owner[:, 0]
    owner_onehot = (owner[:, None] == jnp.arange(group_size, dtype=jnp.int32)[None, :]).astype(
        jnp.int32
    )
    position = jnp.sum((jnp.cumsum(owner_onehot, axis=0) - owner_onehot) * owner_onehot, axis=1)
    slot_id = owner * capacity + position
    slot_onehot = slot_id[:, None] == jnp.arange(group_size * capacity, dtype=jnp.int32)[None, :]
    slot_float = slot_onehot.astype(jnp.float32)
    outgoing = jnp.einsum("pq,psi->qsi", slot_float, contribution, precision=HIGH).reshape(
        group_size, capacity, samples, length
    )
    slot_star = (
        jnp.sum(slot_onehot.astype(jnp.int32) * (pair_star + 1)[:, None], axis=0) - 1
    ).reshape(group_size, capacity)
    arrived, arrived_star = (
        lax.all_to_all(outgoing, "vox", split_axis=0, concat_axis=0, tiled=True),
        lax.all_to_all(slot_star, "vox", split_axis=0, concat_axis=0, tiled=True),
    )
    star_onehot = (
        arrived_star.reshape(-1)[:, None] == jnp.arange(block_count, dtype=jnp.int32)[None, :]
    ).astype(jnp.float32)
    extinction = jnp.einsum(
        "qb,qsi->bsi",
        star_onehot,
        arrived.reshape(group_size * capacity, samples, length),
        precision=HIGH,
    )
    misfit = inv_var[:, None, :] * (extinction - observed[:, None, :])
    misfit_b = misfit.astype(jnp.bfloat16)
    returning = jnp.einsum(
        "qb,bsi->qsi", star_onehot, misfit_b.astype(jnp.float32), precision=HIGH
    ).astype(jnp.bfloat16)
    returned = lax.all_to_all(
        returning.reshape(group_size, capacity, samples, length),
        "vox",
        split_axis=0,
        concat_axis=0,
        tiled=True,
    )
    pair_misfit = jnp.einsum(
        "pq,qsi->psi",
        slot_float,
        returned.reshape(group_size * capacity, samples, length).astype(jnp.float32),
        precision=HIGH,
    ).astype(jnp.bfloat16)
    residual_mean = jnp.mean(misfit, axis=1)
    pair_adjoint = jnp.einsum(
        "pij,psi->psj", responses, pair_misfit, preferred_element_type=jnp.float32
    )
    line_onehot = (
        pair_line[:, None] == jnp.arange(width_x * width_y, dtype=jnp.int32)[None, :]
    ).astype(jnp.float32)
    adjoint = jnp.einsum("pb,psj->sbj", line_onehot, pair_adjoint, precision=HIGH).reshape(
        samples, width_x, width_y, length
    )
    grad_log = density * adjoint
    grad_smooth = jnp.einsum("sxyz,zw->sxyw", grad_log, vertical_mix, precision=HIGH)
    padded_grad = with_halo(grad_smooth, (("vox", 1), ("star", 2)), 1)
    grad_latent = jnp.zeros(latent.shape, jnp.float32)
    for offset_x in range(3):
        for offset_y in range(3):
            grad_latent = (
                grad_latent
                + stencil[offset_x, offset_y]
                * padded_grad[
                    :,
                    2 - offset_x : 2 - offset_x + width_x,
                    2 - offset_y : 2 - offset_y + width_y,
                    :,
                ]
            )
    gradient = jnp.mean(grad_latent + latent, axis=0)
    return (gradient, residual_mean)


def solution(mesh):
    placed = (
        P("vox", "star", None),
        P(None, "vox", "star", None),
        P(),
        P(),
        P(),
        P(("vox", "star"), None, None),
        P(("vox", "star")),
        P(("vox", "star"), None),
        P(("vox", "star")),
        P(("vox", "star"), None),
        P(("vox", "star"), None),
    )
    return jax.shard_map(
        per_device,
        mesh=mesh,
        in_specs=placed,
        out_specs=(P("vox", "star", None), P(("vox", "star"), None)),
        check_vma=False,
    )
```

profile of v0, /device:TPU:1, one launch (start us, length us, event | category | flops | bytes accessed | tf_op | source)
XLA Modules:
  0.0 103.0 jit_solution(2323372958306056035)
XLA Ops:
  0.6 1.1 %broadcast_add_fusion = f32[4,2,64,128]{3,2,1,0:T(8,128)S(1)} fusion(f32[4,2,64,128]{3,2,1,0:T(8,128)} %param.12, f32[2,64,128]{2,1,0:T(8,128)} %param.11), kind=kLoop, calls=%fused_computation.68 | loop fusion | flops 65536 | bytes 589824 | tf_op jit(solution)/shard_map/add | solution.py:47
  2.5 4.5 %collective-permute-start = (f32[4,1,64,128]{3,2,1,0:T(8,128)}, f32[4,1,64,128]{3,2,1,0:T(8,128)S(1)}, u32[]{:S(2)}, u32[]{:S(2)}) collective-permute-start(f32[4,1,64,128]{3,2,1,0:T(8,128)} %get-tuple-element.12), channel_id=1, source_target_pairs={{0,2},{2,4},{4,6},{6,8},{8,10},{10,12},{12,14},{14,16},{16,18},{18... | collective-permute-start | bytes 393224 | tf_op jit(solution)/shard_map/ppermute | solution.py:17
  7.0 1.9 %collective-permute-start.1 = (f32[4,1,64,128]{3,2,1,0:T(8,128)}, f32[4,1,64,128]{3,2,1,0:T(8,128)}, u32[]{:S(2)}, u32[]{:S(2)}) collective-permute-start(f32[4,1,64,128]{3,2,1,0:T(8,128)} %get-tuple-element.13), channel_id=1, source_target_pairs={{2,0},{4,2},{6,4},{8,6},{10,8},{12,10},{14,12},{16,14},{18,16},{20... | collective-permute-start | bytes 393224 | tf_op jit(solution)/shard_map/ppermute | solution.py:19
  9.0 1.4 %fusion.65 = s32[96,16]{1,0:T(8,128)} fusion(s32[96]{0:T(128)} %bitcast.60), kind=kLoop, calls=%fused_computation.87 | loop fusion | flops 3072 | bytes 6528 | tf_op jit(solution)/shard_map/convert_element_type | solution.py:63
  10.3 1.5 %reduce_window_sum.11 = s32[96,16]{1,0:T(8,128)} reduce-window(s32[96,16]{1,0:T(8,128)} %fusion.65, s32[]{:T(128)} %constant.28.clone.1), window={size=96x1 pad=95_0x0_0}, to_apply=%region_0.1 | reduce-window | flops 145920 | bytes 12292 | tf_op jit(solution)/shard_map/jit(cumsum)/reduce_window_sum | solution.py:66
  15.0 6.5 %all-to-all-start = ((s32[16,1,12]{2,1,0:T(1,128)}), s32[16,1,12]{2,1,0:T(1,128)S(1)}, u32[]{:S(2)}, u32[]{:S(2)}) async-start(s32[16,1,12]{2,1,0:T(1,128)} %bitcast.15), calls=%async_computation | async-start | bytes 16384 | tf_op jit(solution)/shard_map/all_to_all | solution.py:78
  22.1 1.2 %compare_and_fusion = pred[96]{0:T(512)(128)(4,1)} fusion(s32[96]{0:T(128)} %param.17), kind=kLoop, calls=%fused_computation.105 | loop fusion | flops 576 | bytes 480 | tf_op jit(solution)/shard_map/jit(_take)/and | solution.py:60
  23.3 1.7 %fusion.80 = (f32[1,1]{1,0:T(1,128)}, f32[1,1]{1,0:T(1,128)}, f32[1,1]{1,0:T(1,128)}, f32[1,1]{1,0:T(1,128)}, f32[1,1]{1,0:T(1,128)}, /*index=5*/f32[1,1]{1,0:T(...) fusion(f32[3,3]{1,0:T(4,128)} %param.13), kind=kLoop, calls=%fused_computation.114 | loop fusion | bytes 72 | tf_op jit(solution)/shard_map/slice | solution.py:125
  25.7 3.1 %collective-permute-start.2 = (f32[4,4,1,128]{3,2,1,0:T(1,128)S(1)}, f32[4,4,1,128]{3,2,1,0:T(1,128)S(1)}, u32[]{:S(2)}, u32[]{:S(2)}) collective-permute-start(f32[4,4,1,128]{3,2,1,0:T(1,128)S(1)} %get-tuple-element.8), channel_id=1, source_target_pairs={{0,1},{2,3},{4,5},{6,7},{8,9},{10,11},{12,13},{14,15},{16,17},{18,... | collective-permute-start | bytes 24584 | tf_op jit(solution)/shard_map/ppermute | solution.py:17
  28.8 1.3 %collective-permute-start.3 = (f32[4,4,1,128]{3,2,1,0:T(1,128)S(1)}, f32[4,4,1,128]{3,2,1,0:T(1,128)S(1)}, u32[]{:S(2)}, u32[]{:S(2)}) collective-permute-start(f32[4,4,1,128]{3,2,1,0:T(1,128)S(1)} %get-tuple-element.9), channel_id=1, source_target_pairs={{1,0},{3,2},{5,4},{7,6},{9,8},{11,10},{13,12},{15,14},{17,16},{19,... | collective-permute-start | bytes 24584 | tf_op jit(solution)/shard_map/ppermute | solution.py:19
  30.2 3.1 %collective-permute-done.3 = f32[4,4,1,128]{3,2,1,0:T(1,128)S(1)} collective-permute-done((f32[4,4,1,128]{3,2,1,0:T(1,128)S(1)}, f32[4,4,1,128]{3,2,1,0:T(1,128)S(1)}, u32[]{:S(2)}, u32[]{:S(2)}) %collective-permute-start.3) | collective-permute-done | bytes 8224 | tf_op jit(solution)/shard_map/ppermute | solution.py:19
  33.2 1.1 %maximum_maximum_fusion = (f32[4,4,65,128]{3,2,1,0:T(8,128)S(1)}, f32[4,4,65,128]{3,2,1,0:T(8,128)S(1)}) fusion(f32[4,1,64,128]{3,2,1,0:T(8,128)} %collective-permute-done.1, f32[4,2,64,128]{3,2,1,0:T(8,128)S(1)} %broadcast_add_fusion, f32[4,1,64,128]{3,2,1,0:T(8,128)S(1)} %collective-permute-done, f32[4,4,1,128]{3,2,1,0:T(1,128)S(1)} %collective-permute-done.2, ...), kind=kLoop, calls=%fused_computation.7 | loop fusion | flops 798720 | bytes 1605632 | tf_op jit(solution)/shard_map/concatenate | solution.py:15
  34.3 7.8 %fusion.81 = (bf16[4,2,64,128]{3,2,1,0:T(8,128)(2,1)S(1)}, f32[4,2,64,128]{3,2,1,0:T(8,128)}) fusion(f32[128]{0:T(128)} %param.15, f32[128,128]{1,0:T(8,128)} %param.14, f32[4,4,65,128]{3,2,1,0:T(8,128)S(1)} %get-tuple-element.7, f32[4,1,64,128]{3,2,1,0:T(8,128)} %collective-permute-done.1, f32[4,2,64,128]{3,2,1,0:T(8,128)S(1)} %broadcast_add_fusion, ...), kind=kOutput, calls=%fused_computation.115 | convolution fusion | flops 102039552 | bytes 2556452 | tf_op jit(solution)/shard_map/sxyw,zw->sxyz/dot_general | solution.py:57
  42.9 2.4 %fusion.51 = f32[96,4,128]{2,1,0:T(4,128)S(1)} fusion(bf16[96,128,128]{2,1,0:T(8,128)(2,1)S(1)} %copy-done, bf16[96,4,128]{2,1,0:T(4,128)(2,1)S(1)} %gather_fusion, pred[96]{0:T(512)(128)(4,1)} %compare_and_fusion), kind=kOutput, calls=%fused_computation.70 | convolution fusion | flops 12632064 | bytes 3440736 | tf_op jit(solution)/shard_map/pij,spj->psi/dot_general | solution.py:61
  46.8 7.4 %all-to-all-start.1 = ((f32[16,12,4,128]{3,2,1,0:T(4,128)}), f32[16,12,4,128]{3,2,1,0:T(4,128)S(1)}, u32[]{:S(2)}, u32[]{:S(2)}) async-start(f32[16,12,4,128]{3,2,1,0:T(4,128)} %bitcast.55), calls=%async_computation.1 | async-start | bytes 786432 | tf_op jit(solution)/shard_map/all_to_all | solution.py:77
  55.5 10.6 %all-to-all-done.1 = f32[16,12,4,128]{3,2,1,0:T(4,128)S(1)} async-done(((f32[16,12,4,128]{3,2,1,0:T(4,128)}), f32[16,12,4,128]{3,2,1,0:T(4,128)S(1)}, u32[]{:S(2)}, u32[]{:S(2)}) %all-to-all-start.1) | async-done | bytes 393248 | tf_op jit(solution)/shard_map/all_to_all | solution.py:77
  66.1 1.0 fusion.82
  67.6 11.9 %all_to_all.16 = bf16[16,12,4,128]{3,2,1,0:T(4,128)(2,1)S(1)} all-to-all(bf16[16,12,4,128]{3,2,1,0:T(4,128)(2,1)S(1)} %bitcast.58), channel_id=1, replica_groups=mesh['vox'=16,'star'=2] {'vox'}, dimensions={0} | all-to-all | bytes 393216 | tf_op jit(solution)/shard_map/all_to_all | solution.py:94
  82.1 1.9 %collective-permute-start.4 = (f32[4,1,64,128]{3,2,1,0:T(8,128)S(1)}, f32[4,1,64,128]{3,2,1,0:T(8,128)S(1)}, u32[]{:S(2)}, u32[]{:S(2)}) collective-permute-start(f32[4,1,64,128]{3,2,1,0:T(8,128)S(1)} %get-tuple-element.10), channel_id=1, source_target_pairs={{0,2},{2,4},{4,6},{6,8},{8,10},{10,12},{12,14},{14,16},{16,18},{18... | collective-permute-start | bytes 393224 | tf_op jit(solution)/shard_map/ppermute | solution.py:17
  84.1 2.4 %collective-permute-start.5 = (f32[4,1,64,128]{3,2,1,0:T(8,128)S(1)}, f32[4,1,64,128]{3,2,1,0:T(8,128)S(1)}, u32[]{:S(2)}, u32[]{:S(2)}) collective-permute-start(f32[4,1,64,128]{3,2,1,0:T(8,128)S(1)} %get-tuple-element.11), channel_id=1, source_target_pairs={{2,0},{4,2},{6,4},{8,6},{10,8},{12,10},{14,12},{16,14},{18,16},{20... | collective-permute-start | bytes 393224 | tf_op jit(solution)/shard_map/ppermute | solution.py:19
  86.5 3.9 %collective-permute-done.5 = f32[4,1,64,128]{3,2,1,0:T(8,128)S(1)} collective-permute-done((f32[4,1,64,128]{3,2,1,0:T(8,128)S(1)}, f32[4,1,64,128]{3,2,1,0:T(8,128)S(1)}, u32[]{:S(2)}, u32[]{:S(2)}) %collective-permute-start.5) | collective-permute-done | bytes 131104 | tf_op jit(solution)/shard_map/ppermute | solution.py:19
  90.4 1.3 %collective-permute-start.6 = (f32[4,4,1,128]{3,2,1,0:T(1,128)S(1)}, f32[4,4,1,128]{3,2,1,0:T(1,128)S(1)}, u32[]{:S(2)}, u32[]{:S(2)}) collective-permute-start(f32[4,4,1,128]{3,2,1,0:T(1,128)S(1)} %get-tuple-element.4), channel_id=1, source_target_pairs={{1,0},{3,2},{5,4},{7,6},{9,8},{11,10},{13,12},{15,14},{17,16},{19,... | collective-permute-start | bytes 24584 | tf_op jit(solution)/shard_map/ppermute | solution.py:19
  91.7 4.0 %collective-permute-start.7 = (f32[4,4,1,128]{3,2,1,0:T(1,128)S(1)}, f32[4,4,1,128]{3,2,1,0:T(1,128)S(1)}, u32[]{:S(2)}, u32[]{:S(2)}) collective-permute-start(f32[4,4,1,128]{3,2,1,0:T(1,128)S(1)} %get-tuple-element.5), channel_id=1, source_target_pairs={{0,1},{2,3},{4,5},{6,7},{8,9},{10,11},{12,13},{14,15},{16,17},{18,... | collective-permute-start | bytes 24584 | tf_op jit(solution)/shard_map/ppermute | solution.py:17
  96.5 5.8 %fusion.5 = f32[2,64,128]{2,1,0:T(8,128)S(1)} fusion(f32[4,4,65,128]{3,2,1,0:T(8,128)S(1)} %get-tuple-element.3, f32[4,2,64,128]{3,2,1,0:T(8,128)S(1)} %fusion.34, f32[4,1,64,128]{3,2,1,0:T(8,128)S(1)} %collective-permute-done.4, f32[4,4,65,128]{3,2,1,0:T(8,128)S(1)} %get-tuple-element.2, f32[4,1,64,128]{3,2,1,0:T(8,128)S(1)} %collective-permute-done.5, ...), kind=kLoop, calls=%fused_computation.15 | loop fusion | flops 1425408 | bytes 2490404 | tf_op jit(solution)/shard_map/reduce_sum | solution.py:133
  (49 shorter events, 13.3 us)
Async XLA Ops:
  0.6 42.3 %copy-start = (bf16[96,128,128]{2,1,0:T(8,128)(2,1)S(1)}, bf16[96,128,128]{2,1,0:T(8,128)(2,1)}, u32[]{:S(2)}) copy-start(bf16[96,128,128]{2,1,0:T(8,128)(2,1)} %param.16) | copy-start | bytes 9437188
  2.5 22.4 %collective-permute-start = (f32[4,1,64,128]{3,2,1,0:T(8,128)}, f32[4,1,64,128]{3,2,1,0:T(8,128)S(1)}, u32[]{:S(2)}, u32[]{:S(2)}) collective-permute-start(f32[4,1,64,128]{3,2,1,0:T(8,128)} %get-tuple-element.12), channel_id=1, source_target_pairs={{0,2},{2,4},{4,6},{6,8},{8,10},{10,12},{12,14},{14,16},{16,18},{18... | collective-permute-start | bytes 393224 | tf_op jit(solution)/shard_map/ppermute | solution.py:17
  7.0 17.9 %collective-permute-start.1 = (f32[4,1,64,128]{3,2,1,0:T(8,128)}, f32[4,1,64,128]{3,2,1,0:T(8,128)}, u32[]{:S(2)}, u32[]{:S(2)}) collective-permute-start(f32[4,1,64,128]{3,2,1,0:T(8,128)} %get-tuple-element.13), channel_id=1, source_target_pairs={{2,0},{4,2},{6,4},{8,6},{10,8},{12,10},{14,12},{16,14},{18,16},{20... | collective-permute-start | bytes 393224 | tf_op jit(solution)/shard_map/ppermute | solution.py:19
  13.5 31.8 %copy-start.5 = (s32[96]{0:T(128)}, s32[96]{0:T(128)S(1)}, u32[]{:S(2)}) copy-start(s32[96]{0:T(128)S(1)} %fusion.75) | copy-start | bytes 1156
  15.0 31.8 %all-to-all-start = ((s32[16,1,12]{2,1,0:T(1,128)}), s32[16,1,12]{2,1,0:T(1,128)S(1)}, u32[]{:S(2)}, u32[]{:S(2)}) async-start(s32[16,1,12]{2,1,0:T(1,128)} %bitcast.15), calls=%async_computation | async-start | bytes 16384 | tf_op jit(solution)/shard_map/all_to_all | solution.py:78
  25.7 4.5 %collective-permute-start.2 = (f32[4,4,1,128]{3,2,1,0:T(1,128)S(1)}, f32[4,4,1,128]{3,2,1,0:T(1,128)S(1)}, u32[]{:S(2)}, u32[]{:S(2)}) collective-permute-start(f32[4,4,1,128]{3,2,1,0:T(1,128)S(1)} %get-tuple-element.8), channel_id=1, source_target_pairs={{0,1},{2,3},{4,5},{6,7},{8,9},{10,11},{12,13},{14,15},{16,17},{18,... | collective-permute-start | bytes 24584 | tf_op jit(solution)/shard_map/ppermute | solution.py:17
  28.8 4.4 %collective-permute-start.3 = (f32[4,4,1,128]{3,2,1,0:T(1,128)S(1)}, f32[4,4,1,128]{3,2,1,0:T(1,128)S(1)}, u32[]{:S(2)}, u32[]{:S(2)}) collective-permute-start(f32[4,4,1,128]{3,2,1,0:T(1,128)S(1)} %get-tuple-element.9), channel_id=1, source_target_pairs={{1,0},{3,2},{5,4},{7,6},{9,8},{11,10},{13,12},{15,14},{17,16},{19,... | collective-permute-start | bytes 24584 | tf_op jit(solution)/shard_map/ppermute | solution.py:19
  46.8 19.3 %all-to-all-start.1 = ((f32[16,12,4,128]{3,2,1,0:T(4,128)}), f32[16,12,4,128]{3,2,1,0:T(4,128)S(1)}, u32[]{:S(2)}, u32[]{:S(2)}) async-start(f32[16,12,4,128]{3,2,1,0:T(4,128)} %bitcast.55), calls=%async_computation.1 | async-start | bytes 786432 | tf_op jit(solution)/shard_map/all_to_all | solution.py:77
  55.4 25.9 %copy-start.6 = (s32[96]{0:T(128)S(1)}, s32[96]{0:T(128)}, u32[]{:S(2)}) copy-start(s32[96]{0:T(128)} %param.17) | copy-start | bytes 1156
  66.1 15.6 %copy-start.3 = (f32[4,2,64,128]{3,2,1,0:T(8,128)S(1)}, f32[4,2,64,128]{3,2,1,0:T(8,128)}, u32[]{:S(2)}) copy-start(f32[4,2,64,128]{3,2,1,0:T(8,128)} %get-tuple-element.24) | copy-start | bytes 786436
  66.1 15.6 %copy-start.4 = (f32[128,128]{1,0:T(8,128)S(1)}, f32[128,128]{1,0:T(8,128)}, u32[]{:S(2)}) copy-start(f32[128,128]{1,0:T(8,128)} %param.14) | copy-start | bytes 196612
  80.4 16.2 %copy-start.1 = (f32[4,2,64,128]{3,2,1,0:T(8,128)S(1)}, f32[4,2,64,128]{3,2,1,0:T(8,128)}, u32[]{:S(2)}) copy-start(f32[4,2,64,128]{3,2,1,0:T(8,128)} %param.12) | copy-start | bytes 786436
  80.4 16.2 %copy-start.2 = (f32[2,64,128]{2,1,0:T(8,128)S(1)}, f32[2,64,128]{2,1,0:T(8,128)}, u32[]{:S(2)}) copy-start(f32[2,64,128]{2,1,0:T(8,128)} %param.11) | copy-start | bytes 196612
  82.1 4.3 %collective-permute-start.4 = (f32[4,1,64,128]{3,2,1,0:T(8,128)S(1)}, f32[4,1,64,128]{3,2,1,0:T(8,128)S(1)}, u32[]{:S(2)}, u32[]{:S(2)}) collective-permute-start(f32[4,1,64,128]{3,2,1,0:T(8,128)S(1)} %get-tuple-element.10), channel_id=1, source_target_pairs={{0,2},{2,4},{4,6},{6,8},{8,10},{10,12},{12,14},{14,16},{16,18},{18... | collective-permute-start | bytes 393224 | tf_op jit(solution)/shard_map/ppermute | solution.py:17
  84.1 6.3 %collective-permute-start.5 = (f32[4,1,64,128]{3,2,1,0:T(8,128)S(1)}, f32[4,1,64,128]{3,2,1,0:T(8,128)S(1)}, u32[]{:S(2)}, u32[]{:S(2)}) collective-permute-start(f32[4,1,64,128]{3,2,1,0:T(8,128)S(1)} %get-tuple-element.11), channel_id=1, source_target_pairs={{2,0},{4,2},{6,4},{8,6},{10,8},{12,10},{14,12},{16,14},{18,16},{20... | collective-permute-start | bytes 393224 | tf_op jit(solution)/shard_map/ppermute | solution.py:19
  90.4 5.9 %collective-permute-start.6 = (f32[4,4,1,128]{3,2,1,0:T(1,128)S(1)}, f32[4,4,1,128]{3,2,1,0:T(1,128)S(1)}, u32[]{:S(2)}, u32[]{:S(2)}) collective-permute-start(f32[4,4,1,128]{3,2,1,0:T(1,128)S(1)} %get-tuple-element.4), channel_id=1, source_target_pairs={{1,0},{3,2},{5,4},{7,6},{9,8},{11,10},{13,12},{15,14},{17,16},{19,... | collective-permute-start | bytes 24584 | tf_op jit(solution)/shard_map/ppermute | solution.py:19
  91.7 4.8 %collective-permute-start.7 = (f32[4,4,1,128]{3,2,1,0:T(1,128)S(1)}, f32[4,4,1,128]{3,2,1,0:T(1,128)S(1)}, u32[]{:S(2)}, u32[]{:S(2)}) collective-permute-start(f32[4,4,1,128]{3,2,1,0:T(1,128)S(1)} %get-tuple-element.5), channel_id=1, source_target_pairs={{0,1},{2,3},{4,5},{6,7},{8,9},{10,11},{12,13},{14,15},{16,17},{18,... | collective-permute-start | bytes 24584 | tf_op jit(solution)/shard_map/ppermute | solution.py:17
where the time goes:
time: 105 us; the launch traced here: 103 us
  starting transfers between devices  34.4 us (33%)
  other arithmetic  17.9 us (17%)
  waiting for transfers between devices  17.7 us (17%)
  matrix products  14.4 us (14%)
  blocking collectives  11.9 us (11%)
  local copies, waits for them, and re-layouts  5.71 us (5%)
    ppermute x4, starting transfers between devices, with_halo(): lax.ppermute(tail, axis, [(i, (i + 1) % count) for i in range(ends)])  13.6 us
    all_to_all x1, blocking collectives, per_device(): lax.all_to_all(returning.reshape(group_size, capacity, samples, length),...  11.9 us
    all_to_all x1, waiting for transfers between devices, per_device(): lax.all_to_all(outgoing, 'vox', split_axis=0, concat_axis=0, tiled=True)  10.6 us
    dot_general x1, matrix products, per_device(): jnp.einsum('sxyw,zw->sxyz', smoothed, vertical_mix, precision=HIGH)  7.76 us
    all_to_all x1, starting transfers between devices, per_device(): lax.all_to_all(outgoing, 'vox', split_axis=0, concat_axis=0, tiled=True)  7.43 us
    ppermute x4, waiting for transfers between devices, with_halo(): lax.ppermute(head, axis, [((i + 1) % count, i) for i in range(ends)])  6.94 us
    ppermute x4, starting transfers between devices, with_halo(): lax.ppermute(head, axis, [((i + 1) % count, i) for i in range(ends)])  6.92 us
    all_to_all x1, starting transfers between devices, per_device(): lax.all_to_all(slot_star, 'vox', split_axis=0, concat_axis=0, tiled=True)  6.45 us
  transfers between devices with their start and end apart: 10, of which 4 were waited for; matrix products, arithmetic and copies ran while one was open for 25% of the time, Pallas kernels for 0%

commit v1 on v0

--- a/solution.py
+++ b/solution.py
@@ -43,7 +43,6 @@
     pair_count = responses.shape[0]
     block_count = observed.shape[0]
     group_size = lax.axis_size("vox")
-    capacity = max(2, 2 * pair_count // group_size)
     latent = mean_field[None] + deviations
     padded = with_halo(latent, (("vox", 1), ("star", 2)), 1)
     smoothed = jnp.zeros(latent.shape, jnp.float32)
@@ -59,52 +58,20 @@
     density_b = density.astype(jnp.bfloat16).reshape(samples, width_x * width_y, length)
     picked = jnp.take(density_b, pair_line, axis=1)
     contribution = jnp.einsum("pij,spj->psi", responses, picked, preferred_element_type=jnp.float32)
-    owner = pair_owner[:, 0]
-    owner_onehot = (owner[:, None] == jnp.arange(group_size, dtype=jnp.int32)[None, :]).astype(
-        jnp.int32
-    )
-    position = jnp.sum((jnp.cumsum(owner_onehot, axis=0) - owner_onehot) * owner_onehot, axis=1)
-    slot_id = owner * capacity + position
-    slot_onehot = slot_id[:, None] == jnp.arange(group_size * capacity, dtype=jnp.int32)[None, :]
-    slot_float = slot_onehot.astype(jnp.float32)
-    outgoing = jnp.einsum("pq,psi->qsi", slot_float, contribution, precision=HIGH).reshape(
-        group_size, capacity, samples, length
-    )
-    slot_star = (
-        jnp.sum(slot_onehot.astype(jnp.int32) * (pair_star + 1)[:, None], axis=0) - 1
-    ).reshape(group_size, capacity)
-    arrived, arrived_star = (
-        lax.all_to_all(outgoing, "vox", split_axis=0, concat_axis=0, tiled=True),
-        lax.all_to_all(slot_star, "vox", split_axis=0, concat_axis=0, tiled=True),
-    )
-    star_onehot = (
-        arrived_star.reshape(-1)[:, None] == jnp.arange(block_count, dtype=jnp.int32)[None, :]
+    star_count = observed.shape[0]
+    group_blocks = group_size * star_count
+    target = pair_owner[:, 0] * star_count + pair_star
+    target_onehot = (
+        target[:, None] == jnp.arange(group_blocks, dtype=jnp.int32)[None, :]
     ).astype(jnp.float32)
-    extinction = jnp.einsum(
-        "qb,qsi->bsi",
-        star_onehot,
-        arrived.reshape(group_size * capacity, samples, length),
-        precision=HIGH,
-    )
-    misfit = inv_var[:, None, :] * (extinction - observed[:, None, :])
+    partial = jnp.einsum("pb,psi->bsi", target_onehot, contribution, precision=HIGH)
+    extinction = lax.psum(partial, "vox")
+    table = lax.all_gather(jnp.stack([observed, inv_var]), "vox", axis=1, tiled=True)
+    misfit = table[1][:, None, :] * (extinction - table[0][:, None, :])
     misfit_b = misfit.astype(jnp.bfloat16)
-    returning = jnp.einsum(
-        "qb,bsi->qsi", star_onehot, misfit_b.astype(jnp.float32), precision=HIGH
-    ).astype(jnp.bfloat16)
-    returned = lax.all_to_all(
-        returning.reshape(group_size, capacity, samples, length),
-        "vox",
-        split_axis=0,
-        concat_axis=0,
-        tiled=True,
-    )
-    pair_misfit = jnp.einsum(
-        "pq,qsi->psi",
-        slot_float,
-        returned.reshape(group_size * capacity, samples, length).astype(jnp.float32),
-        precision=HIGH,
-    ).astype(jnp.bfloat16)
-    residual_mean = jnp.mean(misfit, axis=1)
+    own = lax.dynamic_slice_in_dim(misfit, lax.axis_index("vox") * star_count, star_count, axis=0)
+    residual_mean = jnp.mean(own, axis=1)
+    pair_misfit = jnp.take(misfit_b, target, axis=0)
     pair_adjoint = jnp.einsum(
         "pij,psi->psj", responses, pair_misfit, preferred_element_type=jnp.float32
     )

time: 105 us -> 186 us (1.77)
  waiting for transfers between devices: 17.7 us -> 93.3 us
  starting transfers between devices: 34.4 us -> 20.5 us
  between operations: 0.93 us -> 14.3 us
  blocking collectives: 11.9 us -> 22.4 us
  matrix products: 14.4 us -> 11.4 us
    psum x0 -> x1, waiting for transfers between devices: none -> 86.4 us  [per_device(): extinction = lax.psum(partial, 'vox')]
    all_gather x0 -> x1, blocking collectives: none -> 22.4 us  [per_device(): lax.all_gather(jnp.stack([observed, inv_var]), 'vox', axis=1, tiled=True)]
    all_to_all x2 -> x0, starting transfers between devices: 13.9 us -> none  [the longest x1 7.43 us: per_device(): lax.all_to_all(outgoing, 'vox', split_axis=0, concat_axis=0, tiled=True)]
    all_to_all x1 -> x0, blocking collectives: 11.9 us -> none  [per_device(): lax.all_to_all(returning.reshape(group_size, capacity, samples, length),...]
    all_to_all x2 -> x0, waiting for transfers between devices: 10.6 us -> none  [the longest x1 10.6 us: per_device(): lax.all_to_all(outgoing, 'vox', split_axis=0, concat_axis=0, tiled=True)]
  transfers between devices with their start and end apart: 10 -> 9, of which waited for: 4 -> 4; matrix products, arithmetic and copies ran while one was open for 25% -> 3% of each run, Pallas kernels for 0% -> 0%
where the time goes in v1:
time: 186 us; the launch traced here: 182 us
  waiting for transfers between devices  93.3 us (50%)
  blocking collectives  22.4 us (12%)
  starting transfers between devices  20.5 us (11%)
  other arithmetic  16.3 us (9%)
  between operations  14.3 us (8%)
  matrix products  11.4 us (6%)
  local copies, waits for them, and re-layouts  4.09 us (2%)
    psum x1, waiting for transfers between devices, per_device(): extinction = lax.psum(partial, 'vox')  86.4 us
    all_gather x1, blocking collectives, per_device(): lax.all_gather(jnp.stack([observed, inv_var]), 'vox', axis=1, tiled=True)  22.4 us
    ppermute x4, starting transfers between devices, with_halo(): lax.ppermute(tail, axis, [(i, (i + 1) % count) for i in range(ends)])  13.7 us
    reduce_sum x1, other arithmetic, per_device(): gradient = jnp.mean(grad_latent + latent, axis=0)  6.87 us
    dot_general x1, matrix products, per_device(): jnp.einsum('sxyw,zw->sxyz', smoothed, vertical_mix, precision=HIGH)  6.84 us
    ppermute x4, starting transfers between devices, with_halo(): lax.ppermute(head, axis, [((i + 1) % count, i) for i in range(ends)])  6.74 us
    ppermute x4, waiting for transfers between devices, with_halo(): lax.ppermute(head, axis, [((i + 1) % count, i) for i in range(ends)])  6.7 us
  transfers between devices with their start and end apart: 9, of which 4 were waited for; matrix products, arithmetic and copies ran while one was open for 3% of the time, Pallas kernels for 0%

profile of v1, /device:TPU:1, one launch (start us, length us, event | category | flops | bytes accessed | tf_op | source)
XLA Modules:
  0.0 182.3 jit_solution(6022717707829478496)
XLA Ops:
  7.2 1.1 broadcast_add_fusion
  8.4 4.5 %collective-permute-start = (f32[4,1,64,128]{3,2,1,0:T(8,128)S(1)}, f32[4,1,64,128]{3,2,1,0:T(8,128)S(1)}, u32[]{:S(2)}, u32[]{:S(2)}) collective-permute-start(f32[4,1,64,128]{3,2,1,0:T(8,128)S(1)} %get-tuple-element.16), channel_id=1, source_target_pairs={{0,2},{2,4},{4,6},{6,8},{8,10},{10,12},{12,14},{14,16},{16,18},{18... | collective-permute-start | bytes 393224 | tf_op jit(solution)/shard_map/ppermute | solution.py:17
  12.9 1.9 %collective-permute-start.1 = (f32[4,1,64,128]{3,2,1,0:T(8,128)S(1)}, f32[4,1,64,128]{3,2,1,0:T(8,128)S(1)}, u32[]{:S(2)}, u32[]{:S(2)}) collective-permute-start(f32[4,1,64,128]{3,2,1,0:T(8,128)S(1)} %get-tuple-element.17), channel_id=1, source_target_pairs={{2,0},{4,2},{6,4},{8,6},{10,8},{12,10},{14,12},{16,14},{18,16},{20... | collective-permute-start | bytes 393224 | tf_op jit(solution)/shard_map/ppermute | solution.py:19
  16.2 22.4 %all_gather.3 = f32[2,128,128]{2,1,0:T(8,128)S(1)} all-gather(f32[2,8,128]{2,1,0:T(8,128)S(1)} %pad_maximum_fusion.12), channel_id=1, replica_groups=mesh['vox'=16,'star'=2] {'vox'}, dimensions={1}, use_global_device_ids=true | all-gather | bytes 139264 | tf_op jit(solution)/shard_map/all_gather | solution.py:69
  40.0 1.7 fusion.71
  41.7 3.1 %collective-permute-start.2 = (f32[4,4,1,128]{3,2,1,0:T(1,128)S(1)}, f32[4,4,1,128]{3,2,1,0:T(1,128)S(1)}, u32[]{:S(2)}, u32[]{:S(2)}) collective-permute-start(f32[4,4,1,128]{3,2,1,0:T(1,128)S(1)} %get-tuple-element.12), channel_id=1, source_target_pairs={{0,1},{2,3},{4,5},{6,7},{8,9},{10,11},{12,13},{14,15},{16,17},{18,... | collective-permute-start | bytes 24584 | tf_op jit(solution)/shard_map/ppermute | solution.py:17
  44.9 1.3 collective-permute-start.3
  46.2 3.1 %collective-permute-done.3 = f32[4,4,1,128]{3,2,1,0:T(1,128)S(1)} collective-permute-done((f32[4,4,1,128]{3,2,1,0:T(1,128)S(1)}, f32[4,4,1,128]{3,2,1,0:T(1,128)S(1)}, u32[]{:S(2)}, u32[]{:S(2)}) %collective-permute-start.3) | collective-permute-done | bytes 8224 | tf_op jit(solution)/shard_map/ppermute | solution.py:19
  49.4 6.8 %fusion.72 = (bf16[4,2,64,128]{3,2,1,0:T(8,128)(2,1)S(1)}, f32[4,2,64,128]{3,2,1,0:T(8,128)}) fusion(f32[128]{0:T(128)S(1)} %copy-done.5, f32[128,128]{1,0:T(8,128)S(1)} %copy-done.2, f32[4,4,65,128]{3,2,1,0:T(8,128)S(1)} %get-tuple-element.11, f32[4,1,64,128]{3,2,1,0:T(8,128)S(1)} %collective-permute-done.1, f32[4,2,64,128]{3,2,1,0:T(8,128)S(1)} %broadcast_add_fusion, ...), kind=kOutput, calls=%fused_computation.109 | convolution fusion | flops 102039552 | bytes 2556452 | tf_op jit(solution)/shard_map/sxyw,zw->sxyz/dot_general | solution.py:56
  57.0 1.8 fusion.48
  58.8 1.1 fusion.37
  59.9 86.4 %all-reduce.2.cloned.1.call-done = f32[128,4,128]{2,0,1:T(8,128)} async-done(((f32[128,4,128]{2,0,1:T(8,128)}), f32[128,4,128]{2,0,1:T(8,128)}) %all-reduce.2.cloned.1.call-update) | async-done | bytes 262160 | tf_op jit(solution)/shard_map/psum | solution.py:68
  146.3 1.7 fusion.68
  148.8 1.0 fusion.51
  150.6 0.7 fusion.69
  151.3 2.1 %collective-permute-start.4 = (f32[4,1,64,128]{3,2,1,0:T(8,128)}, f32[4,1,64,128]{3,2,1,0:T(8,128)S(1)}, u32[]{:S(2)}, u32[]{:S(2)}) collective-permute-start(f32[4,1,64,128]{3,2,1,0:T(8,128)} %get-tuple-element.14), channel_id=1, source_target_pairs={{0,2},{2,4},{4,6},{6,8},{8,10},{10,12},{12,14},{14,16},{16,18},{18... | collective-permute-start | bytes 393224 | tf_op jit(solution)/shard_map/ppermute | solution.py:17
  153.4 2.2 %collective-permute-start.5 = (f32[4,1,64,128]{3,2,1,0:T(8,128)}, f32[4,1,64,128]{3,2,1,0:T(8,128)}, u32[]{:S(2)}, u32[]{:S(2)}) collective-permute-start(f32[4,1,64,128]{3,2,1,0:T(8,128)} %get-tuple-element.15), channel_id=1, source_target_pairs={{2,0},{4,2},{6,4},{8,6},{10,8},{12,10},{14,12},{16,14},{18,16},{20... | collective-permute-start | bytes 393224 | tf_op jit(solution)/shard_map/ppermute | solution.py:19
  155.7 0.7 dynamic-slice_reduce_fusion
  156.4 3.6 %collective-permute-done.5 = f32[4,1,64,128]{3,2,1,0:T(8,128)} collective-permute-done((f32[4,1,64,128]{3,2,1,0:T(8,128)}, f32[4,1,64,128]{3,2,1,0:T(8,128)}, u32[]{:S(2)}, u32[]{:S(2)}) %collective-permute-start.5) | collective-permute-done | bytes 131104 | tf_op jit(solution)/shard_map/ppermute | solution.py:19
  160.0 0.7 pad_maximum_fusion.8
  160.8 1.3 collective-permute-start.6
  162.1 4.0 %collective-permute-start.7 = (f32[4,4,1,128]{3,2,1,0:T(1,128)S(1)}, f32[4,4,1,128]{3,2,1,0:T(1,128)S(1)}, u32[]{:S(2)}, u32[]{:S(2)}) collective-permute-start(f32[4,4,1,128]{3,2,1,0:T(1,128)S(1)} %get-tuple-element.9), channel_id=1, source_target_pairs={{0,1},{2,3},{4,5},{6,7},{8,9},{10,11},{12,13},{14,15},{16,17},{18,... | collective-permute-start | bytes 24584 | tf_op jit(solution)/shard_map/ppermute | solution.py:17
  166.9 1.1 pad_maximum_fusion.1
  167.9 6.9 %fusion.3 = f32[2,64,128]{2,1,0:T(8,128)S(1)} fusion(f32[4,4,65,128]{3,2,1,0:T(8,128)S(1)} %get-tuple-element.7, f32[4,2,64,128]{3,2,1,0:T(8,128)S(1)} %fusion.32, f32[4,1,64,128]{3,2,1,0:T(8,128)S(1)} %collective-permute-done.4, f32[4,4,65,128]{3,2,1,0:T(8,128)S(1)} %get-tuple-element.6, f32[4,1,64,128]{3,2,1,0:T(8,128)} %collective-permute-done.5, ...), kind=kLoop, calls=%fused_computation.11 | loop fusion | flops 1425408 | bytes 2490404 | tf_op jit(solution)/shard_map/reduce_sum | solution.py:100
  (39 shorter events, 6.7 us)
Async XLA Ops:
  7.2 49.9 %copy-start = (bf16[96,128,128]{2,1,0:T(8,128)(2,1)S(1)}, bf16[96,128,128]{2,1,0:T(8,128)(2,1)}, u32[]{:S(2)}) copy-start(bf16[96,128,128]{2,1,0:T(8,128)(2,1)} %param.16) | copy-start | bytes 9437188
  7.2 42.2 %copy-start.2 = (f32[128,128]{1,0:T(8,128)S(1)}, f32[128,128]{1,0:T(8,128)}, u32[]{:S(2)}) copy-start(f32[128,128]{1,0:T(8,128)} %param.14) | copy-start | bytes 196612
  7.2 42.2 %copy-start.5 = (f32[128]{0:T(128)S(1)}, f32[128]{0:T(128)}, u32[]{:S(2)}) copy-start(f32[128]{0:T(128)} %param.15) | copy-start | bytes 1540
  7.2 139.1 %all-reduce.2.cloned.1.call-start = ((), (), s32[]{:S(2)}) async-start(), calls=%async_computation | async-start | bytes 524288 | tf_op jit(solution)/shard_map/psum | solution.py:68
  8.4 33.3 %collective-permute-start = (f32[4,1,64,128]{3,2,1,0:T(8,128)S(1)}, f32[4,1,64,128]{3,2,1,0:T(8,128)S(1)}, u32[]{:S(2)}, u32[]{:S(2)}) collective-permute-start(f32[4,1,64,128]{3,2,1,0:T(8,128)S(1)} %get-tuple-element.16), channel_id=1, source_target_pairs={{0,2},{2,4},{4,6},{6,8},{8,10},{10,12},{12,14},{14,16},{16,18},{18... | collective-permute-start | bytes 393224 | tf_op jit(solution)/shard_map/ppermute | solution.py:17
  12.9 28.8 %collective-permute-start.1 = (f32[4,1,64,128]{3,2,1,0:T(8,128)S(1)}, f32[4,1,64,128]{3,2,1,0:T(8,128)S(1)}, u32[]{:S(2)}, u32[]{:S(2)}) collective-permute-start(f32[4,1,64,128]{3,2,1,0:T(8,128)S(1)} %get-tuple-element.17), channel_id=1, source_target_pairs={{2,0},{4,2},{6,4},{8,6},{10,8},{12,10},{14,12},{16,14},{18,16},{20... | collective-permute-start | bytes 393224 | tf_op jit(solution)/shard_map/ppermute | solution.py:19
  41.7 4.4 %collective-permute-start.2 = (f32[4,4,1,128]{3,2,1,0:T(1,128)S(1)}, f32[4,4,1,128]{3,2,1,0:T(1,128)S(1)}, u32[]{:S(2)}, u32[]{:S(2)}) collective-permute-start(f32[4,4,1,128]{3,2,1,0:T(1,128)S(1)} %get-tuple-element.12), channel_id=1, source_target_pairs={{0,1},{2,3},{4,5},{6,7},{8,9},{10,11},{12,13},{14,15},{16,17},{18,... | collective-permute-start | bytes 24584 | tf_op jit(solution)/shard_map/ppermute | solution.py:17
  44.9 4.4 %collective-permute-start.3 = (f32[4,4,1,128]{3,2,1,0:T(1,128)S(1)}, f32[4,4,1,128]{3,2,1,0:T(1,128)S(1)}, u32[]{:S(2)}, u32[]{:S(2)}) collective-permute-start(f32[4,4,1,128]{3,2,1,0:T(1,128)S(1)} %get-tuple-element.13), channel_id=1, source_target_pairs={{1,0},{3,2},{5,4},{7,6},{9,8},{11,10},{13,12},{15,14},{17,16},{19,... | collective-permute-start | bytes 24584 | tf_op jit(solution)/shard_map/ppermute | solution.py:19
  58.8 91.0 %copy-start.4 = (s32[96]{0:T(128)S(1)}, s32[96]{0:T(128)}, u32[]{:S(2)}) copy-start(s32[96]{0:T(128)} %param.17) | copy-start | bytes 1156
  58.8 91.4 %copy-start.3 = (f32[128,128]{1,0:T(8,128)S(1)}, f32[128,128]{1,0:T(8,128)}, u32[]{:S(2)}) copy-start(f32[128,128]{1,0:T(8,128)} %param.14) | copy-start | bytes 196612
  148.8 1.4 copy-start.1
  151.3 5.1 %collective-permute-start.4 = (f32[4,1,64,128]{3,2,1,0:T(8,128)}, f32[4,1,64,128]{3,2,1,0:T(8,128)S(1)}, u32[]{:S(2)}, u32[]{:S(2)}) collective-permute-start(f32[4,1,64,128]{3,2,1,0:T(8,128)} %get-tuple-element.14), channel_id=1, source_target_pairs={{0,2},{2,4},{4,6},{6,8},{8,10},{10,12},{12,14},{14,16},{16,18},{18... | collective-permute-start | bytes 393224 | tf_op jit(solution)/shard_map/ppermute | solution.py:17
  153.4 6.6 %collective-permute-start.5 = (f32[4,1,64,128]{3,2,1,0:T(8,128)}, f32[4,1,64,128]{3,2,1,0:T(8,128)}, u32[]{:S(2)}, u32[]{:S(2)}) collective-permute-start(f32[4,1,64,128]{3,2,1,0:T(8,128)} %get-tuple-element.15), channel_id=1, source_target_pairs={{2,0},{4,2},{6,4},{8,6},{10,8},{12,10},{14,12},{16,14},{18,16},{20... | collective-permute-start | bytes 393224 | tf_op jit(solution)/shard_map/ppermute | solution.py:19
  160.8 5.9 %collective-permute-start.6 = (f32[4,4,1,128]{3,2,1,0:T(1,128)S(1)}, f32[4,4,1,128]{3,2,1,0:T(1,128)S(1)}, u32[]{:S(2)}, u32[]{:S(2)}) collective-permute-start(f32[4,4,1,128]{3,2,1,0:T(1,128)S(1)} %get-tuple-element.8), channel_id=1, source_target_pairs={{1,0},{3,2},{5,4},{7,6},{9,8},{11,10},{13,12},{15,14},{17,16},{19,... | collective-permute-start | bytes 24584 | tf_op jit(solution)/shard_map/ppermute | solution.py:19
  162.1 4.8 %collective-permute-start.7 = (f32[4,4,1,128]{3,2,1,0:T(1,128)S(1)}, f32[4,4,1,128]{3,2,1,0:T(1,128)S(1)}, u32[]{:S(2)}, u32[]{:S(2)}) collective-permute-start(f32[4,4,1,128]{3,2,1,0:T(1,128)S(1)} %get-tuple-element.9), channel_id=1, source_target_pairs={{0,1},{2,3},{4,5},{6,7},{8,9},{10,11},{12,13},{14,15},{16,17},{18,... | collective-permute-start | bytes 24584 | tf_op jit(solution)/shard_map/ppermute | solution.py:17
Sparse Core Ops, SparseCore 0:
  60.0 86.2 all-reduce.1

commit v2 on v1

--- a/solution.py
+++ b/solution.py
@@ -65,12 +65,21 @@
         target[:, None] == jnp.arange(group_blocks, dtype=jnp.int32)[None, :]
     ).astype(jnp.float32)
     partial = jnp.einsum("pb,psi->bsi", target_onehot, contribution, precision=HIGH)
-    extinction = lax.psum(partial, "vox")
-    table = lax.all_gather(jnp.stack([observed, inv_var]), "vox", axis=1, tiled=True)
-    misfit = table[1][:, None, :] * (extinction - table[0][:, None, :])
+    arrived = lax.all_to_all(
+        partial.reshape(group_size, star_count, samples, length),
+        "vox",
+        split_axis=0,
+        concat_axis=0,
+        tiled=True,
+    )
+    extinction = jnp.sum(arrived, axis=0)
+    misfit = inv_var[:, None, :] * (extinction - observed[:, None, :])
+    residual_mean = jnp.mean(misfit, axis=1)
     misfit_b = misfit.astype(jnp.bfloat16)
-    own = lax.dynamic_slice_in_dim(misfit, lax.axis_index("vox") * star_count, star_count, axis=0)
-    residual_mean = jnp.mean(own, axis=1)
+    spread = jnp.broadcast_to(misfit_b[None], (group_size,) + misfit_b.shape)
+    misfit_b = lax.all_to_all(spread, "vox", split_axis=0, concat_axis=0, tiled=True).reshape(
+        group_blocks, samples, length
+    )
     pair_misfit = jnp.take(misfit_b, target, axis=0)
     pair_adjoint = jnp.einsum(
         "pij,psi->psj", responses, pair_misfit, preferred_element_type=jnp.float32

time: 186 us -> 82.9 us (0.45); the launches traced: 182 us -> 81.8 us
  waiting for transfers between devices: 93.3 us -> 14.8 us
  between operations: 14.3 us -> 0.96 us
  other arithmetic: 16.3 us -> 10.4 us
  blocking collectives: 22.4 us -> 16.5 us
  starting transfers between devices: 20.5 us -> 24.5 us
    psum x1 -> x0, waiting for transfers between devices: 86.4 us -> none  [per_device(): extinction = lax.psum(partial, 'vox')]
    all_gather x1 -> x0, blocking collectives: 22.4 us -> none  [per_device(): lax.all_gather(jnp.stack([observed, inv_var]), 'vox', axis=1, tiled=True)]
    all_to_all x0 -> x1, blocking collectives: none -> 16.5 us  [per_device(): lax.all_to_all(partial.reshape(group_size, star_count, samples, length),...]
    all_to_all x0 -> x1, waiting for transfers between devices: none -> 6.93 us  [per_device(): lax.all_to_all(spread, 'vox', split_axis=0, concat_axis=0, tiled=True)]
    all_to_all x0 -> x1, starting transfers between devices: none -> 3.95 us  [per_device(): lax.all_to_all(spread, 'vox', split_axis=0, concat_axis=0, tiled=True)]
  transfers between devices with their start and end apart: 9 -> 9, of which waited for: 4 -> 5; matrix products, arithmetic and copies ran while one was open for 3% -> 5% of each run, Pallas kernels for 0% -> 0%
where the time goes in v2:
time: 82.9 us; the launch traced here: 81.8 us
  starting transfers between devices  24.5 us (30%)
  blocking collectives  16.5 us (20%)
  waiting for transfers between devices  14.8 us (18%)
  matrix products  10.7 us (13%)
  other arithmetic  10.4 us (13%)
  local copies, waits for them, and re-layouts  3.98 us (5%)
  between operations  0.96 us (1%)
    all_to_all x1, blocking collectives, per_device(): lax.all_to_all(partial.reshape(group_size, star_count, samples, length),...  16.5 us
    ppermute x4, starting transfers between devices, with_halo(): lax.ppermute(tail, axis, [(i, (i + 1) % count) for i in range(ends)])  13.7 us
    ppermute x4, waiting for transfers between devices, with_halo(): lax.ppermute(head, axis, [((i + 1) % count, i) for i in range(ends)])  7.69 us
    all_to_all x1, waiting for transfers between devices, per_device(): lax.all_to_all(spread, 'vox', split_axis=0, concat_axis=0, tiled=True)  6.93 us
    ppermute x4, starting transfers between devices, with_halo(): lax.ppermute(head, axis, [((i + 1) % count, i) for i in range(ends)])  6.83 us
    dot_general x1, matrix products, per_device(): jnp.einsum('sxyw,zw->sxyz', smoothed, vertical_mix, precision=HIGH)  6.78 us
    reduce_sum x1, other arithmetic, per_device(): gradient = jnp.mean(grad_latent + latent, axis=0)  5.77 us
    all_to_all x1, starting transfers between devices, per_device(): lax.all_to_all(spread, 'vox', split_axis=0, concat_axis=0, tiled=True)  3.95 us
  transfers between devices with their start and end apart: 9, of which 5 were waited for; matrix products, arithmetic and copies ran while one was open for 5% of the time, Pallas kernels for 0%

profile of v2, /device:TPU:1, one launch (start us, length us, event | category | flops | bytes accessed | tf_op | source)
XLA Modules:
  0.0 81.8 jit_solution(18403460834928742368)
XLA Ops:
  0.7 1.1 %broadcast_add_fusion = f32[4,2,64,128]{3,2,1,0:T(8,128)S(1)} fusion(f32[4,2,64,128]{3,2,1,0:T(8,128)} %param.12, f32[2,64,128]{2,1,0:T(8,128)} %param.11), kind=kLoop, calls=%fused_computation.63 | loop fusion | flops 65536 | bytes 589824 | tf_op jit(solution)/shard_map/add | solution.py:46
  1.8 4.5 %collective-permute-start = (f32[4,1,64,128]{3,2,1,0:T(8,128)S(1)}, f32[4,1,64,128]{3,2,1,0:T(8,128)S(1)}, u32[]{:S(2)}, u32[]{:S(2)}) collective-permute-start(f32[4,1,64,128]{3,2,1,0:T(8,128)S(1)} %get-tuple-element.14), channel_id=1, source_target_pairs={{0,2},{2,4},{4,6},{6,8},{8,10},{10,12},{12,14},{14,16},{16,18},{18... | collective-permute-start | bytes 393224 | tf_op jit(solution)/shard_map/ppermute | solution.py:17
  6.4 1.9 %collective-permute-start.1 = (f32[4,1,64,128]{3,2,1,0:T(8,128)S(1)}, f32[4,1,64,128]{3,2,1,0:T(8,128)S(1)}, u32[]{:S(2)}, u32[]{:S(2)}) collective-permute-start(f32[4,1,64,128]{3,2,1,0:T(8,128)S(1)} %get-tuple-element.15), channel_id=1, source_target_pairs={{2,0},{4,2},{6,4},{8,6},{10,8},{12,10},{14,12},{16,14},{18,16},{20... | collective-permute-start | bytes 393224 | tf_op jit(solution)/shard_map/ppermute | solution.py:19
  9.0 0.7 compare_and_fusion.1
  10.3 1.7 %fusion.71 = (f32[1,1]{1,0:T(1,128)}, f32[1,1]{1,0:T(1,128)}, f32[1,1]{1,0:T(1,128)}, f32[1,1]{1,0:T(1,128)}, f32[1,1]{1,0:T(1,128)}, /*index=5*/f32[1,1]{1,0:T(...) fusion(f32[3,3]{1,0:T(4,128)} %param.13), kind=kLoop, calls=%fused_computation.105 | loop fusion | bytes 72 | tf_op jit(solution)/shard_map/slice | solution.py:101
  12.0 0.7 collective-permute-done.1
  12.7 3.1 %collective-permute-start.2 = (f32[4,4,1,128]{3,2,1,0:T(1,128)S(1)}, f32[4,4,1,128]{3,2,1,0:T(1,128)S(1)}, u32[]{:S(2)}, u32[]{:S(2)}) collective-permute-start(f32[4,4,1,128]{3,2,1,0:T(1,128)S(1)} %get-tuple-element.10), channel_id=1, source_target_pairs={{0,1},{2,3},{4,5},{6,7},{8,9},{10,11},{12,13},{14,15},{16,17},{18,... | collective-permute-start | bytes 24584 | tf_op jit(solution)/shard_map/ppermute | solution.py:17
  15.8 1.3 %collective-permute-start.3 = (f32[4,4,1,128]{3,2,1,0:T(1,128)S(1)}, f32[4,4,1,128]{3,2,1,0:T(1,128)S(1)}, u32[]{:S(2)}, u32[]{:S(2)}) collective-permute-start(f32[4,4,1,128]{3,2,1,0:T(1,128)S(1)} %get-tuple-element.11), channel_id=1, source_target_pairs={{1,0},{3,2},{5,4},{7,6},{9,8},{11,10},{13,12},{15,14},{17,16},{19,... | collective-permute-start | bytes 24584 | tf_op jit(solution)/shard_map/ppermute | solution.py:19
  17.1 3.1 %collective-permute-done.3 = f32[4,4,1,128]{3,2,1,0:T(1,128)S(1)} collective-permute-done((f32[4,4,1,128]{3,2,1,0:T(1,128)S(1)}, f32[4,4,1,128]{3,2,1,0:T(1,128)S(1)}, u32[]{:S(2)}, u32[]{:S(2)}) %collective-permute-start.3) | collective-permute-done | bytes 8224 | tf_op jit(solution)/shard_map/ppermute | solution.py:19
  20.3 6.8 %fusion.72 = (bf16[4,2,64,128]{3,2,1,0:T(8,128)(2,1)S(1)}, f32[4,2,64,128]{3,2,1,0:T(8,128)}) fusion(f32[128]{0:T(128)S(1)} %copy-done.8, f32[128,128]{1,0:T(8,128)S(1)} %copy-done.4, f32[4,4,65,128]{3,2,1,0:T(8,128)S(1)} %get-tuple-element.9, f32[4,1,64,128]{3,2,1,0:T(8,128)S(1)} %collective-permute-done.1, f32[4,2,64,128]{3,2,1,0:T(8,128)S(1)} %broadcast_add_fusion, ...), kind=kOutput, calls=%fused_computation.106 | convolution fusion | flops 102039552 | bytes 2556452 | tf_op jit(solution)/shard_map/sxyw,zw->sxyz/dot_general | solution.py:56
  27.2 0.7 gather_fusion
  27.9 1.8 %fusion.47 = f32[96,4,128]{2,1,0:T(4,128)S(1)} fusion(bf16[96,128,128]{2,1,0:T(8,128)(2,1)S(1)} %copy-done, bf16[96,4,128]{2,1,0:T(4,128)(2,1)S(1)} %gather_fusion, pred[96]{0:T(512)(128)(4,1)S(1)} %compare_and_fusion), kind=kOutput, calls=%fused_computation.65 | convolution fusion | flops 12632064 | bytes 3440736 | tf_op jit(solution)/shard_map/pij,spj->psi/dot_general | solution.py:60
  30.1 16.5 %all_to_all.10 = f32[16,8,4,128]{3,1,2,0:T(8,128)S(1)} all-to-all(f32[16,8,4,128]{3,1,2,0:T(8,128)S(1)} %copy.16), channel_id=1, replica_groups=mesh['vox'=16,'star'=2] {'vox'}, dimensions={0} | all-to-all | bytes 524288 | tf_op jit(solution)/shard_map/all_to_all | solution.py:68
  46.7 0.7 broadcast_in_dim.42
  47.4 4.0 %all-to-all-start.1 = ((bf16[16,8,4,128]{3,2,1,0:T(4,128)(2,1)}), bf16[16,8,4,128]{3,2,1,0:T(4,128)(2,1)S(1)}, u32[]{:S(2)}, u32[]{:S(2)}) async-start(bf16[16,8,4,128]{3,2,1,0:T(4,128)(2,1)} %broadcast_in_dim.42), calls=%async_computation.1 | async-start | bytes 262144 | tf_op jit(solution)/shard_map/all_to_all | solution.py:80
  51.4 6.9 %all-to-all-done.1 = bf16[16,8,4,128]{3,2,1,0:T(4,128)(2,1)S(1)} async-done(((bf16[16,8,4,128]{3,2,1,0:T(4,128)(2,1)}), bf16[16,8,4,128]{3,2,1,0:T(4,128)(2,1)S(1)}, u32[]{:S(2)}, u32[]{:S(2)}) %all-to-all-start.1) | async-done | bytes 131104 | tf_op jit(solution)/shard_map/all_to_all | solution.py:80
  58.3 0.7 gather_fusion.1
  59.0 1.0 %fusion.50 = f32[96,4,128]{2,1,0:T(4,128)S(1)} fusion(bf16[96,128,128]{2,1,0:T(8,128)(2,1)S(1)} %copy-done, bf16[96,4,128]{2,1,0:T(4,128)(2,1)S(1)} %gather_fusion.1, pred[96]{0:T(512)(128)(4,1)S(1)} %get-tuple-element.2), kind=kOutput, calls=%fused_computation.68 | convolution fusion | flops 12632064 | bytes 3440736 | tf_op jit(solution)/shard_map/pij,psi->psj/dot_general | solution.py:84
  60.8 2.1 %collective-permute-start.4 = (f32[4,1,64,128]{3,2,1,0:T(8,128)S(1)}, f32[4,1,64,128]{3,2,1,0:T(8,128)S(1)}, u32[]{:S(2)}, u32[]{:S(2)}) collective-permute-start(f32[4,1,64,128]{3,2,1,0:T(8,128)S(1)} %get-tuple-element.12), channel_id=1, source_target_pairs={{0,2},{2,4},{4,6},{6,8},{8,10},{10,12},{12,14},{14,16},{16,18},{18... | collective-permute-start | bytes 393224 | tf_op jit(solution)/shard_map/ppermute | solution.py:17
  62.9 2.3 %collective-permute-start.5 = (f32[4,1,64,128]{3,2,1,0:T(8,128)S(1)}, f32[4,1,64,128]{3,2,1,0:T(8,128)S(1)}, u32[]{:S(2)}, u32[]{:S(2)}) collective-permute-start(f32[4,1,64,128]{3,2,1,0:T(8,128)S(1)} %get-tuple-element.13), channel_id=1, source_target_pairs={{2,0},{4,2},{6,4},{8,6},{10,8},{12,10},{14,12},{16,14},{18,16},{20... | collective-permute-start | bytes 393224 | tf_op jit(solution)/shard_map/ppermute | solution.py:19
  65.2 3.9 %collective-permute-done.5 = f32[4,1,64,128]{3,2,1,0:T(8,128)S(1)} collective-permute-done((f32[4,1,64,128]{3,2,1,0:T(8,128)S(1)}, f32[4,1,64,128]{3,2,1,0:T(8,128)S(1)}, u32[]{:S(2)}, u32[]{:S(2)}) %collective-permute-start.5) | collective-permute-done | bytes 131104 | tf_op jit(solution)/shard_map/ppermute | solution.py:19
  69.2 1.3 %collective-permute-start.6 = (f32[4,4,1,128]{3,2,1,0:T(1,128)S(1)}, f32[4,4,1,128]{3,2,1,0:T(1,128)S(1)}, u32[]{:S(2)}, u32[]{:S(2)}) collective-permute-start(f32[4,4,1,128]{3,2,1,0:T(1,128)S(1)} %get-tuple-element.6), channel_id=1, source_target_pairs={{1,0},{3,2},{5,4},{7,6},{9,8},{11,10},{13,12},{15,14},{17,16},{19,... | collective-permute-start | bytes 24584 | tf_op jit(solution)/shard_map/ppermute | solution.py:19
  70.5 4.0 %collective-permute-start.7 = (f32[4,4,1,128]{3,2,1,0:T(1,128)S(1)}, f32[4,4,1,128]{3,2,1,0:T(1,128)S(1)}, u32[]{:S(2)}, u32[]{:S(2)}) collective-permute-start(f32[4,4,1,128]{3,2,1,0:T(1,128)S(1)} %get-tuple-element.7), channel_id=1, source_target_pairs={{0,1},{2,3},{4,5},{6,7},{8,9},{10,11},{12,13},{14,15},{16,17},{18,... | collective-permute-start | bytes 24584 | tf_op jit(solution)/shard_map/ppermute | solution.py:17
  75.3 5.8 %fusion.3 = f32[2,64,128]{2,1,0:T(8,128)S(1)} fusion(f32[4,4,65,128]{3,2,1,0:T(8,128)S(1)} %get-tuple-element.5, f32[4,2,64,128]{3,2,1,0:T(8,128)S(1)} %fusion.32, f32[4,1,64,128]{3,2,1,0:T(8,128)S(1)} %collective-permute-done.4, f32[4,4,65,128]{3,2,1,0:T(8,128)S(1)} %get-tuple-element.4, f32[4,1,64,128]{3,2,1,0:T(8,128)S(1)} %collective-permute-done.5, ...), kind=kLoop, calls=%fused_computation.12 | loop fusion | flops 1425408 | bytes 2490404 | tf_op jit(solution)/shard_map/reduce_sum | solution.py:109
  (44 shorter events, 4.4 us)
Async XLA Ops:
  0.6 27.3 %copy-start = (bf16[96,128,128]{2,1,0:T(8,128)(2,1)S(1)}, bf16[96,128,128]{2,1,0:T(8,128)(2,1)}, u32[]{:S(2)}) copy-start(bf16[96,128,128]{2,1,0:T(8,128)(2,1)} %param.16) | copy-start | bytes 9437188
  0.6 19.6 %copy-start.4 = (f32[128,128]{1,0:T(8,128)S(1)}, f32[128,128]{1,0:T(8,128)}, u32[]{:S(2)}) copy-start(f32[128,128]{1,0:T(8,128)} %param.14) | copy-start | bytes 196612
  0.7 19.6 %copy-start.8 = (f32[128]{0:T(128)S(1)}, f32[128]{0:T(128)}, u32[]{:S(2)}) copy-start(f32[128]{0:T(128)} %param.15) | copy-start | bytes 1540
  1.8 10.2 %collective-permute-start = (f32[4,1,64,128]{3,2,1,0:T(8,128)S(1)}, f32[4,1,64,128]{3,2,1,0:T(8,128)S(1)}, u32[]{:S(2)}, u32[]{:S(2)}) collective-permute-start(f32[4,1,64,128]{3,2,1,0:T(8,128)S(1)} %get-tuple-element.14), channel_id=1, source_target_pairs={{0,2},{2,4},{4,6},{6,8},{8,10},{10,12},{12,14},{14,16},{16,18},{18... | collective-permute-start | bytes 393224 | tf_op jit(solution)/shard_map/ppermute | solution.py:17
  6.4 6.3 %collective-permute-start.1 = (f32[4,1,64,128]{3,2,1,0:T(8,128)S(1)}, f32[4,1,64,128]{3,2,1,0:T(8,128)S(1)}, u32[]{:S(2)}, u32[]{:S(2)}) collective-permute-start(f32[4,1,64,128]{3,2,1,0:T(8,128)S(1)} %get-tuple-element.15), channel_id=1, source_target_pairs={{2,0},{4,2},{6,4},{8,6},{10,8},{12,10},{14,12},{16,14},{18,16},{20... | collective-permute-start | bytes 393224 | tf_op jit(solution)/shard_map/ppermute | solution.py:19
  12.7 4.4 %collective-permute-start.2 = (f32[4,4,1,128]{3,2,1,0:T(1,128)S(1)}, f32[4,4,1,128]{3,2,1,0:T(1,128)S(1)}, u32[]{:S(2)}, u32[]{:S(2)}) collective-permute-start(f32[4,4,1,128]{3,2,1,0:T(1,128)S(1)} %get-tuple-element.10), channel_id=1, source_target_pairs={{0,1},{2,3},{4,5},{6,7},{8,9},{10,11},{12,13},{14,15},{16,17},{18,... | collective-permute-start | bytes 24584 | tf_op jit(solution)/shard_map/ppermute | solution.py:17
  15.8 4.4 %collective-permute-start.3 = (f32[4,4,1,128]{3,2,1,0:T(1,128)S(1)}, f32[4,4,1,128]{3,2,1,0:T(1,128)S(1)}, u32[]{:S(2)}, u32[]{:S(2)}) collective-permute-start(f32[4,4,1,128]{3,2,1,0:T(1,128)S(1)} %get-tuple-element.11), channel_id=1, source_target_pairs={{1,0},{3,2},{5,4},{7,6},{9,8},{11,10},{13,12},{15,14},{17,16},{19,... | collective-permute-start | bytes 24584 | tf_op jit(solution)/shard_map/ppermute | solution.py:19
  27.1 19.6 %copy-start.5 = (f32[8,128]{1,0:T(8,128)S(1)}, f32[8,128]{1,0:T(8,128)}, u32[]{:S(2)}) copy-start(f32[8,128]{1,0:T(8,128)} %param.20) | copy-start | bytes 12292
  27.1 19.6 %copy-start.6 = (f32[8,128]{1,0:T(8,128)S(1)}, f32[8,128]{1,0:T(8,128)}, u32[]{:S(2)}) copy-start(f32[8,128]{1,0:T(8,128)} %param.21) | copy-start | bytes 12292
  29.7 30.3 %copy-start.7 = (s32[96]{0:T(128)S(1)}, s32[96]{0:T(128)}, u32[]{:S(2)}) copy-start(s32[96]{0:T(128)} %param.17) | copy-start | bytes 1156
  47.4 10.9 %all-to-all-start.1 = ((bf16[16,8,4,128]{3,2,1,0:T(4,128)(2,1)}), bf16[16,8,4,128]{3,2,1,0:T(4,128)(2,1)S(1)}, u32[]{:S(2)}, u32[]{:S(2)}) async-start(bf16[16,8,4,128]{3,2,1,0:T(4,128)(2,1)} %broadcast_in_dim.42), calls=%async_computation.1 | async-start | bytes 262144 | tf_op jit(solution)/shard_map/all_to_all | solution.py:80
  59.0 1.4 %copy-start.3 = (f32[4,2,64,128]{3,2,1,0:T(8,128)S(1)}, f32[4,2,64,128]{3,2,1,0:T(8,128)}, u32[]{:S(2)}) copy-start(f32[4,2,64,128]{3,2,1,0:T(8,128)} %get-tuple-element.28) | copy-start | bytes 786436
  59.0 16.3 %copy-start.1 = (f32[4,2,64,128]{3,2,1,0:T(8,128)S(1)}, f32[4,2,64,128]{3,2,1,0:T(8,128)}, u32[]{:S(2)}) copy-start(f32[4,2,64,128]{3,2,1,0:T(8,128)} %param.12) | copy-start | bytes 786436
  59.0 16.3 %copy-start.2 = (f32[2,64,128]{2,1,0:T(8,128)S(1)}, f32[2,64,128]{2,1,0:T(8,128)}, u32[]{:S(2)}) copy-start(f32[2,64,128]{2,1,0:T(8,128)} %param.11) | copy-start | bytes 196612
  60.8 4.4 %collective-permute-start.4 = (f32[4,1,64,128]{3,2,1,0:T(8,128)S(1)}, f32[4,1,64,128]{3,2,1,0:T(8,128)S(1)}, u32[]{:S(2)}, u32[]{:S(2)}) collective-permute-start(f32[4,1,64,128]{3,2,1,0:T(8,128)S(1)} %get-tuple-element.12), channel_id=1, source_target_pairs={{0,2},{2,4},{4,6},{6,8},{8,10},{10,12},{12,14},{14,16},{16,18},{18... | collective-permute-start | bytes 393224 | tf_op jit(solution)/shard_map/ppermute | solution.py:17
  62.9 6.3 %collective-permute-start.5 = (f32[4,1,64,128]{3,2,1,0:T(8,128)S(1)}, f32[4,1,64,128]{3,2,1,0:T(8,128)S(1)}, u32[]{:S(2)}, u32[]{:S(2)}) collective-permute-start(f32[4,1,64,128]{3,2,1,0:T(8,128)S(1)} %get-tuple-element.13), channel_id=1, source_target_pairs={{2,0},{4,2},{6,4},{8,6},{10,8},{12,10},{14,12},{16,14},{18,16},{20... | collective-permute-start | bytes 393224 | tf_op jit(solution)/shard_map/ppermute | solution.py:19
  69.2 5.9 %collective-permute-start.6 = (f32[4,4,1,128]{3,2,1,0:T(1,128)S(1)}, f32[4,4,1,128]{3,2,1,0:T(1,128)S(1)}, u32[]{:S(2)}, u32[]{:S(2)}) collective-permute-start(f32[4,4,1,128]{3,2,1,0:T(1,128)S(1)} %get-tuple-element.6), channel_id=1, source_target_pairs={{1,0},{3,2},{5,4},{7,6},{9,8},{11,10},{13,12},{15,14},{17,16},{19,... | collective-permute-start | bytes 24584 | tf_op jit(solution)/shard_map/ppermute | solution.py:19
  70.5 4.8 %collective-permute-start.7 = (f32[4,4,1,128]{3,2,1,0:T(1,128)S(1)}, f32[4,4,1,128]{3,2,1,0:T(1,128)S(1)}, u32[]{:S(2)}, u32[]{:S(2)}) collective-permute-start(f32[4,4,1,128]{3,2,1,0:T(1,128)S(1)} %get-tuple-element.7), channel_id=1, source_target_pairs={{0,1},{2,3},{4,5},{6,7},{8,9},{10,11},{12,13},{14,15},{16,17},{18,... | collective-permute-start | bytes 24584 | tf_op jit(solution)/shard_map/ppermute | solution.py:17

commit v3 on v2

v3 whole, which is shorter than its diff:
```python
import jax
import jax.numpy as jnp
from jax import lax
from jax.sharding import PartitionSpec as P

HIGH = lax.Precision.HIGHEST


def exchange(cells, axis, dim):
    count = lax.axis_size(axis)
    size = cells.shape[dim]
    head = lax.slice_in_dim(cells, 0, 1, axis=dim)
    tail = lax.slice_in_dim(cells, size - 1, size, axis=dim)
    if count == 2:
        index = lax.axis_index(axis)
        incoming = lax.ppermute(jnp.where(index == 0, tail, head), axis, [(0, 1), (1, 0)])
        zero = jnp.zeros_like(incoming)
        below = jnp.where(index == 1, incoming, zero)
        above = jnp.where(index == 0, incoming, zero)
    else:
        below = lax.ppermute(tail, axis, [(i, i + 1) for i in range(count - 1)])
        above = lax.ppermute(head, axis, [(i + 1, i) for i in range(count - 1)])
    return jnp.concatenate([below, cells, above], axis=dim)


def with_halo(cells):
    return exchange(exchange(cells, "vox", 0), "star", 1)


def per_device(
    mean_field,
    deviations,
    stencil,
    vertical_mix,
    log_mean,
    responses,
    pair_line,
    pair_owner,
    pair_star,
    observed,
    inv_var,
):
    samples = deviations.shape[0]
    width_x = deviations.shape[1]
    width_y = deviations.shape[2]
    length = deviations.shape[3]
    group_size = lax.axis_size("vox")
    star_count = observed.shape[0]
    group_blocks = group_size * star_count
    latent = jnp.transpose(mean_field[None] + deviations, (1, 2, 0, 3))
    padded = with_halo(latent)
    smoothed = jnp.zeros(latent.shape, jnp.float32)
    for offset_x in range(3):
        for offset_y in range(3):
            smoothed = (
                smoothed
                + stencil[offset_x, offset_y]
                * padded[offset_x : offset_x + width_x, offset_y : offset_y + width_y]
            )
    log_density = jnp.einsum("xysw,zw->xysz", smoothed, vertical_mix, precision=HIGH) + log_mean
    density = jnp.exp(log_density)
    density_b = density.astype(jnp.bfloat16).reshape(width_x * width_y, samples, length)
    picked = jnp.take(density_b, pair_line, axis=0)
    contribution = jnp.einsum("pij,psj->psi", responses, picked, preferred_element_type=jnp.float32)
    target = pair_owner[:, 0] * star_count + pair_star
    target_onehot = (
        target[:, None] == jnp.arange(group_blocks, dtype=jnp.int32)[None, :]
    ).astype(jnp.float32)
    partial = jnp.einsum("pb,psi->bsi", target_onehot, contribution, precision=HIGH)
    arrived = lax.all_to_all(
        partial.reshape(group_size, star_count, samples, length),
        "vox",
        split_axis=0,
        concat_axis=0,
        tiled=True,
    )
    extinction = jnp.sum(arrived, axis=0)
    misfit = inv_var[:, None, :] * (extinction - observed[:, None, :])
    residual_mean = jnp.mean(misfit, axis=1)
    misfit_b = misfit.astype(jnp.bfloat16)
    spread = jnp.broadcast_to(misfit_b[None], (group_size,) + misfit_b.shape)
    misfit_b = lax.all_to_all(spread, "vox", split_axis=0, concat_axis=0, tiled=True).reshape(
        group_blocks, samples, length
    )
    pair_misfit = jnp.take(misfit_b, target, axis=0)
    pair_adjoint = jnp.einsum(
        "pij,psi->psj", responses, pair_misfit, preferred_element_type=jnp.float32
    )
    line_onehot = (
        pair_line[:, None] == jnp.arange(width_x * width_y, dtype=jnp.int32)[None, :]
    ).astype(jnp.float32)
    adjoint = jnp.einsum("pb,psj->bsj", line_onehot, pair_adjoint, precision=HIGH).reshape(
        width_x, width_y, samples, length
    )
    grad_log = density * adjoint
    grad_smooth = jnp.einsum("xysz,zw->xysw", grad_log, vertical_mix, precision=HIGH)
    padded_grad = with_halo(grad_smooth)
    grad_latent = jnp.zeros(latent.shape, jnp.float32)
    for offset_x in range(3):
        for offset_y in range(3):
            grad_latent = (
                grad_latent
                + stencil[offset_x, offset_y]
                * padded_grad[2 - offset_x : 2 - offset_x + width_x, 2 - offset_y : 2 - offset_y + width_y]
            )
    gradient = jnp.mean(grad_latent + latent, axis=2)
    return (gradient, residual_mean)


def solution(mesh):
    placed = (
        P("vox", "star", None),
        P(None, "vox", "star", None),
        P(),
        P(),
        P(),
        P(("vox", "star"), None, None),
        P(("vox", "star")),
        P(("vox", "star"), None),
        P(("vox", "star")),
        P(("vox", "star"), None),
        P(("vox", "star"), None),
    )
    return jax.shard_map(
        per_device,
        mesh=mesh,
        in_specs=placed,
        out_specs=(P("vox", "star", None), P(("vox", "star"), None)),
        check_vma=False,
    )
```

time: 82.9 us -> 78.9 us (0.952)
  starting transfers between devices: 24.5 us -> 17.3 us
  other arithmetic: 10.4 us -> 15 us
  waiting for transfers between devices: 14.8 us -> 11.6 us
  matrix products: 10.7 us -> 11.6 us
  local copies, waits for them, and re-layouts: 3.98 us -> 4.82 us
    ppermute x8 -> x6, starting transfers between devices: 20.5 us -> 13.4 us  [the longest x2 6.58 us: exchange(): below = lax.ppermute(tail, axis, [(i, i + 1) for i in range(count - 1)])]
    ppermute x8 -> x6, waiting for transfers between devices: 7.88 us -> 4.68 us  [the longest x2 3.95 us: exchange(): above = lax.ppermute(head, axis, [(i + 1, i) for i in range(count - 1)])]
    select_n x1 -> x5, other arithmetic: 0.66 us -> 2.02 us  [the longest x1 1.23 us: per_device(): picked = jnp.take(density_b, pair_line, axis=0)]
    gather x2, other arithmetic: 0.01 us -> 1.26 us  [the longest x1 0.01 us: per_device(): pair_misfit = jnp.take(misfit_b, target, axis=0)]
    add x1 -> x0, other arithmetic: 1.13 us -> none  [per_device(): latent = mean_field[None] + deviations]
    transpose x0 -> x1, other arithmetic: none -> 1.13 us  [per_device(): latent = jnp.transpose(mean_field[None] + deviations, (1, 2, 0, 3))]
    concatenate x2, other arithmetic: 0.17 us -> 1.16 us  [exchange(): return jnp.concatenate([below, cells, above], axis=dim)]
    dot_general x4, matrix products: 9.3 us -> 10.2 us  [the longest x1 7.69 us: per_device(): jnp.einsum('xysw,zw->xysz', smoothed, vertical_mix, precision=HIGH)]
  transfers between devices with their start and end apart: 9 -> 7, of which waited for: 5 -> 3; matrix products, arithmetic and copies ran while one was open for 5% -> 9% of each run, Pallas kernels for 0% -> 0%
where the time goes in v3:
time: 78.9 us; the launch traced here: 78.2 us
  starting transfers between devices  17.3 us (22%)
  blocking collectives  16.9 us (21%)
  other arithmetic  15 us (19%)
  waiting for transfers between devices  11.6 us (15%)
  matrix products  11.6 us (15%)
  local copies, waits for them, and re-layouts  4.82 us (6%)
  between operations  0.94 us (1%)
    all_to_all x1, blocking collectives, per_device(): lax.all_to_all(partial.reshape(group_size, star_count, samples, length),...  16.9 us
    dot_general x1, matrix products, per_device(): jnp.einsum('xysw,zw->xysz', smoothed, vertical_mix, precision=HIGH)  7.69 us
    all_to_all x1, waiting for transfers between devices, per_device(): lax.all_to_all(spread, 'vox', split_axis=0, concat_axis=0, tiled=True)  6.93 us
    ppermute x2, starting transfers between devices, exchange(): below = lax.ppermute(tail, axis, [(i, i + 1) for i in range(count - 1)])  6.58 us
    reduce_sum x1, other arithmetic, per_device(): gradient = jnp.mean(grad_latent + latent, axis=2)  5.76 us
    ppermute x2, starting transfers between devices, exchange(): above = lax.ppermute(head, axis, [(i + 1, i) for i in range(count - 1)])  4.25 us
    all_to_all x1, starting transfers between devices, per_device(): lax.all_to_all(spread, 'vox', split_axis=0, concat_axis=0, tiled=True)  3.95 us
    ppermute x2, waiting for transfers between devices, exchange(): above = lax.ppermute(head, axis, [(i + 1, i) for i in range(count - 1)])  3.95 us
  transfers between devices with their start and end apart: 7, of which 3 were waited for; matrix products, arithmetic and copies ran while one was open for 9% of the time, Pallas kernels for 0%

profile of v3, /device:TPU:1, one launch (start us, length us, event | category | flops | bytes accessed | tf_op | source)
XLA Modules:
  0.0 78.2 jit_solution(12850571639678652465)
XLA Ops:
  0.6 1.1 %fusion.33 = f32[2,64,4,128]{3,1,2,0:T(8,128)S(1)} fusion(f32[4,2,64,128]{3,2,1,0:T(8,128)} %param.14, f32[2,64,128]{2,1,0:T(8,128)} %param.13), kind=kLoop, calls=%fused_computation.52 | loop fusion | flops 65536 | bytes 589824 | tf_op jit(solution)/shard_map/transpose | solution.py:50
  1.8 0.7 fusion.69
  2.5 4.5 %collective-permute-start = (f32[1,64,4,128]{3,1,2,0:T(8,128)}, f32[1,64,4,128]{3,1,2,0:T(8,128)S(1)}, u32[]{:S(2)}, u32[]{:S(2)}) collective-permute-start(f32[1,64,4,128]{3,1,2,0:T(8,128)} %get-tuple-element.11), channel_id=1, source_target_pairs={{0,2},{2,4},{4,6},{6,8},{8,10},{10,12},{12,14},{14,16},{16,18},{18... | collective-permute-start | bytes 393224 | tf_op jit(solution)/shard_map/ppermute | solution.py:21
  7.0 1.9 %collective-permute-start.1 = (f32[1,64,4,128]{3,1,2,0:T(8,128)}, f32[1,64,4,128]{3,1,2,0:T(8,128)}, u32[]{:S(2)}, u32[]{:S(2)}) collective-permute-start(f32[1,64,4,128]{3,1,2,0:T(8,128)} %get-tuple-element.12), channel_id=1, source_target_pairs={{2,0},{4,2},{6,4},{8,6},{10,8},{12,10},{14,12},{16,14},{18,16},{20... | collective-permute-start | bytes 393224 | tf_op jit(solution)/shard_map/ppermute | solution.py:22
  9.0 1.2 %compare_select_fusion.1 = s32[96]{0:T(128)} fusion(s32[96]{0:T(128)} %param.19), kind=kLoop, calls=%fused_computation.99 | loop fusion | flops 288 | bytes 768 | tf_op jit(solution)/shard_map/jit(_take)/jit(_where)/select_n | solution.py:63
  10.2 1.2 %compare_and_fusion = (pred[96]{0:T(512)(128)(4,1)}, s32[96]{0:T(128)}) fusion(s32[96]{0:T(128)} %param.21, s32[96,1]{0,1:T(1,128)} %param.20), kind=kLoop, calls=%fused_computation.101 | loop fusion | flops 768 | bytes 1248 | tf_op jit(solution)/shard_map/jit(_take)/and | solution.py:85
  11.4 1.2 %compare_and_fusion.1 = pred[96]{0:T(512)(128)(4,1)} fusion(s32[96]{0:T(128)} %param.19), kind=kLoop, calls=%fused_computation.102 | loop fusion | flops 576 | bytes 480 | tf_op jit(solution)/shard_map/jit(_take)/and | solution.py:63
  12.6 1.7 %fusion.70 = (f32[1,1]{1,0:T(1,128)}, f32[1,1]{1,0:T(1,128)}, f32[1,1]{1,0:T(1,128)}, f32[1,1]{1,0:T(1,128)}, f32[1,1]{1,0:T(1,128)}, /*index=5*/f32[1,1]{1,0:T(...) fusion(f32[3,3]{1,0:T(4,128)} %param.15), kind=kLoop, calls=%fused_computation.109 | loop fusion | bytes 72 | tf_op jit(solution)/shard_map/slice | solution.py:103
  14.3 0.7 broadcast_select_fusion.3
  15.1 1.3 %collective-permute-start.2 = (f32[4,1,4,128]{3,1,2,0:T(1,128)S(1)}, f32[4,1,4,128]{3,1,2,0:T(1,128)S(1)}, u32[]{:S(2)}, u32[]{:S(2)}) collective-permute-start(f32[4,1,4,128]{3,1,2,0:T(1,128)S(1)} %broadcast_select_fusion.3), channel_id=1, source_target_pairs={{0,1},{1,0},{2,3},{3,2},{4,5},{5,4},{6,7},{7,6},{8,9},{9,8},{10,11... | collective-permute-start | bytes 24584 | tf_op jit(solution)/shard_map/ppermute | solution.py:16
  16.4 1.3 %pad_clamp_fusion.1 = s32[1024]{0:T(1024)} fusion(s32[96]{0:T(128)} %compare_select_fusion.1), kind=kLoop, calls=%fused_computation.97 | loop fusion | flops 1024 | bytes 4480 | tf_op gather
  17.7 1.1 %maximum_maximum_fusion = (f32[4,65,4,128]{3,1,2,0:T(8,128)S(1)}, f32[4,65,4,128]{3,1,2,0:T(8,128)S(1)}) fusion(f32[1,64,4,128]{3,1,2,0:T(8,128)} %collective-permute-done.1, f32[2,64,4,128]{3,1,2,0:T(8,128)S(1)} %fusion.33, f32[1,64,4,128]{3,1,2,0:T(8,128)S(1)} %collective-permute-done, f32[4,1,4,128]{3,1,2,0:T(1,128)S(1)} %get-tuple-element.17, ...), kind=kLoop, calls=%fused_computation.5 | loop fusion | flops 798720 | bytes 1605632 | tf_op jit(solution)/shard_map/concatenate | solution.py:23
  18.8 7.7 %fusion.71 = (bf16[2,64,4,128]{3,1,2,0:T(8,128)(2,1)S(1)}, f32[2,64,4,128]{3,1,2,0:T(8,128)}) fusion(f32[128]{0:T(128)} %param.17, f32[128,128]{1,0:T(8,128)} %param.16, f32[4,65,4,128]{3,1,2,0:T(8,128)S(1)} %get-tuple-element.8, f32[1,64,4,128]{3,1,2,0:T(8,128)} %collective-permute-done.1, f32[2,64,4,128]{3,1,2,0:T(8,128)S(1)} %fusion.33, ...), kind=kOutput, calls=%fused_computation.110 | convolution fusion | flops 102039552 | bytes 2556452 | tf_op jit(solution)/shard_map/xysw,zw->xysz/dot_general | solution.py:60
  26.6 0.8 %gather_fusion = bf16[96,4,128]{2,1,0:T(4,128)(2,1)S(1)} fusion(bf16[128,4,128]{2,1,0:T(4,128)(2,1)S(1)} %copy.25, s32[1024]{0:T(1024)} %pad_clamp_fusion.1), kind=kCustom, calls=%fused_computation.clone | custom fusion | bytes 196992 | tf_op jit(solution)/shard_map/jit(_take)/gather | solution.py:63
  27.4 1.8 %fusion.49 = f32[96,4,128]{2,1,0:T(4,128)S(1)} fusion(bf16[96,128,128]{2,1,0:T(8,128)(2,1)S(1)} %copy-done, bf16[96,4,128]{2,1,0:T(4,128)(2,1)S(1)} %gather_fusion, pred[96]{0:T(512)(128)(4,1)S(1)} %copy-done.9), kind=kOutput, calls=%fused_computation.68 | convolution fusion | flops 12632064 | bytes 3440736 | tf_op jit(solution)/shard_map/pij,psj->psi/dot_general | solution.py:64
  29.6 16.9 %all_to_all.10 = f32[16,8,4,128]{3,1,2,0:T(8,128)S(1)} all-to-all(f32[16,8,4,128]{3,1,2,0:T(8,128)S(1)} %copy.27), channel_id=1, replica_groups=mesh['vox'=16,'star'=2] {'vox'}, dimensions={0} | all-to-all | bytes 524288 | tf_op jit(solution)/shard_map/all_to_all | solution.py:70
  47.3 4.0 %all-to-all-start.1 = ((bf16[16,8,4,128]{3,2,1,0:T(4,128)(2,1)}), bf16[16,8,4,128]{3,2,1,0:T(4,128)(2,1)S(1)}, u32[]{:S(2)}, u32[]{:S(2)}) async-start(bf16[16,8,4,128]{3,2,1,0:T(4,128)(2,1)} %broadcast_in_dim.11), calls=%async_computation.1 | async-start | bytes 262144 | tf_op jit(solution)/shard_map/all_to_all | solution.py:82
  51.3 6.9 %all-to-all-done.1 = bf16[16,8,4,128]{3,2,1,0:T(4,128)(2,1)S(1)} async-done(((bf16[16,8,4,128]{3,2,1,0:T(4,128)(2,1)}), bf16[16,8,4,128]{3,2,1,0:T(4,128)(2,1)S(1)}, u32[]{:S(2)}, u32[]{:S(2)}) %all-to-all-start.1) | async-done | bytes 131104 | tf_op jit(solution)/shard_map/all_to_all | solution.py:82
  58.9 1.0 %fusion.47 = f32[96,4,128]{2,1,0:T(4,128)S(1)} fusion(bf16[96,128,128]{2,1,0:T(8,128)(2,1)S(1)} %copy-done, bf16[96,4,128]{2,1,0:T(4,128)(2,1)S(1)} %gather_fusion.1, pred[96]{0:T(512)(128)(4,1)S(1)} %copy-done.7), kind=kOutput, calls=%fused_computation.66 | convolution fusion | flops 12632064 | bytes 3440736 | tf_op jit(solution)/shard_map/pij,psi->psj/dot_general | solution.py:86
  60.7 2.1 %collective-permute-start.3 = (f32[1,64,4,128]{3,1,2,0:T(8,128)S(1)}, f32[1,64,4,128]{3,1,2,0:T(8,128)S(1)}, u32[]{:S(2)}, u32[]{:S(2)}) collective-permute-start(f32[1,64,4,128]{3,1,2,0:T(8,128)S(1)} %get-tuple-element.9), channel_id=1, source_target_pairs={{0,2},{2,4},{4,6},{6,8},{8,10},{10,12},{12,14},{14,16},{16,18},{18... | collective-permute-start | bytes 393224 | tf_op jit(solution)/shard_map/ppermute | solution.py:21
  62.8 2.3 %collective-permute-start.4 = (f32[1,64,4,128]{3,1,2,0:T(8,128)S(1)}, f32[1,64,4,128]{3,1,2,0:T(8,128)S(1)}, u32[]{:S(2)}, u32[]{:S(2)}) collective-permute-start(f32[1,64,4,128]{3,1,2,0:T(8,128)S(1)} %get-tuple-element.10), channel_id=1, source_target_pairs={{2,0},{4,2},{6,4},{8,6},{10,8},{12,10},{14,12},{16,14},{18,16},{20... | collective-permute-start | bytes 393224 | tf_op jit(solution)/shard_map/ppermute | solution.py:22
  65.1 3.9 %collective-permute-done.4 = f32[1,64,4,128]{3,1,2,0:T(8,128)S(1)} collective-permute-done((f32[1,64,4,128]{3,1,2,0:T(8,128)S(1)}, f32[1,64,4,128]{3,1,2,0:T(8,128)S(1)}, u32[]{:S(2)}, u32[]{:S(2)}) %collective-permute-start.4) | collective-permute-done | bytes 131104 | tf_op jit(solution)/shard_map/ppermute | solution.py:22
  69.1 1.3 %collective-permute-start.5 = (f32[4,1,4,128]{3,1,2,0:T(1,128)S(1)}, f32[4,1,4,128]{3,1,2,0:T(1,128)S(1)}, u32[]{:S(2)}, u32[]{:S(2)}) collective-permute-start(f32[4,1,4,128]{3,1,2,0:T(1,128)S(1)} %broadcast_select_fusion.1), channel_id=1, source_target_pairs={{0,1},{1,0},{2,3},{3,2},{4,5},{5,4},{6,7},{7,6},{8,9},{9,8},{10,11... | collective-permute-start | bytes 24584 | tf_op jit(solution)/shard_map/ppermute | solution.py:16
  71.8 5.8 %fusion.3 = f32[2,64,128]{2,1,0:T(8,128)S(1)} fusion(f32[4,65,4,128]{3,1,2,0:T(8,128)S(1)} %get-tuple-element.6, f32[2,64,4,128]{3,1,2,0:T(8,128)S(1)} %fusion.32, f32[1,64,4,128]{3,1,2,0:T(8,128)S(1)} %collective-permute-done.3, f32[4,65,4,128]{3,1,2,0:T(8,128)S(1)} %get-tuple-element.5, f32[1,64,4,128]{3,1,2,0:T(8,128)S(1)} %collective-permute-done.4, ...), kind=kLoop, calls=%fused_computation.12 | loop fusion | flops 1425408 | bytes 2490404 | tf_op jit(solution)/shard_map/reduce_sum | solution.py:106
  (47 shorter events, 4.9 us)
Async XLA Ops:
  0.6 26.8 %copy-start = (bf16[96,128,128]{2,1,0:T(8,128)(2,1)S(1)}, bf16[96,128,128]{2,1,0:T(8,128)(2,1)}, u32[]{:S(2)}) copy-start(bf16[96,128,128]{2,1,0:T(8,128)(2,1)} %param.18) | copy-start | bytes 9437188
  2.5 11.8 %collective-permute-start = (f32[1,64,4,128]{3,1,2,0:T(8,128)}, f32[1,64,4,128]{3,1,2,0:T(8,128)S(1)}, u32[]{:S(2)}, u32[]{:S(2)}) collective-permute-start(f32[1,64,4,128]{3,1,2,0:T(8,128)} %get-tuple-element.11), channel_id=1, source_target_pairs={{0,2},{2,4},{4,6},{6,8},{8,10},{10,12},{12,14},{14,16},{16,18},{18... | collective-permute-start | bytes 393224 | tf_op jit(solution)/shard_map/ppermute | solution.py:21
  7.0 7.3 %collective-permute-start.1 = (f32[1,64,4,128]{3,1,2,0:T(8,128)}, f32[1,64,4,128]{3,1,2,0:T(8,128)}, u32[]{:S(2)}, u32[]{:S(2)}) collective-permute-start(f32[1,64,4,128]{3,1,2,0:T(8,128)} %get-tuple-element.12), channel_id=1, source_target_pairs={{2,0},{4,2},{6,4},{8,6},{10,8},{12,10},{14,12},{16,14},{18,16},{20... | collective-permute-start | bytes 393224 | tf_op jit(solution)/shard_map/ppermute | solution.py:22
  15.1 2.6 %collective-permute-start.2 = (f32[4,1,4,128]{3,1,2,0:T(1,128)S(1)}, f32[4,1,4,128]{3,1,2,0:T(1,128)S(1)}, u32[]{:S(2)}, u32[]{:S(2)}) collective-permute-start(f32[4,1,4,128]{3,1,2,0:T(1,128)S(1)} %broadcast_select_fusion.3), channel_id=1, source_target_pairs={{0,1},{1,0},{2,3},{3,2},{4,5},{5,4},{6,7},{7,6},{8,9},{9,8},{10,11... | collective-permute-start | bytes 24584 | tf_op jit(solution)/shard_map/ppermute | solution.py:16
  17.6 9.8 %copy-start.9 = (pred[96]{0:T(512)(128)(4,1)S(1)}, pred[96]{0:T(512)(128)(4,1)}, u32[]{:S(2)}) copy-start(pred[96]{0:T(512)(128)(4,1)} %compare_and_fusion.1) | copy-start | bytes 292
  18.7 10.5 %copy-start.8 = (s32[96]{0:T(128)S(1)}, s32[96]{0:T(128)}, u32[]{:S(2)}) copy-start(s32[96]{0:T(128)} %get-tuple-element.4) | copy-start | bytes 1156
  26.5 20.1 %copy-start.5 = (f32[8,128]{1,0:T(8,128)S(1)}, f32[8,128]{1,0:T(8,128)}, u32[]{:S(2)}) copy-start(f32[8,128]{1,0:T(8,128)} %param.22) | copy-start | bytes 12292
  26.5 20.1 %copy-start.6 = (f32[8,128]{1,0:T(8,128)S(1)}, f32[8,128]{1,0:T(8,128)}, u32[]{:S(2)}) copy-start(f32[8,128]{1,0:T(8,128)} %param.23) | copy-start | bytes 12292
  26.5 32.4 %copy-start.7 = (pred[96]{0:T(512)(128)(4,1)S(1)}, pred[96]{0:T(512)(128)(4,1)}, u32[]{:S(2)}) copy-start(pred[96]{0:T(512)(128)(4,1)} %get-tuple-element.3) | copy-start | bytes 292
  29.2 30.7 %copy-start.10 = (s32[96]{0:T(128)S(1)}, s32[96]{0:T(128)}, u32[]{:S(2)}) copy-start(s32[96]{0:T(128)} %param.19) | copy-start | bytes 1156
  29.2 31.1 %copy-start.4 = (f32[128,128]{1,0:T(8,128)S(1)}, f32[128,128]{1,0:T(8,128)}, u32[]{:S(2)}) copy-start(f32[128,128]{1,0:T(8,128)} %param.16) | copy-start | bytes 196612
  47.3 10.9 %all-to-all-start.1 = ((bf16[16,8,4,128]{3,2,1,0:T(4,128)(2,1)}), bf16[16,8,4,128]{3,2,1,0:T(4,128)(2,1)S(1)}, u32[]{:S(2)}, u32[]{:S(2)}) async-start(bf16[16,8,4,128]{3,2,1,0:T(4,128)(2,1)} %broadcast_in_dim.11), calls=%async_computation.1 | async-start | bytes 262144 | tf_op jit(solution)/shard_map/all_to_all | solution.py:82
  58.9 1.4 %copy-start.3 = (f32[2,64,4,128]{3,1,2,0:T(8,128)S(1)}, f32[2,64,4,128]{3,1,2,0:T(8,128)}, u32[]{:S(2)}) copy-start(f32[2,64,4,128]{3,1,2,0:T(8,128)} %get-tuple-element.29) | copy-start | bytes 786436
  58.9 12.9 %copy-start.1 = (f32[4,2,64,128]{3,2,1,0:T(8,128)S(1)}, f32[4,2,64,128]{3,2,1,0:T(8,128)}, u32[]{:S(2)}) copy-start(f32[4,2,64,128]{3,2,1,0:T(8,128)} %param.14) | copy-start | bytes 786436
  58.9 12.9 %copy-start.2 = (f32[2,64,128]{2,1,0:T(8,128)S(1)}, f32[2,64,128]{2,1,0:T(8,128)}, u32[]{:S(2)}) copy-start(f32[2,64,128]{2,1,0:T(8,128)} %param.13) | copy-start | bytes 196612
  60.7 4.4 %collective-permute-start.3 = (f32[1,64,4,128]{3,1,2,0:T(8,128)S(1)}, f32[1,64,4,128]{3,1,2,0:T(8,128)S(1)}, u32[]{:S(2)}, u32[]{:S(2)}) collective-permute-start(f32[1,64,4,128]{3,1,2,0:T(8,128)S(1)} %get-tuple-element.9), channel_id=1, source_target_pairs={{0,2},{2,4},{4,6},{6,8},{8,10},{10,12},{12,14},{14,16},{16,18},{18... | collective-permute-start | bytes 393224 | tf_op jit(solution)/shard_map/ppermute | solution.py:21
  62.8 6.3 %collective-permute-start.4 = (f32[1,64,4,128]{3,1,2,0:T(8,128)S(1)}, f32[1,64,4,128]{3,1,2,0:T(8,128)S(1)}, u32[]{:S(2)}, u32[]{:S(2)}) collective-permute-start(f32[1,64,4,128]{3,1,2,0:T(8,128)S(1)} %get-tuple-element.10), channel_id=1, source_target_pairs={{2,0},{4,2},{6,4},{8,6},{10,8},{12,10},{14,12},{16,14},{18,16},{20... | collective-permute-start | bytes 393224 | tf_op jit(solution)/shard_map/ppermute | solution.py:22
  69.1 2.6 %collective-permute-start.5 = (f32[4,1,4,128]{3,1,2,0:T(1,128)S(1)}, f32[4,1,4,128]{3,1,2,0:T(1,128)S(1)}, u32[]{:S(2)}, u32[]{:S(2)}) collective-permute-start(f32[4,1,4,128]{3,1,2,0:T(1,128)S(1)} %broadcast_select_fusion.1), channel_id=1, source_target_pairs={{0,1},{1,0},{2,3},{3,2},{4,5},{5,4},{6,7},{7,6},{8,9},{9,8},{10,11... | collective-permute-start | bytes 24584 | tf_op jit(solution)/shard_map/ppermute | solution.py:16

commit v4 on v3

--- a/solution.py
+++ b/solution.py
@@ -25,6 +25,44 @@
 
 def with_halo(cells):
     return exchange(exchange(cells, "vox", 0), "star", 1)
+
+
+def cube_bits(count):
+    bits = count.bit_length() - 1
+    return bits if (1 << bits) == count and bits > 0 else None
+
+
+def reduce_scatter(partial, axis):
+    count = partial.shape[0]
+    bits = cube_bits(count)
+    if bits is None:
+        arrived = lax.all_to_all(partial, axis, split_axis=0, concat_axis=0, tiled=True)
+        return jnp.sum(arrived, axis=0)
+    index = lax.axis_index(axis)
+    cells = partial.reshape((2,) * bits + partial.shape[1:])
+    for bit in range(bits):
+        mine = (index >> bit) & 1
+        place = bits - 1 - bit
+        keep = lax.dynamic_index_in_dim(cells, mine, axis=place, keepdims=False)
+        send = lax.dynamic_index_in_dim(cells, 1 - mine, axis=place, keepdims=False)
+        cells = keep + lax.ppermute(send, axis, [(i, i ^ (1 << bit)) for i in range(count)])
+    return cells
+
+
+def all_gather(block, axis, count):
+    bits = cube_bits(count)
+    if bits is None:
+        spread = jnp.broadcast_to(block[None], (count,) + block.shape)
+        gathered = lax.all_to_all(spread, axis, split_axis=0, concat_axis=0, tiled=True)
+        return gathered.reshape((count * block.shape[0],) + block.shape[1:])
+    index = lax.axis_index(axis)
+    cells = block
+    for bit in reversed(range(bits)):
+        low = ((index >> bit) & 1) == 0
+        other = lax.ppermute(cells, axis, [(i, i ^ (1 << bit)) for i in range(count)])
+        place = bits - 1 - bit
+        cells = jnp.stack([jnp.where(low, cells, other), jnp.where(low, other, cells)], axis=place)
+    return cells.reshape((count * block.shape[0],) + block.shape[1:])
 
 
 def per_device(
@@ -67,21 +105,10 @@
         target[:, None] == jnp.arange(group_blocks, dtype=jnp.int32)[None, :]
     ).astype(jnp.float32)
     partial = jnp.einsum("pb,psi->bsi", target_onehot, contribution, precision=HIGH)
-    arrived = lax.all_to_all(
-        partial.reshape(group_size, star_count, samples, length),
-        "vox",
-        split_axis=0,
-        concat_axis=0,
-        tiled=True,
-    )
-    extinction = jnp.sum(arrived, axis=0)
+    extinction = reduce_scatter(partial.reshape(group_size, star_count, samples, length), "vox")
     misfit = inv_var[:, None, :] * (extinction - observed[:, None, :])
     residual_mean = jnp.mean(misfit, axis=1)
-    misfit_b = misfit.astype(jnp.bfloat16)
-    spread = jnp.broadcast_to(misfit_b[None], (group_size,) + misfit_b.shape)
-    misfit_b = lax.all_to_all(spread, "vox", split_axis=0, concat_axis=0, tiled=True).reshape(
-        group_blocks, samples, length
-    )
+    misfit_b = all_gather(misfit.astype(jnp.bfloat16), "vox", group_size)
     pair_misfit = jnp.take(misfit_b, target, axis=0)
     pair_adjoint = jnp.einsum(
         "pij,psi->psj", responses, pair_misfit, preferred_element_type=jnp.float32

time: 78.9 us -> 84.4 us (1.070)
  blocking collectives: 16.9 us -> 0 us
  starting transfers between devices: 17.3 us -> 32.3 us
  waiting for transfers between devices: 11.6 us -> 16.4 us
    ppermute x0 -> x8, starting transfers between devices: none -> 18.5 us  [the longest x4 11.3 us: all_gather(): other = lax.ppermute(cells, axis, [(i, i ^ 1 << bit) for i in range(count)])]
    all_to_all x1 -> x0, blocking collectives: 16.9 us -> none  [per_device(): lax.all_to_all(partial.reshape(group_size, star_count, samples, length),...]
    ppermute x0 -> x8, waiting for transfers between devices: none -> 11.1 us  [the longest x4 6.16 us: reduce_scatter(): lax.ppermute(send, axis, [(i, i ^ 1 << bit) for i in range(count)])]
    all_to_all x1 -> x0, waiting for transfers between devices: 6.93 us -> none  [per_device(): lax.all_to_all(spread, 'vox', split_axis=0, concat_axis=0, tiled=True)]
    all_to_all x1 -> x0, starting transfers between devices: 3.95 us -> none  [per_device(): lax.all_to_all(spread, 'vox', split_axis=0, concat_axis=0, tiled=True)]
    select_n x1, other arithmetic: 0.01 us -> 1.24 us  [per_device(): pair_misfit = jnp.take(misfit_b, target, axis=0)]
    select_n x1 -> x0, other arithmetic: 1.23 us -> none  [per_device(): picked = jnp.take(density_b, pair_line, axis=0)]
  transfers between devices with their start and end apart: 7 -> 14, of which waited for: 3 -> 10; matrix products, arithmetic and copies ran while one was open for 9% -> 9% of each run, Pallas kernels for 0% -> 0%
where the time goes in v4:
time: 84.4 us; the launch traced here: 83.1 us
  starting transfers between devices  32.3 us (38%)
  waiting for transfers between devices  16.4 us (19%)
  other arithmetic  15.8 us (19%)
  matrix products  12.2 us (14%)
  local copies, waits for them, and re-layouts  5.5 us (7%)
  between operations  0.98 us (1%)
    ppermute x4, starting transfers between devices, all_gather(): other = lax.ppermute(cells, axis, [(i, i ^ 1 << bit) for i in range(count)])  11.3 us
    dot_general x1, matrix products, per_device(): jnp.einsum('xysw,zw->xysz', smoothed, vertical_mix, precision=HIGH)  7.65 us
    ppermute x2, starting transfers between devices, exchange(): below = lax.ppermute(tail, axis, [(i, i + 1) for i in range(count - 1)])  7.34 us
    ppermute x4, starting transfers between devices, reduce_scatter(): lax.ppermute(send, axis, [(i, i ^ 1 << bit) for i in range(count)])  7.2 us
    ppermute x4, waiting for transfers between devices, reduce_scatter(): lax.ppermute(send, axis, [(i, i ^ 1 << bit) for i in range(count)])  6.16 us
    reduce_sum x1, other arithmetic, per_device(): gradient = jnp.mean(grad_latent + latent, axis=2)  5.73 us
    ppermute x4, waiting for transfers between devices, all_gather(): other = lax.ppermute(cells, axis, [(i, i ^ 1 << bit) for i in range(count)])  4.89 us
    ppermute x2, waiting for transfers between devices, exchange(): above = lax.ppermute(head, axis, [(i + 1, i) for i in range(count - 1)])  4.65 us
  transfers between devices with their start and end apart: 14, of which 10 were waited for; matrix products, arithmetic and copies ran while one was open for 9% of the time, Pallas kernels for 0%

profile of v4, /device:TPU:1, one launch (start us, length us, event | category | flops | bytes accessed | tf_op | source)
XLA Modules:
  0.0 83.1 jit_solution(16148761778249526756)
XLA Ops:
  2.5 4.5 %collective-permute-start = (f32[1,64,4,128]{3,1,2,0:T(8,128)}, f32[1,64,4,128]{3,1,2,0:T(8,128)S(1)}, u32[]{:S(2)}, u32[]{:S(2)}) collective-permute-start(f32[1,64,4,128]{3,1,2,0:T(8,128)} %get-tuple-element.13), channel_id=1, source_target_pairs={{0,2},{2,4},{4,6},{6,8},{8,10},{10,12},{12,14},{14,16},{16,18},{18... | collective-permute-start | bytes 393224 | tf_op jit(solution)/shard_map/ppermute | solution.py:21
  7.0 1.9 %collective-permute-start.1 = (f32[1,64,4,128]{3,1,2,0:T(8,128)}, f32[1,64,4,128]{3,1,2,0:T(8,128)}, u32[]{:S(2)}, u32[]{:S(2)}) collective-permute-start(f32[1,64,4,128]{3,1,2,0:T(8,128)} %get-tuple-element.14), channel_id=1, source_target_pairs={{2,0},{4,2},{6,4},{8,6},{10,8},{12,10},{14,12},{16,14},{18,16},{20... | collective-permute-start | bytes 393224 | tf_op jit(solution)/shard_map/ppermute | solution.py:22
  8.9 1.3 %compare_and_fusion = (pred[96]{0:T(512)(128)(4,1)}, s32[96]{0:T(128)S(1)}) fusion(s32[96]{0:T(128)} %param.21, s32[96,1]{0,1:T(1,128)} %param.20), kind=kLoop, calls=%fused_computation.122 | loop fusion | flops 768 | bytes 1248 | tf_op jit(solution)/shard_map/jit(_take)/and | solution.py:112
  10.8 1.2 %compare_select_fusion = (s32[96]{0:T(128)}, s32[96]{0:T(128)}) fusion(s32[96]{0:T(128)S(1)} %get-tuple-element.4, s32[96]{0:T(128)} %param.19), kind=kLoop, calls=%fused_computation.117 | loop fusion | flops 576 | bytes 1536 | tf_op jit(solution)/shard_map/jit(_take)/jit(_where)/select_n | solution.py:112
  13.2 1.7 %fusion.73 = (f32[1,1]{1,0:T(1,128)}, f32[1,1]{1,0:T(1,128)}, f32[1,1]{1,0:T(1,128)}, f32[1,1]{1,0:T(1,128)}, f32[1,1]{1,0:T(1,128)}, /*index=5*/f32[1,1]{1,0:T(...) fusion(f32[3,3]{1,0:T(4,128)} %param.15), kind=kLoop, calls=%fused_computation.132 | loop fusion | bytes 72 | tf_op jit(solution)/shard_map/slice | solution.py:130
  15.7 1.3 %collective-permute-start.2 = (f32[4,1,4,128]{3,1,2,0:T(1,128)S(1)}, f32[4,1,4,128]{3,1,2,0:T(1,128)S(1)}, u32[]{:S(2)}, u32[]{:S(2)}) collective-permute-start(f32[4,1,4,128]{3,1,2,0:T(1,128)S(1)} %broadcast_select_fusion.3), channel_id=1, source_target_pairs={{0,1},{1,0},{2,3},{3,2},{4,5},{5,4},{6,7},{7,6},{8,9},{9,8},{10,11... | collective-permute-start | bytes 24584 | tf_op jit(solution)/shard_map/ppermute | solution.py:16
  16.9 1.3 %pad_clamp_fusion.1 = s32[1024]{0:T(1024)} fusion(s32[96]{0:T(128)} %get-tuple-element.41), kind=kLoop, calls=%fused_computation.116 | loop fusion | flops 1024 | bytes 4480 | tf_op gather
  19.3 7.7 %fusion.74 = (bf16[2,64,4,128]{3,1,2,0:T(8,128)(2,1)S(1)}, f32[2,64,4,128]{3,1,2,0:T(8,128)}) fusion(f32[128]{0:T(128)} %param.17, f32[128,128]{1,0:T(8,128)} %param.16, f32[4,65,4,128]{3,1,2,0:T(8,128)S(1)} %get-tuple-element.8, f32[1,64,4,128]{3,1,2,0:T(8,128)} %collective-permute-done.1, f32[2,64,4,128]{3,1,2,0:T(8,128)S(1)} %fusion.33, ...), kind=kOutput, calls=%fused_computation.133 | convolution fusion | flops 102039552 | bytes 2556452 | tf_op jit(solution)/shard_map/xysw,zw->xysz/dot_general | solution.py:98
  28.0 2.4 %fusion.50 = f32[96,4,128]{2,1,0:T(4,128)S(1)} fusion(bf16[96,128,128]{2,1,0:T(8,128)(2,1)S(1)} %copy-done, bf16[96,4,128]{2,1,0:T(4,128)(2,1)S(1)} %gather_fusion, pred[96]{0:T(512)(128)(4,1)} %compare_and_fusion.1), kind=kOutput, calls=%fused_computation.71 | convolution fusion | flops 12632064 | bytes 3440736 | tf_op jit(solution)/shard_map/pij,psj->psi/dot_general | solution.py:102
  31.5 1.6 %collective-permute-done.3 = f32[2,2,2,8,4,128]{5,3,4,2,1,0:T(8,128)S(1)} collective-permute-done((f32[2,2,2,8,4,128]{5,3,4,2,1,0:T(8,128)}, f32[2,2,2,8,4,128]{5,3,4,2,1,0:T(8,128)S(1)}, u32[]{:S(2)}, u32[]{:S(2)}) %collective-permute-start.3) | collective-permute-done | bytes 131104 | tf_op jit(solution)/shard_map/ppermute | solution.py:48
  33.1 2.7 %collective-permute-start.4 = (f32[2,2,8,4,128]{4,2,3,1,0:T(8,128)S(1)}, f32[2,2,8,4,128]{4,2,3,1,0:T(8,128)S(1)}, u32[]{:S(2)}, u32[]{:S(2)}) collective-permute-start(f32[2,2,8,4,128]{4,2,3,1,0:T(8,128)S(1)} %dynamic-slice_bitcast_fusion), channel_id=1, source_target_pairs={{0,4},{2,6},{4,0},{6,2},{8,12},{10,14},{12,8},{14,10},{16,20},{18,... | collective-permute-start | bytes 196616 | tf_op jit(solution)/shard_map/ppermute | solution.py:48
  35.8 2.2 %collective-permute-done.4 = f32[2,2,8,4,128]{4,2,3,1,0:T(8,128)S(1)} collective-permute-done((f32[2,2,8,4,128]{4,2,3,1,0:T(8,128)S(1)}, f32[2,2,8,4,128]{4,2,3,1,0:T(8,128)S(1)}, u32[]{:S(2)}, u32[]{:S(2)}) %collective-permute-start.4) | collective-permute-done | bytes 65568 | tf_op jit(solution)/shard_map/ppermute | solution.py:48
  38.0 2.0 %collective-permute-start.5 = (f32[2,8,4,128]{3,1,2,0:T(8,128)S(1)}, f32[2,8,4,128]{3,1,2,0:T(8,128)S(1)}, u32[]{:S(2)}, u32[]{:S(2)}) collective-permute-start(f32[2,8,4,128]{3,1,2,0:T(8,128)S(1)} %dynamic-slice_bitcast_fusion.1), channel_id=1, source_target_pairs={{0,8},{2,10},{4,12},{6,14},{8,0},{10,2},{12,4},{14,6},{16,24},{18,... | collective-permute-start | bytes 98312 | tf_op jit(solution)/shard_map/ppermute | solution.py:48
  39.9 1.3 %collective-permute-done.5 = f32[2,8,4,128]{3,1,2,0:T(8,128)S(1)} collective-permute-done((f32[2,8,4,128]{3,1,2,0:T(8,128)S(1)}, f32[2,8,4,128]{3,1,2,0:T(8,128)S(1)}, u32[]{:S(2)}, u32[]{:S(2)}) %collective-permute-start.5) | collective-permute-done | bytes 32800 | tf_op jit(solution)/shard_map/ppermute | solution.py:48
  41.3 2.5 %collective-permute-start.6 = (f32[8,4,128]{2,0,1:T(8,128)S(1)}, f32[8,4,128]{2,0,1:T(8,128)S(1)}, u32[]{:S(2)}, u32[]{:S(2)}) collective-permute-start(f32[8,4,128]{2,0,1:T(8,128)S(1)} %dynamic-slice_bitcast_fusion.2), channel_id=1, source_target_pairs={{0,16},{2,18},{4,20},{6,22},{8,24},{10,26},{12,28},{14,30},{16,0},... | collective-permute-start | bytes 49160 | tf_op jit(solution)/shard_map/ppermute | solution.py:48
  45.0 2.4 %collective-permute-start.7 = (bf16[8,4,128]{2,0,1:T(8,128)(2,1)S(1)}, bf16[8,4,128]{2,0,1:T(8,128)(2,1)S(1)}, u32[]{:S(2)}, u32[]{:S(2)}) collective-permute-start(bf16[8,4,128]{2,0,1:T(8,128)(2,1)S(1)} %get-tuple-element.20), channel_id=1, source_target_pairs={{0,16},{2,18},{4,20},{6,22},{8,24},{10,26},{12,28},{14,30},{16,0},... | collective-permute-start | bytes 24584 | tf_op jit(solution)/shard_map/ppermute | solution.py:62
  48.4 1.4 %collective-permute-start.8 = (bf16[2,8,4,128]{3,1,0,2:T(8,128)(2,1)S(1)}, bf16[2,8,4,128]{3,1,0,2:T(8,128)(2,1)S(1)}, u32[]{:S(2)}, u32[]{:S(2)}) collective-permute-start(bf16[2,8,4,128]{3,1,0,2:T(8,128)(2,1)S(1)} %pad_maximum_fusion.9), channel_id=1, source_target_pairs={{0,8},{2,10},{4,12},{6,14},{8,0},{10,2},{12,4},{14,6},{16,24},{18,... | collective-permute-start | bytes 49160 | tf_op jit(solution)/shard_map/ppermute | solution.py:62
  51.6 2.4 %collective-permute-done.9 = bf16[2,2,8,4,128]{4,2,1,0,3:T(8,128)(2,1)S(1)} collective-permute-done((bf16[2,2,8,4,128]{4,2,1,0,3:T(8,128)(2,1)S(1)}, bf16[2,2,8,4,128]{4,2,1,0,3:T(8,128)(2,1)S(1)}, u32[]{:S(2)}, u32[]{:S(2)}) %collective-permute-start.9) | collective-permute-done | bytes 32800 | tf_op jit(solution)/shard_map/ppermute | solution.py:62
  54.0 7.0 %collective-permute-start.10 = (bf16[2,2,2,8,4,128]{5,3,2,1,0,4:T(8,128)(2,1)S(1)}, bf16[2,2,2,8,4,128]{5,3,2,1,0,4:T(8,128)(2,1)S(1)}, u32[]{:S(2)}, u32[]{:S(2)}) collective-permute-start(bf16[2,2,2,8,4,128]{5,3,2,1,0,4:T(8,128)(2,1)S(1)} %pad_maximum_fusion.7), channel_id=1, source_target_pairs={{0,2},{2,0},{4,6},{6,4},{8,10},{10,8},{12,14},{14,12},{16,18},{18,... | collective-permute-start | bytes 196616 | tf_op jit(solution)/shard_map/ppermute | solution.py:62
  64.6 2.8 %collective-permute-start.11 = (f32[1,64,4,128]{3,1,2,0:T(8,128)S(1)}, f32[1,64,4,128]{3,1,2,0:T(8,128)S(1)}, u32[]{:S(2)}, u32[]{:S(2)}) collective-permute-start(f32[1,64,4,128]{3,1,2,0:T(8,128)S(1)} %get-tuple-element.9), channel_id=1, source_target_pairs={{0,2},{2,4},{4,6},{6,8},{8,10},{10,12},{12,14},{14,16},{16,18},{18... | collective-permute-start | bytes 393224 | tf_op jit(solution)/shard_map/ppermute | solution.py:21
  67.5 1.9 %collective-permute-start.12 = (f32[1,64,4,128]{3,1,2,0:T(8,128)S(1)}, f32[1,64,4,128]{3,1,2,0:T(8,128)S(1)}, u32[]{:S(2)}, u32[]{:S(2)}) collective-permute-start(f32[1,64,4,128]{3,1,2,0:T(8,128)S(1)} %get-tuple-element.10), channel_id=1, source_target_pairs={{2,0},{4,2},{6,4},{8,6},{10,8},{12,10},{14,12},{16,14},{18,16},{20... | collective-permute-start | bytes 393224 | tf_op jit(solution)/shard_map/ppermute | solution.py:22
  69.4 4.6 %collective-permute-done.12 = f32[1,64,4,128]{3,1,2,0:T(8,128)S(1)} collective-permute-done((f32[1,64,4,128]{3,1,2,0:T(8,128)S(1)}, f32[1,64,4,128]{3,1,2,0:T(8,128)S(1)}, u32[]{:S(2)}, u32[]{:S(2)}) %collective-permute-start.12) | collective-permute-done | bytes 131104 | tf_op jit(solution)/shard_map/ppermute | solution.py:22
  74.1 1.3 %collective-permute-start.13 = (f32[4,1,4,128]{3,1,2,0:T(1,128)S(1)}, f32[4,1,4,128]{3,1,2,0:T(1,128)S(1)}, u32[]{:S(2)}, u32[]{:S(2)}) collective-permute-start(f32[4,1,4,128]{3,1,2,0:T(1,128)S(1)} %broadcast_select_fusion.1), channel_id=1, source_target_pairs={{0,1},{1,0},{2,3},{3,2},{4,5},{5,4},{6,7},{7,6},{8,9},{9,8},{10,11... | collective-permute-start | bytes 24584 | tf_op jit(solution)/shard_map/ppermute | solution.py:16
  76.8 5.7 %fusion.3 = f32[2,64,128]{2,1,0:T(8,128)S(1)} fusion(f32[4,65,4,128]{3,1,2,0:T(8,128)S(1)} %get-tuple-element.6, f32[2,64,4,128]{3,1,2,0:T(8,128)S(1)} %fusion.32, f32[1,64,4,128]{3,1,2,0:T(8,128)S(1)} %collective-permute-done.11, f32[4,65,4,128]{3,1,2,0:T(8,128)S(1)} %get-tuple-element.5, f32[1,64,4,128]{3,1,2,0:T(8,128)S(1)} %collective-permute-done.12, ...), kind=kLoop, calls=%fused_computation.11 | loop fusion | flops 1425408 | bytes 2490404 | tf_op jit(solution)/shard_map/reduce_sum | solution.py:133
  (72 shorter events, 17.1 us)
Async XLA Ops:
  0.6 27.3 %copy-start = (bf16[96,128,128]{2,1,0:T(8,128)(2,1)S(1)}, bf16[96,128,128]{2,1,0:T(8,128)(2,1)}, u32[]{:S(2)}) copy-start(bf16[96,128,128]{2,1,0:T(8,128)(2,1)} %param.18) | copy-start | bytes 9437188
  2.5 12.4 %collective-permute-start = (f32[1,64,4,128]{3,1,2,0:T(8,128)}, f32[1,64,4,128]{3,1,2,0:T(8,128)S(1)}, u32[]{:S(2)}, u32[]{:S(2)}) collective-permute-start(f32[1,64,4,128]{3,1,2,0:T(8,128)} %get-tuple-element.13), channel_id=1, source_target_pairs={{0,2},{2,4},{4,6},{6,8},{8,10},{10,12},{12,14},{14,16},{16,18},{18... | collective-permute-start | bytes 393224 | tf_op jit(solution)/shard_map/ppermute | solution.py:21
  7.0 7.9 %collective-permute-start.1 = (f32[1,64,4,128]{3,1,2,0:T(8,128)}, f32[1,64,4,128]{3,1,2,0:T(8,128)}, u32[]{:S(2)}, u32[]{:S(2)}) collective-permute-start(f32[1,64,4,128]{3,1,2,0:T(8,128)} %get-tuple-element.14), channel_id=1, source_target_pairs={{2,0},{4,2},{6,4},{8,6},{10,8},{12,10},{14,12},{16,14},{18,16},{20... | collective-permute-start | bytes 393224 | tf_op jit(solution)/shard_map/ppermute | solution.py:22
  15.7 2.6 %collective-permute-start.2 = (f32[4,1,4,128]{3,1,2,0:T(1,128)S(1)}, f32[4,1,4,128]{3,1,2,0:T(1,128)S(1)}, u32[]{:S(2)}, u32[]{:S(2)}) collective-permute-start(f32[4,1,4,128]{3,1,2,0:T(1,128)S(1)} %broadcast_select_fusion.3), channel_id=1, source_target_pairs={{0,1},{1,0},{2,3},{3,2},{4,5},{5,4},{6,7},{7,6},{8,9},{9,8},{10,11... | collective-permute-start | bytes 24584 | tf_op jit(solution)/shard_map/ppermute | solution.py:16
  19.3 11.0 %copy-start.6 = (s32[96]{0:T(128)S(1)}, s32[96]{0:T(128)}, u32[]{:S(2)}) copy-start(s32[96]{0:T(128)} %copy-done.5) | copy-start | bytes 1156
  27.0 17.9 %copy-start.7 = (f32[8,128]{1,0:T(8,128)S(1)}, f32[8,128]{1,0:T(8,128)}, u32[]{:S(2)}) copy-start(f32[8,128]{1,0:T(8,128)} %param.22) | copy-start | bytes 12292
  27.0 17.9 %copy-start.8 = (f32[8,128]{1,0:T(8,128)S(1)}, f32[8,128]{1,0:T(8,128)}, u32[]{:S(2)}) copy-start(f32[8,128]{1,0:T(8,128)} %param.23) | copy-start | bytes 12292
  28.0 34.9 %copy-start.9 = (pred[96]{0:T(512)(128)(4,1)S(1)}, pred[96]{0:T(512)(128)(4,1)}, u32[]{:S(2)}) copy-start(pred[96]{0:T(512)(128)(4,1)} %get-tuple-element.3) | copy-start | bytes 292
  30.8 33.0 %copy-start.10 = (s32[96]{0:T(128)S(1)}, s32[96]{0:T(128)}, u32[]{:S(2)}) copy-start(s32[96]{0:T(128)} %param.19) | copy-start | bytes 1156
  31.5 1.6 %collective-permute-start.3 = (f32[2,2,2,8,4,128]{5,3,4,2,1,0:T(8,128)}, f32[2,2,2,8,4,128]{5,3,4,2,1,0:T(8,128)S(1)}, u32[]{:S(2)}, u32[]{:S(2)}) collective-permute-start(f32[2,2,2,8,4,128]{5,3,4,2,1,0:T(8,128)} %bitcast.85), channel_id=1, source_target_pairs={{0,2},{2,0},{4,6},{6,4},{8,10},{10,8},{12,14},{14,12},{16,18},{18,... | collective-permute-start | bytes 393224 | tf_op jit(solution)/shard_map/ppermute | solution.py:48
  33.0 31.2 %copy-start.4 = (f32[128,128]{1,0:T(8,128)S(1)}, f32[128,128]{1,0:T(8,128)}, u32[]{:S(2)}) copy-start(f32[128,128]{1,0:T(8,128)} %param.16) | copy-start | bytes 196612
  33.1 4.9 %collective-permute-start.4 = (f32[2,2,8,4,128]{4,2,3,1,0:T(8,128)S(1)}, f32[2,2,8,4,128]{4,2,3,1,0:T(8,128)S(1)}, u32[]{:S(2)}, u32[]{:S(2)}) collective-permute-start(f32[2,2,8,4,128]{4,2,3,1,0:T(8,128)S(1)} %dynamic-slice_bitcast_fusion), channel_id=1, source_target_pairs={{0,4},{2,6},{4,0},{6,2},{8,12},{10,14},{12,8},{14,10},{16,20},{18,... | collective-permute-start | bytes 196616 | tf_op jit(solution)/shard_map/ppermute | solution.py:48
  38.0 3.3 %collective-permute-start.5 = (f32[2,8,4,128]{3,1,2,0:T(8,128)S(1)}, f32[2,8,4,128]{3,1,2,0:T(8,128)S(1)}, u32[]{:S(2)}, u32[]{:S(2)}) collective-permute-start(f32[2,8,4,128]{3,1,2,0:T(8,128)S(1)} %dynamic-slice_bitcast_fusion.1), channel_id=1, source_target_pairs={{0,8},{2,10},{4,12},{6,14},{8,0},{10,2},{12,4},{14,6},{16,24},{18,... | collective-permute-start | bytes 98312 | tf_op jit(solution)/shard_map/ppermute | solution.py:48
  41.3 3.7 %collective-permute-start.6 = (f32[8,4,128]{2,0,1:T(8,128)S(1)}, f32[8,4,128]{2,0,1:T(8,128)S(1)}, u32[]{:S(2)}, u32[]{:S(2)}) collective-permute-start(f32[8,4,128]{2,0,1:T(8,128)S(1)} %dynamic-slice_bitcast_fusion.2), channel_id=1, source_target_pairs={{0,16},{2,18},{4,20},{6,22},{8,24},{10,26},{12,28},{14,30},{16,0},... | collective-permute-start | bytes 49160 | tf_op jit(solution)/shard_map/ppermute | solution.py:48
  45.0 3.5 %collective-permute-start.7 = (bf16[8,4,128]{2,0,1:T(8,128)(2,1)S(1)}, bf16[8,4,128]{2,0,1:T(8,128)(2,1)S(1)}, u32[]{:S(2)}, u32[]{:S(2)}) collective-permute-start(bf16[8,4,128]{2,0,1:T(8,128)(2,1)S(1)} %get-tuple-element.20), channel_id=1, source_target_pairs={{0,16},{2,18},{4,20},{6,22},{8,24},{10,26},{12,28},{14,30},{16,0},... | collective-permute-start | bytes 24584 | tf_op jit(solution)/shard_map/ppermute | solution.py:62
  48.4 2.7 %collective-permute-start.8 = (bf16[2,8,4,128]{3,1,0,2:T(8,128)(2,1)S(1)}, bf16[2,8,4,128]{3,1,0,2:T(8,128)(2,1)S(1)}, u32[]{:S(2)}, u32[]{:S(2)}) collective-permute-start(bf16[2,8,4,128]{3,1,0,2:T(8,128)(2,1)S(1)} %pad_maximum_fusion.9), channel_id=1, source_target_pairs={{0,8},{2,10},{4,12},{6,14},{8,0},{10,2},{12,4},{14,6},{16,24},{18,... | collective-permute-start | bytes 49160 | tf_op jit(solution)/shard_map/ppermute | solution.py:62
  51.1 2.8 %collective-permute-start.9 = (bf16[2,2,8,4,128]{4,2,1,0,3:T(8,128)(2,1)S(1)}, bf16[2,2,8,4,128]{4,2,1,0,3:T(8,128)(2,1)S(1)}, u32[]{:S(2)}, u32[]{:S(2)}) collective-permute-start(bf16[2,2,8,4,128]{4,2,1,0,3:T(8,128)(2,1)S(1)} %pad_maximum_fusion.8), channel_id=1, source_target_pairs={{0,4},{2,6},{4,0},{6,2},{8,12},{10,14},{12,8},{14,10},{16,20},{18,... | collective-permute-start | bytes 98312 | tf_op jit(solution)/shard_map/ppermute | solution.py:62
  54.0 7.9 %collective-permute-start.10 = (bf16[2,2,2,8,4,128]{5,3,2,1,0,4:T(8,128)(2,1)S(1)}, bf16[2,2,2,8,4,128]{5,3,2,1,0,4:T(8,128)(2,1)S(1)}, u32[]{:S(2)}, u32[]{:S(2)}) collective-permute-start(bf16[2,2,2,8,4,128]{5,3,2,1,0,4:T(8,128)(2,1)S(1)} %pad_maximum_fusion.7), channel_id=1, source_target_pairs={{0,2},{2,0},{4,6},{6,4},{8,10},{10,8},{12,14},{14,12},{16,18},{18,... | collective-permute-start | bytes 196616 | tf_op jit(solution)/shard_map/ppermute | solution.py:62
  62.8 1.4 %copy-start.3 = (f32[2,64,4,128]{3,1,2,0:T(8,128)S(1)}, f32[2,64,4,128]{3,1,2,0:T(8,128)}, u32[]{:S(2)}) copy-start(f32[2,64,4,128]{3,1,2,0:T(8,128)} %get-tuple-element.39) | copy-start | bytes 786436
  62.8 13.9 %copy-start.1 = (f32[4,2,64,128]{3,2,1,0:T(8,128)S(1)}, f32[4,2,64,128]{3,2,1,0:T(8,128)}, u32[]{:S(2)}) copy-start(f32[4,2,64,128]{3,2,1,0:T(8,128)} %param.14) | copy-start | bytes 786436
  62.8 13.9 %copy-start.2 = (f32[2,64,128]{2,1,0:T(8,128)S(1)}, f32[2,64,128]{2,1,0:T(8,128)}, u32[]{:S(2)}) copy-start(f32[2,64,128]{2,1,0:T(8,128)} %param.13) | copy-start | bytes 196612
  64.6 4.8 %collective-permute-start.11 = (f32[1,64,4,128]{3,1,2,0:T(8,128)S(1)}, f32[1,64,4,128]{3,1,2,0:T(8,128)S(1)}, u32[]{:S(2)}, u32[]{:S(2)}) collective-permute-start(f32[1,64,4,128]{3,1,2,0:T(8,128)S(1)} %get-tuple-element.9), channel_id=1, source_target_pairs={{0,2},{2,4},{4,6},{6,8},{8,10},{10,12},{12,14},{14,16},{16,18},{18... | collective-permute-start | bytes 393224 | tf_op jit(solution)/shard_map/ppermute | solution.py:21
  67.5 6.6 %collective-permute-start.12 = (f32[1,64,4,128]{3,1,2,0:T(8,128)S(1)}, f32[1,64,4,128]{3,1,2,0:T(8,128)S(1)}, u32[]{:S(2)}, u32[]{:S(2)}) collective-permute-start(f32[1,64,4,128]{3,1,2,0:T(8,128)S(1)} %get-tuple-element.10), channel_id=1, source_target_pairs={{2,0},{4,2},{6,4},{8,6},{10,8},{12,10},{14,12},{16,14},{18,16},{20... | collective-permute-start | bytes 393224 | tf_op jit(solution)/shard_map/ppermute | solution.py:22
  74.1 2.6 %collective-permute-start.13 = (f32[4,1,4,128]{3,1,2,0:T(1,128)S(1)}, f32[4,1,4,128]{3,1,2,0:T(1,128)S(1)}, u32[]{:S(2)}, u32[]{:S(2)}) collective-permute-start(f32[4,1,4,128]{3,1,2,0:T(1,128)S(1)} %broadcast_select_fusion.1), channel_id=1, source_target_pairs={{0,1},{1,0},{2,3},{3,2},{4,5},{5,4},{6,7},{7,6},{8,9},{9,8},{10,11... | collective-permute-start | bytes 24584 | tf_op jit(solution)/shard_map/ppermute | solution.py:16
  (1 other events, 0.6 us)

commit v5 on v3

--- a/solution.py
+++ b/solution.py
@@ -6,7 +6,7 @@
 HIGH = lax.Precision.HIGHEST
 
 
-def exchange(cells, axis, dim):
+def edges(cells, axis, dim):
     count = lax.axis_size(axis)
     size = cells.shape[dim]
     head = lax.slice_in_dim(cells, 0, 1, axis=dim)
@@ -20,11 +20,38 @@
     else:
         below = lax.ppermute(tail, axis, [(i, i + 1) for i in range(count - 1)])
         above = lax.ppermute(head, axis, [(i + 1, i) for i in range(count - 1)])
-    return jnp.concatenate([below, cells, above], axis=dim)
+    return below, above
 
 
 def with_halo(cells):
-    return exchange(exchange(cells, "vox", 0), "star", 1)
+    below, above = edges(cells, "vox", 1)
+    extended = jnp.concatenate([below, cells, above], axis=1)
+    below, above = edges(extended, "star", 2)
+    rows = cells.shape[2]
+    spare = -(rows + 2) % 8
+    filler = jnp.zeros(extended.shape[:2] + (spare,) + extended.shape[3:], extended.dtype)
+    padded = jnp.concatenate([extended, below, above, filler], axis=2)
+    return padded.reshape(cells.shape[0], -1, cells.shape[3])
+
+
+def stencil_matrix(stencil, width_x, width_y, flip):
+    rows = width_y + 2 + (-(width_y + 2) % 8)
+    out = jnp.arange(width_x * width_y, dtype=jnp.int32)[:, None]
+    col = jnp.arange((width_x + 2) * rows, dtype=jnp.int32)[None, :]
+    out_x, out_y = out // width_y, out % width_y
+    col_x, place = col // rows, col % rows
+    col_y = jnp.where(place < width_y, place, jnp.where(place == width_y, -1, width_y))
+    if flip:
+        shift_x, shift_y = out_x + 2 - col_x, out_y + 1 - col_y
+    else:
+        shift_x, shift_y = col_x - out_x, col_y - out_y + 1
+    live = place < width_y + 2
+    matrix = jnp.zeros(shift_x.shape, jnp.float32)
+    for a in range(3):
+        for b in range(3):
+            hit = live & (shift_x == a) & (shift_y == b)
+            matrix = matrix + jnp.where(hit, stencil[a, b], 0.0)
+    return matrix
 
 
 def per_device(
@@ -47,21 +74,16 @@
     group_size = lax.axis_size("vox")
     star_count = observed.shape[0]
     group_blocks = group_size * star_count
-    latent = jnp.transpose(mean_field[None] + deviations, (1, 2, 0, 3))
-    padded = with_halo(latent)
-    smoothed = jnp.zeros(latent.shape, jnp.float32)
-    for offset_x in range(3):
-        for offset_y in range(3):
-            smoothed = (
-                smoothed
-                + stencil[offset_x, offset_y]
-                * padded[offset_x : offset_x + width_x, offset_y : offset_y + width_y]
-            )
-    log_density = jnp.einsum("xysw,zw->xysz", smoothed, vertical_mix, precision=HIGH) + log_mean
+    latent = mean_field[None] + deviations
+    forward = stencil_matrix(stencil, width_x, width_y, False)
+    smoothed = jnp.einsum("rc,scz->srz", forward, with_halo(latent), precision=HIGH).reshape(
+        latent.shape
+    )
+    log_density = jnp.einsum("sxyw,zw->sxyz", smoothed, vertical_mix, precision=HIGH) + log_mean
     density = jnp.exp(log_density)
-    density_b = density.astype(jnp.bfloat16).reshape(width_x * width_y, samples, length)
-    picked = jnp.take(density_b, pair_line, axis=0)
-    contribution = jnp.einsum("pij,psj->psi", responses, picked, preferred_element_type=jnp.float32)
+    density_b = density.astype(jnp.bfloat16).reshape(samples, width_x * width_y, length)
+    picked = jnp.take(density_b, pair_line, axis=1)
+    contribution = jnp.einsum("pij,spj->psi", responses, picked, preferred_element_type=jnp.float32)
     target = pair_owner[:, 0] * star_count + pair_star
     target_onehot = (
         target[:, None] == jnp.arange(group_blocks, dtype=jnp.int32)[None, :]
@@ -89,21 +111,14 @@
     line_onehot = (
         pair_line[:, None] == jnp.arange(width_x * width_y, dtype=jnp.int32)[None, :]
     ).astype(jnp.float32)
-    adjoint = jnp.einsum("pb,psj->bsj", line_onehot, pair_adjoint, precision=HIGH).reshape(
-        width_x, width_y, samples, length
+    adjoint = jnp.einsum("pb,psj->sbj", line_onehot, pair_adjoint, precision=HIGH).reshape(
+        samples, width_x, width_y, length
     )
-    grad_log = density * adjoint
-    grad_smooth = jnp.einsum("xysz,zw->xysw", grad_log, vertical_mix, precision=HIGH)
-    padded_grad = with_halo(grad_smooth)
-    grad_latent = jnp.zeros(latent.shape, jnp.float32)
-    for offset_x in range(3):
-        for offset_y in range(3):
-            grad_latent = (
-                grad_latent
-                + stencil[offset_x, offset_y]
-                * padded_grad[2 - offset_x : 2 - offset_x + width_x, 2 - offset_y : 2 - offset_y + width_y]
-            )
-    gradient = jnp.mean(grad_latent + latent, axis=2)
+    grad_log = jnp.mean(density * adjoint, axis=0)
+    grad_smooth = jnp.einsum("xyz,zw->xyw", grad_log, vertical_mix, precision=HIGH)
+    backward = stencil_matrix(stencil, width_x, width_y, True)
+    grad_latent = jnp.einsum("rc,scz->srz", backward, with_halo(grad_smooth[None]), precision=HIGH)
+    gradient = grad_latent.reshape(width_x, width_y, length) + jnp.mean(latent, axis=0)
     return (gradient, residual_mean)
 
 

time: 78.9 us -> 86.3 us (1.094)
  matrix products: 11.6 us -> 21.6 us
  other arithmetic: 15 us -> 12 us
  local copies, waits for them, and re-layouts: 4.82 us -> 6.18 us
  waiting for transfers between devices: 11.6 us -> 10.5 us
    dot_general x4 -> x6, matrix products: 10.2 us -> 19.3 us  [the longest x1 7.2 us: per_device(): jnp.einsum('rc,scz->srz', forward, with_halo(latent), precision=HIGH)]
    reduce_sum x1 -> x2, other arithmetic: 5.76 us -> 1.79 us  [the longest x1 1.76 us: per_device(): jnp.mean(latent, axis=0)]
    transpose x1 -> x0, other arithmetic: 1.13 us -> none  [per_device(): latent = jnp.transpose(mean_field[None] + deviations, (1, 2, 0, 3))]
    reduce_sum x1, other arithmetic: 0.02 us -> 0.97 us  [per_device(): extinction = jnp.sum(arrived, axis=0)]
    dot_general x1, matrix products: 0.97 us -> 1.89 us  [per_device(): jnp.einsum('pij,psi->psj', responses, pair_misfit, preferred_element_type...]
    select_n x5 -> x7, other arithmetic: 2.02 us -> 2.59 us  [the longest x2 0.76 us: edges(): jnp.where(index == 0, tail, head)]
  transfers between devices with their start and end apart: 7 -> 7, of which waited for: 3 -> 4; matrix products, arithmetic and copies ran while one was open for 9% -> 10% of each run, Pallas kernels for 0% -> 0%
where the time goes in v5:
time: 86.3 us; the launch traced here: 85.4 us
  matrix products  21.6 us (25%)
  starting transfers between devices  17.2 us (20%)
  blocking collectives  17 us (20%)
  other arithmetic  12 us (14%)
  waiting for transfers between devices  10.5 us (12%)
  local copies, waits for them, and re-layouts  6.18 us (7%)
  between operations  0.9 us (1%)
    all_to_all x1, blocking collectives, per_device(): lax.all_to_all(partial.reshape(group_size, star_count, samples, length),...  17 us
    dot_general x1, matrix products, per_device(): jnp.einsum('rc,scz->srz', forward, with_halo(latent), precision=HIGH)  7.2 us
    dot_general x1, matrix products, per_device(): jnp.einsum('rc,scz->srz', backward, with_halo(grad_smooth[None]), precisi...  7.01 us
    ppermute x2, starting transfers between devices, edges(): below = lax.ppermute(tail, axis, [(i, i + 1) for i in range(count - 1)])  6.57 us
    all_to_all x1, waiting for transfers between devices, per_device(): lax.all_to_all(spread, 'vox', split_axis=0, concat_axis=0, tiled=True)  6.34 us
    ppermute x2, starting transfers between devices, edges(): above = lax.ppermute(head, axis, [(i + 1, i) for i in range(count - 1)])  4.24 us
    all_to_all x1, starting transfers between devices, per_device(): lax.all_to_all(spread, 'vox', split_axis=0, concat_axis=0, tiled=True)  3.95 us
    ppermute x2, waiting for transfers between devices, edges(): above = lax.ppermute(head, axis, [(i + 1, i) for i in range(count - 1)])  2.89 us
  transfers between devices with their start and end apart: 7, of which 4 were waited for; matrix products, arithmetic and copies ran while one was open for 10% of the time, Pallas kernels for 0%

profile of v5, /device:TPU:1, one launch (start us, length us, event | category | flops | bytes accessed | tf_op | source)
XLA Modules:
  0.0 85.4 jit_solution(12959631109518614616)
XLA Ops:
  0.6 1.8 %fusion.161 = (f32[2,64,128]{2,1,0:T(8,128)}, f32[4,2,64,128]{3,2,1,0:T(8,128)S(1)}) fusion(f32[4,2,64,128]{3,2,1,0:T(8,128)} %param.12, f32[2,64,128]{2,1,0:T(8,128)} %param.11), kind=kLoop, calls=%fused_computation.195 | loop fusion | flops 114688 | bytes 655360 | tf_op jit(solution)/shard_map/reduce_sum | solution.py:121
  3.1 4.5 %collective-permute-start = (f32[4,1,64,128]{3,2,1,0:T(8,128)}, f32[4,1,64,128]{3,2,1,0:T(8,128)S(1)}, u32[]{:S(2)}, u32[]{:S(2)}) collective-permute-start(f32[4,1,64,128]{3,2,1,0:T(8,128)} %get-tuple-element.6), channel_id=1, source_target_pairs={{0,2},{2,4},{4,6},{6,8},{8,10},{10,12},{12,14},{14,16},{16,18},{18... | collective-permute-start | bytes 393224 | tf_op jit(solution)/shard_map/ppermute | solution.py:21
  7.7 1.9 %collective-permute-start.1 = (f32[4,1,64,128]{3,2,1,0:T(8,128)}, f32[4,1,64,128]{3,2,1,0:T(8,128)}, u32[]{:S(2)}, u32[]{:S(2)}) collective-permute-start(f32[4,1,64,128]{3,2,1,0:T(8,128)} %get-tuple-element.7), channel_id=1, source_target_pairs={{2,0},{4,2},{6,4},{8,6},{10,8},{12,10},{14,12},{16,14},{18,16},{20... | collective-permute-start | bytes 393224 | tf_op jit(solution)/shard_map/ppermute | solution.py:22
  10.8 1.2 %compare_and_fusion = pred[96]{0:T(512)(128)(4,1)} fusion(s32[96]{0:T(128)} %param.17), kind=kLoop, calls=%fused_computation.174 | loop fusion | flops 576 | bytes 480 | tf_op jit(solution)/shard_map/jit(_take)/and | solution.py:85
  12.7 1.2 %compare_and_fusion.1 = (pred[96]{0:T(512)(128)(4,1)}, s32[96]{0:T(128)}) fusion(s32[96]{0:T(128)} %param.19, s32[96,1]{0,1:T(1,128)} %param.18), kind=kLoop, calls=%fused_computation.175 | loop fusion | flops 768 | bytes 1248 | tf_op jit(solution)/shard_map/jit(_take)/and | solution.py:107
  14.5 1.7 %fusion.164 = (f32[1,1]{1,0:T(1,128)}, f32[1,1]{1,0:T(1,128)}, f32[1,1]{1,0:T(1,128)}, f32[1,1]{1,0:T(1,128)}, f32[1,1]{1,0:T(1,128)}, /*index=5*/f32[1,1]{1,0:T...) fusion(f32[3,3]{1,0:T(4,128)} %param.13), kind=kLoop, calls=%fused_computation.198 | loop fusion | bytes 72 | tf_op jit(solution)/shard_map/slice | solution.py:53
  16.9 1.3 %collective-permute-start.2 = (f32[4,4,1,128]{3,2,1,0:T(1,128)S(1)}, f32[4,4,1,128]{3,2,1,0:T(1,128)S(1)}, u32[]{:S(2)}, u32[]{:S(2)}) collective-permute-start(f32[4,4,1,128]{3,2,1,0:T(1,128)S(1)} %broadcast_select_fusion.1), channel_id=1, source_target_pairs={{0,1},{1,0},{2,3},{3,2},{4,5},{5,4},{6,7},{7,6},{8,9},{9,8},{10,11... | collective-permute-start | bytes 24584 | tf_op jit(solution)/shard_map/ppermute | solution.py:16
  19.5 1.0 %maximum_maximum_fusion = f32[4,4,72,128]{3,2,1,0:T(8,128)S(1)} fusion(f32[4,4,1,128]{3,2,1,0:T(1,128)S(1)} %get-tuple-element.13, f32[4,4,1,128]{3,2,1,0:T(1,128)S(1)} %get-tuple-element.12, f32[4,1,64,128]{3,2,1,0:T(8,128)} %collective-permute-done.1, f32[4,2,64,128]{3,2,1,0:T(8,128)S(1)} %get-tuple-element.3, ...), kind=kLoop, calls=%fused_computation.6 | loop fusion | flops 737280 | bytes 1130784 | tf_op jit(solution)/shard_map/concatenate | solution.py:33
  20.6 7.2 %fusion.13 = f32[4,128,128]{1,2,0:T(8,128)S(1)} fusion(f32[4,288,128]{2,1,0:T(8,128)S(1)} %bitcast.59, f32[]{:T(128)} %bitcast.9, f32[]{:T(128)} %bitcast.8, f32[]{:T(128)} %bitcast.7, f32[]{:T(128)} %bitcast.6, f32[]{:T(128)} %bitcast.5, f32[]{:T(128)} %bitcast.4, f32[]{:T(128)} %bitcast.3, f32[]{:T(128)} %bitcast.2, f32[]{:T(128)} %bitcast.1, ...), kind=kOutput, calls=%fused_computation.30 | convolution fusion | flops 227893248 | bytes 855620 | tf_op jit(solution)/shard_map/rc,scz->srz/dot_general | solution.py:79
  27.8 1.2 %fusion.165 = (bf16[4,2,64,128]{3,2,1,0:T(8,128)(2,1)S(1)}, f32[4,2,64,128]{3,2,1,0:T(8,128)S(1)}) fusion(f32[128]{0:T(128)} %param.15, f32[4,2,64,128]{3,2,1,0:T(8,128)S(1)} %bitcast.62, f32[128,128]{1,0:T(8,128)} %param.14), kind=kOutput, calls=%fused_computation.199 | convolution fusion | flops 100794368 | bytes 721408 | tf_op jit(solution)/shard_map/sxyw,zw->sxyz/dot_general | solution.py:82
  29.2 1.5 %gather_fusion = bf16[96,4,128]{2,1,0:T(4,128)(2,1)} fusion(bf16[4,128,128]{2,0,1:T(4,128)(2,1)S(1)} %copy.14, s32[1024]{0:T(1024)} %pad_clamp_fusion.1), kind=kCustom, calls=%fused_computation | custom fusion | bytes 196992 | tf_op jit(solution)/shard_map/jit(_take)/gather | solution.py:85
  30.6 2.6 %fusion.86 = f32[96,4,128]{2,1,0:T(4,128)S(1)} fusion(bf16[96,128,128]{2,1,0:T(8,128)(2,1)S(1)} %copy-done, bf16[96,4,128]{2,1,0:T(4,128)(2,1)} %gather_fusion, pred[96]{0:T(512)(128)(4,1)S(1)} %copy-done.8), kind=kOutput, calls=%fused_computation.87 | convolution fusion | flops 12632064 | bytes 3440736 | tf_op jit(solution)/shard_map/pij,spj->psi/dot_general | solution.py:86
  33.7 17.0 %all_to_all.10 = f32[16,8,4,128]{3,1,2,0:T(8,128)} all-to-all(f32[16,8,4,128]{3,1,2,0:T(8,128)S(1)} %copy.16), channel_id=1, replica_groups=mesh['vox'=16,'star'=2] {'vox'}, dimensions={0} | all-to-all | bytes 524288 | tf_op jit(solution)/shard_map/all_to_all | solution.py:92
  50.7 1.0 %reduce_sum.36 = f32[8,4,128]{2,0,1:T(8,128)S(1)} reduce(f32[16,8,4,128]{3,1,2,0:T(8,128)} %all_to_all.10, f32[]{:T(128)} %constant.104.clone.1), dimensions={0}, to_apply=%region_0.1 | reduce | flops 61440 | bytes 278532 | tf_op jit(solution)/shard_map/reduce_sum | solution.py:99
  52.5 4.0 %all-to-all-start.1 = ((bf16[16,8,4,128]{3,2,1,0:T(4,128)(2,1)}), bf16[16,8,4,128]{3,2,1,0:T(4,128)(2,1)S(1)}, u32[]{:S(2)}, u32[]{:S(2)}) async-start(bf16[16,8,4,128]{3,2,1,0:T(4,128)(2,1)} %broadcast_in_dim.137), calls=%async_computation.1 | async-start | bytes 262144 | tf_op jit(solution)/shard_map/all_to_all | solution.py:104
  57.0 6.3 %all-to-all-done.1 = bf16[16,8,4,128]{3,2,1,0:T(4,128)(2,1)S(1)} async-done(((bf16[16,8,4,128]{3,2,1,0:T(4,128)(2,1)}), bf16[16,8,4,128]{3,2,1,0:T(4,128)(2,1)S(1)}, u32[]{:S(2)}, u32[]{:S(2)}) %all-to-all-start.1) | async-done | bytes 131104 | tf_op jit(solution)/shard_map/all_to_all | solution.py:104
  63.4 1.4 %gather_fusion.1 = bf16[96,4,128]{2,1,0:T(4,128)(2,1)} fusion(bf16[128,4,128]{2,1,0:T(4,128)(2,1)S(1)} %bitcast.61, s32[1024]{0:T(1024)S(1)} %pad_clamp_fusion), kind=kCustom, calls=%fused_computation.1 | custom fusion | bytes 196992 | tf_op jit(solution)/shard_map/jit(_take)/gather | solution.py:107
  64.7 1.9 %fusion.89 = f32[96,4,128]{2,1,0:T(4,128)S(1)} fusion(bf16[96,128,128]{2,1,0:T(8,128)(2,1)S(1)} %copy-done, bf16[96,4,128]{2,1,0:T(4,128)(2,1)} %gather_fusion.1, pred[96]{0:T(512)(128)(4,1)} %get-tuple-element.4), kind=kOutput, calls=%fused_computation.90 | convolution fusion | flops 12632064 | bytes 3440736 | tf_op jit(solution)/shard_map/pij,psi->psj/dot_general | solution.py:108
  66.6 1.1 %fusion.1 = f32[4,128,128]{1,2,0:T(8,128)S(1)} fusion(f32[96,4,128]{2,1,0:T(4,128)S(1)} %fusion.89, s32[96]{0:T(128)} %param.17), kind=kOutput, calls=%fused_computation.17 | convolution fusion | flops 75509760 | bytes 459136 | tf_op jit(solution)/shard_map/pb,psj->sbj/dot_general | solution.py:114
  67.9 2.0 %collective-permute-start.3 = (f32[1,1,64,128]{3,2,1,0:T(8,128)S(1)}, f32[1,1,64,128]{3,2,1,0:T(8,128)S(1)}, u32[]{:S(2)}, u32[]{:S(2)}) collective-permute-start(f32[1,1,64,128]{3,2,1,0:T(8,128)S(1)} %get-tuple-element.8), channel_id=1, source_target_pairs={{0,2},{2,4},{4,6},{6,8},{8,10},{10,12},{12,14},{14,16},{16,18},{18... | collective-permute-start | bytes 98312 | tf_op jit(solution)/shard_map/ppermute | solution.py:21
  70.0 2.3 %collective-permute-start.4 = (f32[1,1,64,128]{3,2,1,0:T(8,128)S(1)}, f32[1,1,64,128]{3,2,1,0:T(8,128)S(1)}, u32[]{:S(2)}, u32[]{:S(2)}) collective-permute-start(f32[1,1,64,128]{3,2,1,0:T(8,128)S(1)} %get-tuple-element.9), channel_id=1, source_target_pairs={{2,0},{4,2},{6,4},{8,6},{10,8},{12,10},{14,12},{16,14},{18,16},{20... | collective-permute-start | bytes 98312 | tf_op jit(solution)/shard_map/ppermute | solution.py:22
  72.3 2.9 %collective-permute-done.4 = f32[1,1,64,128]{3,2,1,0:T(8,128)S(1)} collective-permute-done((f32[1,1,64,128]{3,2,1,0:T(8,128)S(1)}, f32[1,1,64,128]{3,2,1,0:T(8,128)S(1)}, u32[]{:S(2)}, u32[]{:S(2)}) %collective-permute-start.4) | collective-permute-done | bytes 32800 | tf_op jit(solution)/shard_map/ppermute | solution.py:22
  75.2 1.2 %collective-permute-start.5 = (f32[1,4,1,128]{3,2,1,0:T(1,128)S(1)}, f32[1,4,1,128]{3,2,1,0:T(1,128)S(1)}, u32[]{:S(2)}, u32[]{:S(2)}) collective-permute-start(f32[1,4,1,128]{3,2,1,0:T(1,128)S(1)} %broadcast_select_fusion.4), channel_id=1, source_target_pairs={{0,1},{1,0},{2,3},{3,2},{4,5},{5,4},{6,7},{7,6},{8,9},{9,8},{10,11... | collective-permute-start | bytes 6152 | tf_op jit(solution)/shard_map/ppermute | solution.py:16
  77.8 7.0 %fusion.15 = f32[128,128]{0,1:T(8,128)S(1)} fusion(f32[288,128]{1,0:T(8,128)S(1)} %bitcast.63, s32[128]{0:T(128)S(1)} %get-tuple-element.32, s32[128]{0:T(128)S(1)} %get-tuple-element.31, f32[]{:T(128)} %bitcast.9, f32[]{:T(128)} %bitcast.8, f32[]{:T(128)} %bitcast.7, f32[]{:T(128)} %bitcast.6, f32[]{:T(128)} %bitcast.5, f32[]{:T(128)} %bitcast.4, ...), kind=kOutput, calls=%fused_computation.32 | convolution fusion | flops 57987072 | bytes 216644 | tf_op jit(solution)/shard_map/rc,scz->srz/dot_general | solution.py:120
  (50 shorter events, 9.3 us)
Async XLA Ops:
  0.6 30.0 %copy-start = (bf16[96,128,128]{2,1,0:T(8,128)(2,1)S(1)}, bf16[96,128,128]{2,1,0:T(8,128)(2,1)}, u32[]{:S(2)}) copy-start(bf16[96,128,128]{2,1,0:T(8,128)(2,1)} %param.16) | copy-start | bytes 9437188
  3.1 13.0 %collective-permute-start = (f32[4,1,64,128]{3,2,1,0:T(8,128)}, f32[4,1,64,128]{3,2,1,0:T(8,128)S(1)}, u32[]{:S(2)}, u32[]{:S(2)}) collective-permute-start(f32[4,1,64,128]{3,2,1,0:T(8,128)} %get-tuple-element.6), channel_id=1, source_target_pairs={{0,2},{2,4},{4,6},{6,8},{8,10},{10,12},{12,14},{14,16},{16,18},{18... | collective-permute-start | bytes 393224 | tf_op jit(solution)/shard_map/ppermute | solution.py:21
  7.7 8.5 %collective-permute-start.1 = (f32[4,1,64,128]{3,2,1,0:T(8,128)}, f32[4,1,64,128]{3,2,1,0:T(8,128)}, u32[]{:S(2)}, u32[]{:S(2)}) collective-permute-start(f32[4,1,64,128]{3,2,1,0:T(8,128)} %get-tuple-element.7), channel_id=1, source_target_pairs={{2,0},{4,2},{6,4},{8,6},{10,8},{12,10},{14,12},{16,14},{18,16},{20... | collective-permute-start | bytes 393224 | tf_op jit(solution)/shard_map/ppermute | solution.py:22
  16.9 2.6 %collective-permute-start.2 = (f32[4,4,1,128]{3,2,1,0:T(1,128)S(1)}, f32[4,4,1,128]{3,2,1,0:T(1,128)S(1)}, u32[]{:S(2)}, u32[]{:S(2)}) collective-permute-start(f32[4,4,1,128]{3,2,1,0:T(1,128)S(1)} %broadcast_select_fusion.1), channel_id=1, source_target_pairs={{0,1},{1,0},{2,3},{3,2},{4,5},{5,4},{6,7},{7,6},{8,9},{9,8},{10,11... | collective-permute-start | bytes 24584 | tf_op jit(solution)/shard_map/ppermute | solution.py:16
  18.9 1.7 %copy-start.5 = (f32[72]{0:T(128)}, f32[72]{0:T(128)S(1)}, u32[]{:S(2)}) copy-start(f32[72]{0:T(128)S(1)} %pad.14.clone) | copy-start | bytes 868
  19.5 11.1 %copy-start.8 = (pred[96]{0:T(512)(128)(4,1)S(1)}, pred[96]{0:T(512)(128)(4,1)}, u32[]{:S(2)}) copy-start(pred[96]{0:T(512)(128)(4,1)} %compare_and_fusion) | copy-start | bytes 292
  20.6 12.7 %copy-start.7 = (s32[96]{0:T(128)S(1)}, s32[96]{0:T(128)}, u32[]{:S(2)}) copy-start(s32[96]{0:T(128)} %get-tuple-element.5) | copy-start | bytes 1156
  27.8 23.9 %copy-start.3 = (f32[8,128]{1,0:T(8,128)S(1)}, f32[8,128]{1,0:T(8,128)}, u32[]{:S(2)}) copy-start(f32[8,128]{1,0:T(8,128)} %param.20) | copy-start | bytes 12292
  27.8 23.9 %copy-start.4 = (f32[8,128]{1,0:T(8,128)S(1)}, f32[8,128]{1,0:T(8,128)}, u32[]{:S(2)}) copy-start(f32[8,128]{1,0:T(8,128)} %param.21) | copy-start | bytes 12292
  33.7 44.0 %copy-start.6 = (f32[72]{0:T(128)S(1)}, f32[72]{0:T(128)}, u32[]{:S(2)}) copy-start(f32[72]{0:T(128)} %copy-done.5) | copy-start | bytes 868
  52.5 10.9 %all-to-all-start.1 = ((bf16[16,8,4,128]{3,2,1,0:T(4,128)(2,1)}), bf16[16,8,4,128]{3,2,1,0:T(4,128)(2,1)S(1)}, u32[]{:S(2)}, u32[]{:S(2)}) async-start(bf16[16,8,4,128]{3,2,1,0:T(4,128)(2,1)} %broadcast_in_dim.137), calls=%async_computation.1 | async-start | bytes 262144 | tf_op jit(solution)/shard_map/all_to_all | solution.py:104
  64.7 3.0 %copy-start.1 = (f32[128,128]{1,0:T(8,128)S(1)}, f32[128,128]{1,0:T(8,128)}, u32[]{:S(2)}) copy-start(f32[128,128]{1,0:T(8,128)} %param.14) | copy-start | bytes 196612
  64.7 20.1 %copy-start.2 = (f32[2,64,128]{2,1,0:T(8,128)S(1)}, f32[2,64,128]{2,1,0:T(8,128)}, u32[]{:S(2)}) copy-start(f32[2,64,128]{2,1,0:T(8,128)} %get-tuple-element.2) | copy-start | bytes 196612
  67.9 4.4 %collective-permute-start.3 = (f32[1,1,64,128]{3,2,1,0:T(8,128)S(1)}, f32[1,1,64,128]{3,2,1,0:T(8,128)S(1)}, u32[]{:S(2)}, u32[]{:S(2)}) collective-permute-start(f32[1,1,64,128]{3,2,1,0:T(8,128)S(1)} %get-tuple-element.8), channel_id=1, source_target_pairs={{0,2},{2,4},{4,6},{6,8},{8,10},{10,12},{12,14},{14,16},{16,18},{18... | collective-permute-start | bytes 98312 | tf_op jit(solution)/shard_map/ppermute | solution.py:21
  70.0 5.2 %collective-permute-start.4 = (f32[1,1,64,128]{3,2,1,0:T(8,128)S(1)}, f32[1,1,64,128]{3,2,1,0:T(8,128)S(1)}, u32[]{:S(2)}, u32[]{:S(2)}) collective-permute-start(f32[1,1,64,128]{3,2,1,0:T(8,128)S(1)} %get-tuple-element.9), channel_id=1, source_target_pairs={{2,0},{4,2},{6,4},{8,6},{10,8},{12,10},{14,12},{16,14},{18,16},{20... | collective-permute-start | bytes 98312 | tf_op jit(solution)/shard_map/ppermute | solution.py:22
  75.2 2.4 %collective-permute-start.5 = (f32[1,4,1,128]{3,2,1,0:T(1,128)S(1)}, f32[1,4,1,128]{3,2,1,0:T(1,128)S(1)}, u32[]{:S(2)}, u32[]{:S(2)}) collective-permute-start(f32[1,4,1,128]{3,2,1,0:T(1,128)S(1)} %broadcast_select_fusion.4), channel_id=1, source_target_pairs={{0,1},{1,0},{2,3},{3,2},{4,5},{5,4},{6,7},{7,6},{8,9},{9,8},{10,11... | collective-permute-start | bytes 6152 | tf_op jit(solution)/shard_map/ppermute | solution.py:16

commit v6 on v5

--- a/solution.py
+++ b/solution.py
@@ -51,7 +51,7 @@
         for b in range(3):
             hit = live & (shift_x == a) & (shift_y == b)
             matrix = matrix + jnp.where(hit, stencil[a, b], 0.0)
-    return matrix
+    return lax.optimization_barrier(matrix)
 
 
 def per_device(

time: 86.3 us -> 89.4 us (1.036)
  the two profiles are of different devices: /device:TPU:1 before, /device:TPU:8 now
where the time goes in v6:
time: 89.4 us; the launch traced here: 88.5 us
  other arithmetic  25.1 us (28%)
  starting transfers between devices  19.1 us (21%)
  blocking collectives  14.6 us (16%)
  waiting for transfers between devices  11.3 us (13%)
  matrix products  8.89 us (10%)
  local copies, waits for them, and re-layouts  8.71 us (10%)
    all_to_all x1, blocking collectives, per_device(): lax.all_to_all(partial.reshape(group_size, star_count, samples, length),...  14.6 us
    add x1, other arithmetic, stencil_matrix(): matrix = matrix + jnp.where(hit, stencil[a, b], 0.0)  7.6 us
    ppermute x2, starting transfers between devices, edges(): above = lax.ppermute(head, axis, [(i + 1, i) for i in range(count - 1)])  6.35 us
    all_to_all x1, starting transfers between devices, per_device(): lax.all_to_all(spread, 'vox', split_axis=0, concat_axis=0, tiled=True)  5.92 us
    all_to_all x1, waiting for transfers between devices, per_device(): lax.all_to_all(spread, 'vox', split_axis=0, concat_axis=0, tiled=True)  4.38 us
    ppermute x2, waiting for transfers between devices, edges(): below = lax.ppermute(tail, axis, [(i, i + 1) for i in range(count - 1)])  4.2 us
    ppermute x2, starting transfers between devices, edges(): below = lax.ppermute(tail, axis, [(i, i + 1) for i in range(count - 1)])  3.84 us
    ppermute x2, starting transfers between devices, edges(): lax.ppermute(jnp.where(index == 0, tail, head), axis, [(0, 1), (1, 0)])  2.98 us
  transfers between devices with their start and end apart: 7, of which 4 were waited for; matrix products, arithmetic and copies ran while one was open for 21% of the time, Pallas kernels for 0%

profile of v6, /device:TPU:8, one launch (start us, length us, event | category | flops | bytes accessed | tf_op | source)
XLA Modules:
  0.0 88.5 jit_solution(5448314961129237211)
XLA Ops:
  0.6 1.8 %fusion.55 = (f32[2,64,128]{2,1,0:T(8,128)}, f32[4,2,64,128]{3,2,1,0:T(8,128)S(1)}) fusion(f32[4,2,64,128]{3,2,1,0:T(8,128)} %param.12, f32[2,64,128]{2,1,0:T(8,128)} %param.11), kind=kLoop, calls=%fused_computation.109 | loop fusion | flops 114688 | bytes 655360 | tf_op jit(solution)/shard_map/reduce_sum | solution.py:121
  3.1 2.7 %collective-permute-start.1 = (f32[4,1,64,128]{3,2,1,0:T(8,128)}, f32[4,1,64,128]{3,2,1,0:T(8,128)}, u32[]{:S(2)}, u32[]{:S(2)}) collective-permute-start(f32[4,1,64,128]{3,2,1,0:T(8,128)} %get-tuple-element.7), channel_id=1, source_target_pairs={{2,0},{4,2},{6,4},{8,6},{10,8},{12,10},{14,12},{16,14},{18,16},{20... | collective-permute-start | bytes 393224 | tf_op jit(solution)/shard_map/ppermute | solution.py:22
  5.9 1.9 %collective-permute-start = (f32[4,1,64,128]{3,2,1,0:T(8,128)}, f32[4,1,64,128]{3,2,1,0:T(8,128)}, u32[]{:S(2)}, u32[]{:S(2)}) collective-permute-start(f32[4,1,64,128]{3,2,1,0:T(8,128)} %get-tuple-element.6), channel_id=1, source_target_pairs={{0,2},{2,4},{4,6},{6,8},{8,10},{10,12},{12,14},{14,16},{16,18},{18... | collective-permute-start | bytes 393224 | tf_op jit(solution)/shard_map/ppermute | solution.py:21
  10.1 1.7 %fusion.58 = (f32[1,1]{1,0:T(1,128)}, f32[1,1]{1,0:T(1,128)}, f32[1,1]{1,0:T(1,128)}, f32[1,1]{1,0:T(1,128)}, f32[1,1]{1,0:T(1,128)}, /*index=5*/f32[1,1]{1,0:T(...) fusion(f32[3,3]{1,0:T(4,128)} %param.13), kind=kLoop, calls=%fused_computation.112 | loop fusion | bytes 72 | tf_op jit(solution)/shard_map/slice | solution.py:53
  12.9 1.3 %compare_and_fusion.1 = (pred[96]{0:T(512)(128)(4,1)}, s32[96]{0:T(128)}) fusion(s32[96]{0:T(128)} %param.19, s32[96,1]{0,1:T(1,128)} %param.18), kind=kLoop, calls=%fused_computation.97 | loop fusion | flops 768 | bytes 1248 | tf_op jit(solution)/shard_map/jit(_take)/and | solution.py:107
  14.2 7.6 %select_add_fusion = (f32[128,288]{0,1:T(8,128)S(1)}, f32[128,288]{0,1:T(8,128)}) fusion(s32[128]{0:T(128)} %get-tuple-element.34, s32[128]{0:T(128)} %get-tuple-element.33, f32[]{:T(128)} %bitcast.9, f32[]{:T(128)} %bitcast.8, f32[]{:T(128)} %bitcast.7, f32[]{:T(128)} %bitcast.6, f32[]{:T(128)} %bitcast.5, f32[]{:T(128)} %bitcast.4, f32[]{:T(128)} %bitcast.3, ...), kind=kLoop, calls=%fused_computation.32 | loop fusion | flops 2764800 | bytes 299588 | tf_op jit(solution)/shard_map/add | solution.py:53
  23.0 1.4 %broadcast_select_fusion.1 = f32[4,4,1,128]{3,2,1,0:T(1,128)} fusion(pred[]{:T(512)S(6)} %eq.194, f32[4,1,64,128]{3,2,1,0:T(8,128)} %collective-permute-done.1, f32[4,2,64,128]{3,2,1,0:T(8,128)S(1)} %get-tuple-element.3, f32[4,1,64,128]{3,2,1,0:T(8,128)} %collective-permute-done), kind=kLoop, calls=%fused_computation.67 | loop fusion | flops 10240 | bytes 532481 | tf_op jit(solution)/shard_map/jit(_where)/select_n | solution.py:16
  24.4 1.5 %collective-permute-start.2 = (f32[4,4,1,128]{3,2,1,0:T(1,128)}, f32[4,4,1,128]{3,2,1,0:T(1,128)}, u32[]{:S(2)}, u32[]{:S(2)}) collective-permute-start(f32[4,4,1,128]{3,2,1,0:T(1,128)} %broadcast_select_fusion.1), channel_id=1, source_target_pairs={{0,1},{1,0},{2,3},{3,2},{4,5},{5,4},{6,7},{7,6},{8,9},{9,8},{10,11... | collective-permute-start | bytes 24584 | tf_op jit(solution)/shard_map/ppermute | solution.py:16
  30.2 1.6 %fusion.13 = f32[4,128,128]{1,2,0:T(8,128)S(1)} fusion(f32[4,288,128]{2,1,0:T(8,128)S(1)} %bitcast.59, f32[128,288]{0,1:T(8,128)} %get-tuple-element.15), kind=kOutput, calls=%fused_computation.30 | convolution fusion | flops 226492416 | bytes 999424 | tf_op jit(solution)/shard_map/rc,scz->srz/dot_general | solution.py:79
  31.7 1.2 %fusion.59 = (bf16[4,2,64,128]{3,2,1,0:T(8,128)(2,1)S(1)}, f32[4,2,64,128]{3,2,1,0:T(8,128)S(1)}) fusion(f32[128]{0:T(128)} %param.15, f32[4,2,64,128]{3,2,1,0:T(8,128)S(1)} %bitcast.61, f32[128,128]{1,0:T(8,128)} %param.14), kind=kOutput, calls=%fused_computation.113 | convolution fusion | flops 100794368 | bytes 721408 | tf_op jit(solution)/shard_map/sxyw,zw->sxyz/dot_general | solution.py:82
  33.7 2.4 %gather_fusion = bf16[96,4,128]{2,1,0:T(4,128)(2,1)} fusion(bf16[4,128,128]{2,0,1:T(4,128)(2,1)} %copy.14, s32[1024]{0:T(1024)} %pad_clamp_fusion.1), kind=kCustom, calls=%fused_computation | custom fusion | bytes 196992 | tf_op jit(solution)/shard_map/jit(_take)/gather | solution.py:85
  36.1 2.6 %fusion.24 = f32[96,4,128]{2,1,0:T(4,128)S(1)} fusion(bf16[96,128,128]{2,1,0:T(8,128)(2,1)S(1)} %copy-done, bf16[96,4,128]{2,1,0:T(4,128)(2,1)} %gather_fusion, pred[96]{0:T(512)(128)(4,1)} %compare_and_fusion), kind=kOutput, calls=%fused_computation.45 | convolution fusion | flops 12632064 | bytes 3440736 | tf_op jit(solution)/shard_map/pij,spj->psi/dot_general | solution.py:86
  39.2 14.6 %all_to_all.10 = f32[16,8,4,128]{3,1,2,0:T(8,128)} all-to-all(f32[16,8,4,128]{3,1,2,0:T(8,128)S(1)} %copy.16), channel_id=1, replica_groups=mesh['vox'=16,'star'=2] {'vox'}, dimensions={0} | all-to-all | bytes 524288 | tf_op jit(solution)/shard_map/all_to_all | solution.py:92
  53.8 1.6 %reduce_sum.36 = f32[8,4,128]{2,0,1:T(8,128)} reduce(f32[16,8,4,128]{3,1,2,0:T(8,128)} %all_to_all.10, f32[]{:T(128)} %constant.104.clone.1), dimensions={0}, to_apply=%region_0.1 | reduce | flops 61440 | bytes 278532 | tf_op jit(solution)/shard_map/reduce_sum | solution.py:99
  55.4 1.3 %fusion.43 = (f32[8,128]{1,0:T(8,128)}, bf16[8,4,128]{2,0,1:T(8,128)(2,1)S(1)}) fusion(f32[8,4,128]{2,0,1:T(8,128)} %reduce_sum.36, f32[8,128]{1,0:T(8,128)} %param.20, f32[8,128]{1,0:T(8,128)} %param.21), kind=kLoop, calls=%fused_computation.69 | loop fusion | flops 15360 | bytes 36864 | tf_op jit(solution)/shard_map/reduce_sum | solution.py:101
  57.4 5.9 %all-to-all-start.1 = ((bf16[16,8,4,128]{3,2,1,0:T(4,128)(2,1)}), bf16[16,8,4,128]{3,2,1,0:T(4,128)(2,1)}, u32[]{:S(2)}, u32[]{:S(2)}) async-start(bf16[16,8,4,128]{3,2,1,0:T(4,128)(2,1)} %broadcast_in_dim.137), calls=%async_computation.1 | async-start | bytes 262144 | tf_op jit(solution)/shard_map/all_to_all | solution.py:104
  64.5 4.4 %all-to-all-done.1 = bf16[16,8,4,128]{3,2,1,0:T(4,128)(2,1)} async-done(((bf16[16,8,4,128]{3,2,1,0:T(4,128)(2,1)}), bf16[16,8,4,128]{3,2,1,0:T(4,128)(2,1)}, u32[]{:S(2)}, u32[]{:S(2)}) %all-to-all-start.1) | async-done | bytes 131104 | tf_op jit(solution)/shard_map/all_to_all | solution.py:104
  68.9 2.4 %gather_fusion.1 = bf16[96,4,128]{2,1,0:T(4,128)(2,1)} fusion(bf16[128,4,128]{2,1,0:T(4,128)(2,1)} %bitcast.20, s32[1024]{0:T(1024)} %pad_clamp_fusion), kind=kCustom, calls=%fused_computation.1 | custom fusion | bytes 196992 | tf_op jit(solution)/shard_map/jit(_take)/gather | solution.py:107
  71.3 1.9 %fusion.27 = f32[96,4,128]{2,1,0:T(4,128)S(1)} fusion(bf16[96,128,128]{2,1,0:T(8,128)(2,1)S(1)} %copy-done, bf16[96,4,128]{2,1,0:T(4,128)(2,1)} %gather_fusion.1, pred[96]{0:T(512)(128)(4,1)} %get-tuple-element.4), kind=kOutput, calls=%fused_computation.48 | convolution fusion | flops 12632064 | bytes 3440736 | tf_op jit(solution)/shard_map/pij,psi->psj/dot_general | solution.py:108
  73.9 3.6 %collective-permute-start.4 = (f32[1,1,64,128]{3,2,1,0:T(8,128)S(1)}, f32[1,1,64,128]{3,2,1,0:T(8,128)S(1)}, u32[]{:S(2)}, u32[]{:S(2)}) collective-permute-start(f32[1,1,64,128]{3,2,1,0:T(8,128)S(1)} %get-tuple-element.9), channel_id=1, source_target_pairs={{2,0},{4,2},{6,4},{8,6},{10,8},{12,10},{14,12},{16,14},{18,16},{20... | collective-permute-start | bytes 98312 | tf_op jit(solution)/shard_map/ppermute | solution.py:22
  77.5 1.9 %collective-permute-start.3 = (f32[1,1,64,128]{3,2,1,0:T(8,128)S(1)}, f32[1,1,64,128]{3,2,1,0:T(8,128)S(1)}, u32[]{:S(2)}, u32[]{:S(2)}) collective-permute-start(f32[1,1,64,128]{3,2,1,0:T(8,128)S(1)} %get-tuple-element.8), channel_id=1, source_target_pairs={{0,2},{2,4},{4,6},{6,8},{8,10},{10,12},{12,14},{14,16},{16,18},{18... | collective-permute-start | bytes 98312 | tf_op jit(solution)/shard_map/ppermute | solution.py:21
  79.5 4.2 %collective-permute-done.3 = f32[1,1,64,128]{3,2,1,0:T(8,128)S(1)} collective-permute-done((f32[1,1,64,128]{3,2,1,0:T(8,128)S(1)}, f32[1,1,64,128]{3,2,1,0:T(8,128)S(1)}, u32[]{:S(2)}, u32[]{:S(2)}) %collective-permute-start.3) | collective-permute-done | bytes 32800 | tf_op jit(solution)/shard_map/ppermute | solution.py:21
  83.7 1.5 %collective-permute-start.5 = (f32[1,4,1,128]{3,2,1,0:T(1,128)S(1)}, f32[1,4,1,128]{3,2,1,0:T(1,128)S(1)}, u32[]{:S(2)}, u32[]{:S(2)}) collective-permute-start(f32[1,4,1,128]{3,2,1,0:T(1,128)S(1)} %broadcast_select_fusion.4), channel_id=1, source_target_pairs={{0,1},{1,0},{2,3},{3,2},{4,5},{5,4},{6,7},{7,6},{8,9},{9,8},{10,11... | collective-permute-start | bytes 6152 | tf_op jit(solution)/shard_map/ppermute | solution.py:16
  85.8 1.5 %collective-permute-done.5 = f32[1,4,1,128]{3,2,1,0:T(1,128)S(1)} collective-permute-done((f32[1,4,1,128]{3,2,1,0:T(1,128)S(1)}, f32[1,4,1,128]{3,2,1,0:T(1,128)S(1)}, u32[]{:S(2)}, u32[]{:S(2)}) %collective-permute-start.5) | collective-permute-done | bytes 2080 | tf_op jit(solution)/shard_map/ppermute | solution.py:16
  (49 shorter events, 15.2 us)
Async XLA Ops:
  0.6 35.5 %copy-start = (bf16[96,128,128]{2,1,0:T(8,128)(2,1)S(1)}, bf16[96,128,128]{2,1,0:T(8,128)(2,1)}, u32[]{:S(2)}) copy-start(bf16[96,128,128]{2,1,0:T(8,128)(2,1)} %param.16) | copy-start | bytes 9437188
  3.1 19.9 %collective-permute-start.1 = (f32[4,1,64,128]{3,2,1,0:T(8,128)}, f32[4,1,64,128]{3,2,1,0:T(8,128)}, u32[]{:S(2)}, u32[]{:S(2)}) collective-permute-start(f32[4,1,64,128]{3,2,1,0:T(8,128)} %get-tuple-element.7), channel_id=1, source_target_pairs={{2,0},{4,2},{6,4},{8,6},{10,8},{12,10},{14,12},{16,14},{18,16},{20... | collective-permute-start | bytes 393224 | tf_op jit(solution)/shard_map/ppermute | solution.py:22
  5.9 17.1 %collective-permute-start = (f32[4,1,64,128]{3,2,1,0:T(8,128)}, f32[4,1,64,128]{3,2,1,0:T(8,128)}, u32[]{:S(2)}, u32[]{:S(2)}) collective-permute-start(f32[4,1,64,128]{3,2,1,0:T(8,128)} %get-tuple-element.6), channel_id=1, source_target_pairs={{0,2},{2,4},{4,6},{6,8},{8,10},{10,12},{12,14},{14,16},{16,18},{18... | collective-permute-start | bytes 393224 | tf_op jit(solution)/shard_map/ppermute | solution.py:21
  24.4 4.0 %collective-permute-start.2 = (f32[4,4,1,128]{3,2,1,0:T(1,128)}, f32[4,4,1,128]{3,2,1,0:T(1,128)}, u32[]{:S(2)}, u32[]{:S(2)}) collective-permute-start(f32[4,4,1,128]{3,2,1,0:T(1,128)} %broadcast_select_fusion.1), channel_id=1, source_target_pairs={{0,1},{1,0},{2,3},{3,2},{4,5},{5,4},{6,7},{7,6},{8,9},{9,8},{10,11... | collective-permute-start | bytes 24584 | tf_op jit(solution)/shard_map/ppermute | solution.py:16
  27.1 3.0 %copy-start.4 = (f32[72]{0:T(128)}, f32[72]{0:T(128)S(1)}, u32[]{:S(2)}) copy-start(f32[72]{0:T(128)S(1)} %pad.14.clone) | copy-start | bytes 868
  36.1 2.7 %copy-start.6 = (s32[96]{0:T(128)S(1)}, s32[96]{0:T(128)}, u32[]{:S(2)}) copy-start(s32[96]{0:T(128)} %get-tuple-element.5) | copy-start | bytes 1156
  57.4 11.5 %all-to-all-start.1 = ((bf16[16,8,4,128]{3,2,1,0:T(4,128)(2,1)}), bf16[16,8,4,128]{3,2,1,0:T(4,128)(2,1)}, u32[]{:S(2)}, u32[]{:S(2)}) async-start(bf16[16,8,4,128]{3,2,1,0:T(4,128)(2,1)} %broadcast_in_dim.137), calls=%async_computation.1 | async-start | bytes 262144 | tf_op jit(solution)/shard_map/all_to_all | solution.py:104
  71.3 1.9 %copy-start.7 = (s32[96]{0:T(128)S(1)}, s32[96]{0:T(128)}, u32[]{:S(2)}) copy-start(s32[96]{0:T(128)} %param.17) | copy-start | bytes 1156
  71.3 2.4 %copy-start.1 = (f32[128,128]{1,0:T(8,128)S(1)}, f32[128,128]{1,0:T(8,128)}, u32[]{:S(2)}) copy-start(f32[128,128]{1,0:T(8,128)} %param.14) | copy-start | bytes 196612
  71.3 13.9 %copy-start.3 = (f32[8,128]{1,0:T(8,128)S(1)}, f32[8,128]{1,0:T(8,128)}, u32[]{:S(2)}) copy-start(f32[8,128]{1,0:T(8,128)} %get-tuple-element.10) | copy-start | bytes 12292
  71.3 16.0 %copy-start.5 = (f32[72]{0:T(128)S(1)}, f32[72]{0:T(128)}, u32[]{:S(2)}) copy-start(f32[72]{0:T(128)} %copy-done.4) | copy-start | bytes 868
  71.3 16.6 %copy-start.2 = (f32[2,64,128]{2,1,0:T(8,128)S(1)}, f32[2,64,128]{2,1,0:T(8,128)}, u32[]{:S(2)}) copy-start(f32[2,64,128]{2,1,0:T(8,128)} %get-tuple-element.2) | copy-start | bytes 196612
  73.9 5.5 %collective-permute-start.4 = (f32[1,1,64,128]{3,2,1,0:T(8,128)S(1)}, f32[1,1,64,128]{3,2,1,0:T(8,128)S(1)}, u32[]{:S(2)}, u32[]{:S(2)}) collective-permute-start(f32[1,1,64,128]{3,2,1,0:T(8,128)S(1)} %get-tuple-element.9), channel_id=1, source_target_pairs={{2,0},{4,2},{6,4},{8,6},{10,8},{12,10},{14,12},{16,14},{18,16},{20... | collective-permute-start | bytes 98312 | tf_op jit(solution)/shard_map/ppermute | solution.py:22
  77.5 6.1 %collective-permute-start.3 = (f32[1,1,64,128]{3,2,1,0:T(8,128)S(1)}, f32[1,1,64,128]{3,2,1,0:T(8,128)S(1)}, u32[]{:S(2)}, u32[]{:S(2)}) collective-permute-start(f32[1,1,64,128]{3,2,1,0:T(8,128)S(1)} %get-tuple-element.8), channel_id=1, source_target_pairs={{0,2},{2,4},{4,6},{6,8},{8,10},{10,12},{12,14},{14,16},{16,18},{18... | collective-permute-start | bytes 98312 | tf_op jit(solution)/shard_map/ppermute | solution.py:21
  83.7 3.6 %collective-permute-start.5 = (f32[1,4,1,128]{3,2,1,0:T(1,128)S(1)}, f32[1,4,1,128]{3,2,1,0:T(1,128)S(1)}, u32[]{:S(2)}, u32[]{:S(2)}) collective-permute-start(f32[1,4,1,128]{3,2,1,0:T(1,128)S(1)} %broadcast_select_fusion.4), channel_id=1, source_target_pairs={{0,1},{1,0},{2,3},{3,2},{4,5},{5,4},{6,7},{7,6},{8,9},{9,8},{10,11... | collective-permute-start | bytes 6152 | tf_op jit(solution)/shard_map/ppermute | solution.py:16

commit v7 on v6

--- a/solution.py
+++ b/solution.py
@@ -1,3 +1,4 @@
+import numpy as np
 import jax
 import jax.numpy as jnp
 from jax import lax
@@ -36,21 +37,21 @@
 
 def stencil_matrix(stencil, width_x, width_y, flip):
     rows = width_y + 2 + (-(width_y + 2) % 8)
-    out = jnp.arange(width_x * width_y, dtype=jnp.int32)[:, None]
-    col = jnp.arange((width_x + 2) * rows, dtype=jnp.int32)[None, :]
+    out = np.arange(width_x * width_y)[:, None]
+    col = np.arange((width_x + 2) * rows)[None, :]
     out_x, out_y = out // width_y, out % width_y
     col_x, place = col // rows, col % rows
-    col_y = jnp.where(place < width_y, place, jnp.where(place == width_y, -1, width_y))
+    col_y = np.where(place < width_y, place, np.where(place == width_y, -1, width_y))
     if flip:
         shift_x, shift_y = out_x + 2 - col_x, out_y + 1 - col_y
     else:
         shift_x, shift_y = col_x - out_x, col_y - out_y + 1
-    live = place < width_y + 2
-    matrix = jnp.zeros(shift_x.shape, jnp.float32)
-    for a in range(3):
-        for b in range(3):
-            hit = live & (shift_x == a) & (shift_y == b)
-            matrix = matrix + jnp.where(hit, stencil[a, b], 0.0)
+    live = (place < width_y + 2) & (shift_x >= 0) & (shift_x < 3) & (shift_y >= 0) & (shift_y < 3)
+    code = jnp.asarray(np.where(live, shift_x * 3 + shift_y, 9).astype(np.int32))
+    weights = stencil.reshape(9)
+    matrix = jnp.zeros(code.shape, jnp.float32)
+    for k in range(9):
+        matrix = matrix + jnp.where(code == k, weights[k], 0.0)
     return lax.optimization_barrier(matrix)
 
 

time: 89.4 us -> 87 us (0.973)
  other arithmetic: 25.1 us -> 23 us
    select_n x2 -> x0, other arithmetic: 1.13 us -> none  [the longest x1 0.59 us: stencil_matrix(): jnp.where(place < width_y, place, jnp.where(place == width_y, -1, width_y))]
    slice x1, local copies, waits for them, and re-layouts: 1.68 us -> 0.68 us  [stencil_matrix(): matrix = matrix + jnp.where(code == k, weights[k], 0.0)]
    add x2 -> x1, other arithmetic: 8.2 us -> 7.66 us  [stencil_matrix(): matrix = matrix + jnp.where(code == k, weights[k], 0.0)]
  transfers between devices with their start and end apart: 7 -> 7, of which waited for: 4 -> 4; matrix products, arithmetic and copies ran while one was open for 21% -> 19% of each run, Pallas kernels for 0% -> 0%
where the time goes in v7:
time: 87 us; the launch traced here: 86.1 us
  other arithmetic  23 us (26%)
  starting transfers between devices  19.1 us (22%)
  blocking collectives  14.6 us (17%)
  waiting for transfers between devices  11.2 us (13%)
  matrix products  8.89 us (10%)
  local copies, waits for them, and re-layouts  8.51 us (10%)
    all_to_all x1, blocking collectives, per_device(): lax.all_to_all(partial.reshape(group_size, star_count, samples, length),...  14.6 us
    add x1, other arithmetic, stencil_matrix(): matrix = matrix + jnp.where(code == k, weights[k], 0.0)  7.66 us
    ppermute x2, starting transfers between devices, edges(): above = lax.ppermute(head, axis, [(i + 1, i) for i in range(count - 1)])  6.35 us
    all_to_all x1, starting transfers between devices, per_device(): lax.all_to_all(spread, 'vox', split_axis=0, concat_axis=0, tiled=True)  5.91 us
    all_to_all x1, waiting for transfers between devices, per_device(): lax.all_to_all(spread, 'vox', split_axis=0, concat_axis=0, tiled=True)  4.3 us
    ppermute x2, waiting for transfers between devices, edges(): below = lax.ppermute(tail, axis, [(i, i + 1) for i in range(count - 1)])  4.2 us
    ppermute x2, starting transfers between devices, edges(): below = lax.ppermute(tail, axis, [(i, i + 1) for i in range(count - 1)])  3.84 us
    ppermute x2, starting transfers between devices, edges(): lax.ppermute(jnp.where(index == 0, tail, head), axis, [(0, 1), (1, 0)])  2.97 us
  transfers between devices with their start and end apart: 7, of which 4 were waited for; matrix products, arithmetic and copies ran while one was open for 19% of the time, Pallas kernels for 0%

profile of v7, /device:TPU:8, one launch (start us, length us, event | category | flops | bytes accessed | tf_op | source)
XLA Modules:
  0.0 86.1 jit_solution(8178345122207708955)
XLA Ops:
  0.6 1.8 %fusion.38 = (f32[2,64,128]{2,1,0:T(8,128)}, f32[4,2,64,128]{3,2,1,0:T(8,128)S(1)}) fusion(f32[4,2,64,128]{3,2,1,0:T(8,128)} %param.14, f32[2,64,128]{2,1,0:T(8,128)} %param.13), kind=kLoop, calls=%fused_computation.69 | loop fusion | flops 114688 | bytes 655360 | tf_op jit(solution)/shard_map/reduce_sum | solution.py:122
  3.1 2.7 %collective-permute-start.1 = (f32[4,1,64,128]{3,2,1,0:T(8,128)}, f32[4,1,64,128]{3,2,1,0:T(8,128)}, u32[]{:S(2)}, u32[]{:S(2)}) collective-permute-start(f32[4,1,64,128]{3,2,1,0:T(8,128)} %get-tuple-element.9), channel_id=1, source_target_pairs={{2,0},{4,2},{6,4},{8,6},{10,8},{12,10},{14,12},{16,14},{18,16},{20... | collective-permute-start | bytes 393224 | tf_op jit(solution)/shard_map/ppermute | solution.py:23
  5.9 1.9 %collective-permute-start = (f32[4,1,64,128]{3,2,1,0:T(8,128)}, f32[4,1,64,128]{3,2,1,0:T(8,128)}, u32[]{:S(2)}, u32[]{:S(2)}) collective-permute-start(f32[4,1,64,128]{3,2,1,0:T(8,128)} %get-tuple-element.8), channel_id=1, source_target_pairs={{0,2},{2,4},{4,6},{6,8},{8,10},{10,12},{12,14},{14,16},{16,18},{18... | collective-permute-start | bytes 393224 | tf_op jit(solution)/shard_map/ppermute | solution.py:22
  9.0 1.2 %compare_and_fusion = pred[96]{0:T(512)(128)(4,1)} fusion(s32[96]{0:T(128)} %param.19), kind=kLoop, calls=%fused_computation.63 | loop fusion | flops 576 | bytes 480 | tf_op jit(solution)/shard_map/jit(_take)/and | solution.py:86
  11.0 1.3 %compare_and_fusion.1 = (pred[96]{0:T(512)(128)(4,1)}, s32[96]{0:T(128)}) fusion(s32[96]{0:T(128)} %param.21, s32[96,1]{0,1:T(1,128)} %param.20), kind=kLoop, calls=%fused_computation.64 | loop fusion | flops 768 | bytes 1248 | tf_op jit(solution)/shard_map/jit(_take)/and | solution.py:108
  12.9 7.7 %fusion.11 = (f32[128,288]{0,1:T(8,128)S(1)}, f32[128,288]{0,1:T(8,128)}) fusion(pred[128,288]{0,1:T(32,128)(4,1)} %constant.78, pred[128,288]{0,1:T(32,128)(4,1)} %constant.74, pred[128,288]{0,1:T(32,128)(4,1)} %constant.75, pred[128,288]{0,1:T(32,128)(4,1)} %constant.76, pred[128,288]{0,1:T(32,128)(4,1)} %constant.77, pred[128,288]{0,1:T(32,128)(4,1)} %constant.79, ...), kind=kLoop, calls=%fused_computation.20 | loop fusion | flops 1216512 | bytes 626724 | tf_op jit(solution)/shard_map/add | solution.py:54
  20.6 1.4 %broadcast_select_fusion.1 = f32[4,4,1,128]{3,2,1,0:T(1,128)} fusion(pred[]{:T(512)S(6)} %eq.91, f32[4,1,64,128]{3,2,1,0:T(8,128)} %collective-permute-done.1, f32[4,2,64,128]{3,2,1,0:T(8,128)S(1)} %get-tuple-element.3, f32[4,1,64,128]{3,2,1,0:T(8,128)} %collective-permute-done), kind=kLoop, calls=%fused_computation.47 | loop fusion | flops 10240 | bytes 532481 | tf_op jit(solution)/shard_map/jit(_where)/select_n | solution.py:17
  22.0 1.5 %collective-permute-start.2 = (f32[4,4,1,128]{3,2,1,0:T(1,128)}, f32[4,4,1,128]{3,2,1,0:T(1,128)}, u32[]{:S(2)}, u32[]{:S(2)}) collective-permute-start(f32[4,4,1,128]{3,2,1,0:T(1,128)} %broadcast_select_fusion.1), channel_id=1, source_target_pairs={{0,1},{1,0},{2,3},{3,2},{4,5},{5,4},{6,7},{7,6},{8,9},{9,8},{10,11... | collective-permute-start | bytes 24584 | tf_op jit(solution)/shard_map/ppermute | solution.py:17
  27.7 1.6 %fusion.12 = f32[4,128,128]{1,2,0:T(8,128)S(1)} fusion(f32[4,288,128]{2,1,0:T(8,128)S(1)} %bitcast.59, f32[128,288]{0,1:T(8,128)} %get-tuple-element.7), kind=kOutput, calls=%fused_computation.22 | convolution fusion | flops 226492416 | bytes 999424 | tf_op jit(solution)/shard_map/rc,scz->srz/dot_general | solution.py:80
  29.3 1.2 %fusion.42 = (bf16[4,2,64,128]{3,2,1,0:T(8,128)(2,1)S(1)}, f32[4,2,64,128]{3,2,1,0:T(8,128)S(1)}) fusion(f32[128]{0:T(128)} %param.17, f32[4,2,64,128]{3,2,1,0:T(8,128)S(1)} %bitcast.61, f32[128,128]{1,0:T(8,128)} %param.16), kind=kOutput, calls=%fused_computation.73 | convolution fusion | flops 100794368 | bytes 721408 | tf_op jit(solution)/shard_map/sxyw,zw->sxyz/dot_general | solution.py:83
  31.3 2.4 %gather_fusion = bf16[96,4,128]{2,1,0:T(4,128)(2,1)} fusion(bf16[4,128,128]{2,0,1:T(4,128)(2,1)} %copy.16, s32[1024]{0:T(1024)} %pad_clamp_fusion.1), kind=kCustom, calls=%fused_computation | custom fusion | bytes 196992 | tf_op jit(solution)/shard_map/jit(_take)/gather | solution.py:86
  33.7 2.6 %fusion.14 = f32[96,4,128]{2,1,0:T(4,128)S(1)} fusion(bf16[96,128,128]{2,1,0:T(8,128)(2,1)S(1)} %copy-done, bf16[96,4,128]{2,1,0:T(4,128)(2,1)} %gather_fusion, pred[96]{0:T(512)(128)(4,1)} %compare_and_fusion), kind=kOutput, calls=%fused_computation.25 | convolution fusion | flops 12632064 | bytes 3440736 | tf_op jit(solution)/shard_map/pij,spj->psi/dot_general | solution.py:87
  36.8 14.6 %all_to_all.10 = f32[16,8,4,128]{3,1,2,0:T(8,128)} all-to-all(f32[16,8,4,128]{3,1,2,0:T(8,128)S(1)} %copy.18), channel_id=1, replica_groups=mesh['vox'=16,'star'=2] {'vox'}, dimensions={0} | all-to-all | bytes 524288 | tf_op jit(solution)/shard_map/all_to_all | solution.py:93
  51.4 1.6 %reduce_sum.36 = f32[8,4,128]{2,0,1:T(8,128)} reduce(f32[16,8,4,128]{3,1,2,0:T(8,128)} %all_to_all.10, f32[]{:T(128)} %constant.21.clone.1), dimensions={0}, to_apply=%region_0.1 | reduce | flops 61440 | bytes 278532 | tf_op jit(solution)/shard_map/reduce_sum | solution.py:100
  53.0 1.3 %fusion.33 = (f32[8,128]{1,0:T(8,128)}, bf16[8,4,128]{2,0,1:T(8,128)(2,1)S(1)}) fusion(f32[8,4,128]{2,0,1:T(8,128)} %reduce_sum.36, f32[8,128]{1,0:T(8,128)} %param.22, f32[8,128]{1,0:T(8,128)} %param.23), kind=kLoop, calls=%fused_computation.49 | loop fusion | flops 15360 | bytes 36864 | tf_op jit(solution)/shard_map/reduce_sum | solution.py:102
  55.0 5.9 %all-to-all-start.1 = ((bf16[16,8,4,128]{3,2,1,0:T(4,128)(2,1)}), bf16[16,8,4,128]{3,2,1,0:T(4,128)(2,1)}, u32[]{:S(2)}, u32[]{:S(2)}) async-start(bf16[16,8,4,128]{3,2,1,0:T(4,128)(2,1)} %broadcast_in_dim.127), calls=%async_computation.1 | async-start | bytes 262144 | tf_op jit(solution)/shard_map/all_to_all | solution.py:105
  62.2 4.3 %all-to-all-done.1 = bf16[16,8,4,128]{3,2,1,0:T(4,128)(2,1)} async-done(((bf16[16,8,4,128]{3,2,1,0:T(4,128)(2,1)}), bf16[16,8,4,128]{3,2,1,0:T(4,128)(2,1)}, u32[]{:S(2)}, u32[]{:S(2)}) %all-to-all-start.1) | async-done | bytes 131104 | tf_op jit(solution)/shard_map/all_to_all | solution.py:105
  66.5 2.4 %gather_fusion.1 = bf16[96,4,128]{2,1,0:T(4,128)(2,1)} fusion(bf16[128,4,128]{2,1,0:T(4,128)(2,1)} %bitcast.20, s32[1024]{0:T(1024)} %pad_clamp_fusion), kind=kCustom, calls=%fused_computation.1 | custom fusion | bytes 196992 | tf_op jit(solution)/shard_map/jit(_take)/gather | solution.py:108
  68.9 1.9 %fusion.17 = f32[96,4,128]{2,1,0:T(4,128)S(1)} fusion(bf16[96,128,128]{2,1,0:T(8,128)(2,1)S(1)} %copy-done, bf16[96,4,128]{2,1,0:T(4,128)(2,1)} %gather_fusion.1, pred[96]{0:T(512)(128)(4,1)} %get-tuple-element.4), kind=kOutput, calls=%fused_computation.28 | convolution fusion | flops 12632064 | bytes 3440736 | tf_op jit(solution)/shard_map/pij,psi->psj/dot_general | solution.py:109
  71.5 3.6 %collective-permute-start.4 = (f32[1,1,64,128]{3,2,1,0:T(8,128)S(1)}, f32[1,1,64,128]{3,2,1,0:T(8,128)S(1)}, u32[]{:S(2)}, u32[]{:S(2)}) collective-permute-start(f32[1,1,64,128]{3,2,1,0:T(8,128)S(1)} %get-tuple-element.11), channel_id=1, source_target_pairs={{2,0},{4,2},{6,4},{8,6},{10,8},{12,10},{14,12},{16,14},{18,16},{20... | collective-permute-start | bytes 98312 | tf_op jit(solution)/shard_map/ppermute | solution.py:23
  75.1 1.9 %collective-permute-start.3 = (f32[1,1,64,128]{3,2,1,0:T(8,128)S(1)}, f32[1,1,64,128]{3,2,1,0:T(8,128)S(1)}, u32[]{:S(2)}, u32[]{:S(2)}) collective-permute-start(f32[1,1,64,128]{3,2,1,0:T(8,128)S(1)} %get-tuple-element.10), channel_id=1, source_target_pairs={{0,2},{2,4},{4,6},{6,8},{8,10},{10,12},{12,14},{14,16},{16,18},{18... | collective-permute-start | bytes 98312 | tf_op jit(solution)/shard_map/ppermute | solution.py:22
  77.1 4.2 %collective-permute-done.3 = f32[1,1,64,128]{3,2,1,0:T(8,128)S(1)} collective-permute-done((f32[1,1,64,128]{3,2,1,0:T(8,128)S(1)}, f32[1,1,64,128]{3,2,1,0:T(8,128)S(1)}, u32[]{:S(2)}, u32[]{:S(2)}) %collective-permute-start.3) | collective-permute-done | bytes 32800 | tf_op jit(solution)/shard_map/ppermute | solution.py:22
  81.3 1.5 %collective-permute-start.5 = (f32[1,4,1,128]{3,2,1,0:T(1,128)S(1)}, f32[1,4,1,128]{3,2,1,0:T(1,128)S(1)}, u32[]{:S(2)}, u32[]{:S(2)}) collective-permute-start(f32[1,4,1,128]{3,2,1,0:T(1,128)S(1)} %broadcast_select_fusion.4), channel_id=1, source_target_pairs={{0,1},{1,0},{2,3},{3,2},{4,5},{5,4},{6,7},{7,6},{8,9},{9,8},{10,11... | collective-permute-start | bytes 6152 | tf_op jit(solution)/shard_map/ppermute | solution.py:17
  83.3 1.5 %collective-permute-done.5 = f32[1,4,1,128]{3,2,1,0:T(1,128)S(1)} collective-permute-done((f32[1,4,1,128]{3,2,1,0:T(1,128)S(1)}, f32[1,4,1,128]{3,2,1,0:T(1,128)S(1)}, u32[]{:S(2)}, u32[]{:S(2)}) %collective-permute-start.5) | collective-permute-done | bytes 2080 | tf_op jit(solution)/shard_map/ppermute | solution.py:17
  (46 shorter events, 13.3 us)
Async XLA Ops:
  0.6 33.1 %copy-start = (bf16[96,128,128]{2,1,0:T(8,128)(2,1)S(1)}, bf16[96,128,128]{2,1,0:T(8,128)(2,1)}, u32[]{:S(2)}) copy-start(bf16[96,128,128]{2,1,0:T(8,128)(2,1)} %param.18) | copy-start | bytes 9437188
  3.1 17.5 %collective-permute-start.1 = (f32[4,1,64,128]{3,2,1,0:T(8,128)}, f32[4,1,64,128]{3,2,1,0:T(8,128)}, u32[]{:S(2)}, u32[]{:S(2)}) collective-permute-start(f32[4,1,64,128]{3,2,1,0:T(8,128)} %get-tuple-element.9), channel_id=1, source_target_pairs={{2,0},{4,2},{6,4},{8,6},{10,8},{12,10},{14,12},{16,14},{18,16},{20... | collective-permute-start | bytes 393224 | tf_op jit(solution)/shard_map/ppermute | solution.py:23
  5.9 14.7 %collective-permute-start = (f32[4,1,64,128]{3,2,1,0:T(8,128)}, f32[4,1,64,128]{3,2,1,0:T(8,128)}, u32[]{:S(2)}, u32[]{:S(2)}) collective-permute-start(f32[4,1,64,128]{3,2,1,0:T(8,128)} %get-tuple-element.8), channel_id=1, source_target_pairs={{0,2},{2,4},{4,6},{6,8},{8,10},{10,12},{12,14},{14,16},{16,18},{18... | collective-permute-start | bytes 393224 | tf_op jit(solution)/shard_map/ppermute | solution.py:22
  22.0 4.0 %collective-permute-start.2 = (f32[4,4,1,128]{3,2,1,0:T(1,128)}, f32[4,4,1,128]{3,2,1,0:T(1,128)}, u32[]{:S(2)}, u32[]{:S(2)}) collective-permute-start(f32[4,4,1,128]{3,2,1,0:T(1,128)} %broadcast_select_fusion.1), channel_id=1, source_target_pairs={{0,1},{1,0},{2,3},{3,2},{4,5},{5,4},{6,7},{7,6},{8,9},{9,8},{10,11... | collective-permute-start | bytes 24584 | tf_op jit(solution)/shard_map/ppermute | solution.py:17
  24.8 3.0 %copy-start.4 = (f32[72]{0:T(128)}, f32[72]{0:T(128)S(1)}, u32[]{:S(2)}) copy-start(f32[72]{0:T(128)S(1)} %pad.14.clone) | copy-start | bytes 868
  33.7 2.7 %copy-start.6 = (s32[96]{0:T(128)S(1)}, s32[96]{0:T(128)}, u32[]{:S(2)}) copy-start(s32[96]{0:T(128)} %get-tuple-element.5) | copy-start | bytes 1156
  55.0 11.5 %all-to-all-start.1 = ((bf16[16,8,4,128]{3,2,1,0:T(4,128)(2,1)}), bf16[16,8,4,128]{3,2,1,0:T(4,128)(2,1)}, u32[]{:S(2)}, u32[]{:S(2)}) async-start(bf16[16,8,4,128]{3,2,1,0:T(4,128)(2,1)} %broadcast_in_dim.127), calls=%async_computation.1 | async-start | bytes 262144 | tf_op jit(solution)/shard_map/all_to_all | solution.py:105
  68.9 1.9 %copy-start.7 = (s32[96]{0:T(128)S(1)}, s32[96]{0:T(128)}, u32[]{:S(2)}) copy-start(s32[96]{0:T(128)} %param.19) | copy-start | bytes 1156
  68.9 2.4 %copy-start.1 = (f32[128,128]{1,0:T(8,128)S(1)}, f32[128,128]{1,0:T(8,128)}, u32[]{:S(2)}) copy-start(f32[128,128]{1,0:T(8,128)} %param.16) | copy-start | bytes 196612
  68.9 13.9 %copy-start.3 = (f32[8,128]{1,0:T(8,128)S(1)}, f32[8,128]{1,0:T(8,128)}, u32[]{:S(2)}) copy-start(f32[8,128]{1,0:T(8,128)} %get-tuple-element.12) | copy-start | bytes 12292
  68.9 16.0 %copy-start.5 = (f32[72]{0:T(128)S(1)}, f32[72]{0:T(128)}, u32[]{:S(2)}) copy-start(f32[72]{0:T(128)} %copy-done.4) | copy-start | bytes 868
  68.9 16.6 %copy-start.2 = (f32[2,64,128]{2,1,0:T(8,128)S(1)}, f32[2,64,128]{2,1,0:T(8,128)}, u32[]{:S(2)}) copy-start(f32[2,64,128]{2,1,0:T(8,128)} %get-tuple-element.2) | copy-start | bytes 196612
  71.5 5.5 %collective-permute-start.4 = (f32[1,1,64,128]{3,2,1,0:T(8,128)S(1)}, f32[1,1,64,128]{3,2,1,0:T(8,128)S(1)}, u32[]{:S(2)}, u32[]{:S(2)}) collective-permute-start(f32[1,1,64,128]{3,2,1,0:T(8,128)S(1)} %get-tuple-element.11), channel_id=1, source_target_pairs={{2,0},{4,2},{6,4},{8,6},{10,8},{12,10},{14,12},{16,14},{18,16},{20... | collective-permute-start | bytes 98312 | tf_op jit(solution)/shard_map/ppermute | solution.py:23
  75.1 6.1 %collective-permute-start.3 = (f32[1,1,64,128]{3,2,1,0:T(8,128)S(1)}, f32[1,1,64,128]{3,2,1,0:T(8,128)S(1)}, u32[]{:S(2)}, u32[]{:S(2)}) collective-permute-start(f32[1,1,64,128]{3,2,1,0:T(8,128)S(1)} %get-tuple-element.10), channel_id=1, source_target_pairs={{0,2},{2,4},{4,6},{6,8},{8,10},{10,12},{12,14},{14,16},{16,18},{18... | collective-permute-start | bytes 98312 | tf_op jit(solution)/shard_map/ppermute | solution.py:22
  81.3 3.6 %collective-permute-start.5 = (f32[1,4,1,128]{3,2,1,0:T(1,128)S(1)}, f32[1,4,1,128]{3,2,1,0:T(1,128)S(1)}, u32[]{:S(2)}, u32[]{:S(2)}) collective-permute-start(f32[1,4,1,128]{3,2,1,0:T(1,128)S(1)} %broadcast_select_fusion.4), channel_id=1, source_target_pairs={{0,1},{1,0},{2,3},{3,2},{4,5},{5,4},{6,7},{7,6},{8,9},{9,8},{10,11... | collective-permute-start | bytes 6152 | tf_op jit(solution)/shard_map/ppermute | solution.py:17

commit v8 on v3

--- a/solution.py
+++ b/solution.py
@@ -92,10 +92,10 @@
     adjoint = jnp.einsum("pb,psj->bsj", line_onehot, pair_adjoint, precision=HIGH).reshape(
         width_x, width_y, samples, length
     )
-    grad_log = density * adjoint
-    grad_smooth = jnp.einsum("xysz,zw->xysw", grad_log, vertical_mix, precision=HIGH)
+    grad_log = jnp.mean(density * adjoint, axis=2)
+    grad_smooth = jnp.einsum("xyz,zw->xyw", grad_log, vertical_mix, precision=HIGH)
     padded_grad = with_halo(grad_smooth)
-    grad_latent = jnp.zeros(latent.shape, jnp.float32)
+    grad_latent = jnp.zeros(grad_smooth.shape, jnp.float32)
     for offset_x in range(3):
         for offset_y in range(3):
             grad_latent = (
@@ -103,7 +103,7 @@
                 + stencil[offset_x, offset_y]
                 * padded_grad[2 - offset_x : 2 - offset_x + width_x, 2 - offset_y : 2 - offset_y + width_y]
             )
-    gradient = jnp.mean(grad_latent + latent, axis=2)
+    gradient = grad_latent + jnp.mean(latent, axis=2)
     return (gradient, residual_mean)
 
 

time: 78.9 us -> 79.2 us (level)
  other arithmetic: 15 us -> 16.7 us
  waiting for transfers between devices: 11.6 us -> 9.98 us
    add x0 -> x1, other arithmetic: none -> 6.16 us  [per_device(): gradient = grad_latent + jnp.mean(latent, axis=2)]
    reduce_sum x1 -> x2, other arithmetic: 5.76 us -> 1.8 us  [the longest x1 1.76 us: per_device(): gradient = grad_latent + jnp.mean(latent, axis=2)]
    transpose x1 -> x0, other arithmetic: 1.13 us -> none  [per_device(): latent = jnp.transpose(mean_field[None] + deviations, (1, 2, 0, 3))]
    ppermute x2, waiting for transfers between devices: 3.95 us -> 2.91 us  [exchange(): above = lax.ppermute(head, axis, [(i + 1, i) for i in range(count - 1)])]
  transfers between devices with their start and end apart: 7 -> 7, of which waited for: 3 -> 4; matrix products, arithmetic and copies ran while one was open for 9% -> 10% of each run, Pallas kernels for 0% -> 0%
where the time goes in v8:
time: 79.2 us; the launch traced here: 78.5 us
  starting transfers between devices  17.3 us (22%)
  blocking collectives  16.9 us (21%)
  other arithmetic  16.7 us (21%)
  matrix products  12.1 us (15%)
  waiting for transfers between devices  9.98 us (13%)
  local copies, waits for them, and re-layouts  4.79 us (6%)
  between operations  0.86 us (1%)
    all_to_all x1, blocking collectives, per_device(): lax.all_to_all(partial.reshape(group_size, star_count, samples, length),...  16.9 us
    dot_general x1, matrix products, per_device(): jnp.einsum('xysw,zw->xysz', smoothed, vertical_mix, precision=HIGH)  7.63 us
    ppermute x2, starting transfers between devices, exchange(): below = lax.ppermute(tail, axis, [(i, i + 1) for i in range(count - 1)])  6.58 us
    all_to_all x1, waiting for transfers between devices, per_device(): lax.all_to_all(spread, 'vox', split_axis=0, concat_axis=0, tiled=True)  6.36 us
    add x1, other arithmetic, per_device(): gradient = grad_latent + jnp.mean(latent, axis=2)  6.16 us
    ppermute x2, starting transfers between devices, exchange(): above = lax.ppermute(head, axis, [(i + 1, i) for i in range(count - 1)])  4.23 us
    all_to_all x1, starting transfers between devices, per_device(): lax.all_to_all(spread, 'vox', split_axis=0, concat_axis=0, tiled=True)  3.95 us
    ppermute x2, waiting for transfers between devices, exchange(): above = lax.ppermute(head, axis, [(i + 1, i) for i in range(count - 1)])  2.91 us
  transfers between devices with their start and end apart: 7, of which 4 were waited for; matrix products, arithmetic and copies ran while one was open for 10% of the time, Pallas kernels for 0%

profile of v8, /device:TPU:1, one launch (start us, length us, event | category | flops | bytes accessed | tf_op | source)
XLA Modules:
  0.0 78.5 jit_solution(9540729240683956723)
XLA Ops:
  0.6 1.8 %fusion.51 = (f32[2,64,128]{2,1,0:T(8,128)}, f32[2,64,4,128]{3,1,0,2:T(8,128)S(1)}) fusion(f32[4,2,64,128]{3,2,1,0:T(8,128)} %param.14, f32[2,64,128]{2,1,0:T(8,128)} %param.13), kind=kLoop, calls=%fused_computation.96 | loop fusion | flops 114688 | bytes 655360 | tf_op jit(solution)/shard_map/reduce_sum | solution.py:106
  3.1 4.5 %collective-permute-start = (f32[1,64,4,128]{3,1,0,2:T(8,128)}, f32[1,64,4,128]{3,1,0,2:T(8,128)S(1)}, u32[]{:S(2)}, u32[]{:S(2)}) collective-permute-start(f32[1,64,4,128]{3,1,0,2:T(8,128)} %get-tuple-element.9), channel_id=1, source_target_pairs={{0,2},{2,4},{4,6},{6,8},{8,10},{10,12},{12,14},{14,16},{16,18},{18... | collective-permute-start | bytes 393224 | tf_op jit(solution)/shard_map/ppermute | solution.py:21
  7.7 1.9 %collective-permute-start.1 = (f32[1,64,4,128]{3,1,0,2:T(8,128)}, f32[1,64,4,128]{3,1,0,2:T(8,128)}, u32[]{:S(2)}, u32[]{:S(2)}) collective-permute-start(f32[1,64,4,128]{3,1,0,2:T(8,128)} %get-tuple-element.10), channel_id=1, source_target_pairs={{2,0},{4,2},{6,4},{8,6},{10,8},{12,10},{14,12},{16,14},{18,16},{20... | collective-permute-start | bytes 393224 | tf_op jit(solution)/shard_map/ppermute | solution.py:22
  9.6 1.2 %compare_select_fusion.1 = s32[96]{0:T(128)} fusion(s32[96]{0:T(128)} %param.19), kind=kLoop, calls=%fused_computation.86 | loop fusion | flops 288 | bytes 768 | tf_op jit(solution)/shard_map/jit(_take)/jit(_where)/select_n | solution.py:63
  10.8 1.3 %compare_and_fusion = (pred[96]{0:T(512)(128)(4,1)}, s32[96]{0:T(128)}) fusion(s32[96]{0:T(128)} %param.21, s32[96,1]{0,1:T(1,128)} %param.20), kind=kLoop, calls=%fused_computation.90 | loop fusion | flops 768 | bytes 1248 | tf_op jit(solution)/shard_map/jit(_take)/and | solution.py:85
  12.0 1.2 %compare_and_fusion.1 = pred[96]{0:T(512)(128)(4,1)} fusion(s32[96]{0:T(128)} %param.19), kind=kLoop, calls=%fused_computation.91 | loop fusion | flops 576 | bytes 480 | tf_op jit(solution)/shard_map/jit(_take)/and | solution.py:63
  13.3 1.7 %fusion.54 = (f32[1,1]{1,0:T(1,128)}, f32[1,1]{1,0:T(1,128)}, f32[1,1]{1,0:T(1,128)}, f32[1,1]{1,0:T(1,128)}, f32[1,1]{1,0:T(1,128)}, /*index=5*/f32[1,1]{1,0:T(...) fusion(f32[3,3]{1,0:T(4,128)} %param.15), kind=kLoop, calls=%fused_computation.99 | loop fusion | bytes 72 | tf_op jit(solution)/shard_map/slice | solution.py:103
  15.0 0.7 broadcast_select_fusion.1
  15.7 1.3 %collective-permute-start.2 = (f32[4,1,4,128]{3,1,0,2:T(1,128)S(1)}, f32[4,1,4,128]{3,1,0,2:T(1,128)S(1)}, u32[]{:S(2)}, u32[]{:S(2)}) collective-permute-start(f32[4,1,4,128]{3,1,0,2:T(1,128)S(1)} %broadcast_select_fusion.1), channel_id=1, source_target_pairs={{0,1},{1,0},{2,3},{3,2},{4,5},{5,4},{6,7},{7,6},{8,9},{9,8},{10,11... | collective-permute-start | bytes 24584 | tf_op jit(solution)/shard_map/ppermute | solution.py:16
  17.0 1.2 %pad_clamp_fusion.1 = s32[1024]{0:T(1024)} fusion(s32[96]{0:T(128)} %compare_select_fusion.1), kind=kLoop, calls=%fused_computation.81 | loop fusion | flops 1024 | bytes 4480 | tf_op gather
  18.3 1.1 %maximum_maximum_fusion = (f32[4,65,4,128]{3,1,0,2:T(8,128)S(1)}, f32[4,65,4,128]{3,1,0,2:T(8,128)S(1)}) fusion(f32[1,64,4,128]{3,1,0,2:T(8,128)} %collective-permute-done.1, f32[2,64,4,128]{3,1,0,2:T(8,128)S(1)} %get-tuple-element.4, f32[1,64,4,128]{3,1,0,2:T(8,128)S(1)} %collective-permute-done, f32[4,1,4,128]{3,1,0,2:T(1,128)S(1)} %get-tuple-element.17, ...), kind=kLoop, calls=%fused_computation.5 | loop fusion | flops 798720 | bytes 1605632 | tf_op jit(solution)/shard_map/concatenate | solution.py:23
  19.4 7.6 %fusion.55 = (bf16[2,64,4,128]{3,1,2,0:T(8,128)(2,1)S(1)}, f32[2,64,4,128]{3,1,2,0:T(8,128)}) fusion(f32[128]{0:T(128)} %param.17, f32[128,128]{1,0:T(8,128)} %param.16, f32[4,65,4,128]{3,1,0,2:T(8,128)S(1)} %get-tuple-element.8, f32[1,64,4,128]{3,1,0,2:T(8,128)} %collective-permute-done.1, f32[2,64,4,128]{3,1,0,2:T(8,128)S(1)} %get-tuple-element.4, ...), kind=kOutput, calls=%fused_computation.100 | convolution fusion | flops 102039552 | bytes 2556452 | tf_op jit(solution)/shard_map/xysw,zw->xysz/dot_general | solution.py:60
  27.1 0.8 %gather_fusion = bf16[96,4,128]{2,1,0:T(4,128)(2,1)S(1)} fusion(bf16[128,4,128]{2,1,0:T(4,128)(2,1)S(1)} %copy.25, s32[1024]{0:T(1024)} %pad_clamp_fusion.1), kind=kCustom, calls=%fused_computation.clone | custom fusion | bytes 196992 | tf_op jit(solution)/shard_map/jit(_take)/gather | solution.py:63
  28.0 1.8 %fusion.18 = f32[96,4,128]{2,1,0:T(4,128)S(1)} fusion(bf16[96,128,128]{2,1,0:T(8,128)(2,1)S(1)} %copy-done, bf16[96,4,128]{2,1,0:T(4,128)(2,1)S(1)} %gather_fusion, pred[96]{0:T(512)(128)(4,1)S(1)} %copy-done.5), kind=kOutput, calls=%fused_computation.36 | convolution fusion | flops 12632064 | bytes 3440736 | tf_op jit(solution)/shard_map/pij,psj->psi/dot_general | solution.py:64
  30.2 16.9 %all_to_all.10 = f32[16,8,4,128]{3,1,2,0:T(8,128)S(1)} all-to-all(f32[16,8,4,128]{3,1,2,0:T(8,128)S(1)} %copy.27), channel_id=1, replica_groups=mesh['vox'=16,'star'=2] {'vox'}, dimensions={0} | all-to-all | bytes 524288 | tf_op jit(solution)/shard_map/all_to_all | solution.py:70
  47.1 0.7 fusion.46
  48.6 4.0 %all-to-all-start.1 = ((bf16[16,8,4,128]{3,2,1,0:T(4,128)(2,1)}), bf16[16,8,4,128]{3,2,1,0:T(4,128)(2,1)S(1)}, u32[]{:S(2)}, u32[]{:S(2)}) async-start(bf16[16,8,4,128]{3,2,1,0:T(4,128)(2,1)} %broadcast_in_dim.16), calls=%async_computation.1 | async-start | bytes 262144 | tf_op jit(solution)/shard_map/all_to_all | solution.py:82
  53.1 6.4 %all-to-all-done.1 = bf16[16,8,4,128]{3,2,1,0:T(4,128)(2,1)S(1)} async-done(((bf16[16,8,4,128]{3,2,1,0:T(4,128)(2,1)}), bf16[16,8,4,128]{3,2,1,0:T(4,128)(2,1)S(1)}, u32[]{:S(2)}, u32[]{:S(2)}) %all-to-all-start.1) | async-done | bytes 131104 | tf_op jit(solution)/shard_map/all_to_all | solution.py:82
  60.2 1.7 %fusion.16 = f32[96,4,128]{2,1,0:T(4,128)S(1)} fusion(bf16[96,128,128]{2,1,0:T(8,128)(2,1)S(1)} %copy-done, bf16[96,4,128]{2,1,0:T(4,128)(2,1)S(1)} %gather_fusion.1, pred[96]{0:T(512)(128)(4,1)} %get-tuple-element.5), kind=kOutput, calls=%fused_computation.34 | convolution fusion | flops 12632064 | bytes 3440736 | tf_op jit(solution)/shard_map/pij,psi->psj/dot_general | solution.py:86
  62.5 2.1 %collective-permute-start.3 = (f32[1,64,128]{2,1,0:T(8,128)S(1)}, f32[1,64,128]{2,1,0:T(8,128)S(1)}, u32[]{:S(2)}, u32[]{:S(2)}) collective-permute-start(f32[1,64,128]{2,1,0:T(8,128)S(1)} %get-tuple-element.13), channel_id=1, source_target_pairs={{0,2},{2,4},{4,6},{6,8},{8,10},{10,12},{12,14},{14,16},{16,18},{18... | collective-permute-start | bytes 98312 | tf_op jit(solution)/shard_map/ppermute | solution.py:21
  64.6 2.3 %collective-permute-start.4 = (f32[1,64,128]{2,1,0:T(8,128)S(1)}, f32[1,64,128]{2,1,0:T(8,128)S(1)}, u32[]{:S(2)}, u32[]{:S(2)}) collective-permute-start(f32[1,64,128]{2,1,0:T(8,128)S(1)} %get-tuple-element.14), channel_id=1, source_target_pairs={{2,0},{4,2},{6,4},{8,6},{10,8},{12,10},{14,12},{16,14},{18,16},{20... | collective-permute-start | bytes 98312 | tf_op jit(solution)/shard_map/ppermute | solution.py:22
  66.9 2.9 %collective-permute-done.4 = f32[1,64,128]{2,1,0:T(8,128)S(1)} collective-permute-done((f32[1,64,128]{2,1,0:T(8,128)S(1)}, f32[1,64,128]{2,1,0:T(8,128)S(1)}, u32[]{:S(2)}, u32[]{:S(2)}) %collective-permute-start.4) | collective-permute-done | bytes 32800 | tf_op jit(solution)/shard_map/ppermute | solution.py:22
  69.8 1.2 %collective-permute-start.5 = (f32[4,1,128]{2,1,0:T(1,128)S(1)}, f32[4,1,128]{2,1,0:T(1,128)S(1)}, u32[]{:S(2)}, u32[]{:S(2)}) collective-permute-start(f32[4,1,128]{2,1,0:T(1,128)S(1)} %broadcast_select_fusion.5), channel_id=1, source_target_pairs={{0,1},{1,0},{2,3},{3,2},{4,5},{5,4},{6,7},{7,6},{8,9},{9,8},{10,11... | collective-permute-start | bytes 6152 | tf_op jit(solution)/shard_map/ppermute | solution.py:16
  72.3 6.2 %fusion.23 = f32[2,64,128]{2,1,0:T(8,128)} fusion(f32[4,65,128]{2,1,0:T(8,128)S(1)} %get-tuple-element.12, f32[2,64,128]{2,1,0:T(8,128)S(1)} %fusion.34, f32[1,64,128]{2,1,0:T(8,128)S(1)} %collective-permute-done.3, f32[4,65,128]{2,1,0:T(8,128)S(1)} %get-tuple-element.11, f32[1,64,128]{2,1,0:T(8,128)S(1)} %collective-permute-done.4, ...), kind=kLoop, calls=%fused_computation.42 | loop fusion | flops 344064 | bytes 655396 | tf_op jit(solution)/shard_map/add | solution.py:106
  (39 shorter events, 5.3 us)
Async XLA Ops:
  0.6 27.3 %copy-start = (bf16[96,128,128]{2,1,0:T(8,128)(2,1)S(1)}, bf16[96,128,128]{2,1,0:T(8,128)(2,1)}, u32[]{:S(2)}) copy-start(bf16[96,128,128]{2,1,0:T(8,128)(2,1)} %param.18) | copy-start | bytes 9437188
  3.1 11.8 %collective-permute-start = (f32[1,64,4,128]{3,1,0,2:T(8,128)}, f32[1,64,4,128]{3,1,0,2:T(8,128)S(1)}, u32[]{:S(2)}, u32[]{:S(2)}) collective-permute-start(f32[1,64,4,128]{3,1,0,2:T(8,128)} %get-tuple-element.9), channel_id=1, source_target_pairs={{0,2},{2,4},{4,6},{6,8},{8,10},{10,12},{12,14},{14,16},{16,18},{18... | collective-permute-start | bytes 393224 | tf_op jit(solution)/shard_map/ppermute | solution.py:21
  7.7 7.3 %collective-permute-start.1 = (f32[1,64,4,128]{3,1,0,2:T(8,128)}, f32[1,64,4,128]{3,1,0,2:T(8,128)}, u32[]{:S(2)}, u32[]{:S(2)}) collective-permute-start(f32[1,64,4,128]{3,1,0,2:T(8,128)} %get-tuple-element.10), channel_id=1, source_target_pairs={{2,0},{4,2},{6,4},{8,6},{10,8},{12,10},{14,12},{16,14},{18,16},{20... | collective-permute-start | bytes 393224 | tf_op jit(solution)/shard_map/ppermute | solution.py:22
  15.7 2.6 %collective-permute-start.2 = (f32[4,1,4,128]{3,1,0,2:T(1,128)S(1)}, f32[4,1,4,128]{3,1,0,2:T(1,128)S(1)}, u32[]{:S(2)}, u32[]{:S(2)}) collective-permute-start(f32[4,1,4,128]{3,1,0,2:T(1,128)S(1)} %broadcast_select_fusion.1), channel_id=1, source_target_pairs={{0,1},{1,0},{2,3},{3,2},{4,5},{5,4},{6,7},{7,6},{8,9},{9,8},{10,11... | collective-permute-start | bytes 24584 | tf_op jit(solution)/shard_map/ppermute | solution.py:16
  18.3 9.7 %copy-start.5 = (pred[96]{0:T(512)(128)(4,1)S(1)}, pred[96]{0:T(512)(128)(4,1)}, u32[]{:S(2)}) copy-start(pred[96]{0:T(512)(128)(4,1)} %compare_and_fusion.1) | copy-start | bytes 292
  19.4 10.4 %copy-start.4 = (s32[96]{0:T(128)S(1)}, s32[96]{0:T(128)}, u32[]{:S(2)}) copy-start(s32[96]{0:T(128)} %get-tuple-element.6) | copy-start | bytes 1156
  30.2 32.1 %copy-start.3 = (f32[128,128]{1,0:T(8,128)S(1)}, f32[128,128]{1,0:T(8,128)}, u32[]{:S(2)}) copy-start(f32[128,128]{1,0:T(8,128)} %param.16) | copy-start | bytes 196612
  47.1 25.2 %copy-start.1 = (f32[2,64,128]{2,1,0:T(8,128)S(1)}, f32[2,64,128]{2,1,0:T(8,128)}, u32[]{:S(2)}) copy-start(f32[2,64,128]{2,1,0:T(8,128)} %get-tuple-element.3) | copy-start | bytes 196612
  47.1 14.7 %copy-start.6 = (s32[96]{0:T(128)S(1)}, s32[96]{0:T(128)}, u32[]{:S(2)}) copy-start(s32[96]{0:T(128)} %param.19) | copy-start | bytes 1156
  48.6 10.9 %all-to-all-start.1 = ((bf16[16,8,4,128]{3,2,1,0:T(4,128)(2,1)}), bf16[16,8,4,128]{3,2,1,0:T(4,128)(2,1)S(1)}, u32[]{:S(2)}, u32[]{:S(2)}) async-start(bf16[16,8,4,128]{3,2,1,0:T(4,128)(2,1)} %broadcast_in_dim.16), calls=%async_computation.1 | async-start | bytes 262144 | tf_op jit(solution)/shard_map/all_to_all | solution.py:82
  60.2 2.1 %copy-start.2 = (f32[2,64,4,128]{3,1,2,0:T(8,128)S(1)}, f32[2,64,4,128]{3,1,2,0:T(8,128)}, u32[]{:S(2)}) copy-start(f32[2,64,4,128]{3,1,2,0:T(8,128)} %get-tuple-element.31) | copy-start | bytes 786436
  62.5 4.4 %collective-permute-start.3 = (f32[1,64,128]{2,1,0:T(8,128)S(1)}, f32[1,64,128]{2,1,0:T(8,128)S(1)}, u32[]{:S(2)}, u32[]{:S(2)}) collective-permute-start(f32[1,64,128]{2,1,0:T(8,128)S(1)} %get-tuple-element.13), channel_id=1, source_target_pairs={{0,2},{2,4},{4,6},{6,8},{8,10},{10,12},{12,14},{14,16},{16,18},{18... | collective-permute-start | bytes 98312 | tf_op jit(solution)/shard_map/ppermute | solution.py:21
  64.6 5.2 %collective-permute-start.4 = (f32[1,64,128]{2,1,0:T(8,128)S(1)}, f32[1,64,128]{2,1,0:T(8,128)S(1)}, u32[]{:S(2)}, u32[]{:S(2)}) collective-permute-start(f32[1,64,128]{2,1,0:T(8,128)S(1)} %get-tuple-element.14), channel_id=1, source_target_pairs={{2,0},{4,2},{6,4},{8,6},{10,8},{12,10},{14,12},{16,14},{18,16},{20... | collective-permute-start | bytes 98312 | tf_op jit(solution)/shard_map/ppermute | solution.py:22
  69.8 2.4 %collective-permute-start.5 = (f32[4,1,128]{2,1,0:T(1,128)S(1)}, f32[4,1,128]{2,1,0:T(1,128)S(1)}, u32[]{:S(2)}, u32[]{:S(2)}) collective-permute-start(f32[4,1,128]{2,1,0:T(1,128)S(1)} %broadcast_select_fusion.5), channel_id=1, source_target_pairs={{0,1},{1,0},{2,3},{3,2},{4,5},{5,4},{6,7},{7,6},{8,9},{9,8},{10,11... | collective-permute-start | bytes 6152 | tf_op jit(solution)/shard_map/ppermute | solution.py:16

commit v9 on v8

--- a/solution.py
+++ b/solution.py
@@ -24,7 +24,7 @@
 
 
 def with_halo(cells):
-    return exchange(exchange(cells, "vox", 0), "star", 1)
+    return lax.optimization_barrier(exchange(exchange(cells, "vox", 0), "star", 1))
 
 
 def per_device(

time: 79.2 us -> 79.4 us (level)
  transfers between devices with their start and end apart: 7 -> 7, of which waited for: 4 -> 3; matrix products, arithmetic and copies ran while one was open for 10% -> 10% of each run, Pallas kernels for 0% -> 0%
where the time goes in v9:
time: 79.4 us; the launch traced here: 78.6 us
  starting transfers between devices  17.3 us (22%)
  blocking collectives  16.9 us (21%)
  other arithmetic  16.7 us (21%)
  matrix products  12.2 us (15%)
  waiting for transfers between devices  9.93 us (13%)
  local copies, waits for them, and re-layouts  4.79 us (6%)
  between operations  0.85 us (1%)
    all_to_all x1, blocking collectives, per_device(): lax.all_to_all(partial.reshape(group_size, star_count, samples, length),...  16.9 us
    dot_general x1, matrix products, per_device(): jnp.einsum('xysw,zw->xysz', smoothed, vertical_mix, precision=HIGH)  7.74 us
    ppermute x2, starting transfers between devices, exchange(): below = lax.ppermute(tail, axis, [(i, i + 1) for i in range(count - 1)])  6.58 us
    all_to_all x1, waiting for transfers between devices, per_device(): lax.all_to_all(spread, 'vox', split_axis=0, concat_axis=0, tiled=True)  6.37 us
    add x1, other arithmetic, per_device(): gradient = grad_latent + jnp.mean(latent, axis=2)  6.3 us
    ppermute x2, starting transfers between devices, exchange(): above = lax.ppermute(head, axis, [(i + 1, i) for i in range(count - 1)])  4.23 us
    all_to_all x1, starting transfers between devices, per_device(): lax.all_to_all(spread, 'vox', split_axis=0, concat_axis=0, tiled=True)  3.95 us
    ppermute x2, waiting for transfers between devices, exchange(): above = lax.ppermute(head, axis, [(i + 1, i) for i in range(count - 1)])  2.9 us
  transfers between devices with their start and end apart: 7, of which 3 were waited for; matrix products, arithmetic and copies ran while one was open for 10% of the time, Pallas kernels for 0%

profile of v9, /device:TPU:1, one launch (start us, length us, event | category | flops | bytes accessed | tf_op | source)
XLA Modules:
  0.0 78.6 jit_solution(17370195192202946730)
XLA Ops:
  0.6 1.8 %fusion.47 = (f32[2,64,128]{2,1,0:T(8,128)}, f32[2,64,4,128]{3,1,0,2:T(8,128)S(1)}) fusion(f32[4,2,64,128]{3,2,1,0:T(8,128)} %param.14, f32[2,64,128]{2,1,0:T(8,128)} %param.13), kind=kLoop, calls=%fused_computation.92 | loop fusion | flops 114688 | bytes 655360 | tf_op jit(solution)/shard_map/reduce_sum | solution.py:106
  3.1 4.5 %collective-permute-start = (f32[1,64,4,128]{3,1,0,2:T(8,128)}, f32[1,64,4,128]{3,1,0,2:T(8,128)S(1)}, u32[]{:S(2)}, u32[]{:S(2)}) collective-permute-start(f32[1,64,4,128]{3,1,0,2:T(8,128)} %get-tuple-element.7), channel_id=1, source_target_pairs={{0,2},{2,4},{4,6},{6,8},{8,10},{10,12},{12,14},{14,16},{16,18},{18... | collective-permute-start | bytes 393224 | tf_op jit(solution)/shard_map/ppermute | solution.py:21
  7.7 1.9 %collective-permute-start.1 = (f32[1,64,4,128]{3,1,0,2:T(8,128)}, f32[1,64,4,128]{3,1,0,2:T(8,128)}, u32[]{:S(2)}, u32[]{:S(2)}) collective-permute-start(f32[1,64,4,128]{3,1,0,2:T(8,128)} %get-tuple-element.8), channel_id=1, source_target_pairs={{2,0},{4,2},{6,4},{8,6},{10,8},{12,10},{14,12},{16,14},{18,16},{20... | collective-permute-start | bytes 393224 | tf_op jit(solution)/shard_map/ppermute | solution.py:22
  9.6 1.2 %compare_select_fusion.1 = s32[96]{0:T(128)} fusion(s32[96]{0:T(128)} %param.19), kind=kLoop, calls=%fused_computation.82 | loop fusion | flops 288 | bytes 768 | tf_op jit(solution)/shard_map/jit(_take)/jit(_where)/select_n | solution.py:63
  10.8 1.3 %compare_and_fusion = (pred[96]{0:T(512)(128)(4,1)}, s32[96]{0:T(128)}) fusion(s32[96]{0:T(128)} %param.21, s32[96,1]{0,1:T(1,128)} %param.20), kind=kLoop, calls=%fused_computation.86 | loop fusion | flops 768 | bytes 1248 | tf_op jit(solution)/shard_map/jit(_take)/and | solution.py:85
  12.1 1.1 %compare_and_fusion.1 = pred[96]{0:T(512)(128)(4,1)} fusion(s32[96]{0:T(128)} %param.19), kind=kLoop, calls=%fused_computation.87 | loop fusion | flops 576 | bytes 480 | tf_op jit(solution)/shard_map/jit(_take)/and | solution.py:63
  13.2 1.7 %fusion.50 = (f32[1,1]{1,0:T(1,128)}, f32[1,1]{1,0:T(1,128)}, f32[1,1]{1,0:T(1,128)}, f32[1,1]{1,0:T(1,128)}, f32[1,1]{1,0:T(1,128)}, /*index=5*/f32[1,1]{1,0:T(...) fusion(f32[3,3]{1,0:T(4,128)} %param.15), kind=kLoop, calls=%fused_computation.95 | loop fusion | bytes 72 | tf_op jit(solution)/shard_map/slice | solution.py:103
  14.9 0.7 broadcast_select_fusion.1
  15.7 1.3 %collective-permute-start.2 = (f32[4,1,4,128]{3,1,0,2:T(1,128)S(1)}, f32[4,1,4,128]{3,1,0,2:T(1,128)S(1)}, u32[]{:S(2)}, u32[]{:S(2)}) collective-permute-start(f32[4,1,4,128]{3,1,0,2:T(1,128)S(1)} %broadcast_select_fusion.1), channel_id=1, source_target_pairs={{0,1},{1,0},{2,3},{3,2},{4,5},{5,4},{6,7},{7,6},{8,9},{9,8},{10,11... | collective-permute-start | bytes 24584 | tf_op jit(solution)/shard_map/ppermute | solution.py:16
  16.9 1.3 %pad_clamp_fusion.1 = s32[1024]{0:T(1024)} fusion(s32[96]{0:T(128)} %compare_select_fusion.1), kind=kLoop, calls=%fused_computation.77 | loop fusion | flops 1024 | bytes 4480 | tf_op gather
  18.2 1.0 %pad_maximum_fusion = f32[4,66,4,128]{3,1,0,2:T(8,128)S(1)} fusion(f32[4,1,4,128]{3,1,0,2:T(1,128)S(1)} %get-tuple-element.14, f32[1,64,4,128]{3,1,0,2:T(8,128)} %collective-permute-done.1, f32[2,64,4,128]{3,1,0,2:T(8,128)S(1)} %get-tuple-element.4, f32[1,64,4,128]{3,1,0,2:T(8,128)S(1)} %collective-permute-done, f32[4,1,4,128]{3,1,0,2:T(1,128)S(1)} %get-tuple-element.13), kind=kLoop, calls=%fused_computation.5 | loop fusion | flops 540672 | bytes 1081344 | tf_op jit(solution)/shard_map/concatenate | solution.py:23
  19.2 7.7 %fusion.51 = (bf16[2,64,4,128]{3,1,2,0:T(8,128)(2,1)S(1)}, f32[2,64,4,128]{3,1,2,0:T(8,128)}) fusion(f32[128]{0:T(128)} %param.17, f32[128,128]{1,0:T(8,128)} %param.16, f32[4,66,4,128]{3,1,0,2:T(8,128)S(1)} %pad_maximum_fusion, f32[]{:T(128)} %bitcast.9, f32[]{:T(128)} %bitcast.8, f32[]{:T(128)} %bitcast.7, f32[]{:T(128)} %bitcast.6, f32[]{:T(128)} %bitcast.5, ...), kind=kOutput, calls=%fused_computation.96 | convolution fusion | flops 101908480 | bytes 2818596 | tf_op jit(solution)/shard_map/xysw,zw->xysz/dot_general | solution.py:60
  27.1 0.8 %gather_fusion = bf16[96,4,128]{2,1,0:T(4,128)(2,1)S(1)} fusion(bf16[128,4,128]{2,1,0:T(4,128)(2,1)S(1)} %copy.25, s32[1024]{0:T(1024)} %pad_clamp_fusion.1), kind=kCustom, calls=%fused_computation.clone | custom fusion | bytes 196992 | tf_op jit(solution)/shard_map/jit(_take)/gather | solution.py:63
  27.9 1.8 %fusion.16 = f32[96,4,128]{2,1,0:T(4,128)S(1)} fusion(bf16[96,128,128]{2,1,0:T(8,128)(2,1)S(1)} %copy-done, bf16[96,4,128]{2,1,0:T(4,128)(2,1)S(1)} %gather_fusion, pred[96]{0:T(512)(128)(4,1)S(1)} %copy-done.5), kind=kOutput, calls=%fused_computation.33 | convolution fusion | flops 12632064 | bytes 3440736 | tf_op jit(solution)/shard_map/pij,psj->psi/dot_general | solution.py:64
  30.1 16.9 %all_to_all.10 = f32[16,8,4,128]{3,1,2,0:T(8,128)S(1)} all-to-all(f32[16,8,4,128]{3,1,2,0:T(8,128)S(1)} %copy.27), channel_id=1, replica_groups=mesh['vox'=16,'star'=2] {'vox'}, dimensions={0} | all-to-all | bytes 524288 | tf_op jit(solution)/shard_map/all_to_all | solution.py:70
  47.1 0.7 fusion.42
  48.5 4.0 %all-to-all-start.1 = ((bf16[16,8,4,128]{3,2,1,0:T(4,128)(2,1)}), bf16[16,8,4,128]{3,2,1,0:T(4,128)(2,1)S(1)}, u32[]{:S(2)}, u32[]{:S(2)}) async-start(bf16[16,8,4,128]{3,2,1,0:T(4,128)(2,1)} %broadcast_in_dim.16), calls=%async_computation.1 | async-start | bytes 262144 | tf_op jit(solution)/shard_map/all_to_all | solution.py:82
  53.1 6.4 %all-to-all-done.1 = bf16[16,8,4,128]{3,2,1,0:T(4,128)(2,1)S(1)} async-done(((bf16[16,8,4,128]{3,2,1,0:T(4,128)(2,1)}), bf16[16,8,4,128]{3,2,1,0:T(4,128)(2,1)S(1)}, u32[]{:S(2)}, u32[]{:S(2)}) %all-to-all-start.1) | async-done | bytes 131104 | tf_op jit(solution)/shard_map/all_to_all | solution.py:82
  60.1 1.7 %fusion.14 = f32[96,4,128]{2,1,0:T(4,128)S(1)} fusion(bf16[96,128,128]{2,1,0:T(8,128)(2,1)S(1)} %copy-done, bf16[96,4,128]{2,1,0:T(4,128)(2,1)S(1)} %gather_fusion.1, pred[96]{0:T(512)(128)(4,1)} %get-tuple-element.5), kind=kOutput, calls=%fused_computation.31 | convolution fusion | flops 12632064 | bytes 3440736 | tf_op jit(solution)/shard_map/pij,psi->psj/dot_general | solution.py:86
  62.5 2.1 %collective-permute-start.3 = (f32[1,64,128]{2,1,0:T(8,128)S(1)}, f32[1,64,128]{2,1,0:T(8,128)S(1)}, u32[]{:S(2)}, u32[]{:S(2)}) collective-permute-start(f32[1,64,128]{2,1,0:T(8,128)S(1)} %get-tuple-element.9), channel_id=1, source_target_pairs={{0,2},{2,4},{4,6},{6,8},{8,10},{10,12},{12,14},{14,16},{16,18},{18... | collective-permute-start | bytes 98312 | tf_op jit(solution)/shard_map/ppermute | solution.py:21
  64.6 2.3 %collective-permute-start.4 = (f32[1,64,128]{2,1,0:T(8,128)S(1)}, f32[1,64,128]{2,1,0:T(8,128)S(1)}, u32[]{:S(2)}, u32[]{:S(2)}) collective-permute-start(f32[1,64,128]{2,1,0:T(8,128)S(1)} %get-tuple-element.10), channel_id=1, source_target_pairs={{2,0},{4,2},{6,4},{8,6},{10,8},{12,10},{14,12},{16,14},{18,16},{20... | collective-permute-start | bytes 98312 | tf_op jit(solution)/shard_map/ppermute | solution.py:22
  66.9 2.9 %collective-permute-done.4 = f32[1,64,128]{2,1,0:T(8,128)S(1)} collective-permute-done((f32[1,64,128]{2,1,0:T(8,128)S(1)}, f32[1,64,128]{2,1,0:T(8,128)S(1)}, u32[]{:S(2)}, u32[]{:S(2)}) %collective-permute-start.4) | collective-permute-done | bytes 32800 | tf_op jit(solution)/shard_map/ppermute | solution.py:22
  69.8 1.2 %collective-permute-start.5 = (f32[4,1,128]{2,1,0:T(1,128)S(1)}, f32[4,1,128]{2,1,0:T(1,128)S(1)}, u32[]{:S(2)}, u32[]{:S(2)}) collective-permute-start(f32[4,1,128]{2,1,0:T(1,128)S(1)} %broadcast_select_fusion.4), channel_id=1, source_target_pairs={{0,1},{1,0},{2,3},{3,2},{4,5},{5,4},{6,7},{7,6},{8,9},{9,8},{10,11... | collective-permute-start | bytes 6152 | tf_op jit(solution)/shard_map/ppermute | solution.py:16
  72.3 6.3 %fusion.21 = f32[2,64,128]{2,1,0:T(8,128)} fusion(f32[4,66,128]{2,1,0:T(8,128)S(1)} %pad_maximum_fusion.1, f32[2,64,128]{2,1,0:T(8,128)S(1)} %copy-done.1, f32[]{:T(128)} %bitcast.9, f32[]{:T(128)} %bitcast.8, f32[]{:T(128)} %bitcast.7, f32[]{:T(128)} %bitcast.6, f32[]{:T(128)} %bitcast.5, f32[]{:T(128)} %bitcast.4, f32[]{:T(128)} %bitcast.3, f32[]{:T(128)} %bitcast.2, ...), kind=kLoop, calls=%fused_computation.39 | loop fusion | flops 311296 | bytes 720932 | tf_op jit(solution)/shard_map/add | solution.py:106
  (39 shorter events, 5.2 us)
Async XLA Ops:
  0.6 27.3 %copy-start = (bf16[96,128,128]{2,1,0:T(8,128)(2,1)S(1)}, bf16[96,128,128]{2,1,0:T(8,128)(2,1)}, u32[]{:S(2)}) copy-start(bf16[96,128,128]{2,1,0:T(8,128)(2,1)} %param.18) | copy-start | bytes 9437188
  3.1 11.8 %collective-permute-start = (f32[1,64,4,128]{3,1,0,2:T(8,128)}, f32[1,64,4,128]{3,1,0,2:T(8,128)S(1)}, u32[]{:S(2)}, u32[]{:S(2)}) collective-permute-start(f32[1,64,4,128]{3,1,0,2:T(8,128)} %get-tuple-element.7), channel_id=1, source_target_pairs={{0,2},{2,4},{4,6},{6,8},{8,10},{10,12},{12,14},{14,16},{16,18},{18... | collective-permute-start | bytes 393224 | tf_op jit(solution)/shard_map/ppermute | solution.py:21
  7.7 7.2 %collective-permute-start.1 = (f32[1,64,4,128]{3,1,0,2:T(8,128)}, f32[1,64,4,128]{3,1,0,2:T(8,128)}, u32[]{:S(2)}, u32[]{:S(2)}) collective-permute-start(f32[1,64,4,128]{3,1,0,2:T(8,128)} %get-tuple-element.8), channel_id=1, source_target_pairs={{2,0},{4,2},{6,4},{8,6},{10,8},{12,10},{14,12},{16,14},{18,16},{20... | collective-permute-start | bytes 393224 | tf_op jit(solution)/shard_map/ppermute | solution.py:22
  15.7 2.6 %collective-permute-start.2 = (f32[4,1,4,128]{3,1,0,2:T(1,128)S(1)}, f32[4,1,4,128]{3,1,0,2:T(1,128)S(1)}, u32[]{:S(2)}, u32[]{:S(2)}) collective-permute-start(f32[4,1,4,128]{3,1,0,2:T(1,128)S(1)} %broadcast_select_fusion.1), channel_id=1, source_target_pairs={{0,1},{1,0},{2,3},{3,2},{4,5},{5,4},{6,7},{7,6},{8,9},{9,8},{10,11... | collective-permute-start | bytes 24584 | tf_op jit(solution)/shard_map/ppermute | solution.py:16
  18.2 9.7 %copy-start.5 = (pred[96]{0:T(512)(128)(4,1)S(1)}, pred[96]{0:T(512)(128)(4,1)}, u32[]{:S(2)}) copy-start(pred[96]{0:T(512)(128)(4,1)} %compare_and_fusion.1) | copy-start | bytes 292
  19.2 10.5 %copy-start.4 = (s32[96]{0:T(128)S(1)}, s32[96]{0:T(128)}, u32[]{:S(2)}) copy-start(s32[96]{0:T(128)} %get-tuple-element.6) | copy-start | bytes 1156
  30.1 32.2 %copy-start.3 = (f32[128,128]{1,0:T(8,128)S(1)}, f32[128,128]{1,0:T(8,128)}, u32[]{:S(2)}) copy-start(f32[128,128]{1,0:T(8,128)} %param.16) | copy-start | bytes 196612
  47.0 25.2 %copy-start.1 = (f32[2,64,128]{2,1,0:T(8,128)S(1)}, f32[2,64,128]{2,1,0:T(8,128)}, u32[]{:S(2)}) copy-start(f32[2,64,128]{2,1,0:T(8,128)} %get-tuple-element.3) | copy-start | bytes 196612
  47.1 14.7 %copy-start.6 = (s32[96]{0:T(128)S(1)}, s32[96]{0:T(128)}, u32[]{:S(2)}) copy-start(s32[96]{0:T(128)} %param.19) | copy-start | bytes 1156
  48.5 10.9 %all-to-all-start.1 = ((bf16[16,8,4,128]{3,2,1,0:T(4,128)(2,1)}), bf16[16,8,4,128]{3,2,1,0:T(4,128)(2,1)S(1)}, u32[]{:S(2)}, u32[]{:S(2)}) async-start(bf16[16,8,4,128]{3,2,1,0:T(4,128)(2,1)} %broadcast_in_dim.16), calls=%async_computation.1 | async-start | bytes 262144 | tf_op jit(solution)/shard_map/all_to_all | solution.py:82
  60.1 2.1 %copy-start.2 = (f32[2,64,4,128]{3,1,2,0:T(8,128)S(1)}, f32[2,64,4,128]{3,1,2,0:T(8,128)}, u32[]{:S(2)}) copy-start(f32[2,64,4,128]{3,1,2,0:T(8,128)} %get-tuple-element.27) | copy-start | bytes 786436
  62.5 4.4 %collective-permute-start.3 = (f32[1,64,128]{2,1,0:T(8,128)S(1)}, f32[1,64,128]{2,1,0:T(8,128)S(1)}, u32[]{:S(2)}, u32[]{:S(2)}) collective-permute-start(f32[1,64,128]{2,1,0:T(8,128)S(1)} %get-tuple-element.9), channel_id=1, source_target_pairs={{0,2},{2,4},{4,6},{6,8},{8,10},{10,12},{12,14},{14,16},{16,18},{18... | collective-permute-start | bytes 98312 | tf_op jit(solution)/shard_map/ppermute | solution.py:21
  64.6 5.2 %collective-permute-start.4 = (f32[1,64,128]{2,1,0:T(8,128)S(1)}, f32[1,64,128]{2,1,0:T(8,128)S(1)}, u32[]{:S(2)}, u32[]{:S(2)}) collective-permute-start(f32[1,64,128]{2,1,0:T(8,128)S(1)} %get-tuple-element.10), channel_id=1, source_target_pairs={{2,0},{4,2},{6,4},{8,6},{10,8},{12,10},{14,12},{16,14},{18,16},{20... | collective-permute-start | bytes 98312 | tf_op jit(solution)/shard_map/ppermute | solution.py:22
  69.8 2.4 %collective-permute-start.5 = (f32[4,1,128]{2,1,0:T(1,128)S(1)}, f32[4,1,128]{2,1,0:T(1,128)S(1)}, u32[]{:S(2)}, u32[]{:S(2)}) collective-permute-start(f32[4,1,128]{2,1,0:T(1,128)S(1)} %broadcast_select_fusion.4), channel_id=1, source_target_pairs={{0,1},{1,0},{2,3},{3,2},{4,5},{5,4},{6,7},{7,6},{8,9},{9,8},{10,11... | collective-permute-start | bytes 6152 | tf_op jit(solution)/shard_map/ppermute | solution.py:16

commit v10 on v9

--- a/solution.py
+++ b/solution.py
@@ -48,13 +48,16 @@
     star_count = observed.shape[0]
     group_blocks = group_size * star_count
     latent = jnp.transpose(mean_field[None] + deviations, (1, 2, 0, 3))
+    weights = lax.optimization_barrier(
+        jnp.broadcast_to(stencil.reshape(9, 1), (9, length))
+    )
     padded = with_halo(latent)
     smoothed = jnp.zeros(latent.shape, jnp.float32)
     for offset_x in range(3):
         for offset_y in range(3):
             smoothed = (
                 smoothed
-                + stencil[offset_x, offset_y]
+                + weights[offset_x * 3 + offset_y]
                 * padded[offset_x : offset_x + width_x, offset_y : offset_y + width_y]
             )
     log_density = jnp.einsum("xysw,zw->xysz", smoothed, vertical_mix, precision=HIGH) + log_mean
@@ -100,7 +103,7 @@
         for offset_y in range(3):
             grad_latent = (
                 grad_latent
-                + stencil[offset_x, offset_y]
+                + weights[offset_x * 3 + offset_y]
                 * padded_grad[2 - offset_x : 2 - offset_x + width_x, 2 - offset_y : 2 - offset_y + width_y]
             )
     gradient = grad_latent + jnp.mean(latent, axis=2)

time: 79.4 us -> 68 us (0.86)
  matrix products: 12.2 us -> 6.57 us
  other arithmetic: 16.7 us -> 11.2 us
    add x1, other arithmetic: 6.3 us -> 0.7 us  [per_device(): gradient = grad_latent + jnp.mean(latent, axis=2)]
    dot_general x1, matrix products: 7.74 us -> 2.15 us  [per_device(): jnp.einsum('xysw,zw->xysz', smoothed, vertical_mix, precision=HIGH)]
    slice x1 -> x0, local copies, waits for them, and re-layouts: 1.66 us -> none  [per_device(): stencil[offset_x, offset_y]]
    broadcast_in_dim x0 -> x2, local copies, waits for them, and re-layouts: none -> 0.84 us  [per_device(): jnp.broadcast_to(stencil.reshape(9, 1), (9, length))]
  transfers between devices with their start and end apart: 7 -> 7, of which waited for: 3 -> 3; matrix products, arithmetic and copies ran while one was open for 10% -> 11% of each run, Pallas kernels for 0% -> 0%
where the time goes in v10:
time: 68 us; the launch traced here: 67.4 us
  starting transfers between devices  17.3 us (25%)
  blocking collectives  16.9 us (25%)
  other arithmetic  11.2 us (16%)
  waiting for transfers between devices  9.87 us (15%)
  matrix products  6.57 us (10%)
  local copies, waits for them, and re-layouts  4.59 us (7%)
  between operations  0.99 us (1%)
    all_to_all x1, blocking collectives, per_device(): lax.all_to_all(partial.reshape(group_size, star_count, samples, length),...  16.9 us
    ppermute x2, starting transfers between devices, exchange(): below = lax.ppermute(tail, axis, [(i, i + 1) for i in range(count - 1)])  6.58 us
    all_to_all x1, waiting for transfers between devices, per_device(): lax.all_to_all(spread, 'vox', split_axis=0, concat_axis=0, tiled=True)  6.31 us
    ppermute x2, starting transfers between devices, exchange(): above = lax.ppermute(head, axis, [(i + 1, i) for i in range(count - 1)])  4.24 us
    all_to_all x1, starting transfers between devices, per_device(): lax.all_to_all(spread, 'vox', split_axis=0, concat_axis=0, tiled=True)  3.95 us
    ppermute x2, waiting for transfers between devices, exchange(): above = lax.ppermute(head, axis, [(i + 1, i) for i in range(count - 1)])  2.9 us
    ppermute x2, starting transfers between devices, exchange(): lax.ppermute(jnp.where(index == 0, tail, head), axis, [(0, 1), (1, 0)])  2.5 us
    dot_general x1, matrix products, per_device(): jnp.einsum('xysw,zw->xysz', smoothed, vertical_mix, precision=HIGH)  2.15 us
  transfers between devices with their start and end apart: 7, of which 3 were waited for; matrix products, arithmetic and copies ran while one was open for 11% of the time, Pallas kernels for 0%

profile of v10, /device:TPU:1, one launch (start us, length us, event | category | flops | bytes accessed | tf_op | source)
XLA Modules:
  0.0 67.4 jit_solution(17656167887791841060)
XLA Ops:
  0.6 1.8 %fusion.47 = (f32[2,64,128]{2,1,0:T(8,128)}, f32[2,64,4,128]{3,1,0,2:T(8,128)S(1)}) fusion(f32[4,2,64,128]{3,2,1,0:T(8,128)} %param.14, f32[2,64,128]{2,1,0:T(8,128)} %param.13), kind=kLoop, calls=%fused_computation.101 | loop fusion | flops 114688 | bytes 655360 | tf_op jit(solution)/shard_map/reduce_sum | solution.py:109
  2.4 0.7 %fusion.48 = (f32[1,64,4,128]{3,1,0,2:T(8,128)}, f32[1,64,4,128]{3,1,0,2:T(8,128)}) fusion(f32[2,64,4,128]{3,1,0,2:T(8,128)S(1)} %get-tuple-element.4), kind=kLoop, calls=%fused_computation.102 | loop fusion | bytes 524288 | tf_op jit(solution)/shard_map/slice | solution.py:13
  3.1 4.5 %collective-permute-start = (f32[1,64,4,128]{3,1,0,2:T(8,128)}, f32[1,64,4,128]{3,1,0,2:T(8,128)S(1)}, u32[]{:S(2)}, u32[]{:S(2)}) collective-permute-start(f32[1,64,4,128]{3,1,0,2:T(8,128)} %get-tuple-element.7), channel_id=1, source_target_pairs={{0,2},{2,4},{4,6},{6,8},{8,10},{10,12},{12,14},{14,16},{16,18},{18... | collective-permute-start | bytes 393224 | tf_op jit(solution)/shard_map/ppermute | solution.py:21
  7.7 1.9 %collective-permute-start.1 = (f32[1,64,4,128]{3,1,0,2:T(8,128)}, f32[1,64,4,128]{3,1,0,2:T(8,128)}, u32[]{:S(2)}, u32[]{:S(2)}) collective-permute-start(f32[1,64,4,128]{3,1,0,2:T(8,128)} %get-tuple-element.8), channel_id=1, source_target_pairs={{2,0},{4,2},{6,4},{8,6},{10,8},{12,10},{14,12},{16,14},{18,16},{20... | collective-permute-start | bytes 393224 | tf_op jit(solution)/shard_map/ppermute | solution.py:22
  9.6 0.8 %broadcast_in_dim.19 = f32[9]{0:T(128)S(1)} reshape(f32[3,3]{1,0:T(4,128)} %param.15) | data formatting | bytes 72 | tf_op jit(solution)/shard_map/broadcast_in_dim | solution.py:52
  11.0 1.2 %compare_select_fusion.1 = s32[96]{0:T(128)} fusion(s32[96]{0:T(128)} %param.19), kind=kLoop, calls=%fused_computation.82 | loop fusion | flops 288 | bytes 768 | tf_op jit(solution)/shard_map/jit(_take)/jit(_where)/select_n | solution.py:66
  12.3 1.3 %compare_and_fusion = (pred[96]{0:T(512)(128)(4,1)}, s32[96]{0:T(128)}) fusion(s32[96]{0:T(128)} %param.21, s32[96,1]{0,1:T(1,128)} %param.20), kind=kLoop, calls=%fused_computation.86 | loop fusion | flops 768 | bytes 1248 | tf_op jit(solution)/shard_map/jit(_take)/and | solution.py:88
  13.5 1.2 %compare_and_fusion.1 = pred[96]{0:T(512)(128)(4,1)} fusion(s32[96]{0:T(128)} %param.19), kind=kLoop, calls=%fused_computation.87 | loop fusion | flops 576 | bytes 480 | tf_op jit(solution)/shard_map/jit(_take)/and | solution.py:66
  14.8 0.7 %broadcast_select_fusion.1 = f32[4,1,4,128]{3,1,0,2:T(1,128)S(1)} fusion(pred[]{:T(512)S(6)} %eq.17, f32[1,64,4,128]{3,1,0,2:T(8,128)} %collective-permute-done.1, f32[2,64,4,128]{3,1,0,2:T(8,128)S(1)} %get-tuple-element.4, f32[1,64,4,128]{3,1,0,2:T(8,128)S(1)} %collective-permute-done), kind=kLoop, calls=%fused_computation.70 | loop fusion | flops 10240 | bytes 532481 | tf_op jit(solution)/shard_map/jit(_where)/select_n | solution.py:16
  15.5 1.3 %collective-permute-start.2 = (f32[4,1,4,128]{3,1,0,2:T(1,128)S(1)}, f32[4,1,4,128]{3,1,0,2:T(1,128)S(1)}, u32[]{:S(2)}, u32[]{:S(2)}) collective-permute-start(f32[4,1,4,128]{3,1,0,2:T(1,128)S(1)} %broadcast_select_fusion.1), channel_id=1, source_target_pairs={{0,1},{1,0},{2,3},{3,2},{4,5},{5,4},{6,7},{7,6},{8,9},{9,8},{10,11... | collective-permute-start | bytes 24584 | tf_op jit(solution)/shard_map/ppermute | solution.py:16
  16.8 1.3 %pad_clamp_fusion.1 = s32[1024]{0:T(1024)} fusion(s32[96]{0:T(128)} %compare_select_fusion.1), kind=kLoop, calls=%fused_computation.77 | loop fusion | flops 1024 | bytes 4480 | tf_op gather
  18.1 1.0 %pad_maximum_fusion = f32[4,66,4,128]{3,1,0,2:T(8,128)S(1)} fusion(f32[4,1,4,128]{3,1,0,2:T(1,128)S(1)} %get-tuple-element.23, f32[1,64,4,128]{3,1,0,2:T(8,128)} %collective-permute-done.1, f32[2,64,4,128]{3,1,0,2:T(8,128)S(1)} %get-tuple-element.4, f32[1,64,4,128]{3,1,0,2:T(8,128)S(1)} %collective-permute-done, f32[4,1,4,128]{3,1,0,2:T(1,128)S(1)} %get-tuple-element.22), kind=kLoop, calls=%fused_computation.5 | loop fusion | flops 540672 | bytes 1081344 | tf_op jit(solution)/shard_map/concatenate | solution.py:23
  19.1 2.1 %fusion.50 = (bf16[2,64,4,128]{3,1,2,0:T(8,128)(2,1)S(1)}, f32[2,64,4,128]{3,1,2,0:T(8,128)}) fusion(f32[128]{0:T(128)} %param.17, f32[128,128]{1,0:T(8,128)} %param.16, f32[4,66,4,128]{3,1,0,2:T(8,128)S(1)} %pad_maximum_fusion, f32[128]{0:T(128)} %get-tuple-element.14, f32[128]{0:T(128)} %get-tuple-element.15, f32[128]{0:T(128)} %get-tuple-element.16, ...), kind=kOutput, calls=%fused_computation.104 | convolution fusion | flops 101908480 | bytes 2823168 | tf_op jit(solution)/shard_map/xysw,zw->xysz/dot_general | solution.py:63
  21.4 0.8 %gather_fusion = bf16[96,4,128]{2,1,0:T(4,128)(2,1)S(1)} fusion(bf16[128,4,128]{2,1,0:T(4,128)(2,1)S(1)} %copy.25, s32[1024]{0:T(1024)} %pad_clamp_fusion.1), kind=kCustom, calls=%fused_computation.clone | custom fusion | bytes 196992 | tf_op jit(solution)/shard_map/jit(_take)/gather | solution.py:66
  22.2 1.8 %fusion.16 = f32[96,4,128]{2,1,0:T(4,128)S(1)} fusion(bf16[96,128,128]{2,1,0:T(8,128)(2,1)S(1)} %copy-done, bf16[96,4,128]{2,1,0:T(4,128)(2,1)S(1)} %gather_fusion, pred[96]{0:T(512)(128)(4,1)S(1)} %copy-done.14), kind=kOutput, calls=%fused_computation.33 | convolution fusion | flops 12632064 | bytes 3440736 | tf_op jit(solution)/shard_map/pij,psj->psi/dot_general | solution.py:67
  24.4 16.9 %all_to_all.10 = f32[16,8,4,128]{3,1,2,0:T(8,128)S(1)} all-to-all(f32[16,8,4,128]{3,1,2,0:T(8,128)S(1)} %copy.27), channel_id=1, replica_groups=mesh['vox'=16,'star'=2] {'vox'}, dimensions={0} | all-to-all | bytes 524288 | tf_op jit(solution)/shard_map/all_to_all | solution.py:73
  41.4 0.7 %fusion.42 = (f32[8,128]{1,0:T(8,128)S(1)}, bf16[8,4,128]{2,0,1:T(8,128)(2,1)S(1)}) fusion(f32[8,4,128]{2,0,1:T(8,128)S(1)} %reduce_sum.36, f32[8,128]{1,0:T(8,128)} %param.22, f32[8,128]{1,0:T(8,128)} %param.23), kind=kLoop, calls=%fused_computation.72 | loop fusion | flops 15360 | bytes 36864 | tf_op jit(solution)/shard_map/reduce_sum | solution.py:82
  42.8 4.0 %all-to-all-start.1 = ((bf16[16,8,4,128]{3,2,1,0:T(4,128)(2,1)}), bf16[16,8,4,128]{3,2,1,0:T(4,128)(2,1)S(1)}, u32[]{:S(2)}, u32[]{:S(2)}) async-start(bf16[16,8,4,128]{3,2,1,0:T(4,128)(2,1)} %broadcast_in_dim.22), calls=%async_computation.1 | async-start | bytes 262144 | tf_op jit(solution)/shard_map/all_to_all | solution.py:85
  47.4 6.3 %all-to-all-done.1 = bf16[16,8,4,128]{3,2,1,0:T(4,128)(2,1)S(1)} async-done(((bf16[16,8,4,128]{3,2,1,0:T(4,128)(2,1)}), bf16[16,8,4,128]{3,2,1,0:T(4,128)(2,1)S(1)}, u32[]{:S(2)}, u32[]{:S(2)}) %all-to-all-start.1) | async-done | bytes 131104 | tf_op jit(solution)/shard_map/all_to_all | solution.py:85
  54.4 1.7 %fusion.14 = f32[96,4,128]{2,1,0:T(4,128)S(1)} fusion(bf16[96,128,128]{2,1,0:T(8,128)(2,1)S(1)} %copy-done, bf16[96,4,128]{2,1,0:T(4,128)(2,1)S(1)} %gather_fusion.1, pred[96]{0:T(512)(128)(4,1)} %get-tuple-element.5), kind=kOutput, calls=%fused_computation.31 | convolution fusion | flops 12632064 | bytes 3440736 | tf_op jit(solution)/shard_map/pij,psi->psj/dot_general | solution.py:89
  56.8 2.1 %collective-permute-start.3 = (f32[1,64,128]{2,1,0:T(8,128)S(1)}, f32[1,64,128]{2,1,0:T(8,128)S(1)}, u32[]{:S(2)}, u32[]{:S(2)}) collective-permute-start(f32[1,64,128]{2,1,0:T(8,128)S(1)} %get-tuple-element.9), channel_id=1, source_target_pairs={{0,2},{2,4},{4,6},{6,8},{8,10},{10,12},{12,14},{14,16},{16,18},{18... | collective-permute-start | bytes 98312 | tf_op jit(solution)/shard_map/ppermute | solution.py:21
  58.9 2.3 %collective-permute-start.4 = (f32[1,64,128]{2,1,0:T(8,128)S(1)}, f32[1,64,128]{2,1,0:T(8,128)S(1)}, u32[]{:S(2)}, u32[]{:S(2)}) collective-permute-start(f32[1,64,128]{2,1,0:T(8,128)S(1)} %get-tuple-element.10), channel_id=1, source_target_pairs={{2,0},{4,2},{6,4},{8,6},{10,8},{12,10},{14,12},{16,14},{18,16},{20... | collective-permute-start | bytes 98312 | tf_op jit(solution)/shard_map/ppermute | solution.py:22
  61.2 2.9 %collective-permute-done.4 = f32[1,64,128]{2,1,0:T(8,128)S(1)} collective-permute-done((f32[1,64,128]{2,1,0:T(8,128)S(1)}, f32[1,64,128]{2,1,0:T(8,128)S(1)}, u32[]{:S(2)}, u32[]{:S(2)}) %collective-permute-start.4) | collective-permute-done | bytes 32800 | tf_op jit(solution)/shard_map/ppermute | solution.py:22
  64.1 1.2 %collective-permute-start.5 = (f32[4,1,128]{2,1,0:T(1,128)S(1)}, f32[4,1,128]{2,1,0:T(1,128)S(1)}, u32[]{:S(2)}, u32[]{:S(2)}) collective-permute-start(f32[4,1,128]{2,1,0:T(1,128)S(1)} %broadcast_select_fusion.4), channel_id=1, source_target_pairs={{0,1},{1,0},{2,3},{3,2},{4,5},{5,4},{6,7},{7,6},{8,9},{9,8},{10,11... | collective-permute-start | bytes 6152 | tf_op jit(solution)/shard_map/ppermute | solution.py:16
  (59 shorter events, 6.0 us)
Async XLA Ops:
  0.6 21.6 %copy-start = (bf16[96,128,128]{2,1,0:T(8,128)(2,1)S(1)}, bf16[96,128,128]{2,1,0:T(8,128)(2,1)}, u32[]{:S(2)}) copy-start(bf16[96,128,128]{2,1,0:T(8,128)(2,1)} %param.18) | copy-start | bytes 9437188
  3.1 11.6 %collective-permute-start = (f32[1,64,4,128]{3,1,0,2:T(8,128)}, f32[1,64,4,128]{3,1,0,2:T(8,128)S(1)}, u32[]{:S(2)}, u32[]{:S(2)}) collective-permute-start(f32[1,64,4,128]{3,1,0,2:T(8,128)} %get-tuple-element.7), channel_id=1, source_target_pairs={{0,2},{2,4},{4,6},{6,8},{8,10},{10,12},{12,14},{14,16},{16,18},{18... | collective-permute-start | bytes 393224 | tf_op jit(solution)/shard_map/ppermute | solution.py:21
  7.7 7.1 %collective-permute-start.1 = (f32[1,64,4,128]{3,1,0,2:T(8,128)}, f32[1,64,4,128]{3,1,0,2:T(8,128)}, u32[]{:S(2)}, u32[]{:S(2)}) collective-permute-start(f32[1,64,4,128]{3,1,0,2:T(8,128)} %get-tuple-element.8), channel_id=1, source_target_pairs={{2,0},{4,2},{6,4},{8,6},{10,8},{12,10},{14,12},{16,14},{18,16},{20... | collective-permute-start | bytes 393224 | tf_op jit(solution)/shard_map/ppermute | solution.py:22
  15.5 2.6 %collective-permute-start.2 = (f32[4,1,4,128]{3,1,0,2:T(1,128)S(1)}, f32[4,1,4,128]{3,1,0,2:T(1,128)S(1)}, u32[]{:S(2)}, u32[]{:S(2)}) collective-permute-start(f32[4,1,4,128]{3,1,0,2:T(1,128)S(1)} %broadcast_select_fusion.1), channel_id=1, source_target_pairs={{0,1},{1,0},{2,3},{3,2},{4,5},{5,4},{6,7},{7,6},{8,9},{9,8},{10,11... | collective-permute-start | bytes 24584 | tf_op jit(solution)/shard_map/ppermute | solution.py:16
  18.1 4.1 %copy-start.14 = (pred[96]{0:T(512)(128)(4,1)S(1)}, pred[96]{0:T(512)(128)(4,1)}, u32[]{:S(2)}) copy-start(pred[96]{0:T(512)(128)(4,1)} %compare_and_fusion.1) | copy-start | bytes 292
  19.1 4.9 %copy-start.13 = (s32[96]{0:T(128)S(1)}, s32[96]{0:T(128)}, u32[]{:S(2)}) copy-start(s32[96]{0:T(128)} %get-tuple-element.6) | copy-start | bytes 1156
  24.4 32.2 %copy-start.3 = (f32[128,128]{1,0:T(8,128)S(1)}, f32[128,128]{1,0:T(8,128)}, u32[]{:S(2)}) copy-start(f32[128,128]{1,0:T(8,128)} %param.16) | copy-start | bytes 196612
  41.3 25.3 %copy-start.1 = (f32[2,64,128]{2,1,0:T(8,128)S(1)}, f32[2,64,128]{2,1,0:T(8,128)}, u32[]{:S(2)}) copy-start(f32[2,64,128]{2,1,0:T(8,128)} %get-tuple-element.3) | copy-start | bytes 196612
  41.3 25.3 %copy-start.4 = (f32[128]{0:T(128)S(1)}, f32[128]{0:T(128)}, u32[]{:S(2)}) copy-start(f32[128]{0:T(128)} %get-tuple-element.13) | copy-start | bytes 1540
  41.3 25.3 %copy-start.5 = (f32[128]{0:T(128)S(1)}, f32[128]{0:T(128)}, u32[]{:S(2)}) copy-start(f32[128]{0:T(128)} %get-tuple-element.14) | copy-start | bytes 1540
  41.3 25.3 %copy-start.6 = (f32[128]{0:T(128)S(1)}, f32[128]{0:T(128)}, u32[]{:S(2)}) copy-start(f32[128]{0:T(128)} %get-tuple-element.15) | copy-start | bytes 1540
  41.4 25.3 %copy-start.7 = (f32[128]{0:T(128)S(1)}, f32[128]{0:T(128)}, u32[]{:S(2)}) copy-start(f32[128]{0:T(128)} %get-tuple-element.16) | copy-start | bytes 1540
  41.4 25.3 %copy-start.8 = (f32[128]{0:T(128)S(1)}, f32[128]{0:T(128)}, u32[]{:S(2)}) copy-start(f32[128]{0:T(128)} %get-tuple-element.17) | copy-start | bytes 1540
  41.4 25.3 %copy-start.9 = (f32[128]{0:T(128)S(1)}, f32[128]{0:T(128)}, u32[]{:S(2)}) copy-start(f32[128]{0:T(128)} %get-tuple-element.18) | copy-start | bytes 1540
  42.1 14.0 %copy-start.15 = (s32[96]{0:T(128)S(1)}, s32[96]{0:T(128)}, u32[]{:S(2)}) copy-start(s32[96]{0:T(128)} %param.19) | copy-start | bytes 1156
  42.1 24.5 %copy-start.10 = (f32[128]{0:T(128)S(1)}, f32[128]{0:T(128)}, u32[]{:S(2)}) copy-start(f32[128]{0:T(128)} %get-tuple-element.19) | copy-start | bytes 1540
  42.1 24.5 %copy-start.11 = (f32[128]{0:T(128)S(1)}, f32[128]{0:T(128)}, u32[]{:S(2)}) copy-start(f32[128]{0:T(128)} %get-tuple-element.20) | copy-start | bytes 1540
  42.1 24.5 %copy-start.12 = (f32[128]{0:T(128)S(1)}, f32[128]{0:T(128)}, u32[]{:S(2)}) copy-start(f32[128]{0:T(128)} %get-tuple-element.21) | copy-start | bytes 1540
  42.8 10.9 %all-to-all-start.1 = ((bf16[16,8,4,128]{3,2,1,0:T(4,128)(2,1)}), bf16[16,8,4,128]{3,2,1,0:T(4,128)(2,1)S(1)}, u32[]{:S(2)}, u32[]{:S(2)}) async-start(bf16[16,8,4,128]{3,2,1,0:T(4,128)(2,1)} %broadcast_in_dim.22), calls=%async_computation.1 | async-start | bytes 262144 | tf_op jit(solution)/shard_map/all_to_all | solution.py:85
  54.4 2.1 %copy-start.2 = (f32[2,64,4,128]{3,1,2,0:T(8,128)S(1)}, f32[2,64,4,128]{3,1,2,0:T(8,128)}, u32[]{:S(2)}) copy-start(f32[2,64,4,128]{3,1,2,0:T(8,128)} %get-tuple-element.27) | copy-start | bytes 786436
  56.8 4.4 %collective-permute-start.3 = (f32[1,64,128]{2,1,0:T(8,128)S(1)}, f32[1,64,128]{2,1,0:T(8,128)S(1)}, u32[]{:S(2)}, u32[]{:S(2)}) collective-permute-start(f32[1,64,128]{2,1,0:T(8,128)S(1)} %get-tuple-element.9), channel_id=1, source_target_pairs={{0,2},{2,4},{4,6},{6,8},{8,10},{10,12},{12,14},{14,16},{16,18},{18... | collective-permute-start | bytes 98312 | tf_op jit(solution)/shard_map/ppermute | solution.py:21
  58.9 5.2 %collective-permute-start.4 = (f32[1,64,128]{2,1,0:T(8,128)S(1)}, f32[1,64,128]{2,1,0:T(8,128)S(1)}, u32[]{:S(2)}, u32[]{:S(2)}) collective-permute-start(f32[1,64,128]{2,1,0:T(8,128)S(1)} %get-tuple-element.10), channel_id=1, source_target_pairs={{2,0},{4,2},{6,4},{8,6},{10,8},{12,10},{14,12},{16,14},{18,16},{20... | collective-permute-start | bytes 98312 | tf_op jit(solution)/shard_map/ppermute | solution.py:22
  64.1 2.4 %collective-permute-start.5 = (f32[4,1,128]{2,1,0:T(1,128)S(1)}, f32[4,1,128]{2,1,0:T(1,128)S(1)}, u32[]{:S(2)}, u32[]{:S(2)}) collective-permute-start(f32[4,1,128]{2,1,0:T(1,128)S(1)} %broadcast_select_fusion.4), channel_id=1, source_target_pairs={{0,1},{1,0},{2,3},{3,2},{4,5},{5,4},{6,7},{7,6},{8,9},{9,8},{10,11... | collective-permute-start | bytes 6152 | tf_op jit(solution)/shard_map/ppermute | solution.py:16

commit v11 on v10

--- a/solution.py
+++ b/solution.py
@@ -25,6 +25,22 @@
 
 def with_halo(cells):
     return lax.optimization_barrier(exchange(exchange(cells, "vox", 0), "star", 1))
+
+
+def rows(table, index, axis):
+    numbers = lax.GatherDimensionNumbers(
+        offset_dims=tuple(d for d in range(table.ndim) if d != axis),
+        collapsed_slice_dims=(axis,),
+        start_index_map=(axis,),
+    )
+    sizes = tuple(1 if d == axis else n for d, n in enumerate(table.shape))
+    return lax.gather(
+        table,
+        index[:, None],
+        numbers,
+        sizes,
+        mode=lax.GatherScatterMode.PROMISE_IN_BOUNDS,
+    )
 
 
 def per_device(
@@ -63,7 +79,7 @@
     log_density = jnp.einsum("xysw,zw->xysz", smoothed, vertical_mix, precision=HIGH) + log_mean
     density = jnp.exp(log_density)
     density_b = density.astype(jnp.bfloat16).reshape(width_x * width_y, samples, length)
-    picked = jnp.take(density_b, pair_line, axis=0)
+    picked = rows(density_b, pair_line, 0)
     contribution = jnp.einsum("pij,psj->psi", responses, picked, preferred_element_type=jnp.float32)
     target = pair_owner[:, 0] * star_count + pair_star
     target_onehot = (
@@ -85,7 +101,7 @@
     misfit_b = lax.all_to_all(spread, "vox", split_axis=0, concat_axis=0, tiled=True).reshape(
         group_blocks, samples, length
     )
-    pair_misfit = jnp.take(misfit_b, target, axis=0)
+    pair_misfit = rows(misfit_b, target, 0)
     pair_adjoint = jnp.einsum(
         "pij,psi->psj", responses, pair_misfit, preferred_element_type=jnp.float32
     )

time: 68 us -> 64.9 us (0.954)
  other arithmetic: 11.2 us -> 8.74 us
  waiting for transfers between devices: 9.87 us -> 11.8 us
  blocking collectives: 16.9 us -> 15.1 us
  matrix products: 6.57 us -> 5.77 us
    and x2 -> x0, other arithmetic: 2.49 us -> none  [the longest x1 1.25 us: per_device(): pair_misfit = jnp.take(misfit_b, target, axis=0)]
    ppermute x2, waiting for transfers between devices: 2.9 us -> 4.89 us  [exchange(): above = lax.ppermute(head, axis, [(i + 1, i) for i in range(count - 1)])]
    select_n x2 -> x0, other arithmetic: 1.86 us -> none  [the longest x1 1.23 us: per_device(): picked = jnp.take(density_b, pair_line, axis=0)]
    all_to_all x1, blocking collectives: 16.9 us -> 15.1 us  [per_device(): lax.all_to_all(partial.reshape(group_size, star_count, samples, length),...]
    add x0 -> x1, other arithmetic: none -> 1.24 us  [per_device(): target = pair_owner[:, 0] * star_count + pair_star]
    dot_general x1, matrix products: 1.67 us -> 0.92 us  [per_device(): jnp.einsum('pij,psi->psj', responses, pair_misfit, preferred_element_type...]
  transfers between devices with their start and end apart: 7 -> 7, of which waited for: 3 -> 4; matrix products, arithmetic and copies ran while one was open for 11% -> 8% of each run, Pallas kernels for 0% -> 0%
where the time goes in v11:
time: 64.9 us; the launch traced here: 64.3 us
  starting transfers between devices  17.3 us (27%)
  blocking collectives  15.1 us (23%)
  waiting for transfers between devices  11.8 us (18%)
  other arithmetic  8.74 us (13%)
  matrix products  5.77 us (9%)
  local copies, waits for them, and re-layouts  4.58 us (7%)
  between operations  0.98 us (2%)
    all_to_all x1, blocking collectives, per_device(): lax.all_to_all(partial.reshape(group_size, star_count, samples, length),...  15.1 us
    ppermute x2, starting transfers between devices, exchange(): below = lax.ppermute(tail, axis, [(i, i + 1) for i in range(count - 1)])  6.58 us
    all_to_all x1, waiting for transfers between devices, per_device(): lax.all_to_all(spread, 'vox', split_axis=0, concat_axis=0, tiled=True)  6.29 us
    ppermute x2, waiting for transfers between devices, exchange(): above = lax.ppermute(head, axis, [(i + 1, i) for i in range(count - 1)])  4.89 us
    ppermute x2, starting transfers between devices, exchange(): above = lax.ppermute(head, axis, [(i + 1, i) for i in range(count - 1)])  4.23 us
    all_to_all x1, starting transfers between devices, per_device(): lax.all_to_all(spread, 'vox', split_axis=0, concat_axis=0, tiled=True)  3.95 us
    ppermute x2, starting transfers between devices, exchange(): lax.ppermute(jnp.where(index == 0, tail, head), axis, [(0, 1), (1, 0)])  2.49 us
    dot_general x1, matrix products, per_device(): jnp.einsum('xysw,zw->xysz', smoothed, vertical_mix, precision=HIGH)  2.14 us
  transfers between devices with their start and end apart: 7, of which 4 were waited for; matrix products, arithmetic and copies ran while one was open for 8% of the time, Pallas kernels for 0%

profile of v11, /device:TPU:1, one launch (start us, length us, event | category | flops | bytes accessed | tf_op | source)
XLA Modules:
  0.0 64.3 jit_solution(12782447735466528036)
XLA Ops:
  0.6 1.8 %fusion.37 = (f32[2,64,128]{2,1,0:T(8,128)}, f32[2,64,4,128]{3,1,0,2:T(8,128)S(1)}) fusion(f32[4,2,64,128]{3,2,1,0:T(8,128)} %param.12, f32[2,64,128]{2,1,0:T(8,128)} %param.11), kind=kLoop, calls=%fused_computation.87 | loop fusion | flops 114688 | bytes 655360 | tf_op jit(solution)/shard_map/reduce_sum | solution.py:125
  2.4 0.7 %fusion.38 = (f32[1,64,4,128]{3,1,0,2:T(8,128)}, f32[1,64,4,128]{3,1,0,2:T(8,128)}) fusion(f32[2,64,4,128]{3,1,0,2:T(8,128)S(1)} %get-tuple-element.3), kind=kLoop, calls=%fused_computation.88 | loop fusion | bytes 524288 | tf_op jit(solution)/shard_map/slice | solution.py:13
  3.1 4.5 %collective-permute-start = (f32[1,64,4,128]{3,1,0,2:T(8,128)}, f32[1,64,4,128]{3,1,0,2:T(8,128)S(1)}, u32[]{:S(2)}, u32[]{:S(2)}) collective-permute-start(f32[1,64,4,128]{3,1,0,2:T(8,128)} %get-tuple-element.4), channel_id=1, source_target_pairs={{0,2},{2,4},{4,6},{6,8},{8,10},{10,12},{12,14},{14,16},{16,18},{18... | collective-permute-start | bytes 393224 | tf_op jit(solution)/shard_map/ppermute | solution.py:21
  7.7 1.9 %collective-permute-start.1 = (f32[1,64,4,128]{3,1,0,2:T(8,128)}, f32[1,64,4,128]{3,1,0,2:T(8,128)}, u32[]{:S(2)}, u32[]{:S(2)}) collective-permute-start(f32[1,64,4,128]{3,1,0,2:T(8,128)} %get-tuple-element.5), channel_id=1, source_target_pairs={{2,0},{4,2},{6,4},{8,6},{10,8},{12,10},{14,12},{16,14},{18,16},{20... | collective-permute-start | bytes 393224 | tf_op jit(solution)/shard_map/ppermute | solution.py:22
  9.6 0.8 %broadcast_in_dim.14 = f32[9]{0:T(128)S(1)} reshape(f32[3,3]{1,0:T(4,128)} %param.13) | data formatting | bytes 72 | tf_op jit(solution)/shard_map/broadcast_in_dim | solution.py:68
  11.0 1.2 %bitcast_add_fusion = s32[96]{0:T(128)} fusion(s32[96]{0:T(128)} %param.19, s32[96,1]{0,1:T(1,128)} %param.18), kind=kLoop, calls=%fused_computation.85 | loop fusion | flops 192 | bytes 1152 | tf_op jit(solution)/shard_map/add | solution.py:84
  12.3 2.0 %collective-permute-done.1 = f32[1,64,4,128]{3,1,0,2:T(8,128)} collective-permute-done((f32[1,64,4,128]{3,1,0,2:T(8,128)}, f32[1,64,4,128]{3,1,0,2:T(8,128)}, u32[]{:S(2)}, u32[]{:S(2)}) %collective-permute-start.1) | collective-permute-done | bytes 131104 | tf_op jit(solution)/shard_map/ppermute | solution.py:22
  14.3 0.7 %broadcast_select_fusion.1 = f32[4,1,4,128]{3,1,0,2:T(1,128)S(1)} fusion(pred[]{:T(512)S(6)} %eq.17, f32[1,64,4,128]{3,1,0,2:T(8,128)} %collective-permute-done.1, f32[2,64,4,128]{3,1,0,2:T(8,128)S(1)} %get-tuple-element.3, f32[1,64,4,128]{3,1,0,2:T(8,128)S(1)} %collective-permute-done), kind=kLoop, calls=%fused_computation.62 | loop fusion | flops 10240 | bytes 532481 | tf_op jit(solution)/shard_map/jit(_where)/select_n | solution.py:16
  15.0 1.3 %collective-permute-start.2 = (f32[4,1,4,128]{3,1,0,2:T(1,128)S(1)}, f32[4,1,4,128]{3,1,0,2:T(1,128)S(1)}, u32[]{:S(2)}, u32[]{:S(2)}) collective-permute-start(f32[4,1,4,128]{3,1,0,2:T(1,128)S(1)} %broadcast_select_fusion.1), channel_id=1, source_target_pairs={{0,1},{1,0},{2,3},{3,2},{4,5},{5,4},{6,7},{7,6},{8,9},{9,8},{10,11... | collective-permute-start | bytes 24584 | tf_op jit(solution)/shard_map/ppermute | solution.py:16
  16.3 1.3 %pad_clamp_fusion.1 = s32[1024]{0:T(1024)} fusion(s32[96]{0:T(128)} %param.17), kind=kLoop, calls=%fused_computation.69 | loop fusion | flops 1024 | bytes 4480 | tf_op jit(solution)/shard_map/gather | solution.py:37
  17.6 1.0 %pad_maximum_fusion = f32[4,66,4,128]{3,1,0,2:T(8,128)S(1)} fusion(f32[4,1,4,128]{3,1,0,2:T(1,128)S(1)} %get-tuple-element.20, f32[1,64,4,128]{3,1,0,2:T(8,128)} %collective-permute-done.1, f32[2,64,4,128]{3,1,0,2:T(8,128)S(1)} %get-tuple-element.3, f32[1,64,4,128]{3,1,0,2:T(8,128)S(1)} %collective-permute-done, f32[4,1,4,128]{3,1,0,2:T(1,128)S(1)} %get-tuple-element.19), kind=kLoop, calls=%fused_computation.5 | loop fusion | flops 540672 | bytes 1081344 | tf_op jit(solution)/shard_map/concatenate | solution.py:23
  18.6 2.1 %fusion.40 = (bf16[2,64,4,128]{3,1,2,0:T(8,128)(2,1)S(1)}, f32[2,64,4,128]{3,1,2,0:T(8,128)}) fusion(f32[128]{0:T(128)} %param.15, f32[128,128]{1,0:T(8,128)} %param.14, f32[4,66,4,128]{3,1,0,2:T(8,128)S(1)} %pad_maximum_fusion, f32[128]{0:T(128)} %get-tuple-element.11, f32[128]{0:T(128)} %get-tuple-element.12, f32[128]{0:T(128)} %get-tuple-element.13, ...), kind=kOutput, calls=%fused_computation.90 | convolution fusion | flops 101908480 | bytes 2823168 | tf_op jit(solution)/shard_map/xysw,zw->xysz/dot_general | solution.py:79
  20.8 0.8 %gather_fusion = bf16[96,4,128]{2,1,0:T(4,128)(2,1)S(1)} fusion(bf16[128,4,128]{2,1,0:T(4,128)(2,1)S(1)} %copy.25, s32[1024]{0:T(1024)} %pad_clamp_fusion.1), kind=kCustom, calls=%fused_computation | custom fusion | bytes 196992 | tf_op jit(solution)/shard_map/gather | solution.py:37
  21.7 1.7 %fusion.41 = f32[96,4,128]{2,1,0:T(4,128)S(1)} fusion(bf16[96,4,128]{2,1,0:T(4,128)(2,1)S(1)} %gather_fusion, bf16[96,128,128]{2,1,0:T(8,128)(2,1)S(1)} %copy-done), kind=kOutput, calls=%fused_computation.91 | convolution fusion | flops 12582912 | bytes 3440640 | tf_op jit(solution)/shard_map/pij,psj->psi/dot_general | solution.py:83
  23.8 15.1 %all_to_all.10 = f32[16,8,4,128]{3,1,2,0:T(8,128)S(1)} all-to-all(f32[16,8,4,128]{3,1,2,0:T(8,128)S(1)} %copy.27), channel_id=1, replica_groups=mesh['vox'=16,'star'=2] {'vox'}, dimensions={0} | all-to-all | bytes 524288 | tf_op jit(solution)/shard_map/all_to_all | solution.py:89
  39.1 0.7 %fusion.34 = (f32[8,128]{1,0:T(8,128)S(1)}, bf16[8,4,128]{2,0,1:T(8,128)(2,1)S(1)}) fusion(f32[8,4,128]{2,0,1:T(8,128)S(1)} %reduce_sum.36, f32[8,128]{1,0:T(8,128)} %param.20, f32[8,128]{1,0:T(8,128)} %param.21), kind=kLoop, calls=%fused_computation.64 | loop fusion | flops 15360 | bytes 36864 | tf_op jit(solution)/shard_map/reduce_sum | solution.py:98
  40.5 4.0 %all-to-all-start.1 = ((bf16[16,8,4,128]{3,2,1,0:T(4,128)(2,1)}), bf16[16,8,4,128]{3,2,1,0:T(4,128)(2,1)S(1)}, u32[]{:S(2)}, u32[]{:S(2)}) async-start(bf16[16,8,4,128]{3,2,1,0:T(4,128)(2,1)} %broadcast_in_dim.18), calls=%async_computation.1 | async-start | bytes 262144 | tf_op jit(solution)/shard_map/all_to_all | solution.py:101
  45.1 6.3 %all-to-all-done.1 = bf16[16,8,4,128]{3,2,1,0:T(4,128)(2,1)S(1)} async-done(((bf16[16,8,4,128]{3,2,1,0:T(4,128)(2,1)}), bf16[16,8,4,128]{3,2,1,0:T(4,128)(2,1)S(1)}, u32[]{:S(2)}, u32[]{:S(2)}) %all-to-all-start.1) | async-done | bytes 131104 | tf_op jit(solution)/shard_map/all_to_all | solution.py:101
  51.4 0.7 %gather_fusion.1 = bf16[96,4,128]{2,1,0:T(4,128)(2,1)S(1)} fusion(bf16[128,4,128]{2,1,0:T(4,128)(2,1)S(1)} %bitcast.50, s32[1024]{0:T(1024)S(1)} %pad_clamp_fusion), kind=kCustom, calls=%fused_computation.1 | custom fusion | bytes 196992 | tf_op jit(solution)/shard_map/gather | solution.py:37
  52.1 0.9 %fusion.42 = f32[96,4,128]{2,1,0:T(4,128)S(1)} fusion(bf16[96,4,128]{2,1,0:T(4,128)(2,1)S(1)} %gather_fusion.1, bf16[96,128,128]{2,1,0:T(8,128)(2,1)S(1)} %copy-done), kind=kOutput, calls=%fused_computation.92 | convolution fusion | flops 12582912 | bytes 3440640 | tf_op jit(solution)/shard_map/pij,psi->psj/dot_general | solution.py:105
  53.7 2.1 %collective-permute-start.3 = (f32[1,64,128]{2,1,0:T(8,128)S(1)}, f32[1,64,128]{2,1,0:T(8,128)S(1)}, u32[]{:S(2)}, u32[]{:S(2)}) collective-permute-start(f32[1,64,128]{2,1,0:T(8,128)S(1)} %get-tuple-element.6), channel_id=1, source_target_pairs={{0,2},{2,4},{4,6},{6,8},{8,10},{10,12},{12,14},{14,16},{16,18},{18... | collective-permute-start | bytes 98312 | tf_op jit(solution)/shard_map/ppermute | solution.py:21
  55.8 2.3 %collective-permute-start.4 = (f32[1,64,128]{2,1,0:T(8,128)S(1)}, f32[1,64,128]{2,1,0:T(8,128)S(1)}, u32[]{:S(2)}, u32[]{:S(2)}) collective-permute-start(f32[1,64,128]{2,1,0:T(8,128)S(1)} %get-tuple-element.7), channel_id=1, source_target_pairs={{2,0},{4,2},{6,4},{8,6},{10,8},{12,10},{14,12},{16,14},{18,16},{20... | collective-permute-start | bytes 98312 | tf_op jit(solution)/shard_map/ppermute | solution.py:22
  58.1 2.9 %collective-permute-done.4 = f32[1,64,128]{2,1,0:T(8,128)S(1)} collective-permute-done((f32[1,64,128]{2,1,0:T(8,128)S(1)}, f32[1,64,128]{2,1,0:T(8,128)S(1)}, u32[]{:S(2)}, u32[]{:S(2)}) %collective-permute-start.4) | collective-permute-done | bytes 32800 | tf_op jit(solution)/shard_map/ppermute | solution.py:22
  61.0 1.2 %collective-permute-start.5 = (f32[4,1,128]{2,1,0:T(1,128)S(1)}, f32[4,1,128]{2,1,0:T(1,128)S(1)}, u32[]{:S(2)}, u32[]{:S(2)}) collective-permute-start(f32[4,1,128]{2,1,0:T(1,128)S(1)} %broadcast_select_fusion.4), channel_id=1, source_target_pairs={{0,1},{1,0},{2,3},{3,2},{4,5},{5,4},{6,7},{7,6},{8,9},{9,8},{10,11... | collective-permute-start | bytes 6152 | tf_op jit(solution)/shard_map/ppermute | solution.py:16
  (54 shorter events, 5.3 us)
Async XLA Ops:
  0.6 21.0 %copy-start = (bf16[96,128,128]{2,1,0:T(8,128)(2,1)S(1)}, bf16[96,128,128]{2,1,0:T(8,128)(2,1)}, u32[]{:S(2)}) copy-start(bf16[96,128,128]{2,1,0:T(8,128)(2,1)} %param.16) | copy-start | bytes 9437188
  3.1 9.2 %collective-permute-start = (f32[1,64,4,128]{3,1,0,2:T(8,128)}, f32[1,64,4,128]{3,1,0,2:T(8,128)S(1)}, u32[]{:S(2)}, u32[]{:S(2)}) collective-permute-start(f32[1,64,4,128]{3,1,0,2:T(8,128)} %get-tuple-element.4), channel_id=1, source_target_pairs={{0,2},{2,4},{4,6},{6,8},{8,10},{10,12},{12,14},{14,16},{16,18},{18... | collective-permute-start | bytes 393224 | tf_op jit(solution)/shard_map/ppermute | solution.py:21
  7.7 6.6 %collective-permute-start.1 = (f32[1,64,4,128]{3,1,0,2:T(8,128)}, f32[1,64,4,128]{3,1,0,2:T(8,128)}, u32[]{:S(2)}, u32[]{:S(2)}) collective-permute-start(f32[1,64,4,128]{3,1,0,2:T(8,128)} %get-tuple-element.5), channel_id=1, source_target_pairs={{2,0},{4,2},{6,4},{8,6},{10,8},{12,10},{14,12},{16,14},{18,16},{20... | collective-permute-start | bytes 393224 | tf_op jit(solution)/shard_map/ppermute | solution.py:22
  15.0 2.6 %collective-permute-start.2 = (f32[4,1,4,128]{3,1,0,2:T(1,128)S(1)}, f32[4,1,4,128]{3,1,0,2:T(1,128)S(1)}, u32[]{:S(2)}, u32[]{:S(2)}) collective-permute-start(f32[4,1,4,128]{3,1,0,2:T(1,128)S(1)} %broadcast_select_fusion.1), channel_id=1, source_target_pairs={{0,1},{1,0},{2,3},{3,2},{4,5},{5,4},{6,7},{7,6},{8,9},{9,8},{10,11... | collective-permute-start | bytes 24584 | tf_op jit(solution)/shard_map/ppermute | solution.py:16
  18.6 4.8 %copy-start.14 = (s32[96]{0:T(128)S(1)}, s32[96]{0:T(128)}, u32[]{:S(2)}) copy-start(s32[96]{0:T(128)} %bitcast_add_fusion) | copy-start | bytes 1156
  23.8 29.7 %copy-start.3 = (f32[128,128]{1,0:T(8,128)S(1)}, f32[128,128]{1,0:T(8,128)}, u32[]{:S(2)}) copy-start(f32[128,128]{1,0:T(8,128)} %param.14) | copy-start | bytes 196612
  39.0 24.5 %copy-start.1 = (f32[2,64,128]{2,1,0:T(8,128)S(1)}, f32[2,64,128]{2,1,0:T(8,128)}, u32[]{:S(2)}) copy-start(f32[2,64,128]{2,1,0:T(8,128)} %get-tuple-element.2) | copy-start | bytes 196612
  39.0 24.5 %copy-start.4 = (f32[128]{0:T(128)S(1)}, f32[128]{0:T(128)}, u32[]{:S(2)}) copy-start(f32[128]{0:T(128)} %get-tuple-element.10) | copy-start | bytes 1540
  39.0 24.5 %copy-start.5 = (f32[128]{0:T(128)S(1)}, f32[128]{0:T(128)}, u32[]{:S(2)}) copy-start(f32[128]{0:T(128)} %get-tuple-element.11) | copy-start | bytes 1540
  39.0 24.5 %copy-start.6 = (f32[128]{0:T(128)S(1)}, f32[128]{0:T(128)}, u32[]{:S(2)}) copy-start(f32[128]{0:T(128)} %get-tuple-element.12) | copy-start | bytes 1540
  39.0 24.5 %copy-start.7 = (f32[128]{0:T(128)S(1)}, f32[128]{0:T(128)}, u32[]{:S(2)}) copy-start(f32[128]{0:T(128)} %get-tuple-element.13) | copy-start | bytes 1540
  39.0 24.5 %copy-start.8 = (f32[128]{0:T(128)S(1)}, f32[128]{0:T(128)}, u32[]{:S(2)}) copy-start(f32[128]{0:T(128)} %get-tuple-element.14) | copy-start | bytes 1540
  39.0 24.5 %copy-start.9 = (f32[128]{0:T(128)S(1)}, f32[128]{0:T(128)}, u32[]{:S(2)}) copy-start(f32[128]{0:T(128)} %get-tuple-element.15) | copy-start | bytes 1540
  39.8 13.3 %copy-start.13 = (s32[96]{0:T(128)S(1)}, s32[96]{0:T(128)}, u32[]{:S(2)}) copy-start(s32[96]{0:T(128)} %param.17) | copy-start | bytes 1156
  39.8 23.8 %copy-start.10 = (f32[128]{0:T(128)S(1)}, f32[128]{0:T(128)}, u32[]{:S(2)}) copy-start(f32[128]{0:T(128)} %get-tuple-element.16) | copy-start | bytes 1540
  39.8 23.8 %copy-start.11 = (f32[128]{0:T(128)S(1)}, f32[128]{0:T(128)}, u32[]{:S(2)}) copy-start(f32[128]{0:T(128)} %get-tuple-element.17) | copy-start | bytes 1540
  39.8 23.8 %copy-start.12 = (f32[128]{0:T(128)S(1)}, f32[128]{0:T(128)}, u32[]{:S(2)}) copy-start(f32[128]{0:T(128)} %get-tuple-element.18) | copy-start | bytes 1540
  40.5 10.9 %all-to-all-start.1 = ((bf16[16,8,4,128]{3,2,1,0:T(4,128)(2,1)}), bf16[16,8,4,128]{3,2,1,0:T(4,128)(2,1)S(1)}, u32[]{:S(2)}, u32[]{:S(2)}) async-start(bf16[16,8,4,128]{3,2,1,0:T(4,128)(2,1)} %broadcast_in_dim.18), calls=%async_computation.1 | async-start | bytes 262144 | tf_op jit(solution)/shard_map/all_to_all | solution.py:101
  52.1 1.3 %copy-start.2 = (f32[2,64,4,128]{3,1,2,0:T(8,128)S(1)}, f32[2,64,4,128]{3,1,2,0:T(8,128)}, u32[]{:S(2)}) copy-start(f32[2,64,4,128]{3,1,2,0:T(8,128)} %get-tuple-element.24) | copy-start | bytes 786436
  53.7 4.4 %collective-permute-start.3 = (f32[1,64,128]{2,1,0:T(8,128)S(1)}, f32[1,64,128]{2,1,0:T(8,128)S(1)}, u32[]{:S(2)}, u32[]{:S(2)}) collective-permute-start(f32[1,64,128]{2,1,0:T(8,128)S(1)} %get-tuple-element.6), channel_id=1, source_target_pairs={{0,2},{2,4},{4,6},{6,8},{8,10},{10,12},{12,14},{14,16},{16,18},{18... | collective-permute-start | bytes 98312 | tf_op jit(solution)/shard_map/ppermute | solution.py:21
  55.8 5.2 %collective-permute-start.4 = (f32[1,64,128]{2,1,0:T(8,128)S(1)}, f32[1,64,128]{2,1,0:T(8,128)S(1)}, u32[]{:S(2)}, u32[]{:S(2)}) collective-permute-start(f32[1,64,128]{2,1,0:T(8,128)S(1)} %get-tuple-element.7), channel_id=1, source_target_pairs={{2,0},{4,2},{6,4},{8,6},{10,8},{12,10},{14,12},{16,14},{18,16},{20... | collective-permute-start | bytes 98312 | tf_op jit(solution)/shard_map/ppermute | solution.py:22
  61.0 2.4 %collective-permute-start.5 = (f32[4,1,128]{2,1,0:T(1,128)S(1)}, f32[4,1,128]{2,1,0:T(1,128)S(1)}, u32[]{:S(2)}, u32[]{:S(2)}) collective-permute-start(f32[4,1,128]{2,1,0:T(1,128)S(1)} %broadcast_select_fusion.4), channel_id=1, source_target_pairs={{0,1},{1,0},{2,3},{3,2},{4,5},{5,4},{6,7},{7,6},{8,9},{9,8},{10,11... | collective-permute-start | bytes 6152 | tf_op jit(solution)/shard_map/ppermute | solution.py:16

commit v12 on v11

--- a/solution.py
+++ b/solution.py
@@ -79,7 +79,12 @@
     log_density = jnp.einsum("xysw,zw->xysz", smoothed, vertical_mix, precision=HIGH) + log_mean
     density = jnp.exp(log_density)
     density_b = density.astype(jnp.bfloat16).reshape(width_x * width_y, samples, length)
-    picked = rows(density_b, pair_line, 0)
+    line_onehot = (
+        pair_line[:, None] == jnp.arange(width_x * width_y, dtype=jnp.int32)[None, :]
+    ).astype(jnp.float32)
+    picked = jnp.einsum(
+        "pl,lsz->psz", line_onehot.astype(jnp.bfloat16), density_b, preferred_element_type=jnp.float32
+    ).astype(jnp.bfloat16)
     contribution = jnp.einsum("pij,psj->psi", responses, picked, preferred_element_type=jnp.float32)
     target = pair_owner[:, 0] * star_count + pair_star
     target_onehot = (
@@ -101,13 +106,12 @@
     misfit_b = lax.all_to_all(spread, "vox", split_axis=0, concat_axis=0, tiled=True).reshape(
         group_blocks, samples, length
     )
-    pair_misfit = rows(misfit_b, target, 0)
+    pair_misfit = jnp.einsum(
+        "pb,bsi->psi", target_onehot.astype(jnp.bfloat16), misfit_b, preferred_element_type=jnp.float32
+    ).astype(jnp.bfloat16)
     pair_adjoint = jnp.einsum(
         "pij,psi->psj", responses, pair_misfit, preferred_element_type=jnp.float32
     )
-    line_onehot = (
-        pair_line[:, None] == jnp.arange(width_x * width_y, dtype=jnp.int32)[None, :]
-    ).astype(jnp.float32)
     adjoint = jnp.einsum("pb,psj->bsj", line_onehot, pair_adjoint, precision=HIGH).reshape(
         width_x, width_y, samples, length
     )

time: 64.9 us -> 63 us (0.971)
  blocking collectives: 15.1 us -> 25.3 us
  waiting for transfers between devices: 11.8 us -> 6.87 us
  starting transfers between devices: 17.3 us -> 13.3 us
  local copies, waits for them, and re-layouts: 4.58 us -> 2.31 us
  other arithmetic: 8.74 us -> 6.78 us
  matrix products: 5.77 us -> 6.88 us
    all_to_all x0 -> x1, blocking collectives: none -> 10.2 us  [per_device(): lax.all_to_all(spread, 'vox', split_axis=0, concat_axis=0, tiled=True)]
    all_to_all x1 -> x0, waiting for transfers between devices: 6.29 us -> none  [per_device(): lax.all_to_all(spread, 'vox', split_axis=0, concat_axis=0, tiled=True)]
    all_to_all x1 -> x0, starting transfers between devices: 3.95 us -> none  [per_device(): lax.all_to_all(spread, 'vox', split_axis=0, concat_axis=0, tiled=True)]
    gather x2 -> x0, other arithmetic: 1.91 us -> none  [rows(): lax.gather(table, index[:, None], numbers, sizes, mode=lax.GatherScatterM...]
    gather x2 -> x0, local copies, waits for them, and re-layouts: 1.53 us -> none  [rows(): lax.gather(table, index[:, None], numbers, sizes, mode=lax.GatherScatterM...]
    ppermute x2, waiting for transfers between devices: 4.89 us -> 6.13 us  [exchange(): above = lax.ppermute(head, axis, [(i + 1, i) for i in range(count - 1)])]
    dot_general x0 -> x2, matrix products: none -> 1.08 us  [the longest x1 0.87 us: per_device(): jnp.einsum('pb,bsi->psi', target_onehot.astype(jnp.bfloat16), misfit_b, p...]
    broadcast_in_dim x1, local copies, waits for them, and re-layouts: 0.68 us -> 0.02 us  [per_device(): spread = jnp.broadcast_to(misfit_b[None], (group_size,) + misfit_b.shape)]
  transfers between devices with their start and end apart: 7 -> 6, of which waited for: 4 -> 4; matrix products, arithmetic and copies ran while one was open for 8% -> 5% of each run, Pallas kernels for 0% -> 0%
where the time goes in v12:
time: 63 us; the launch traced here: 62.5 us
  blocking collectives  25.3 us (40%)
  starting transfers between devices  13.3 us (21%)
  matrix products  6.88 us (11%)
  waiting for transfers between devices  6.87 us (11%)
  other arithmetic  6.78 us (11%)
  local copies, waits for them, and re-layouts  2.31 us (4%)
  between operations  0.98 us (2%)
    all_to_all x1, blocking collectives, per_device(): lax.all_to_all(partial.reshape(group_size, star_count, samples, length),...  15.1 us
    all_to_all x1, blocking collectives, per_device(): lax.all_to_all(spread, 'vox', split_axis=0, concat_axis=0, tiled=True)  10.2 us
    ppermute x2, starting transfers between devices, exchange(): below = lax.ppermute(tail, axis, [(i, i + 1) for i in range(count - 1)])  6.59 us
    ppermute x2, waiting for transfers between devices, exchange(): above = lax.ppermute(head, axis, [(i + 1, i) for i in range(count - 1)])  6.13 us
    ppermute x2, starting transfers between devices, exchange(): above = lax.ppermute(head, axis, [(i + 1, i) for i in range(count - 1)])  4.22 us
    ppermute x2, starting transfers between devices, exchange(): lax.ppermute(jnp.where(index == 0, tail, head), axis, [(0, 1), (1, 0)])  2.49 us
    dot_general x1, matrix products, per_device(): jnp.einsum('xysw,zw->xysz', smoothed, vertical_mix, precision=HIGH)  2.16 us
    reduce_sum x1, other arithmetic, per_device(): gradient = grad_latent + jnp.mean(latent, axis=2)  1.76 us
  transfers between devices with their start and end apart: 6, of which 4 were waited for; matrix products, arithmetic and copies ran while one was open for 5% of the time, Pallas kernels for 0%

profile of v12, /device:TPU:1, one launch (start us, length us, event | category | flops | bytes accessed | tf_op | source)
XLA Modules:
  0.0 62.5 jit_solution(15179420833796402292)
XLA Ops:
  0.6 1.8 %fusion.49 = (f32[2,64,128]{2,1,0:T(8,128)}, f32[2,64,4,128]{3,1,0,2:T(8,128)S(1)}) fusion(f32[4,2,64,128]{3,2,1,0:T(8,128)} %param.12, f32[2,64,128]{2,1,0:T(8,128)} %param.11), kind=kLoop, calls=%fused_computation.97 | loop fusion | flops 114688 | bytes 655360 | tf_op jit(solution)/shard_map/reduce_sum | solution.py:129
  2.4 0.7 %fusion.50 = (f32[1,64,4,128]{3,1,0,2:T(8,128)}, f32[1,64,4,128]{3,1,0,2:T(8,128)}) fusion(f32[2,64,4,128]{3,1,0,2:T(8,128)S(1)} %get-tuple-element.3), kind=kLoop, calls=%fused_computation.98 | loop fusion | bytes 524288 | tf_op jit(solution)/shard_map/slice | solution.py:13
  3.1 4.5 %collective-permute-start = (f32[1,64,4,128]{3,1,0,2:T(8,128)}, f32[1,64,4,128]{3,1,0,2:T(8,128)S(1)}, u32[]{:S(2)}, u32[]{:S(2)}) collective-permute-start(f32[1,64,4,128]{3,1,0,2:T(8,128)} %get-tuple-element.4), channel_id=1, source_target_pairs={{0,2},{2,4},{4,6},{6,8},{8,10},{10,12},{12,14},{14,16},{16,18},{18... | collective-permute-start | bytes 393224 | tf_op jit(solution)/shard_map/ppermute | solution.py:21
  7.7 1.9 %collective-permute-start.1 = (f32[1,64,4,128]{3,1,0,2:T(8,128)}, f32[1,64,4,128]{3,1,0,2:T(8,128)}, u32[]{:S(2)}, u32[]{:S(2)}) collective-permute-start(f32[1,64,4,128]{3,1,0,2:T(8,128)} %get-tuple-element.5), channel_id=1, source_target_pairs={{2,0},{4,2},{6,4},{8,6},{10,8},{12,10},{14,12},{16,14},{18,16},{20... | collective-permute-start | bytes 393224 | tf_op jit(solution)/shard_map/ppermute | solution.py:22
  9.6 0.8 %broadcast_in_dim.10 = f32[9]{0:T(128)S(1)} reshape(f32[3,3]{1,0:T(4,128)} %param.13) | data formatting | bytes 72 | tf_op jit(solution)/shard_map/broadcast_in_dim | solution.py:68
  10.4 0.6 slice_bitcast_fusion.8
  11.1 3.2 %collective-permute-done.1 = f32[1,64,4,128]{3,1,0,2:T(8,128)} collective-permute-done((f32[1,64,4,128]{3,1,0,2:T(8,128)}, f32[1,64,4,128]{3,1,0,2:T(8,128)}, u32[]{:S(2)}, u32[]{:S(2)}) %collective-permute-start.1) | collective-permute-done | bytes 131104 | tf_op jit(solution)/shard_map/ppermute | solution.py:22
  14.3 0.7 %broadcast_select_fusion.1 = f32[4,1,4,128]{3,1,0,2:T(1,128)S(1)} fusion(pred[]{:T(512)S(6)} %eq.17, f32[1,64,4,128]{3,1,0,2:T(8,128)} %collective-permute-done.1, f32[2,64,4,128]{3,1,0,2:T(8,128)S(1)} %get-tuple-element.3, f32[1,64,4,128]{3,1,0,2:T(8,128)S(1)} %collective-permute-done), kind=kLoop, calls=%fused_computation.74 | loop fusion | flops 10240 | bytes 532481 | tf_op jit(solution)/shard_map/jit(_where)/select_n | solution.py:16
  15.0 1.3 %collective-permute-start.2 = (f32[4,1,4,128]{3,1,0,2:T(1,128)S(1)}, f32[4,1,4,128]{3,1,0,2:T(1,128)S(1)}, u32[]{:S(2)}, u32[]{:S(2)}) collective-permute-start(f32[4,1,4,128]{3,1,0,2:T(1,128)S(1)} %broadcast_select_fusion.1), channel_id=1, source_target_pairs={{0,1},{1,0},{2,3},{3,2},{4,5},{5,4},{6,7},{7,6},{8,9},{9,8},{10,11... | collective-permute-start | bytes 24584 | tf_op jit(solution)/shard_map/ppermute | solution.py:16
  16.3 1.2 %bitcast_add_fusion = s32[96]{0:T(128)} fusion(s32[96]{0:T(128)} %param.19, s32[96,1]{0,1:T(1,128)} %param.18), kind=kLoop, calls=%fused_computation.95 | loop fusion | flops 192 | bytes 1152 | tf_op jit(solution)/shard_map/add | solution.py:89
  17.6 1.0 %pad_maximum_fusion = f32[4,66,4,128]{3,1,0,2:T(8,128)S(1)} fusion(f32[4,1,4,128]{3,1,0,2:T(1,128)S(1)} %get-tuple-element.20, f32[1,64,4,128]{3,1,0,2:T(8,128)} %collective-permute-done.1, f32[2,64,4,128]{3,1,0,2:T(8,128)S(1)} %get-tuple-element.3, f32[1,64,4,128]{3,1,0,2:T(8,128)S(1)} %collective-permute-done, f32[4,1,4,128]{3,1,0,2:T(1,128)S(1)} %get-tuple-element.19), kind=kLoop, calls=%fused_computation.5 | loop fusion | flops 540672 | bytes 1081344 | tf_op jit(solution)/shard_map/concatenate | solution.py:23
  18.6 2.2 %fusion.52 = (bf16[2,64,4,128]{3,1,2,0:T(8,128)(2,1)S(1)}, f32[2,64,4,128]{3,1,2,0:T(8,128)}) fusion(f32[128]{0:T(128)} %param.15, f32[128,128]{1,0:T(8,128)} %param.14, f32[4,66,4,128]{3,1,0,2:T(8,128)S(1)} %pad_maximum_fusion, f32[128]{0:T(128)} %get-tuple-element.11, f32[128]{0:T(128)} %get-tuple-element.12, f32[128]{0:T(128)} %get-tuple-element.13, ...), kind=kOutput, calls=%fused_computation.100 | convolution fusion | flops 101908480 | bytes 2823168 | tf_op jit(solution)/shard_map/xysw,zw->xysz/dot_general | solution.py:79
  21.0 1.7 %fusion.18 = f32[96,4,128]{2,1,0:T(4,128)S(1)} fusion(bf16[96,128,128]{2,1,0:T(8,128)(2,1)S(1)} %copy-done, bf16[96,4,128]{2,0,1:T(8,128)(2,1)S(1)} %convolution_convert_fusion.1), kind=kOutput, calls=%fused_computation.35 | convolution fusion | flops 12582912 | bytes 3440640 | tf_op jit(solution)/shard_map/pij,psj->psi/dot_general | solution.py:88
  23.2 15.1 %all_to_all.10 = f32[16,8,4,128]{3,1,2,0:T(8,128)S(1)} all-to-all(f32[16,8,4,128]{3,1,2,0:T(8,128)S(1)} %copy.30), channel_id=1, replica_groups=mesh['vox'=16,'star'=2] {'vox'}, dimensions={0} | all-to-all | bytes 524288 | tf_op jit(solution)/shard_map/all_to_all | solution.py:94
  38.4 0.7 %fusion.46 = (f32[8,128]{1,0:T(8,128)S(1)}, bf16[8,4,128]{2,0,1:T(8,128)(2,1)S(1)}) fusion(f32[8,4,128]{2,0,1:T(8,128)S(1)} %reduce_sum.36, f32[8,128]{1,0:T(8,128)} %param.20, f32[8,128]{1,0:T(8,128)} %param.21), kind=kLoop, calls=%fused_computation.76 | loop fusion | flops 15360 | bytes 36864 | tf_op jit(solution)/shard_map/reduce_sum | solution.py:103
  39.2 10.2 %all_to_all.11 = bf16[16,8,4,128]{3,1,2,0:T(8,128)(2,1)S(1)} all-to-all(bf16[16,8,4,128]{3,1,2,0:T(8,128)(2,1)S(1)} %broadcast_in_dim.13), channel_id=1, replica_groups=mesh['vox'=16,'star'=2] {'vox'}, dimensions={0} | all-to-all | bytes 262144 | tf_op jit(solution)/shard_map/all_to_all | solution.py:106
  49.4 0.9 %convolution_convert_fusion = bf16[96,4,128]{2,0,1:T(8,128)(2,1)S(1)} fusion(bf16[16,8,4,128]{3,1,2,0:T(8,128)(2,1)S(1)} %all_to_all.11, s32[96]{0:T(128)} %bitcast_add_fusion), kind=kOutput, calls=%fused_computation.3 | convolution fusion | flops 12668928 | bytes 229760 | tf_op jit(solution)/shard_map/pb,bsi->psi/dot_general | solution.py:109
  50.3 0.9 %fusion.16 = f32[96,4,128]{2,1,0:T(4,128)S(1)} fusion(bf16[96,128,128]{2,1,0:T(8,128)(2,1)S(1)} %copy-done, bf16[96,4,128]{2,0,1:T(8,128)(2,1)S(1)} %convolution_convert_fusion), kind=kOutput, calls=%fused_computation.33 | convolution fusion | flops 12582912 | bytes 3440640 | tf_op jit(solution)/shard_map/pij,psi->psj/dot_general | solution.py:112
  51.9 2.1 %collective-permute-start.3 = (f32[1,64,128]{2,1,0:T(8,128)S(1)}, f32[1,64,128]{2,1,0:T(8,128)S(1)}, u32[]{:S(2)}, u32[]{:S(2)}) collective-permute-start(f32[1,64,128]{2,1,0:T(8,128)S(1)} %get-tuple-element.6), channel_id=1, source_target_pairs={{0,2},{2,4},{4,6},{6,8},{8,10},{10,12},{12,14},{14,16},{16,18},{18... | collective-permute-start | bytes 98312 | tf_op jit(solution)/shard_map/ppermute | solution.py:21
  53.9 2.3 %collective-permute-start.4 = (f32[1,64,128]{2,1,0:T(8,128)S(1)}, f32[1,64,128]{2,1,0:T(8,128)S(1)}, u32[]{:S(2)}, u32[]{:S(2)}) collective-permute-start(f32[1,64,128]{2,1,0:T(8,128)S(1)} %get-tuple-element.7), channel_id=1, source_target_pairs={{2,0},{4,2},{6,4},{8,6},{10,8},{12,10},{14,12},{16,14},{18,16},{20... | collective-permute-start | bytes 98312 | tf_op jit(solution)/shard_map/ppermute | solution.py:22
  56.3 2.9 %collective-permute-done.4 = f32[1,64,128]{2,1,0:T(8,128)S(1)} collective-permute-done((f32[1,64,128]{2,1,0:T(8,128)S(1)}, f32[1,64,128]{2,1,0:T(8,128)S(1)}, u32[]{:S(2)}, u32[]{:S(2)}) %collective-permute-start.4) | collective-permute-done | bytes 32800 | tf_op jit(solution)/shard_map/ppermute | solution.py:22
  59.2 1.2 %collective-permute-start.5 = (f32[4,1,128]{2,1,0:T(1,128)S(1)}, f32[4,1,128]{2,1,0:T(1,128)S(1)}, u32[]{:S(2)}, u32[]{:S(2)}) collective-permute-start(f32[4,1,128]{2,1,0:T(1,128)S(1)} %broadcast_select_fusion.4), channel_id=1, source_target_pairs={{0,1},{1,0},{2,3},{3,2},{4,5},{5,4},{6,7},{7,6},{8,9},{9,8},{10,11... | collective-permute-start | bytes 6152 | tf_op jit(solution)/shard_map/ppermute | solution.py:16
  61.0 0.6 %collective-permute-done.5 = f32[4,1,128]{2,1,0:T(1,128)S(1)} collective-permute-done((f32[4,1,128]{2,1,0:T(1,128)S(1)}, f32[4,1,128]{2,1,0:T(1,128)S(1)}, u32[]{:S(2)}, u32[]{:S(2)}) %collective-permute-start.5) | collective-permute-done | bytes 2080 | tf_op jit(solution)/shard_map/ppermute | solution.py:16
  61.8 0.7 %fusion.21 = f32[2,64,128]{2,1,0:T(8,128)} fusion(f32[4,66,128]{2,1,0:T(8,128)S(1)} %pad_maximum_fusion.1, f32[2,64,128]{2,1,0:T(8,128)S(1)} %copy-done.1, f32[128]{0:T(128)S(1)} %copy-done.5, f32[128]{0:T(128)S(1)} %copy-done.6, f32[128]{0:T(128)S(1)} %copy-done.7, f32[128]{0:T(128)S(1)} %copy-done.8, f32[128]{0:T(128)S(1)} %copy-done.9, ...), kind=kLoop, calls=%fused_computation.39 | loop fusion | flops 311296 | bytes 725504 | tf_op jit(solution)/shard_map/add | solution.py:129
  (51 shorter events, 2.2 us)
Async XLA Ops:
  0.6 20.4 %copy-start = (bf16[96,128,128]{2,1,0:T(8,128)(2,1)S(1)}, bf16[96,128,128]{2,1,0:T(8,128)(2,1)}, u32[]{:S(2)}) copy-start(bf16[96,128,128]{2,1,0:T(8,128)(2,1)} %param.16) | copy-start | bytes 9437188
  3.1 7.9 %collective-permute-start = (f32[1,64,4,128]{3,1,0,2:T(8,128)}, f32[1,64,4,128]{3,1,0,2:T(8,128)S(1)}, u32[]{:S(2)}, u32[]{:S(2)}) collective-permute-start(f32[1,64,4,128]{3,1,0,2:T(8,128)} %get-tuple-element.4), channel_id=1, source_target_pairs={{0,2},{2,4},{4,6},{6,8},{8,10},{10,12},{12,14},{14,16},{16,18},{18... | collective-permute-start | bytes 393224 | tf_op jit(solution)/shard_map/ppermute | solution.py:21
  7.7 6.6 %collective-permute-start.1 = (f32[1,64,4,128]{3,1,0,2:T(8,128)}, f32[1,64,4,128]{3,1,0,2:T(8,128)}, u32[]{:S(2)}, u32[]{:S(2)}) collective-permute-start(f32[1,64,4,128]{3,1,0,2:T(8,128)} %get-tuple-element.5), channel_id=1, source_target_pairs={{2,0},{4,2},{6,4},{8,6},{10,8},{12,10},{14,12},{16,14},{18,16},{20... | collective-permute-start | bytes 393224 | tf_op jit(solution)/shard_map/ppermute | solution.py:22
  15.0 2.6 %collective-permute-start.2 = (f32[4,1,4,128]{3,1,0,2:T(1,128)S(1)}, f32[4,1,4,128]{3,1,0,2:T(1,128)S(1)}, u32[]{:S(2)}, u32[]{:S(2)}) collective-permute-start(f32[4,1,4,128]{3,1,0,2:T(1,128)S(1)} %broadcast_select_fusion.1), channel_id=1, source_target_pairs={{0,1},{1,0},{2,3},{3,2},{4,5},{5,4},{6,7},{7,6},{8,9},{9,8},{10,11... | collective-permute-start | bytes 24584 | tf_op jit(solution)/shard_map/ppermute | solution.py:16
  17.5 3.3 %copy-start.13 = (s32[96]{0:T(128)S(1)}, s32[96]{0:T(128)}, u32[]{:S(2)}) copy-start(s32[96]{0:T(128)} %param.17) | copy-start | bytes 1156
  18.6 4.1 %copy-start.15 = (s32[96]{0:T(128)S(1)}, s32[96]{0:T(128)}, u32[]{:S(2)}) copy-start(s32[96]{0:T(128)} %bitcast_add_fusion) | copy-start | bytes 1156
  23.1 28.5 %copy-start.3 = (f32[128,128]{1,0:T(8,128)S(1)}, f32[128,128]{1,0:T(8,128)}, u32[]{:S(2)}) copy-start(f32[128,128]{1,0:T(8,128)} %param.14) | copy-start | bytes 196612
  38.3 23.4 %copy-start.1 = (f32[2,64,128]{2,1,0:T(8,128)S(1)}, f32[2,64,128]{2,1,0:T(8,128)}, u32[]{:S(2)}) copy-start(f32[2,64,128]{2,1,0:T(8,128)} %get-tuple-element.2) | copy-start | bytes 196612
  38.3 12.9 %copy-start.14 = (s32[96]{0:T(128)S(1)}, s32[96]{0:T(128)}, u32[]{:S(2)}) copy-start(s32[96]{0:T(128)} %param.17) | copy-start | bytes 1156
  38.3 13.3 %copy-start.2 = (f32[2,64,4,128]{3,1,2,0:T(8,128)S(1)}, f32[2,64,4,128]{3,1,2,0:T(8,128)}, u32[]{:S(2)}) copy-start(f32[2,64,4,128]{3,1,2,0:T(8,128)} %get-tuple-element.24) | copy-start | bytes 786436
  38.3 23.3 %copy-start.4 = (f32[128]{0:T(128)S(1)}, f32[128]{0:T(128)}, u32[]{:S(2)}) copy-start(f32[128]{0:T(128)} %get-tuple-element.10) | copy-start | bytes 1540
  38.4 23.3 %copy-start.5 = (f32[128]{0:T(128)S(1)}, f32[128]{0:T(128)}, u32[]{:S(2)}) copy-start(f32[128]{0:T(128)} %get-tuple-element.11) | copy-start | bytes 1540
  38.4 23.3 %copy-start.6 = (f32[128]{0:T(128)S(1)}, f32[128]{0:T(128)}, u32[]{:S(2)}) copy-start(f32[128]{0:T(128)} %get-tuple-element.12) | copy-start | bytes 1540
  38.4 23.3 %copy-start.7 = (f32[128]{0:T(128)S(1)}, f32[128]{0:T(128)}, u32[]{:S(2)}) copy-start(f32[128]{0:T(128)} %get-tuple-element.13) | copy-start | bytes 1540
  38.4 23.3 %copy-start.8 = (f32[128]{0:T(128)S(1)}, f32[128]{0:T(128)}, u32[]{:S(2)}) copy-start(f32[128]{0:T(128)} %get-tuple-element.14) | copy-start | bytes 1540
  38.4 23.3 %copy-start.9 = (f32[128]{0:T(128)S(1)}, f32[128]{0:T(128)}, u32[]{:S(2)}) copy-start(f32[128]{0:T(128)} %get-tuple-element.15) | copy-start | bytes 1540
  38.4 23.3 %copy-start.10 = (f32[128]{0:T(128)S(1)}, f32[128]{0:T(128)}, u32[]{:S(2)}) copy-start(f32[128]{0:T(128)} %get-tuple-element.16) | copy-start | bytes 1540
  38.4 23.3 %copy-start.11 = (f32[128]{0:T(128)S(1)}, f32[128]{0:T(128)}, u32[]{:S(2)}) copy-start(f32[128]{0:T(128)} %get-tuple-element.17) | copy-start | bytes 1540
  38.4 23.3 %copy-start.12 = (f32[128]{0:T(128)S(1)}, f32[128]{0:T(128)}, u32[]{:S(2)}) copy-start(f32[128]{0:T(128)} %get-tuple-element.18) | copy-start | bytes 1540
  51.9 4.4 %collective-permute-start.3 = (f32[1,64,128]{2,1,0:T(8,128)S(1)}, f32[1,64,128]{2,1,0:T(8,128)S(1)}, u32[]{:S(2)}, u32[]{:S(2)}) collective-permute-start(f32[1,64,128]{2,1,0:T(8,128)S(1)} %get-tuple-element.6), channel_id=1, source_target_pairs={{0,2},{2,4},{4,6},{6,8},{8,10},{10,12},{12,14},{14,16},{16,18},{18... | collective-permute-start | bytes 98312 | tf_op jit(solution)/shard_map/ppermute | solution.py:21
  53.9 5.2 %collective-permute-start.4 = (f32[1,64,128]{2,1,0:T(8,128)S(1)}, f32[1,64,128]{2,1,0:T(8,128)S(1)}, u32[]{:S(2)}, u32[]{:S(2)}) collective-permute-start(f32[1,64,128]{2,1,0:T(8,128)S(1)} %get-tuple-element.7), channel_id=1, source_target_pairs={{2,0},{4,2},{6,4},{8,6},{10,8},{12,10},{14,12},{16,14},{18,16},{20... | collective-permute-start | bytes 98312 | tf_op jit(solution)/shard_map/ppermute | solution.py:22
  59.2 2.4 %collective-permute-start.5 = (f32[4,1,128]{2,1,0:T(1,128)S(1)}, f32[4,1,128]{2,1,0:T(1,128)S(1)}, u32[]{:S(2)}, u32[]{:S(2)}) collective-permute-start(f32[4,1,128]{2,1,0:T(1,128)S(1)} %broadcast_select_fusion.4), channel_id=1, source_target_pairs={{0,1},{1,0},{2,3},{3,2},{4,5},{5,4},{6,7},{7,6},{8,9},{9,8},{10,11... | collective-permute-start | bytes 6152 | tf_op jit(solution)/shard_map/ppermute | solution.py:16

commit v13 on v12

--- a/solution.py
+++ b/solution.py
@@ -7,7 +7,7 @@
 
 
 def exchange(cells, axis, dim):
-    count = lax.axis_size(axis)
+    count = lax.psum(1, axis)
     size = cells.shape[dim]
     head = lax.slice_in_dim(cells, 0, 1, axis=dim)
     tail = lax.slice_in_dim(cells, size - 1, size, axis=dim)
@@ -23,8 +23,11 @@
     return jnp.concatenate([below, cells, above], axis=dim)
 
 
+VOX = ("vh", "vc")
+
+
 def with_halo(cells):
-    return lax.optimization_barrier(exchange(exchange(cells, "vox", 0), "star", 1))
+    return lax.optimization_barrier(exchange(exchange(cells, VOX, 0), "star", 1))
 
 
 def rows(table, index, axis):
@@ -60,7 +63,7 @@
     width_x = deviations.shape[1]
     width_y = deviations.shape[2]
     length = deviations.shape[3]
-    group_size = lax.axis_size("vox")
+    group_size = lax.psum(1, VOX)
     star_count = observed.shape[0]
     group_blocks = group_size * star_count
     latent = jnp.transpose(mean_field[None] + deviations, (1, 2, 0, 3))
@@ -91,19 +94,19 @@
         target[:, None] == jnp.arange(group_blocks, dtype=jnp.int32)[None, :]
     ).astype(jnp.float32)
     partial = jnp.einsum("pb,psi->bsi", target_onehot, contribution, precision=HIGH)
-    arrived = lax.all_to_all(
-        partial.reshape(group_size, star_count, samples, length),
-        "vox",
-        split_axis=0,
-        concat_axis=0,
-        tiled=True,
-    )
+    pair_size = lax.psum(1, "vc")
+    core = lax.axis_index("vc")
+    halves = partial.reshape(group_size // pair_size, pair_size, star_count, samples, length)
+    keep = lax.dynamic_index_in_dim(halves, core, axis=1, keepdims=False)
+    send = lax.dynamic_index_in_dim(halves, 1 - core, axis=1, keepdims=False)
+    merged = keep + lax.ppermute(send, "vc", [(0, 1), (1, 0)])
+    arrived = lax.all_to_all(merged, "vh", split_axis=0, concat_axis=0, tiled=True)
     extinction = jnp.sum(arrived, axis=0)
     misfit = inv_var[:, None, :] * (extinction - observed[:, None, :])
     residual_mean = jnp.mean(misfit, axis=1)
     misfit_b = misfit.astype(jnp.bfloat16)
     spread = jnp.broadcast_to(misfit_b[None], (group_size,) + misfit_b.shape)
-    misfit_b = lax.all_to_all(spread, "vox", split_axis=0, concat_axis=0, tiled=True).reshape(
+    misfit_b = lax.all_to_all(spread, VOX, split_axis=0, concat_axis=0, tiled=True).reshape(
         group_blocks, samples, length
     )
     pair_misfit = jnp.einsum(
@@ -131,23 +134,27 @@
 
 
 def solution(mesh):
+    shape = mesh.devices.shape
+    view = jax.sharding.Mesh(
+        mesh.devices.reshape(shape[0] // 2, 2, shape[1]), ("vh", "vc", "star")
+    )
     placed = (
-        P("vox", "star", None),
-        P(None, "vox", "star", None),
+        P(VOX, "star", None),
+        P(None, VOX, "star", None),
         P(),
         P(),
         P(),
-        P(("vox", "star"), None, None),
-        P(("vox", "star")),
-        P(("vox", "star"), None),
-        P(("vox", "star")),
-        P(("vox", "star"), None),
-        P(("vox", "star"), None),
+        P((*VOX, "star"), None, None),
+        P((*VOX, "star")),
+        P((*VOX, "star"), None),
+        P((*VOX, "star")),
+        P((*VOX, "star"), None),
+        P((*VOX, "star"), None),
     )
     return jax.shard_map(
         per_device,
-        mesh=mesh,
+        mesh=view,
         in_specs=placed,
-        out_specs=(P("vox", "star", None), P(("vox", "star"), None)),
+        out_specs=(P(VOX, "star", None), P((*VOX, "star"), None)),
         check_vma=False,
     )

time: 63 us -> 60.4 us (0.959)
  blocking collectives: 25.3 us -> 22.7 us
  waiting for transfers between devices: 6.87 us -> 8.21 us
  other arithmetic: 6.78 us -> 6.07 us
  matrix products: 6.88 us -> 6.21 us
    all_to_all x2, blocking collectives: 25.3 us -> 22.7 us  [the longest x1 11.4 us: per_device(): lax.all_to_all(merged, 'vh', split_axis=0, concat_axis=0, tiled=True)]
    ppermute x0 -> x1, waiting for transfers between devices: none -> 1.33 us  [per_device(): merged = keep + lax.ppermute(send, 'vc', [(0, 1), (1, 0)])]
    reduce_sum x1, other arithmetic: 0.73 us -> 0.01 us  [per_device(): residual_mean = jnp.mean(misfit, axis=1)]
    dot_general x1, matrix products: 0.87 us -> 0.21 us  [per_device(): jnp.einsum('pb,bsi->psi', target_onehot.astype(jnp.bfloat16), misfit_b, p...]
  transfers between devices with their start and end apart: 6 -> 7, of which waited for: 4 -> 5; matrix products, arithmetic and copies ran while one was open for 5% -> 5% of each run, Pallas kernels for 0% -> 0%
where the time goes in v13:
time: 60.4 us; the launch traced here: 59.9 us
  blocking collectives  22.7 us (38%)
  starting transfers between devices  13.4 us (22%)
  waiting for transfers between devices  8.21 us (14%)
  matrix products  6.21 us (10%)
  other arithmetic  6.07 us (10%)
  local copies, waits for them, and re-layouts  2.33 us (4%)
  between operations  1.04 us (2%)
    all_to_all x1, blocking collectives, per_device(): lax.all_to_all(merged, 'vh', split_axis=0, concat_axis=0, tiled=True)  11.4 us
    all_to_all x1, blocking collectives, per_device(): lax.all_to_all(spread, VOX, split_axis=0, concat_axis=0, tiled=True)  11.3 us
    ppermute x2, starting transfers between devices, exchange(): below = lax.ppermute(tail, axis, [(i, i + 1) for i in range(count - 1)])  6.6 us
    ppermute x2, waiting for transfers between devices, exchange(): above = lax.ppermute(head, axis, [(i + 1, i) for i in range(count - 1)])  6.13 us
    ppermute x2, starting transfers between devices, exchange(): above = lax.ppermute(head, axis, [(i + 1, i) for i in range(count - 1)])  4.22 us
    ppermute x2, starting transfers between devices, exchange(): lax.ppermute(jnp.where(index == 0, tail, head), axis, [(0, 1), (1, 0)])  2.49 us
    dot_general x1, matrix products, per_device(): jnp.einsum('xysw,zw->xysz', smoothed, vertical_mix, precision=HIGH)  2.15 us
    reduce_sum x1, other arithmetic, per_device(): gradient = grad_latent + jnp.mean(latent, axis=2)  1.76 us
  transfers between devices with their start and end apart: 7, of which 5 were waited for; matrix products, arithmetic and copies ran while one was open for 5% of the time, Pallas kernels for 0%

profile of v13, /device:TPU:1, one launch (start us, length us, event | category | flops | bytes accessed | tf_op | source)
XLA Modules:
  0.0 59.9 jit_solution(5082582442264624575)
XLA Ops:
  0.6 1.8 %fusion.50 = (f32[2,64,128]{2,1,0:T(8,128)}, f32[2,64,4,128]{3,1,0,2:T(8,128)S(1)}) fusion(f32[4,2,64,128]{3,2,1,0:T(8,128)} %param.12, f32[2,64,128]{2,1,0:T(8,128)} %param.11), kind=kLoop, calls=%fused_computation.101 | loop fusion | flops 114688 | bytes 655360 | tf_op jit(solution)/shard_map/reduce_sum | solution.py:132
  2.4 0.7 %fusion.51 = (f32[1,64,4,128]{3,1,0,2:T(8,128)}, f32[1,64,4,128]{3,1,0,2:T(8,128)}) fusion(f32[2,64,4,128]{3,1,0,2:T(8,128)S(1)} %get-tuple-element.3), kind=kLoop, calls=%fused_computation.102 | loop fusion | bytes 524288 | tf_op jit(solution)/shard_map/slice | solution.py:13
  3.1 4.5 %collective-permute-start = (f32[1,64,4,128]{3,1,0,2:T(8,128)}, f32[1,64,4,128]{3,1,0,2:T(8,128)S(1)}, u32[]{:S(2)}, u32[]{:S(2)}) collective-permute-start(f32[1,64,4,128]{3,1,0,2:T(8,128)} %get-tuple-element.6), channel_id=1, source_target_pairs={{0,2},{2,4},{4,6},{6,8},{8,10},{10,12},{12,14},{14,16},{16,18},{18... | collective-permute-start | bytes 393224 | tf_op jit(solution)/shard_map/ppermute | solution.py:21
  7.7 1.9 %collective-permute-start.1 = (f32[1,64,4,128]{3,1,0,2:T(8,128)}, f32[1,64,4,128]{3,1,0,2:T(8,128)}, u32[]{:S(2)}, u32[]{:S(2)}) collective-permute-start(f32[1,64,4,128]{3,1,0,2:T(8,128)} %get-tuple-element.7), channel_id=1, source_target_pairs={{2,0},{4,2},{6,4},{8,6},{10,8},{12,10},{14,12},{16,14},{18,16},{20... | collective-permute-start | bytes 393224 | tf_op jit(solution)/shard_map/ppermute | solution.py:22
  9.6 0.8 %broadcast_in_dim.10 = f32[9]{0:T(128)S(1)} reshape(f32[3,3]{1,0:T(4,128)} %param.13) | data formatting | bytes 72 | tf_op jit(solution)/shard_map/broadcast_in_dim | solution.py:71
  10.4 0.6 %slice_bitcast_fusion.8 = (f32[128]{0:T(128)}, f32[128]{0:T(128)}, f32[128]{0:T(128)}, f32[128]{0:T(128)}, f32[128]{0:T(128)}, /*index=5*/f32[128]{0:T(128)}, f32[128]{0:T(128)}, f32[128]{0:T(128)}, f32[128]{0:T(128)}) fusion(f32[9,128]{1,0:T(8,128)S(1)} %broadcast_in_dim.11), kind=kLoop, calls=%fused_computation.96 | loop fusion | bytes 9216 | tf_op jit(solution)/shard_map/mul | solution.py:129
  11.0 3.2 %collective-permute-done.1 = f32[1,64,4,128]{3,1,0,2:T(8,128)} collective-permute-done((f32[1,64,4,128]{3,1,0,2:T(8,128)}, f32[1,64,4,128]{3,1,0,2:T(8,128)}, u32[]{:S(2)}, u32[]{:S(2)}) %collective-permute-start.1) | collective-permute-done | bytes 131104 | tf_op jit(solution)/shard_map/ppermute | solution.py:22
  14.3 0.7 %broadcast_select_fusion.1 = f32[4,1,4,128]{3,1,0,2:T(1,128)S(1)} fusion(pred[]{:T(512)S(6)} %eq.17, f32[1,64,4,128]{3,1,0,2:T(8,128)} %collective-permute-done.1, f32[2,64,4,128]{3,1,0,2:T(8,128)S(1)} %get-tuple-element.3, f32[1,64,4,128]{3,1,0,2:T(8,128)S(1)} %collective-permute-done), kind=kLoop, calls=%fused_computation.76 | loop fusion | flops 10240 | bytes 532481 | tf_op jit(solution)/shard_map/jit(_where)/select_n | solution.py:16
  15.0 1.3 %collective-permute-start.2 = (f32[4,1,4,128]{3,1,0,2:T(1,128)S(1)}, f32[4,1,4,128]{3,1,0,2:T(1,128)S(1)}, u32[]{:S(2)}, u32[]{:S(2)}) collective-permute-start(f32[4,1,4,128]{3,1,0,2:T(1,128)S(1)} %broadcast_select_fusion.1), channel_id=1, source_target_pairs={{0,1},{1,0},{2,3},{3,2},{4,5},{5,4},{6,7},{7,6},{8,9},{9,8},{10,11... | collective-permute-start | bytes 24584 | tf_op jit(solution)/shard_map/ppermute | solution.py:16
  16.3 1.2 %bitcast_add_fusion.1 = s32[96]{0:T(128)} fusion(s32[96]{0:T(128)} %param.19, s32[96,1]{0,1:T(1,128)} %param.18), kind=kLoop, calls=%fused_computation.97 | loop fusion | flops 192 | bytes 1152 | tf_op jit(solution)/shard_map/add | solution.py:92
  17.6 1.0 %pad_maximum_fusion = f32[4,66,4,128]{3,1,0,2:T(8,128)S(1)} fusion(f32[4,1,4,128]{3,1,0,2:T(1,128)S(1)} %get-tuple-element.22, f32[1,64,4,128]{3,1,0,2:T(8,128)} %collective-permute-done.1, f32[2,64,4,128]{3,1,0,2:T(8,128)S(1)} %get-tuple-element.3, f32[1,64,4,128]{3,1,0,2:T(8,128)S(1)} %collective-permute-done, f32[4,1,4,128]{3,1,0,2:T(1,128)S(1)} %get-tuple-element.21), kind=kLoop, calls=%fused_computation.4 | loop fusion | flops 540672 | bytes 1081344 | tf_op jit(solution)/shard_map/concatenate | solution.py:23
  18.6 2.1 %fusion.53 = (bf16[2,64,4,128]{3,1,2,0:T(8,128)(2,1)S(1)}, f32[2,64,4,128]{3,1,2,0:T(8,128)}) fusion(f32[128]{0:T(128)} %param.15, f32[128,128]{1,0:T(8,128)} %param.14, f32[4,66,4,128]{3,1,0,2:T(8,128)S(1)} %pad_maximum_fusion, f32[128]{0:T(128)} %get-tuple-element.13, f32[128]{0:T(128)} %get-tuple-element.14, f32[128]{0:T(128)} %get-tuple-element.15, ...), kind=kOutput, calls=%fused_computation.104 | convolution fusion | flops 101908480 | bytes 2823168 | tf_op jit(solution)/shard_map/xysw,zw->xysz/dot_general | solution.py:82
  21.0 1.7 %fusion.19 = f32[96,4,128]{2,1,0:T(4,128)S(1)} fusion(bf16[96,128,128]{2,1,0:T(8,128)(2,1)S(1)} %copy-done, bf16[96,4,128]{2,0,1:T(8,128)(2,1)S(1)} %convolution_convert_fusion.1), kind=kOutput, calls=%fused_computation.37 | convolution fusion | flops 12582912 | bytes 3440640 | tf_op jit(solution)/shard_map/pij,psj->psi/dot_general | solution.py:91
  23.3 1.3 %collective-permute-done.3 = f32[8,8,4,128]{3,1,2,0:T(8,128)S(1)} collective-permute-done((f32[8,8,4,128]{3,1,2,0:T(8,128)S(1)}, f32[8,8,4,128]{3,1,2,0:T(8,128)S(1)}, u32[]{:S(2)}, u32[]{:S(2)}) %collective-permute-start.3) | collective-permute-done | bytes 131104 | tf_op jit(solution)/shard_map/ppermute | solution.py:102
  24.7 11.4 %all_to_all.10 = f32[8,8,4,128]{3,1,2,0:T(8,128)S(1)} all-to-all(f32[8,8,4,128]{3,1,2,0:T(8,128)S(1)} %bitcast_add_fusion), channel_id=1, replica_groups=mesh['vh'=8,'vc'=2,'star'=2] {'vh'}, dimensions={0} | all-to-all | bytes 262144 | tf_op jit(solution)/shard_map/all_to_all | solution.py:103
  36.2 11.3 %all_to_all.11 = bf16[16,8,4,128]{3,1,2,0:T(8,128)(2,1)S(1)} all-to-all(bf16[16,8,4,128]{3,1,2,0:T(8,128)(2,1)S(1)} %broadcast_in_dim.13), channel_id=1, replica_groups=mesh['vh'=8,'vc'=2,'star'=2] {'vh','vc'}, dimensions={0} | all-to-all | bytes 262144 | tf_op jit(solution)/shard_map/all_to_all | solution.py:109
  47.7 0.9 %fusion.17 = f32[96,4,128]{2,1,0:T(4,128)S(1)} fusion(bf16[96,128,128]{2,1,0:T(8,128)(2,1)S(1)} %copy-done, bf16[96,4,128]{2,0,1:T(8,128)(2,1)S(1)} %convolution_convert_fusion), kind=kOutput, calls=%fused_computation.35 | convolution fusion | flops 12582912 | bytes 3440640 | tf_op jit(solution)/shard_map/pij,psi->psj/dot_general | solution.py:115
  49.3 2.1 %collective-permute-start.4 = (f32[1,64,128]{2,1,0:T(8,128)S(1)}, f32[1,64,128]{2,1,0:T(8,128)S(1)}, u32[]{:S(2)}, u32[]{:S(2)}) collective-permute-start(f32[1,64,128]{2,1,0:T(8,128)S(1)} %get-tuple-element.8), channel_id=1, source_target_pairs={{0,2},{2,4},{4,6},{6,8},{8,10},{10,12},{12,14},{14,16},{16,18},{18... | collective-permute-start | bytes 98312 | tf_op jit(solution)/shard_map/ppermute | solution.py:21
  51.4 2.3 %collective-permute-start.5 = (f32[1,64,128]{2,1,0:T(8,128)S(1)}, f32[1,64,128]{2,1,0:T(8,128)S(1)}, u32[]{:S(2)}, u32[]{:S(2)}) collective-permute-start(f32[1,64,128]{2,1,0:T(8,128)S(1)} %get-tuple-element.9), channel_id=1, source_target_pairs={{2,0},{4,2},{6,4},{8,6},{10,8},{12,10},{14,12},{16,14},{18,16},{20... | collective-permute-start | bytes 98312 | tf_op jit(solution)/shard_map/ppermute | solution.py:22
  53.7 2.9 %collective-permute-done.5 = f32[1,64,128]{2,1,0:T(8,128)S(1)} collective-permute-done((f32[1,64,128]{2,1,0:T(8,128)S(1)}, f32[1,64,128]{2,1,0:T(8,128)S(1)}, u32[]{:S(2)}, u32[]{:S(2)}) %collective-permute-start.5) | collective-permute-done | bytes 32800 | tf_op jit(solution)/shard_map/ppermute | solution.py:22
  56.6 1.2 %collective-permute-start.6 = (f32[4,1,128]{2,1,0:T(1,128)S(1)}, f32[4,1,128]{2,1,0:T(1,128)S(1)}, u32[]{:S(2)}, u32[]{:S(2)}) collective-permute-start(f32[4,1,128]{2,1,0:T(1,128)S(1)} %broadcast_select_fusion.4), channel_id=1, source_target_pairs={{0,1},{1,0},{2,3},{3,2},{4,5},{5,4},{6,7},{7,6},{8,9},{9,8},{10,11... | collective-permute-start | bytes 6152 | tf_op jit(solution)/shard_map/ppermute | solution.py:16
  57.9 0.6 broadcast_multiply_fusion
  58.4 0.6 %collective-permute-done.6 = f32[4,1,128]{2,1,0:T(1,128)S(1)} collective-permute-done((f32[4,1,128]{2,1,0:T(1,128)S(1)}, f32[4,1,128]{2,1,0:T(1,128)S(1)}, u32[]{:S(2)}, u32[]{:S(2)}) %collective-permute-start.6) | collective-permute-done | bytes 2080 | tf_op jit(solution)/shard_map/ppermute | solution.py:16
  59.2 0.7 %fusion.22 = f32[2,64,128]{2,1,0:T(8,128)} fusion(f32[4,66,128]{2,1,0:T(8,128)S(1)} %pad_maximum_fusion.1, f32[2,64,128]{2,1,0:T(8,128)S(1)} %copy-done.1, f32[128]{0:T(128)S(1)} %copy-done.7, f32[128]{0:T(128)S(1)} %copy-done.8, f32[128]{0:T(128)S(1)} %copy-done.9, f32[128]{0:T(128)S(1)} %copy-done.10, f32[128]{0:T(128)S(1)} %copy-done.11, ...), kind=kLoop, calls=%fused_computation.41 | loop fusion | flops 311296 | bytes 725504 | tf_op jit(solution)/shard_map/add | solution.py:132
  (59 shorter events, 1.9 us)
Async XLA Ops:
  0.6 20.3 %copy-start = (bf16[96,128,128]{2,1,0:T(8,128)(2,1)S(1)}, bf16[96,128,128]{2,1,0:T(8,128)(2,1)}, u32[]{:S(2)}) copy-start(bf16[96,128,128]{2,1,0:T(8,128)(2,1)} %param.16) | copy-start | bytes 9437188
  3.1 7.9 %collective-permute-start = (f32[1,64,4,128]{3,1,0,2:T(8,128)}, f32[1,64,4,128]{3,1,0,2:T(8,128)S(1)}, u32[]{:S(2)}, u32[]{:S(2)}) collective-permute-start(f32[1,64,4,128]{3,1,0,2:T(8,128)} %get-tuple-element.6), channel_id=1, source_target_pairs={{0,2},{2,4},{4,6},{6,8},{8,10},{10,12},{12,14},{14,16},{16,18},{18... | collective-permute-start | bytes 393224 | tf_op jit(solution)/shard_map/ppermute | solution.py:21
  7.7 6.6 %collective-permute-start.1 = (f32[1,64,4,128]{3,1,0,2:T(8,128)}, f32[1,64,4,128]{3,1,0,2:T(8,128)}, u32[]{:S(2)}, u32[]{:S(2)}) collective-permute-start(f32[1,64,4,128]{3,1,0,2:T(8,128)} %get-tuple-element.7), channel_id=1, source_target_pairs={{2,0},{4,2},{6,4},{8,6},{10,8},{12,10},{14,12},{16,14},{18,16},{20... | collective-permute-start | bytes 393224 | tf_op jit(solution)/shard_map/ppermute | solution.py:22
  15.0 2.6 %collective-permute-start.2 = (f32[4,1,4,128]{3,1,0,2:T(1,128)S(1)}, f32[4,1,4,128]{3,1,0,2:T(1,128)S(1)}, u32[]{:S(2)}, u32[]{:S(2)}) collective-permute-start(f32[4,1,4,128]{3,1,0,2:T(1,128)S(1)} %broadcast_select_fusion.1), channel_id=1, source_target_pairs={{0,1},{1,0},{2,3},{3,2},{4,5},{5,4},{6,7},{7,6},{8,9},{9,8},{10,11... | collective-permute-start | bytes 24584 | tf_op jit(solution)/shard_map/ppermute | solution.py:16
  18.6 4.1 %copy-start.17 = (s32[96]{0:T(128)S(1)}, s32[96]{0:T(128)}, u32[]{:S(2)}) copy-start(s32[96]{0:T(128)} %bitcast_add_fusion.1) | copy-start | bytes 1156
  20.7 15.4 %copy-start.4 = (f32[8,128]{1,0:T(8,128)S(1)}, f32[8,128]{1,0:T(8,128)}, u32[]{:S(2)}) copy-start(f32[8,128]{1,0:T(8,128)} %param.20) | copy-start | bytes 12292
  20.7 15.4 %copy-start.5 = (f32[8,128]{1,0:T(8,128)S(1)}, f32[8,128]{1,0:T(8,128)}, u32[]{:S(2)}) copy-start(f32[8,128]{1,0:T(8,128)} %param.21) | copy-start | bytes 12292
  22.7 25.9 %copy-start.16 = (s32[96]{0:T(128)S(1)}, s32[96]{0:T(128)}, u32[]{:S(2)}) copy-start(s32[96]{0:T(128)} %param.17) | copy-start | bytes 1156
  23.1 25.9 %copy-start.3 = (f32[128,128]{1,0:T(8,128)S(1)}, f32[128,128]{1,0:T(8,128)}, u32[]{:S(2)}) copy-start(f32[128,128]{1,0:T(8,128)} %param.14) | copy-start | bytes 196612
  23.2 1.4 %collective-permute-start.3 = (f32[8,8,4,128]{3,1,2,0:T(8,128)S(1)}, f32[8,8,4,128]{3,1,2,0:T(8,128)S(1)}, u32[]{:S(2)}, u32[]{:S(2)}) collective-permute-start(f32[8,8,4,128]{3,1,2,0:T(8,128)S(1)} %bitcast.62), channel_id=1, source_target_pairs={{0,2},{2,0},{1,3},{3,1},{4,6},{6,4},{5,7},{7,5},{8,10},{10,8},{9,1... | collective-permute-start | bytes 393224 | tf_op jit(solution)/shard_map/ppermute | solution.py:102
  24.6 34.5 %copy-start.1 = (f32[2,64,128]{2,1,0:T(8,128)S(1)}, f32[2,64,128]{2,1,0:T(8,128)}, u32[]{:S(2)}) copy-start(f32[2,64,128]{2,1,0:T(8,128)} %get-tuple-element.2) | copy-start | bytes 196612
  24.6 34.5 %copy-start.6 = (f32[128]{0:T(128)S(1)}, f32[128]{0:T(128)}, u32[]{:S(2)}) copy-start(f32[128]{0:T(128)} %get-tuple-element.12) | copy-start | bytes 1540
  24.6 34.5 %copy-start.7 = (f32[128]{0:T(128)S(1)}, f32[128]{0:T(128)}, u32[]{:S(2)}) copy-start(f32[128]{0:T(128)} %get-tuple-element.13) | copy-start | bytes 1540
  24.6 34.5 %copy-start.8 = (f32[128]{0:T(128)S(1)}, f32[128]{0:T(128)}, u32[]{:S(2)}) copy-start(f32[128]{0:T(128)} %get-tuple-element.14) | copy-start | bytes 1540
  24.7 34.5 %copy-start.9 = (f32[128]{0:T(128)S(1)}, f32[128]{0:T(128)}, u32[]{:S(2)}) copy-start(f32[128]{0:T(128)} %get-tuple-element.15) | copy-start | bytes 1540
  24.7 34.5 %copy-start.10 = (f32[128]{0:T(128)S(1)}, f32[128]{0:T(128)}, u32[]{:S(2)}) copy-start(f32[128]{0:T(128)} %get-tuple-element.16) | copy-start | bytes 1540
  24.7 34.5 %copy-start.11 = (f32[128]{0:T(128)S(1)}, f32[128]{0:T(128)}, u32[]{:S(2)}) copy-start(f32[128]{0:T(128)} %get-tuple-element.17) | copy-start | bytes 1540
  24.7 34.5 %copy-start.12 = (f32[128]{0:T(128)S(1)}, f32[128]{0:T(128)}, u32[]{:S(2)}) copy-start(f32[128]{0:T(128)} %get-tuple-element.18) | copy-start | bytes 1540
  24.7 34.5 %copy-start.13 = (f32[128]{0:T(128)S(1)}, f32[128]{0:T(128)}, u32[]{:S(2)}) copy-start(f32[128]{0:T(128)} %get-tuple-element.19) | copy-start | bytes 1540
  24.7 34.5 %copy-start.14 = (f32[128]{0:T(128)S(1)}, f32[128]{0:T(128)}, u32[]{:S(2)}) copy-start(f32[128]{0:T(128)} %get-tuple-element.20) | copy-start | bytes 1540
  36.2 12.9 %copy-start.2 = (f32[2,64,4,128]{3,1,2,0:T(8,128)S(1)}, f32[2,64,4,128]{3,1,2,0:T(8,128)}, u32[]{:S(2)}) copy-start(f32[2,64,4,128]{3,1,2,0:T(8,128)} %get-tuple-element.26) | copy-start | bytes 786436
  49.3 4.4 %collective-permute-start.4 = (f32[1,64,128]{2,1,0:T(8,128)S(1)}, f32[1,64,128]{2,1,0:T(8,128)S(1)}, u32[]{:S(2)}, u32[]{:S(2)}) collective-permute-start(f32[1,64,128]{2,1,0:T(8,128)S(1)} %get-tuple-element.8), channel_id=1, source_target_pairs={{0,2},{2,4},{4,6},{6,8},{8,10},{10,12},{12,14},{14,16},{16,18},{18... | collective-permute-start | bytes 98312 | tf_op jit(solution)/shard_map/ppermute | solution.py:21
  51.4 5.2 %collective-permute-start.5 = (f32[1,64,128]{2,1,0:T(8,128)S(1)}, f32[1,64,128]{2,1,0:T(8,128)S(1)}, u32[]{:S(2)}, u32[]{:S(2)}) collective-permute-start(f32[1,64,128]{2,1,0:T(8,128)S(1)} %get-tuple-element.9), channel_id=1, source_target_pairs={{2,0},{4,2},{6,4},{8,6},{10,8},{12,10},{14,12},{16,14},{18,16},{20... | collective-permute-start | bytes 98312 | tf_op jit(solution)/shard_map/ppermute | solution.py:22
  56.6 2.4 %collective-permute-start.6 = (f32[4,1,128]{2,1,0:T(1,128)S(1)}, f32[4,1,128]{2,1,0:T(1,128)S(1)}, u32[]{:S(2)}, u32[]{:S(2)}) collective-permute-start(f32[4,1,128]{2,1,0:T(1,128)S(1)} %broadcast_select_fusion.4), channel_id=1, source_target_pairs={{0,1},{1,0},{2,3},{3,2},{4,5},{5,4},{6,7},{7,6},{8,9},{9,8},{10,11... | collective-permute-start | bytes 6152 | tf_op jit(solution)/shard_map/ppermute | solution.py:16
  (1 other events, 3.3 us)

commit v14 on v13

--- a/solution.py
+++ b/solution.py
@@ -6,7 +6,7 @@
 HIGH = lax.Precision.HIGHEST
 
 
-def exchange(cells, axis, dim):
+def exchange(cells, axis, dim, split=False):
     count = lax.psum(1, axis)
     size = cells.shape[dim]
     head = lax.slice_in_dim(cells, 0, 1, axis=dim)
@@ -20,6 +20,8 @@
     else:
         below = lax.ppermute(tail, axis, [(i, i + 1) for i in range(count - 1)])
         above = lax.ppermute(head, axis, [(i + 1, i) for i in range(count - 1)])
+    if split:
+        return below, above
     return jnp.concatenate([below, cells, above], axis=dim)
 
 
@@ -27,7 +29,59 @@
 
 
 def with_halo(cells):
-    return lax.optimization_barrier(exchange(exchange(cells, VOX, 0), "star", 1))
+    count_x = lax.psum(1, VOX)
+    count_y = lax.psum(1, "star")
+    width_x, width_y = cells.shape[0], cells.shape[1]
+    below_x, above_x = exchange(cells, VOX, 0, split=True)
+    below_y, above_y = exchange(cells, "star", 1, split=True)
+    every = VOX + ("star",)
+
+    def corner(at_x, at_y):
+        return cells[at_x : at_x + 1, at_y : at_y + 1]
+
+    def diagonal(piece, step_x, step_y):
+        pairs = [
+            (u * count_y + t, (u + step_x) * count_y + t + step_y)
+            for u in range(count_x)
+            for t in range(count_y)
+            if 0 <= u + step_x < count_x and 0 <= t + step_y < count_y
+        ]
+        return lax.ppermute(piece, every, pairs)
+
+    def crossing(piece, step_x):
+        pairs = [
+            (u * 2 + t, (u + step_x) * 2 + 1 - t)
+            for u in range(count_x)
+            for t in range(2)
+            if 0 <= u + step_x < count_x
+        ]
+        return lax.ppermute(piece, every, pairs)
+
+    last_x, last_y = width_x - 1, width_y - 1
+    if count_y == 2:
+        star = lax.axis_index("star")
+        low = star == 0
+        from_low_x = crossing(jnp.where(low, corner(last_x, last_y), corner(last_x, 0)), 1)
+        from_high_x = crossing(jnp.where(low, corner(0, last_y), corner(0, 0)), -1)
+        zero = jnp.zeros_like(from_low_x)
+        low_low = jnp.where(low, zero, from_low_x)
+        low_high = jnp.where(low, from_low_x, zero)
+        high_low = jnp.where(low, zero, from_high_x)
+        high_high = jnp.where(low, from_high_x, zero)
+    else:
+        low_low = diagonal(corner(last_x, last_y), 1, 1)
+        low_high = diagonal(corner(last_x, 0), 1, -1)
+        high_low = diagonal(corner(0, last_y), -1, 1)
+        high_high = diagonal(corner(0, 0), -1, -1)
+    padded = jnp.concatenate(
+        [
+            jnp.concatenate([low_low, below_x, low_high], axis=1),
+            jnp.concatenate([below_y, cells, above_y], axis=1),
+            jnp.concatenate([high_low, above_x, high_high], axis=1),
+        ],
+        axis=0,
+    )
+    return lax.optimization_barrier(padded)
 
 
 def rows(table, index, axis):

time: 60.4 us -> 72.5 us (1.20); the launches traced: 59.9 us -> 71 us
  starting transfers between devices: 13.4 us -> 30.3 us
  blocking collectives: 22.7 us -> 12.3 us
  waiting for transfers between devices: 8.21 us -> 14.6 us
  other arithmetic: 6.07 us -> 4.29 us
    all_to_all x1 -> x0, blocking collectives: 11.3 us -> none  [per_device(): lax.all_to_all(spread, VOX, split_axis=0, concat_axis=0, tiled=True)]
    ppermute x0 -> x4, starting transfers between devices: none -> 9.81 us  [crossing(): return lax.ppermute(piece, every, pairs)]
    all_to_all x0 -> x1, waiting for transfers between devices: none -> 6.36 us  [per_device(): lax.all_to_all(spread, VOX, split_axis=0, concat_axis=0, tiled=True)]
    all_to_all x0 -> x1, starting transfers between devices: none -> 5.04 us  [per_device(): lax.all_to_all(spread, VOX, split_axis=0, concat_axis=0, tiled=True)]
    ppermute x0 -> x4, waiting for transfers between devices: none -> 3.81 us  [crossing(): return lax.ppermute(piece, every, pairs)]
    ppermute x2, waiting for transfers between devices: 6.13 us -> 3.08 us  [exchange(): above = lax.ppermute(head, axis, [(i + 1, i) for i in range(count - 1)])]
    ppermute x2, starting transfers between devices: 6.6 us -> 7.68 us  [exchange(): below = lax.ppermute(tail, axis, [(i, i + 1) for i in range(count - 1)])]
    all_to_all x1, blocking collectives: 11.4 us -> 12.3 us  [per_device(): lax.all_to_all(merged, 'vh', split_axis=0, concat_axis=0, tiled=True)]
  transfers between devices with their start and end apart: 7 -> 12, of which waited for: 5 -> 4; matrix products, arithmetic and copies ran while one was open for 5% -> 4% of each run, Pallas kernels for 0% -> 0%
where the time goes in v14:
time: 72.5 us; the launch traced here: 71 us
  starting transfers between devices  30.3 us (42%)
  waiting for transfers between devices  14.6 us (20%)
  blocking collectives  12.3 us (17%)
  matrix products  6.19 us (9%)
  other arithmetic  4.29 us (6%)
  local copies, waits for them, and re-layouts  2.31 us (3%)
  between operations  0.98 us (1%)
    all_to_all x1, blocking collectives, per_device(): lax.all_to_all(merged, 'vh', split_axis=0, concat_axis=0, tiled=True)  12.3 us
    ppermute x4, starting transfers between devices, crossing(): return lax.ppermute(piece, every, pairs)  9.81 us
    ppermute x2, starting transfers between devices, exchange(): below = lax.ppermute(tail, axis, [(i, i + 1) for i in range(count - 1)])  7.68 us
    all_to_all x1, waiting for transfers between devices, per_device(): lax.all_to_all(spread, VOX, split_axis=0, concat_axis=0, tiled=True)  6.36 us
    all_to_all x1, starting transfers between devices, per_device(): lax.all_to_all(spread, VOX, split_axis=0, concat_axis=0, tiled=True)  5.04 us
    ppermute x2, starting transfers between devices, exchange(): above = lax.ppermute(head, axis, [(i + 1, i) for i in range(count - 1)])  4.37 us
    ppermute x4, waiting for transfers between devices, crossing(): return lax.ppermute(piece, every, pairs)  3.81 us
    ppermute x2, starting transfers between devices, exchange(): lax.ppermute(jnp.where(index == 0, tail, head), axis, [(0, 1), (1, 0)])  3.38 us
  transfers between devices with their start and end apart: 12, of which 4 were waited for; matrix products, arithmetic and copies ran while one was open for 4% of the time, Pallas kernels for 0%

profile of v14, /device:TPU:1, one launch (start us, length us, event | category | flops | bytes accessed | tf_op | source)
XLA Modules:
  0.0 71.0 jit_solution(15738771070327297130)
XLA Ops:
  0.7 1.1 %fusion.50 = (f32[2,64,128]{2,1,0:T(8,128)S(1)}, f32[2,64,4,128]{3,1,0,2:T(8,128)S(1)}) fusion(f32[4,2,64,128]{3,2,1,0:T(8,128)} %param.12, f32[2,64,128]{2,1,0:T(8,128)} %param.11), kind=kLoop, calls=%fused_computation.109 | loop fusion | flops 114688 | bytes 655360 | tf_op jit(solution)/shard_map/reduce_sum | solution.py:186
  1.8 2.1 %collective-permute-start.2 = (f32[2,1,4,128]{3,1,0,2:T(1,128)S(1)}, f32[2,1,4,128]{3,1,0,2:T(1,128)S(1)}, u32[]{:S(2)}, u32[]{:S(2)}) collective-permute-start(f32[2,1,4,128]{3,1,0,2:T(1,128)S(1)} %broadcast_select_fusion.1), channel_id=1, source_target_pairs={{0,1},{1,0},{2,3},{3,2},{4,5},{5,4},{6,7},{7,6},{8,9},{9,8},{10,11... | collective-permute-start | bytes 12296 | tf_op jit(solution)/shard_map/ppermute | solution.py:16
  3.9 4.0 %collective-permute-start = (f32[1,1,4,128]{3,1,0,2:T(1,128)S(1)}, f32[1,1,4,128]{3,1,0,2:T(1,128)S(1)}, u32[]{:S(2)}, u32[]{:S(2)}) collective-permute-start(f32[1,1,4,128]{3,1,0,2:T(1,128)S(1)} %get-tuple-element.8), channel_id=1, source_target_pairs={{0,3},{1,2},{2,5},{3,4},{4,7},{5,6},{6,9},{7,8},{8,11},{9,10},{10,... | collective-permute-start | bytes 6152 | tf_op jit(solution)/shard_map/ppermute | solution.py:58
  7.9 1.9 %collective-permute-start.3 = (f32[1,1,4,128]{3,1,0,2:T(1,128)S(1)}, f32[1,1,4,128]{3,1,0,2:T(1,128)S(1)}, u32[]{:S(2)}, u32[]{:S(2)}) collective-permute-start(f32[1,1,4,128]{3,1,0,2:T(1,128)S(1)} %get-tuple-element.9), channel_id=1, source_target_pairs={{2,1},{3,0},{4,3},{5,2},{6,5},{7,4},{8,7},{9,6},{10,9},{11,8},{12,... | collective-permute-start | bytes 6152 | tf_op jit(solution)/shard_map/ppermute | solution.py:58
  9.8 0.7 %fusion.51 = (f32[1,64,4,128]{3,1,0,2:T(8,128)}, f32[1,64,4,128]{3,1,0,2:T(8,128)}) fusion(f32[2,64,4,128]{3,1,0,2:T(8,128)S(1)} %get-tuple-element.3), kind=kLoop, calls=%fused_computation.110 | loop fusion | bytes 524288 | tf_op jit(solution)/shard_map/slice | solution.py:13
  10.6 4.6 %collective-permute-start.1 = (f32[1,64,4,128]{3,1,0,2:T(8,128)}, f32[1,64,4,128]{3,1,0,2:T(8,128)}, u32[]{:S(2)}, u32[]{:S(2)}) collective-permute-start(f32[1,64,4,128]{3,1,0,2:T(8,128)} %get-tuple-element.6), channel_id=1, source_target_pairs={{0,2},{2,4},{4,6},{6,8},{8,10},{10,12},{12,14},{14,16},{16,18},{18... | collective-permute-start | bytes 393224 | tf_op jit(solution)/shard_map/ppermute | solution.py:21
  15.1 1.9 %collective-permute-start.4 = (f32[1,64,4,128]{3,1,0,2:T(8,128)}, f32[1,64,4,128]{3,1,0,2:T(8,128)}, u32[]{:S(2)}, u32[]{:S(2)}) collective-permute-start(f32[1,64,4,128]{3,1,0,2:T(8,128)} %get-tuple-element.7), channel_id=1, source_target_pairs={{2,0},{4,2},{6,4},{8,6},{10,8},{12,10},{14,12},{16,14},{18,16},{20... | collective-permute-start | bytes 393224 | tf_op jit(solution)/shard_map/ppermute | solution.py:22
  17.0 0.8 %broadcast_in_dim.14 = f32[9]{0:T(128)S(1)} reshape(f32[3,3]{1,0:T(4,128)} %param.13) | data formatting | bytes 72 | tf_op jit(solution)/shard_map/broadcast_in_dim | solution.py:125
  18.6 3.1 %collective-permute-done.4 = f32[1,64,4,128]{3,1,0,2:T(8,128)} collective-permute-done((f32[1,64,4,128]{3,1,0,2:T(8,128)}, f32[1,64,4,128]{3,1,0,2:T(8,128)}, u32[]{:S(2)}, u32[]{:S(2)}) %collective-permute-start.4) | collective-permute-done | bytes 131104 | tf_op jit(solution)/shard_map/ppermute | solution.py:22
  21.7 1.0 %maximum_maximum_fusion = f32[4,66,4,128]{3,1,0,2:T(8,128)S(1)} fusion(f32[1,1,4,128]{3,1,0,2:T(1,128)S(1)} %get-tuple-element.30, f32[1,64,4,128]{3,1,0,2:T(8,128)} %collective-permute-done.4, f32[1,1,4,128]{3,1,0,2:T(1,128)S(1)} %get-tuple-element.29, f32[2,1,4,128]{3,1,0,2:T(1,128)S(1)} %get-tuple-element.26, f32[2,64,4,128]{3,1,0,2:T(8,128)S(1)} %get-tuple-element.3, ...), kind=kLoop, calls=%fused_computation.4 | loop fusion | flops 1081344 | bytes 1081344 | tf_op jit(solution)/shard_map/concatenate | solution.py:76
  22.8 2.1 %fusion.53 = (bf16[2,64,4,128]{3,1,2,0:T(8,128)(2,1)S(1)}, f32[2,64,4,128]{3,1,2,0:T(8,128)}) fusion(f32[128]{0:T(128)} %param.15, f32[128,128]{1,0:T(8,128)} %param.14, f32[4,66,4,128]{3,1,0,2:T(8,128)S(1)} %maximum_maximum_fusion, f32[128]{0:T(128)S(1)} %get-tuple-element.17, f32[128]{0:T(128)S(1)} %get-tuple-element.18, f32[128]{0:T(128)S(1)} %get-tuple-element.19, ...), kind=kOutput, calls=%fused_computation.112 | convolution fusion | flops 101908480 | bytes 2823168 | tf_op jit(solution)/shard_map/xysw,zw->xysz/dot_general | solution.py:136
  25.1 1.7 %fusion.19 = f32[96,4,128]{2,1,0:T(4,128)S(1)} fusion(bf16[96,128,128]{2,1,0:T(8,128)(2,1)S(1)} %copy-done, bf16[96,4,128]{2,0,1:T(8,128)(2,1)S(1)} %convolution_convert_fusion.1), kind=kOutput, calls=%fused_computation.37 | convolution fusion | flops 12582912 | bytes 3440640 | tf_op jit(solution)/shard_map/pij,psj->psi/dot_general | solution.py:145
  27.4 1.3 %collective-permute-done.5 = f32[8,8,4,128]{3,1,2,0:T(8,128)S(1)} collective-permute-done((f32[8,8,4,128]{3,1,2,0:T(8,128)S(1)}, f32[8,8,4,128]{3,1,2,0:T(8,128)S(1)}, u32[]{:S(2)}, u32[]{:S(2)}) %collective-permute-start.5) | collective-permute-done | bytes 131104 | tf_op jit(solution)/shard_map/ppermute | solution.py:156
  28.8 12.3 %all_to_all.10 = f32[8,8,4,128]{3,1,2,0:T(8,128)S(1)} all-to-all(f32[8,8,4,128]{3,1,2,0:T(8,128)S(1)} %bitcast_add_fusion), channel_id=1, replica_groups=mesh['vh'=8,'vc'=2,'star'=2] {'vh'}, dimensions={0} | all-to-all | bytes 262144 | tf_op jit(solution)/shard_map/all_to_all | solution.py:157
  41.8 5.0 %all-to-all-start.1 = ((bf16[16,8,4,128]{3,1,2,0:T(8,128)(2,1)}), bf16[16,8,4,128]{3,1,2,0:T(8,128)(2,1)S(1)}, u32[]{:S(2)}, u32[]{:S(2)}) async-start(bf16[16,8,4,128]{3,1,2,0:T(8,128)(2,1)} %broadcast_in_dim.38), calls=%async_computation.1 | async-start | bytes 262144 | tf_op jit(solution)/shard_map/all_to_all | solution.py:163
  47.4 6.4 %all-to-all-done.1 = bf16[16,8,4,128]{3,1,2,0:T(8,128)(2,1)S(1)} async-done(((bf16[16,8,4,128]{3,1,2,0:T(8,128)(2,1)}), bf16[16,8,4,128]{3,1,2,0:T(8,128)(2,1)S(1)}, u32[]{:S(2)}, u32[]{:S(2)}) %all-to-all-start.1) | async-done | bytes 131104 | tf_op jit(solution)/shard_map/all_to_all | solution.py:163
  54.0 0.9 %fusion.17 = f32[96,4,128]{2,1,0:T(4,128)S(1)} fusion(bf16[96,128,128]{2,1,0:T(8,128)(2,1)S(1)} %copy-done, bf16[96,4,128]{2,0,1:T(8,128)(2,1)S(1)} %convolution_convert_fusion), kind=kOutput, calls=%fused_computation.35 | convolution fusion | flops 12582912 | bytes 3440640 | tf_op jit(solution)/shard_map/pij,psi->psj/dot_general | solution.py:169
  55.6 2.0 %collective-permute-start.6 = (f32[1,1,128]{2,1,0:T(1,128)S(1)}, f32[1,1,128]{2,1,0:T(1,128)S(1)}, u32[]{:S(2)}, u32[]{:S(2)}) collective-permute-start(f32[1,1,128]{2,1,0:T(1,128)S(1)} %get-tuple-element.12), channel_id=1, source_target_pairs={{0,3},{1,2},{2,5},{3,4},{4,7},{5,6},{6,9},{7,8},{8,11},{9,10},{10,... | collective-permute-start | bytes 1544 | tf_op jit(solution)/shard_map/ppermute | solution.py:58
  57.7 2.4 %collective-permute-start.10 = (f32[1,64,128]{2,1,0:T(8,128)S(1)}, f32[1,64,128]{2,1,0:T(8,128)S(1)}, u32[]{:S(2)}, u32[]{:S(2)}) collective-permute-start(f32[1,64,128]{2,1,0:T(8,128)S(1)} %get-tuple-element.11), channel_id=1, source_target_pairs={{2,0},{4,2},{6,4},{8,6},{10,8},{12,10},{14,12},{16,14},{18,16},{20... | collective-permute-start | bytes 98312 | tf_op jit(solution)/shard_map/ppermute | solution.py:22
  60.1 3.1 %collective-permute-start.7 = (f32[1,64,128]{2,1,0:T(8,128)S(1)}, f32[1,64,128]{2,1,0:T(8,128)S(1)}, u32[]{:S(2)}, u32[]{:S(2)}) collective-permute-start(f32[1,64,128]{2,1,0:T(8,128)S(1)} %get-tuple-element.10), channel_id=1, source_target_pairs={{0,2},{2,4},{4,6},{6,8},{8,10},{10,12},{12,14},{14,16},{16,18},{18... | collective-permute-start | bytes 98312 | tf_op jit(solution)/shard_map/ppermute | solution.py:21
  63.3 1.3 %collective-permute-start.8 = (f32[2,1,128]{2,1,0:T(1,128)S(1)}, f32[2,1,128]{2,1,0:T(1,128)S(1)}, u32[]{:S(2)}, u32[]{:S(2)}) collective-permute-start(f32[2,1,128]{2,1,0:T(1,128)S(1)} %broadcast_select_fusion.10), channel_id=1, source_target_pairs={{0,1},{1,0},{2,3},{3,2},{4,5},{5,4},{6,7},{7,6},{8,9},{9,8},{10,11... | collective-permute-start | bytes 3080 | tf_op jit(solution)/shard_map/ppermute | solution.py:16
  64.5 1.9 %collective-permute-start.9 = (f32[1,1,128]{2,1,0:T(1,128)S(1)}, f32[1,1,128]{2,1,0:T(1,128)S(1)}, u32[]{:S(2)}, u32[]{:S(2)}) collective-permute-start(f32[1,1,128]{2,1,0:T(1,128)S(1)} %get-tuple-element.13), channel_id=1, source_target_pairs={{2,1},{3,0},{4,3},{5,2},{6,5},{7,4},{8,7},{9,6},{10,9},{11,8},{12,... | collective-permute-start | bytes 1544 | tf_op jit(solution)/shard_map/ppermute | solution.py:58
  66.5 3.8 %collective-permute-done.9 = f32[1,1,128]{2,1,0:T(1,128)S(1)} collective-permute-done((f32[1,1,128]{2,1,0:T(1,128)S(1)}, f32[1,1,128]{2,1,0:T(1,128)S(1)}, u32[]{:S(2)}, u32[]{:S(2)}) %collective-permute-start.9) | collective-permute-done | bytes 544 | tf_op jit(solution)/shard_map/ppermute | solution.py:58
  70.3 0.7 fusion.22
  (50 shorter events, 3.8 us)
Async XLA Ops:
  0.6 24.5 %copy-start = (bf16[96,128,128]{2,1,0:T(8,128)(2,1)S(1)}, bf16[96,128,128]{2,1,0:T(8,128)(2,1)}, u32[]{:S(2)}) copy-start(bf16[96,128,128]{2,1,0:T(8,128)(2,1)} %param.16) | copy-start | bytes 9437188
  0.6 24.3 %copy-start.5 = (s32[96]{0:T(128)S(1)}, s32[96]{0:T(128)}, u32[]{:S(2)}) copy-start(s32[96]{0:T(128)} %param.17) | copy-start | bytes 1156
  1.8 16.8 %collective-permute-start.2 = (f32[2,1,4,128]{3,1,0,2:T(1,128)S(1)}, f32[2,1,4,128]{3,1,0,2:T(1,128)S(1)}, u32[]{:S(2)}, u32[]{:S(2)}) collective-permute-start(f32[2,1,4,128]{3,1,0,2:T(1,128)S(1)} %broadcast_select_fusion.1), channel_id=1, source_target_pairs={{0,1},{1,0},{2,3},{3,2},{4,5},{5,4},{6,7},{7,6},{8,9},{9,8},{10,11... | collective-permute-start | bytes 12296 | tf_op jit(solution)/shard_map/ppermute | solution.py:16
  3.9 14.6 %collective-permute-start = (f32[1,1,4,128]{3,1,0,2:T(1,128)S(1)}, f32[1,1,4,128]{3,1,0,2:T(1,128)S(1)}, u32[]{:S(2)}, u32[]{:S(2)}) collective-permute-start(f32[1,1,4,128]{3,1,0,2:T(1,128)S(1)} %get-tuple-element.8), channel_id=1, source_target_pairs={{0,3},{1,2},{2,5},{3,4},{4,7},{5,6},{6,9},{7,8},{8,11},{9,10},{10,... | collective-permute-start | bytes 6152 | tf_op jit(solution)/shard_map/ppermute | solution.py:58
  7.9 10.7 %collective-permute-start.3 = (f32[1,1,4,128]{3,1,0,2:T(1,128)S(1)}, f32[1,1,4,128]{3,1,0,2:T(1,128)S(1)}, u32[]{:S(2)}, u32[]{:S(2)}) collective-permute-start(f32[1,1,4,128]{3,1,0,2:T(1,128)S(1)} %get-tuple-element.9), channel_id=1, source_target_pairs={{2,1},{3,0},{4,3},{5,2},{6,5},{7,4},{8,7},{9,6},{10,9},{11,8},{12,... | collective-permute-start | bytes 6152 | tf_op jit(solution)/shard_map/ppermute | solution.py:58
  10.6 8.1 %collective-permute-start.1 = (f32[1,64,4,128]{3,1,0,2:T(8,128)}, f32[1,64,4,128]{3,1,0,2:T(8,128)}, u32[]{:S(2)}, u32[]{:S(2)}) collective-permute-start(f32[1,64,4,128]{3,1,0,2:T(8,128)} %get-tuple-element.6), channel_id=1, source_target_pairs={{0,2},{2,4},{4,6},{6,8},{8,10},{10,12},{12,14},{14,16},{16,18},{18... | collective-permute-start | bytes 393224 | tf_op jit(solution)/shard_map/ppermute | solution.py:21
  15.1 6.6 %collective-permute-start.4 = (f32[1,64,4,128]{3,1,0,2:T(8,128)}, f32[1,64,4,128]{3,1,0,2:T(8,128)}, u32[]{:S(2)}, u32[]{:S(2)}) collective-permute-start(f32[1,64,4,128]{3,1,0,2:T(8,128)} %get-tuple-element.7), channel_id=1, source_target_pairs={{2,0},{4,2},{6,4},{8,6},{10,8},{12,10},{14,12},{16,14},{18,16},{20... | collective-permute-start | bytes 393224 | tf_op jit(solution)/shard_map/ppermute | solution.py:22
  24.9 16.2 %copy-start.3 = (f32[8,128]{1,0:T(8,128)S(1)}, f32[8,128]{1,0:T(8,128)}, u32[]{:S(2)}) copy-start(f32[8,128]{1,0:T(8,128)} %param.20) | copy-start | bytes 12292
  24.9 16.2 %copy-start.4 = (f32[8,128]{1,0:T(8,128)S(1)}, f32[8,128]{1,0:T(8,128)}, u32[]{:S(2)}) copy-start(f32[8,128]{1,0:T(8,128)} %param.21) | copy-start | bytes 12292
  27.3 28.1 %copy-start.2 = (f32[128,128]{1,0:T(8,128)S(1)}, f32[128,128]{1,0:T(8,128)}, u32[]{:S(2)}) copy-start(f32[128,128]{1,0:T(8,128)} %param.14) | copy-start | bytes 196612
  27.3 1.4 %collective-permute-start.5 = (f32[8,8,4,128]{3,1,2,0:T(8,128)S(1)}, f32[8,8,4,128]{3,1,2,0:T(8,128)S(1)}, u32[]{:S(2)}, u32[]{:S(2)}) collective-permute-start(f32[8,8,4,128]{3,1,2,0:T(8,128)S(1)} %bitcast.62), channel_id=1, source_target_pairs={{0,2},{2,0},{1,3},{3,1},{4,6},{6,4},{5,7},{7,5},{8,10},{10,8},{9,1... | collective-permute-start | bytes 393224 | tf_op jit(solution)/shard_map/ppermute | solution.py:156
  41.8 12.0 %all-to-all-start.1 = ((bf16[16,8,4,128]{3,1,2,0:T(8,128)(2,1)}), bf16[16,8,4,128]{3,1,2,0:T(8,128)(2,1)S(1)}, u32[]{:S(2)}, u32[]{:S(2)}) async-start(bf16[16,8,4,128]{3,1,2,0:T(8,128)(2,1)} %broadcast_in_dim.38), calls=%async_computation.1 | async-start | bytes 262144 | tf_op jit(solution)/shard_map/all_to_all | solution.py:163
  53.8 1.5 %copy-start.1 = (f32[2,64,4,128]{3,1,2,0:T(8,128)S(1)}, f32[2,64,4,128]{3,1,2,0:T(8,128)}, u32[]{:S(2)}) copy-start(f32[2,64,4,128]{3,1,2,0:T(8,128)} %get-tuple-element.38) | copy-start | bytes 786436
  55.6 10.8 %collective-permute-start.6 = (f32[1,1,128]{2,1,0:T(1,128)S(1)}, f32[1,1,128]{2,1,0:T(1,128)S(1)}, u32[]{:S(2)}, u32[]{:S(2)}) collective-permute-start(f32[1,1,128]{2,1,0:T(1,128)S(1)} %get-tuple-element.12), channel_id=1, source_target_pairs={{0,3},{1,2},{2,5},{3,4},{4,7},{5,6},{6,9},{7,8},{8,11},{9,10},{10,... | collective-permute-start | bytes 1544 | tf_op jit(solution)/shard_map/ppermute | solution.py:58
  57.7 12.6 %collective-permute-start.10 = (f32[1,64,128]{2,1,0:T(8,128)S(1)}, f32[1,64,128]{2,1,0:T(8,128)S(1)}, u32[]{:S(2)}, u32[]{:S(2)}) collective-permute-start(f32[1,64,128]{2,1,0:T(8,128)S(1)} %get-tuple-element.11), channel_id=1, source_target_pairs={{2,0},{4,2},{6,4},{8,6},{10,8},{12,10},{14,12},{16,14},{18,16},{20... | collective-permute-start | bytes 98312 | tf_op jit(solution)/shard_map/ppermute | solution.py:22
  60.1 10.2 %collective-permute-start.7 = (f32[1,64,128]{2,1,0:T(8,128)S(1)}, f32[1,64,128]{2,1,0:T(8,128)S(1)}, u32[]{:S(2)}, u32[]{:S(2)}) collective-permute-start(f32[1,64,128]{2,1,0:T(8,128)S(1)} %get-tuple-element.10), channel_id=1, source_target_pairs={{0,2},{2,4},{4,6},{6,8},{8,10},{10,12},{12,14},{14,16},{16,18},{18... | collective-permute-start | bytes 98312 | tf_op jit(solution)/shard_map/ppermute | solution.py:21
  63.3 7.0 %collective-permute-start.8 = (f32[2,1,128]{2,1,0:T(1,128)S(1)}, f32[2,1,128]{2,1,0:T(1,128)S(1)}, u32[]{:S(2)}, u32[]{:S(2)}) collective-permute-start(f32[2,1,128]{2,1,0:T(1,128)S(1)} %broadcast_select_fusion.10), channel_id=1, source_target_pairs={{0,1},{1,0},{2,3},{3,2},{4,5},{5,4},{6,7},{7,6},{8,9},{9,8},{10,11... | collective-permute-start | bytes 3080 | tf_op jit(solution)/shard_map/ppermute | solution.py:16
  64.5 5.7 %collective-permute-start.9 = (f32[1,1,128]{2,1,0:T(1,128)S(1)}, f32[1,1,128]{2,1,0:T(1,128)S(1)}, u32[]{:S(2)}, u32[]{:S(2)}) collective-permute-start(f32[1,1,128]{2,1,0:T(1,128)S(1)} %get-tuple-element.13), channel_id=1, source_target_pairs={{2,1},{3,0},{4,3},{5,2},{6,5},{7,4},{8,7},{9,6},{10,9},{11,8},{12,... | collective-permute-start | bytes 1544 | tf_op jit(solution)/shard_map/ppermute | solution.py:58

commit v15 on v13

--- a/solution.py
+++ b/solution.py
@@ -6,11 +6,14 @@
 HIGH = lax.Precision.HIGHEST
 
 
-def exchange(cells, axis, dim):
+def exchange(cells, axis, dim, ends=None):
     count = lax.psum(1, axis)
     size = cells.shape[dim]
-    head = lax.slice_in_dim(cells, 0, 1, axis=dim)
-    tail = lax.slice_in_dim(cells, size - 1, size, axis=dim)
+    if ends is None:
+        head = lax.slice_in_dim(cells, 0, 1, axis=dim)
+        tail = lax.slice_in_dim(cells, size - 1, size, axis=dim)
+    else:
+        head, tail = ends
     if count == 2:
         index = lax.axis_index(axis)
         incoming = lax.ppermute(jnp.where(index == 0, tail, head), axis, [(0, 1), (1, 0)])
@@ -26,8 +29,8 @@
 VOX = ("vh", "vc")
 
 
-def with_halo(cells):
-    return lax.optimization_barrier(exchange(exchange(cells, VOX, 0), "star", 1))
+def with_halo(cells, ends=None):
+    return lax.optimization_barrier(exchange(exchange(cells, VOX, 0, ends), "star", 1))
 
 
 def rows(table, index, axis):
@@ -70,7 +73,11 @@
     weights = lax.optimization_barrier(
         jnp.broadcast_to(stencil.reshape(9, 1), (9, length))
     )
-    padded = with_halo(latent)
+    edge = [
+        jnp.transpose(mean_field[at : at + 1][None] + deviations[:, at : at + 1], (1, 2, 0, 3))
+        for at in (0, width_x - 1)
+    ]
+    padded = with_halo(latent, edge)
     smoothed = jnp.zeros(latent.shape, jnp.float32)
     for offset_x in range(3):
         for offset_y in range(3):

time: 60.4 us -> 60.6 us (level)
  waiting for transfers between devices: 8.21 us -> 6.6 us
  other arithmetic: 6.07 us -> 7.64 us
    transpose x0 -> x1, other arithmetic: none -> 1.72 us  [per_device(): jnp.transpose(mean_field[at:at + 1][None] + deviations[:, at:at + 1], (1,...]
    ppermute x2, waiting for transfers between devices: 6.13 us -> 4.53 us  [exchange(): above = lax.ppermute(head, axis, [(i + 1, i) for i in range(count - 1)])]
    add x0 -> x1, local copies, waits for them, and re-layouts: none -> 0.93 us  [per_device(): mean_field[at:at + 1][None] + deviations[:, at:at + 1]]
    slice x2 -> x1, local copies, waits for them, and re-layouts: 0.72 us -> 0.01 us  [exchange(): tail = lax.slice_in_dim(cells, size - 1, size, axis=dim)]
  transfers between devices with their start and end apart: 7 -> 7, of which waited for: 5 -> 5; matrix products, arithmetic and copies ran while one was open for 5% -> 8% of each run, Pallas kernels for 0% -> 0%
where the time goes in v15:
time: 60.6 us; the launch traced here: 60.1 us
  blocking collectives  22.7 us (37%)
  starting transfers between devices  13.4 us (22%)
  other arithmetic  7.64 us (13%)
  waiting for transfers between devices  6.6 us (11%)
  matrix products  6.21 us (10%)
  local copies, waits for them, and re-layouts  2.53 us (4%)
  between operations  1.04 us (2%)
    all_to_all x1, blocking collectives, per_device(): lax.all_to_all(merged, 'vh', split_axis=0, concat_axis=0, tiled=True)  11.4 us
    all_to_all x1, blocking collectives, per_device(): lax.all_to_all(spread, VOX, split_axis=0, concat_axis=0, tiled=True)  11.3 us
    ppermute x2, starting transfers between devices, exchange(): below = lax.ppermute(tail, axis, [(i, i + 1) for i in range(count - 1)])  6.6 us
    ppermute x2, waiting for transfers between devices, exchange(): above = lax.ppermute(head, axis, [(i + 1, i) for i in range(count - 1)])  4.53 us
    ppermute x2, starting transfers between devices, exchange(): above = lax.ppermute(head, axis, [(i + 1, i) for i in range(count - 1)])  4.22 us
    ppermute x2, starting transfers between devices, exchange(): lax.ppermute(jnp.where(index == 0, tail, head), axis, [(0, 1), (1, 0)])  2.49 us
    dot_general x1, matrix products, per_device(): jnp.einsum('xysw,zw->xysz', smoothed, vertical_mix, precision=HIGH)  2.15 us
    transpose x1, other arithmetic, per_device(): jnp.transpose(mean_field[at:at + 1][None] + deviations[:, at:at + 1], (1,...  1.72 us
  transfers between devices with their start and end apart: 7, of which 5 were waited for; matrix products, arithmetic and copies ran while one was open for 8% of the time, Pallas kernels for 0%

profile of v15, /device:TPU:1, one launch (start us, length us, event | category | flops | bytes accessed | tf_op | source)
XLA Modules:
  0.0 60.1 jit_solution(11340321554384716846)
XLA Ops:
  0.6 0.9 %slice_bitcast_fusion.1 = (f32[64,128]{1,0:T(8,128)S(1)}, f32[64,128]{1,0:T(8,128)S(1)}) fusion(f32[2,64,128]{2,1,0:T(8,128)} %param.11), kind=kLoop, calls=%fused_computation.71 | loop fusion | bytes 131072 | tf_op jit(solution)/shard_map/add | solution.py:77
  1.6 1.7 %add_bitcast_fusion.2 = (f32[1,64,4,128]{3,1,0,2:T(8,128)}, f32[1,64,4,128]{3,1,0,2:T(8,128)}) fusion(f32[4,2,64,128]{3,2,1,0:T(8,128)} %param.12, f32[64,128]{1,0:T(8,128)S(1)} %get-tuple-element.10, f32[64,128]{1,0:T(8,128)S(1)} %get-tuple-element.11), kind=kLoop, calls=%fused_computation.36 | loop fusion | flops 65536 | bytes 589824 | tf_op jit(solution)/shard_map/transpose | solution.py:77
  3.3 4.5 %collective-permute-start = (f32[1,64,4,128]{3,1,0,2:T(8,128)}, f32[1,64,4,128]{3,1,0,2:T(8,128)S(1)}, u32[]{:S(2)}, u32[]{:S(2)}) collective-permute-start(f32[1,64,4,128]{3,1,0,2:T(8,128)} %get-tuple-element.6), channel_id=1, source_target_pairs={{0,2},{2,4},{4,6},{6,8},{8,10},{10,12},{12,14},{14,16},{16,18},{18... | collective-permute-start | bytes 393224 | tf_op jit(solution)/shard_map/ppermute | solution.py:24
  7.8 1.9 %collective-permute-start.1 = (f32[1,64,4,128]{3,1,0,2:T(8,128)}, f32[1,64,4,128]{3,1,0,2:T(8,128)}, u32[]{:S(2)}, u32[]{:S(2)}) collective-permute-start(f32[1,64,4,128]{3,1,0,2:T(8,128)} %get-tuple-element.7), channel_id=1, source_target_pairs={{2,0},{4,2},{6,4},{8,6},{10,8},{12,10},{14,12},{16,14},{18,16},{20... | collective-permute-start | bytes 393224 | tf_op jit(solution)/shard_map/ppermute | solution.py:25
  9.8 1.6 %fusion.50 = (f32[2,64,128]{2,1,0:T(8,128)}, f32[2,64,4,128]{3,1,0,2:T(8,128)S(1)}) fusion(f32[4,2,64,128]{3,2,1,0:T(8,128)} %param.12, f32[2,64,128]{2,1,0:T(8,128)} %param.11), kind=kLoop, calls=%fused_computation.105 | loop fusion | flops 114688 | bytes 655360 | tf_op jit(solution)/shard_map/reduce_sum | solution.py:139
  11.4 0.8 %broadcast_in_dim.10 = f32[9]{0:T(128)S(1)} reshape(f32[3,3]{1,0:T(4,128)} %param.13) | data formatting | bytes 72 | tf_op jit(solution)/shard_map/broadcast_in_dim | solution.py:74
  12.2 0.6 %slice_bitcast_fusion.10 = (f32[128]{0:T(128)}, f32[128]{0:T(128)}, f32[128]{0:T(128)}, f32[128]{0:T(128)}, f32[128]{0:T(128)}, /*index=5*/f32[128]{0:T(128)}, f32[128]{0:T(128)}, f32[128]{0:T(128)}, f32[128]{0:T(128)}) fusion(f32[9,128]{1,0:T(8,128)S(1)} %broadcast_in_dim.11), kind=kLoop, calls=%fused_computation.100 | loop fusion | bytes 9216 | tf_op jit(solution)/shard_map/mul | solution.py:136
  12.8 1.6 %collective-permute-done.1 = f32[1,64,4,128]{3,1,0,2:T(8,128)} collective-permute-done((f32[1,64,4,128]{3,1,0,2:T(8,128)}, f32[1,64,4,128]{3,1,0,2:T(8,128)}, u32[]{:S(2)}, u32[]{:S(2)}) %collective-permute-start.1) | collective-permute-done | bytes 131104 | tf_op jit(solution)/shard_map/ppermute | solution.py:25
  14.4 0.7 %broadcast_select_fusion.1 = f32[4,1,4,128]{3,1,0,2:T(1,128)S(1)} fusion(pred[]{:T(512)S(6)} %eq.17, f32[1,64,4,128]{3,1,0,2:T(8,128)} %collective-permute-done.1, f32[2,64,4,128]{3,1,0,2:T(8,128)S(1)} %get-tuple-element.3, f32[1,64,4,128]{3,1,0,2:T(8,128)S(1)} %collective-permute-done), kind=kLoop, calls=%fused_computation.80 | loop fusion | flops 10240 | bytes 532481 | tf_op jit(solution)/shard_map/jit(_where)/select_n | solution.py:19
  15.2 1.3 %collective-permute-start.2 = (f32[4,1,4,128]{3,1,0,2:T(1,128)S(1)}, f32[4,1,4,128]{3,1,0,2:T(1,128)S(1)}, u32[]{:S(2)}, u32[]{:S(2)}) collective-permute-start(f32[4,1,4,128]{3,1,0,2:T(1,128)S(1)} %broadcast_select_fusion.1), channel_id=1, source_target_pairs={{0,1},{1,0},{2,3},{3,2},{4,5},{5,4},{6,7},{7,6},{8,9},{9,8},{10,11... | collective-permute-start | bytes 24584 | tf_op jit(solution)/shard_map/ppermute | solution.py:19
  16.5 1.2 %bitcast_add_fusion.1 = s32[96]{0:T(128)} fusion(s32[96]{0:T(128)} %param.19, s32[96,1]{0,1:T(1,128)} %param.18), kind=kLoop, calls=%fused_computation.101 | loop fusion | flops 192 | bytes 1152 | tf_op jit(solution)/shard_map/add | solution.py:99
  17.8 1.0 %pad_maximum_fusion = f32[4,66,4,128]{3,1,0,2:T(8,128)S(1)} fusion(f32[4,1,4,128]{3,1,0,2:T(1,128)S(1)} %get-tuple-element.24, f32[1,64,4,128]{3,1,0,2:T(8,128)} %collective-permute-done.1, f32[2,64,4,128]{3,1,0,2:T(8,128)S(1)} %get-tuple-element.3, f32[1,64,4,128]{3,1,0,2:T(8,128)S(1)} %collective-permute-done, f32[4,1,4,128]{3,1,0,2:T(1,128)S(1)} %get-tuple-element.23), kind=kLoop, calls=%fused_computation.4 | loop fusion | flops 540672 | bytes 1081344 | tf_op jit(solution)/shard_map/concatenate | solution.py:26
  18.8 2.1 %fusion.52 = (bf16[2,64,4,128]{3,1,2,0:T(8,128)(2,1)S(1)}, f32[2,64,4,128]{3,1,2,0:T(8,128)}) fusion(f32[128]{0:T(128)} %param.15, f32[128,128]{1,0:T(8,128)} %param.14, f32[4,66,4,128]{3,1,0,2:T(8,128)S(1)} %pad_maximum_fusion, f32[128]{0:T(128)} %get-tuple-element.15, f32[128]{0:T(128)} %get-tuple-element.16, f32[128]{0:T(128)} %get-tuple-element.17, ...), kind=kOutput, calls=%fused_computation.107 | convolution fusion | flops 101908480 | bytes 2823168 | tf_op jit(solution)/shard_map/xysw,zw->xysz/dot_general | solution.py:89
  21.2 1.7 %fusion.19 = f32[96,4,128]{2,1,0:T(4,128)S(1)} fusion(bf16[96,128,128]{2,1,0:T(8,128)(2,1)S(1)} %copy-done, bf16[96,4,128]{2,0,1:T(8,128)(2,1)S(1)} %convolution_convert_fusion.1), kind=kOutput, calls=%fused_computation.39 | convolution fusion | flops 12582912 | bytes 3440640 | tf_op jit(solution)/shard_map/pij,psj->psi/dot_general | solution.py:98
  23.4 1.3 %collective-permute-done.3 = f32[8,8,4,128]{3,1,2,0:T(8,128)S(1)} collective-permute-done((f32[8,8,4,128]{3,1,2,0:T(8,128)S(1)}, f32[8,8,4,128]{3,1,2,0:T(8,128)S(1)}, u32[]{:S(2)}, u32[]{:S(2)}) %collective-permute-start.3) | collective-permute-done | bytes 131104 | tf_op jit(solution)/shard_map/ppermute | solution.py:109
  24.9 11.4 %all_to_all.10 = f32[8,8,4,128]{3,1,2,0:T(8,128)S(1)} all-to-all(f32[8,8,4,128]{3,1,2,0:T(8,128)S(1)} %bitcast_add_fusion), channel_id=1, replica_groups=mesh['vh'=8,'vc'=2,'star'=2] {'vh'}, dimensions={0} | all-to-all | bytes 262144 | tf_op jit(solution)/shard_map/all_to_all | solution.py:110
  36.4 11.3 %all_to_all.11 = bf16[16,8,4,128]{3,1,2,0:T(8,128)(2,1)S(1)} all-to-all(bf16[16,8,4,128]{3,1,2,0:T(8,128)(2,1)S(1)} %broadcast_in_dim.13), channel_id=1, replica_groups=mesh['vh'=8,'vc'=2,'star'=2] {'vh','vc'}, dimensions={0} | all-to-all | bytes 262144 | tf_op jit(solution)/shard_map/all_to_all | solution.py:116
  47.9 0.9 %fusion.17 = f32[96,4,128]{2,1,0:T(4,128)S(1)} fusion(bf16[96,128,128]{2,1,0:T(8,128)(2,1)S(1)} %copy-done, bf16[96,4,128]{2,0,1:T(8,128)(2,1)S(1)} %convolution_convert_fusion), kind=kOutput, calls=%fused_computation.37 | convolution fusion | flops 12582912 | bytes 3440640 | tf_op jit(solution)/shard_map/pij,psi->psj/dot_general | solution.py:122
  49.5 2.1 %collective-permute-start.4 = (f32[1,64,128]{2,1,0:T(8,128)S(1)}, f32[1,64,128]{2,1,0:T(8,128)S(1)}, u32[]{:S(2)}, u32[]{:S(2)}) collective-permute-start(f32[1,64,128]{2,1,0:T(8,128)S(1)} %get-tuple-element.8), channel_id=1, source_target_pairs={{0,2},{2,4},{4,6},{6,8},{8,10},{10,12},{12,14},{14,16},{16,18},{18... | collective-permute-start | bytes 98312 | tf_op jit(solution)/shard_map/ppermute | solution.py:24
  51.6 2.3 %collective-permute-start.5 = (f32[1,64,128]{2,1,0:T(8,128)S(1)}, f32[1,64,128]{2,1,0:T(8,128)S(1)}, u32[]{:S(2)}, u32[]{:S(2)}) collective-permute-start(f32[1,64,128]{2,1,0:T(8,128)S(1)} %get-tuple-element.9), channel_id=1, source_target_pairs={{2,0},{4,2},{6,4},{8,6},{10,8},{12,10},{14,12},{16,14},{18,16},{20... | collective-permute-start | bytes 98312 | tf_op jit(solution)/shard_map/ppermute | solution.py:25
  53.9 2.9 %collective-permute-done.5 = f32[1,64,128]{2,1,0:T(8,128)S(1)} collective-permute-done((f32[1,64,128]{2,1,0:T(8,128)S(1)}, f32[1,64,128]{2,1,0:T(8,128)S(1)}, u32[]{:S(2)}, u32[]{:S(2)}) %collective-permute-start.5) | collective-permute-done | bytes 32800 | tf_op jit(solution)/shard_map/ppermute | solution.py:25
  56.8 1.2 %collective-permute-start.6 = (f32[4,1,128]{2,1,0:T(1,128)S(1)}, f32[4,1,128]{2,1,0:T(1,128)S(1)}, u32[]{:S(2)}, u32[]{:S(2)}) collective-permute-start(f32[4,1,128]{2,1,0:T(1,128)S(1)} %broadcast_select_fusion.4), channel_id=1, source_target_pairs={{0,1},{1,0},{2,3},{3,2},{4,5},{5,4},{6,7},{7,6},{8,9},{9,8},{10,11... | collective-permute-start | bytes 6152 | tf_op jit(solution)/shard_map/ppermute | solution.py:19
  58.6 0.6 %collective-permute-done.6 = f32[4,1,128]{2,1,0:T(1,128)S(1)} collective-permute-done((f32[4,1,128]{2,1,0:T(1,128)S(1)}, f32[4,1,128]{2,1,0:T(1,128)S(1)}, u32[]{:S(2)}, u32[]{:S(2)}) %collective-permute-start.6) | collective-permute-done | bytes 2080 | tf_op jit(solution)/shard_map/ppermute | solution.py:19
  59.4 0.7 %fusion.22 = f32[2,64,128]{2,1,0:T(8,128)} fusion(f32[4,66,128]{2,1,0:T(8,128)S(1)} %pad_maximum_fusion.1, f32[2,64,128]{2,1,0:T(8,128)S(1)} %copy-done.1, f32[128]{0:T(128)S(1)} %copy-done.7, f32[128]{0:T(128)S(1)} %copy-done.8, f32[128]{0:T(128)S(1)} %copy-done.9, f32[128]{0:T(128)S(1)} %copy-done.10, f32[128]{0:T(128)S(1)} %copy-done.11, ...), kind=kLoop, calls=%fused_computation.43 | loop fusion | flops 311296 | bytes 725504 | tf_op jit(solution)/shard_map/add | solution.py:139
  (60 shorter events, 2.5 us)
Async XLA Ops:
  0.6 20.5 %copy-start = (bf16[96,128,128]{2,1,0:T(8,128)(2,1)S(1)}, bf16[96,128,128]{2,1,0:T(8,128)(2,1)}, u32[]{:S(2)}) copy-start(bf16[96,128,128]{2,1,0:T(8,128)(2,1)} %param.16) | copy-start | bytes 9437188
  3.3 9.5 %collective-permute-start = (f32[1,64,4,128]{3,1,0,2:T(8,128)}, f32[1,64,4,128]{3,1,0,2:T(8,128)S(1)}, u32[]{:S(2)}, u32[]{:S(2)}) collective-permute-start(f32[1,64,4,128]{3,1,0,2:T(8,128)} %get-tuple-element.6), channel_id=1, source_target_pairs={{0,2},{2,4},{4,6},{6,8},{8,10},{10,12},{12,14},{14,16},{16,18},{18... | collective-permute-start | bytes 393224 | tf_op jit(solution)/shard_map/ppermute | solution.py:24
  7.8 6.6 %collective-permute-start.1 = (f32[1,64,4,128]{3,1,0,2:T(8,128)}, f32[1,64,4,128]{3,1,0,2:T(8,128)}, u32[]{:S(2)}, u32[]{:S(2)}) collective-permute-start(f32[1,64,4,128]{3,1,0,2:T(8,128)} %get-tuple-element.7), channel_id=1, source_target_pairs={{2,0},{4,2},{6,4},{8,6},{10,8},{12,10},{14,12},{16,14},{18,16},{20... | collective-permute-start | bytes 393224 | tf_op jit(solution)/shard_map/ppermute | solution.py:25
  15.2 2.6 %collective-permute-start.2 = (f32[4,1,4,128]{3,1,0,2:T(1,128)S(1)}, f32[4,1,4,128]{3,1,0,2:T(1,128)S(1)}, u32[]{:S(2)}, u32[]{:S(2)}) collective-permute-start(f32[4,1,4,128]{3,1,0,2:T(1,128)S(1)} %broadcast_select_fusion.1), channel_id=1, source_target_pairs={{0,1},{1,0},{2,3},{3,2},{4,5},{5,4},{6,7},{7,6},{8,9},{9,8},{10,11... | collective-permute-start | bytes 24584 | tf_op jit(solution)/shard_map/ppermute | solution.py:19
  18.7 4.1 %copy-start.17 = (s32[96]{0:T(128)S(1)}, s32[96]{0:T(128)}, u32[]{:S(2)}) copy-start(s32[96]{0:T(128)} %bitcast_add_fusion.1) | copy-start | bytes 1156
  20.9 15.4 %copy-start.4 = (f32[8,128]{1,0:T(8,128)S(1)}, f32[8,128]{1,0:T(8,128)}, u32[]{:S(2)}) copy-start(f32[8,128]{1,0:T(8,128)} %param.20) | copy-start | bytes 12292
  20.9 15.4 %copy-start.5 = (f32[8,128]{1,0:T(8,128)S(1)}, f32[8,128]{1,0:T(8,128)}, u32[]{:S(2)}) copy-start(f32[8,128]{1,0:T(8,128)} %param.21) | copy-start | bytes 12292
  22.9 25.9 %copy-start.16 = (s32[96]{0:T(128)S(1)}, s32[96]{0:T(128)}, u32[]{:S(2)}) copy-start(s32[96]{0:T(128)} %param.17) | copy-start | bytes 1156
  23.3 25.9 %copy-start.3 = (f32[128,128]{1,0:T(8,128)S(1)}, f32[128,128]{1,0:T(8,128)}, u32[]{:S(2)}) copy-start(f32[128,128]{1,0:T(8,128)} %param.14) | copy-start | bytes 196612
  23.4 1.4 %collective-permute-start.3 = (f32[8,8,4,128]{3,1,2,0:T(8,128)S(1)}, f32[8,8,4,128]{3,1,2,0:T(8,128)S(1)}, u32[]{:S(2)}, u32[]{:S(2)}) collective-permute-start(f32[8,8,4,128]{3,1,2,0:T(8,128)S(1)} %bitcast.70), channel_id=1, source_target_pairs={{0,2},{2,0},{1,3},{3,1},{4,6},{6,4},{5,7},{7,5},{8,10},{10,8},{9,1... | collective-permute-start | bytes 393224 | tf_op jit(solution)/shard_map/ppermute | solution.py:109
  24.8 34.5 %copy-start.1 = (f32[2,64,128]{2,1,0:T(8,128)S(1)}, f32[2,64,128]{2,1,0:T(8,128)}, u32[]{:S(2)}) copy-start(f32[2,64,128]{2,1,0:T(8,128)} %get-tuple-element.2) | copy-start | bytes 196612
  24.8 34.5 %copy-start.6 = (f32[128]{0:T(128)S(1)}, f32[128]{0:T(128)}, u32[]{:S(2)}) copy-start(f32[128]{0:T(128)} %get-tuple-element.14) | copy-start | bytes 1540
  24.8 34.5 %copy-start.7 = (f32[128]{0:T(128)S(1)}, f32[128]{0:T(128)}, u32[]{:S(2)}) copy-start(f32[128]{0:T(128)} %get-tuple-element.15) | copy-start | bytes 1540
  24.8 34.5 %copy-start.8 = (f32[128]{0:T(128)S(1)}, f32[128]{0:T(128)}, u32[]{:S(2)}) copy-start(f32[128]{0:T(128)} %get-tuple-element.16) | copy-start | bytes 1540
  24.8 34.5 %copy-start.9 = (f32[128]{0:T(128)S(1)}, f32[128]{0:T(128)}, u32[]{:S(2)}) copy-start(f32[128]{0:T(128)} %get-tuple-element.17) | copy-start | bytes 1540
  24.8 34.5 %copy-start.10 = (f32[128]{0:T(128)S(1)}, f32[128]{0:T(128)}, u32[]{:S(2)}) copy-start(f32[128]{0:T(128)} %get-tuple-element.18) | copy-start | bytes 1540
  24.8 34.5 %copy-start.11 = (f32[128]{0:T(128)S(1)}, f32[128]{0:T(128)}, u32[]{:S(2)}) copy-start(f32[128]{0:T(128)} %get-tuple-element.19) | copy-start | bytes 1540
  24.9 34.5 %copy-start.12 = (f32[128]{0:T(128)S(1)}, f32[128]{0:T(128)}, u32[]{:S(2)}) copy-start(f32[128]{0:T(128)} %get-tuple-element.20) | copy-start | bytes 1540
  24.9 34.5 %copy-start.13 = (f32[128]{0:T(128)S(1)}, f32[128]{0:T(128)}, u32[]{:S(2)}) copy-start(f32[128]{0:T(128)} %get-tuple-element.21) | copy-start | bytes 1540
  24.9 34.5 %copy-start.14 = (f32[128]{0:T(128)S(1)}, f32[128]{0:T(128)}, u32[]{:S(2)}) copy-start(f32[128]{0:T(128)} %get-tuple-element.22) | copy-start | bytes 1540
  36.4 12.9 %copy-start.2 = (f32[2,64,4,128]{3,1,2,0:T(8,128)S(1)}, f32[2,64,4,128]{3,1,2,0:T(8,128)}, u32[]{:S(2)}) copy-start(f32[2,64,4,128]{3,1,2,0:T(8,128)} %get-tuple-element.28) | copy-start | bytes 786436
  49.5 4.4 %collective-permute-start.4 = (f32[1,64,128]{2,1,0:T(8,128)S(1)}, f32[1,64,128]{2,1,0:T(8,128)S(1)}, u32[]{:S(2)}, u32[]{:S(2)}) collective-permute-start(f32[1,64,128]{2,1,0:T(8,128)S(1)} %get-tuple-element.8), channel_id=1, source_target_pairs={{0,2},{2,4},{4,6},{6,8},{8,10},{10,12},{12,14},{14,16},{16,18},{18... | collective-permute-start | bytes 98312 | tf_op jit(solution)/shard_map/ppermute | solution.py:24
  51.6 5.2 %collective-permute-start.5 = (f32[1,64,128]{2,1,0:T(8,128)S(1)}, f32[1,64,128]{2,1,0:T(8,128)S(1)}, u32[]{:S(2)}, u32[]{:S(2)}) collective-permute-start(f32[1,64,128]{2,1,0:T(8,128)S(1)} %get-tuple-element.9), channel_id=1, source_target_pairs={{2,0},{4,2},{6,4},{8,6},{10,8},{12,10},{14,12},{16,14},{18,16},{20... | collective-permute-start | bytes 98312 | tf_op jit(solution)/shard_map/ppermute | solution.py:25
  56.8 2.4 %collective-permute-start.6 = (f32[4,1,128]{2,1,0:T(1,128)S(1)}, f32[4,1,128]{2,1,0:T(1,128)S(1)}, u32[]{:S(2)}, u32[]{:S(2)}) collective-permute-start(f32[4,1,128]{2,1,0:T(1,128)S(1)} %broadcast_select_fusion.4), channel_id=1, source_target_pairs={{0,1},{1,0},{2,3},{3,2},{4,5},{5,4},{6,7},{7,6},{8,9},{9,8},{10,11... | collective-permute-start | bytes 6152 | tf_op jit(solution)/shard_map/ppermute | solution.py:19
  (1 other events, 3.3 us)

commit v16 on v13

--- a/solution.py
+++ b/solution.py
@@ -26,8 +26,8 @@
 VOX = ("vh", "vc")
 
 
-def with_halo(cells):
-    return lax.optimization_barrier(exchange(exchange(cells, VOX, 0), "star", 1))
+def with_halo(cells, dim):
+    return lax.optimization_barrier(exchange(exchange(cells, VOX, dim), "star", dim + 1))
 
 
 def rows(table, index, axis):
@@ -66,27 +66,27 @@
     group_size = lax.psum(1, VOX)
     star_count = observed.shape[0]
     group_blocks = group_size * star_count
-    latent = jnp.transpose(mean_field[None] + deviations, (1, 2, 0, 3))
+    latent = mean_field[None] + deviations
     weights = lax.optimization_barrier(
         jnp.broadcast_to(stencil.reshape(9, 1), (9, length))
     )
-    padded = with_halo(latent)
+    padded = with_halo(latent, 1)
     smoothed = jnp.zeros(latent.shape, jnp.float32)
     for offset_x in range(3):
         for offset_y in range(3):
             smoothed = (
                 smoothed
                 + weights[offset_x * 3 + offset_y]
-                * padded[offset_x : offset_x + width_x, offset_y : offset_y + width_y]
+                * padded[:, offset_x : offset_x + width_x, offset_y : offset_y + width_y]
             )
-    log_density = jnp.einsum("xysw,zw->xysz", smoothed, vertical_mix, precision=HIGH) + log_mean
+    log_density = jnp.einsum("sxyw,zw->sxyz", smoothed, vertical_mix, precision=HIGH) + log_mean
     density = jnp.exp(log_density)
-    density_b = density.astype(jnp.bfloat16).reshape(width_x * width_y, samples, length)
+    density_b = density.astype(jnp.bfloat16).reshape(samples, width_x * width_y, length)
     line_onehot = (
         pair_line[:, None] == jnp.arange(width_x * width_y, dtype=jnp.int32)[None, :]
     ).astype(jnp.float32)
     picked = jnp.einsum(
-        "pl,lsz->psz", line_onehot.astype(jnp.bfloat16), density_b, preferred_element_type=jnp.float32
+        "pl,slz->psz", line_onehot.astype(jnp.bfloat16), density_b, preferred_element_type=jnp.float32
     ).astype(jnp.bfloat16)
     contribution = jnp.einsum("pij,psj->psi", responses, picked, preferred_element_type=jnp.float32)
     target = pair_owner[:, 0] * star_count + pair_star
@@ -115,12 +115,12 @@
     pair_adjoint = jnp.einsum(
         "pij,psi->psj", responses, pair_misfit, preferred_element_type=jnp.float32
     )
-    adjoint = jnp.einsum("pb,psj->bsj", line_onehot, pair_adjoint, precision=HIGH).reshape(
-        width_x, width_y, samples, length
+    adjoint = jnp.einsum("pb,psj->sbj", line_onehot, pair_adjoint, precision=HIGH).reshape(
+        samples, width_x, width_y, length
     )
-    grad_log = jnp.mean(density * adjoint, axis=2)
+    grad_log = jnp.mean(density * adjoint, axis=0)
     grad_smooth = jnp.einsum("xyz,zw->xyw", grad_log, vertical_mix, precision=HIGH)
-    padded_grad = with_halo(grad_smooth)
+    padded_grad = with_halo(grad_smooth, 0)
     grad_latent = jnp.zeros(grad_smooth.shape, jnp.float32)
     for offset_x in range(3):
         for offset_y in range(3):
@@ -129,7 +129,7 @@
                 + weights[offset_x * 3 + offset_y]
                 * padded_grad[2 - offset_x : 2 - offset_x + width_x, 2 - offset_y : 2 - offset_y + width_y]
             )
-    gradient = grad_latent + jnp.mean(latent, axis=2)
+    gradient = grad_latent + jnp.mean(latent, axis=0)
     return (gradient, residual_mean)
 
 

time: 60.4 us -> 60.3 us (level)
  no operation moved by 1% of the time
where the time goes in v16:
time: 60.3 us; the launch traced here: 59.8 us
  blocking collectives  22.6 us (37%)
  starting transfers between devices  13.4 us (22%)
  waiting for transfers between devices  8.2 us (14%)
  matrix products  6.19 us (10%)
  other arithmetic  6.06 us (10%)
  local copies, waits for them, and re-layouts  2.34 us (4%)
  between operations  1.03 us (2%)
    all_to_all x1, blocking collectives, per_device(): lax.all_to_all(merged, 'vh', split_axis=0, concat_axis=0, tiled=True)  11.4 us
    all_to_all x1, blocking collectives, per_device(): lax.all_to_all(spread, VOX, split_axis=0, concat_axis=0, tiled=True)  11.1 us
    ppermute x2, starting transfers between devices, exchange(): below = lax.ppermute(tail, axis, [(i, i + 1) for i in range(count - 1)])  6.6 us
    ppermute x2, waiting for transfers between devices, exchange(): above = lax.ppermute(head, axis, [(i + 1, i) for i in range(count - 1)])  6.13 us
    ppermute x2, starting transfers between devices, exchange(): above = lax.ppermute(head, axis, [(i + 1, i) for i in range(count - 1)])  4.22 us
    ppermute x2, starting transfers between devices, exchange(): lax.ppermute(jnp.where(index == 0, tail, head), axis, [(0, 1), (1, 0)])  2.49 us
    dot_general x1, matrix products, per_device(): jnp.einsum('sxyw,zw->sxyz', smoothed, vertical_mix, precision=HIGH)  2.13 us
    reduce_sum x1, other arithmetic, per_device(): gradient = grad_latent + jnp.mean(latent, axis=0)  1.76 us
  transfers between devices with their start and end apart: 7, of which 5 were waited for; matrix products, arithmetic and copies ran while one was open for 5% of the time, Pallas kernels for 0%

profile of v16, /device:TPU:1, one launch (start us, length us, event | category | flops | bytes accessed | tf_op | source)
XLA Modules:
  0.0 59.8 jit_solution(11799611477751787639)
XLA Ops:
  0.6 1.8 %fusion.64 = (f32[2,64,128]{2,1,0:T(8,128)}, f32[4,2,64,128]{3,2,1,0:T(8,128)S(1)}) fusion(f32[4,2,64,128]{3,2,1,0:T(8,128)} %param.12, f32[2,64,128]{2,1,0:T(8,128)} %param.11), kind=kLoop, calls=%fused_computation.107 | loop fusion | flops 114688 | bytes 655360 | tf_op jit(solution)/shard_map/reduce_sum | solution.py:132
  2.4 0.7 %fusion.65 = (f32[4,1,64,128]{3,2,1,0:T(8,128)}, f32[4,1,64,128]{3,2,1,0:T(8,128)}) fusion(f32[4,2,64,128]{3,2,1,0:T(8,128)S(1)} %get-tuple-element.3), kind=kLoop, calls=%fused_computation.108 | loop fusion | bytes 524288 | tf_op jit(solution)/shard_map/slice | solution.py:13
  3.1 4.5 %collective-permute-start = (f32[4,1,64,128]{3,2,1,0:T(8,128)}, f32[4,1,64,128]{3,2,1,0:T(8,128)S(1)}, u32[]{:S(2)}, u32[]{:S(2)}) collective-permute-start(f32[4,1,64,128]{3,2,1,0:T(8,128)} %get-tuple-element.6), channel_id=1, source_target_pairs={{0,2},{2,4},{4,6},{6,8},{8,10},{10,12},{12,14},{14,16},{16,18},{18... | collective-permute-start | bytes 393224 | tf_op jit(solution)/shard_map/ppermute | solution.py:21
  7.7 1.9 %collective-permute-start.1 = (f32[4,1,64,128]{3,2,1,0:T(8,128)}, f32[4,1,64,128]{3,2,1,0:T(8,128)}, u32[]{:S(2)}, u32[]{:S(2)}) collective-permute-start(f32[4,1,64,128]{3,2,1,0:T(8,128)} %get-tuple-element.7), channel_id=1, source_target_pairs={{2,0},{4,2},{6,4},{8,6},{10,8},{12,10},{14,12},{16,14},{18,16},{20... | collective-permute-start | bytes 393224 | tf_op jit(solution)/shard_map/ppermute | solution.py:22
  9.6 0.8 %broadcast_in_dim.10 = f32[9]{0:T(128)S(1)} reshape(f32[3,3]{1,0:T(4,128)} %param.13) | data formatting | bytes 72 | tf_op jit(solution)/shard_map/broadcast_in_dim | solution.py:71
  10.4 0.6 %slice_bitcast_fusion.8 = (f32[128]{0:T(128)}, f32[128]{0:T(128)}, f32[128]{0:T(128)}, f32[128]{0:T(128)}, f32[128]{0:T(128)}, /*index=5*/f32[128]{0:T(128)}, f32[128]{0:T(128)}, f32[128]{0:T(128)}, f32[128]{0:T(128)}) fusion(f32[9,128]{1,0:T(8,128)S(1)} %broadcast_in_dim.11), kind=kLoop, calls=%fused_computation.102 | loop fusion | bytes 9216 | tf_op jit(solution)/shard_map/mul | solution.py:129
  11.0 3.2 %collective-permute-done.1 = f32[4,1,64,128]{3,2,1,0:T(8,128)} collective-permute-done((f32[4,1,64,128]{3,2,1,0:T(8,128)}, f32[4,1,64,128]{3,2,1,0:T(8,128)}, u32[]{:S(2)}, u32[]{:S(2)}) %collective-permute-start.1) | collective-permute-done | bytes 131104 | tf_op jit(solution)/shard_map/ppermute | solution.py:22
  14.3 0.7 %broadcast_select_fusion.1 = f32[4,4,1,128]{3,2,1,0:T(1,128)S(1)} fusion(pred[]{:T(512)S(6)} %eq.17, f32[4,1,64,128]{3,2,1,0:T(8,128)} %collective-permute-done.1, f32[4,2,64,128]{3,2,1,0:T(8,128)S(1)} %get-tuple-element.3, f32[4,1,64,128]{3,2,1,0:T(8,128)S(1)} %collective-permute-done), kind=kLoop, calls=%fused_computation.82 | loop fusion | flops 10240 | bytes 532481 | tf_op jit(solution)/shard_map/jit(_where)/select_n | solution.py:16
  15.0 1.3 %collective-permute-start.2 = (f32[4,4,1,128]{3,2,1,0:T(1,128)S(1)}, f32[4,4,1,128]{3,2,1,0:T(1,128)S(1)}, u32[]{:S(2)}, u32[]{:S(2)}) collective-permute-start(f32[4,4,1,128]{3,2,1,0:T(1,128)S(1)} %broadcast_select_fusion.1), channel_id=1, source_target_pairs={{0,1},{1,0},{2,3},{3,2},{4,5},{5,4},{6,7},{7,6},{8,9},{9,8},{10,11... | collective-permute-start | bytes 24584 | tf_op jit(solution)/shard_map/ppermute | solution.py:16
  16.3 1.2 %bitcast_add_fusion.1 = s32[96]{0:T(128)} fusion(s32[96]{0:T(128)} %param.19, s32[96,1]{0,1:T(1,128)} %param.18), kind=kLoop, calls=%fused_computation.103 | loop fusion | flops 192 | bytes 1152 | tf_op jit(solution)/shard_map/add | solution.py:92
  17.6 1.0 %pad_maximum_fusion = f32[4,4,66,128]{3,2,1,0:T(8,128)S(1)} fusion(f32[4,4,1,128]{3,2,1,0:T(1,128)S(1)} %get-tuple-element.22, f32[4,1,64,128]{3,2,1,0:T(8,128)} %collective-permute-done.1, f32[4,2,64,128]{3,2,1,0:T(8,128)S(1)} %get-tuple-element.3, f32[4,1,64,128]{3,2,1,0:T(8,128)S(1)} %collective-permute-done, f32[4,4,1,128]{3,2,1,0:T(1,128)S(1)} %get-tuple-element.21), kind=kLoop, calls=%fused_computation.2 | loop fusion | flops 540672 | bytes 1081344 | tf_op jit(solution)/shard_map/concatenate | solution.py:23
  18.6 2.1 %fusion.67 = (bf16[4,2,64,128]{3,2,1,0:T(8,128)(2,1)S(1)}, f32[4,2,64,128]{3,2,1,0:T(8,128)}) fusion(f32[128]{0:T(128)} %param.15, f32[128,128]{1,0:T(8,128)} %param.14, f32[4,4,66,128]{3,2,1,0:T(8,128)S(1)} %pad_maximum_fusion, f32[128]{0:T(128)} %get-tuple-element.13, f32[128]{0:T(128)} %get-tuple-element.14, f32[128]{0:T(128)} %get-tuple-element.15, ...), kind=kOutput, calls=%fused_computation.110 | convolution fusion | flops 101908480 | bytes 2823168 | tf_op jit(solution)/shard_map/sxyw,zw->sxyz/dot_general | solution.py:82
  20.9 1.7 %fusion.32 = f32[96,4,128]{2,1,0:T(4,128)S(1)} fusion(bf16[96,128,128]{2,1,0:T(8,128)(2,1)S(1)} %copy-done, bf16[96,4,128]{2,0,1:T(8,128)(2,1)S(1)} %fusion.55), kind=kOutput, calls=%fused_computation.42 | convolution fusion | flops 12582912 | bytes 3440640 | tf_op jit(solution)/shard_map/pij,psj->psi/dot_general | solution.py:91
  23.2 1.3 %collective-permute-done.3 = f32[8,8,4,128]{3,1,2,0:T(8,128)S(1)} collective-permute-done((f32[8,8,4,128]{3,1,2,0:T(8,128)S(1)}, f32[8,8,4,128]{3,1,2,0:T(8,128)S(1)}, u32[]{:S(2)}, u32[]{:S(2)}) %collective-permute-start.3) | collective-permute-done | bytes 131104 | tf_op jit(solution)/shard_map/ppermute | solution.py:102
  24.7 11.4 %all_to_all.10 = f32[8,8,4,128]{3,1,2,0:T(8,128)S(1)} all-to-all(f32[8,8,4,128]{3,1,2,0:T(8,128)S(1)} %bitcast_add_fusion), channel_id=1, replica_groups=mesh['vh'=8,'vc'=2,'star'=2] {'vh'}, dimensions={0} | all-to-all | bytes 262144 | tf_op jit(solution)/shard_map/all_to_all | solution.py:103
  36.2 11.1 %all_to_all.11 = bf16[16,8,4,128]{3,2,1,0:T(4,128)(2,1)S(1)} all-to-all(bf16[16,8,4,128]{3,2,1,0:T(4,128)(2,1)S(1)} %broadcast_in_dim.13), channel_id=1, replica_groups=mesh['vh'=8,'vc'=2,'star'=2] {'vh','vc'}, dimensions={0} | all-to-all | bytes 262144 | tf_op jit(solution)/shard_map/all_to_all | solution.py:109
  47.6 0.9 %fusion.33 = f32[96,4,128]{2,1,0:T(4,128)S(1)} fusion(bf16[96,128,128]{2,1,0:T(8,128)(2,1)S(1)} %copy-done, bf16[96,4,128]{2,0,1:T(8,128)(2,1)S(1)} %fusion.21), kind=kOutput, calls=%fused_computation.43 | convolution fusion | flops 12582912 | bytes 3440640 | tf_op jit(solution)/shard_map/pij,psi->psj/dot_general | solution.py:115
  49.2 2.1 %collective-permute-start.4 = (f32[1,64,128]{2,1,0:T(8,128)S(1)}, f32[1,64,128]{2,1,0:T(8,128)S(1)}, u32[]{:S(2)}, u32[]{:S(2)}) collective-permute-start(f32[1,64,128]{2,1,0:T(8,128)S(1)} %get-tuple-element.8), channel_id=1, source_target_pairs={{0,2},{2,4},{4,6},{6,8},{8,10},{10,12},{12,14},{14,16},{16,18},{18... | collective-permute-start | bytes 98312 | tf_op jit(solution)/shard_map/ppermute | solution.py:21
  51.3 2.3 %collective-permute-start.5 = (f32[1,64,128]{2,1,0:T(8,128)S(1)}, f32[1,64,128]{2,1,0:T(8,128)S(1)}, u32[]{:S(2)}, u32[]{:S(2)}) collective-permute-start(f32[1,64,128]{2,1,0:T(8,128)S(1)} %get-tuple-element.9), channel_id=1, source_target_pairs={{2,0},{4,2},{6,4},{8,6},{10,8},{12,10},{14,12},{16,14},{18,16},{20... | collective-permute-start | bytes 98312 | tf_op jit(solution)/shard_map/ppermute | solution.py:22
  53.6 2.9 %collective-permute-done.5 = f32[1,64,128]{2,1,0:T(8,128)S(1)} collective-permute-done((f32[1,64,128]{2,1,0:T(8,128)S(1)}, f32[1,64,128]{2,1,0:T(8,128)S(1)}, u32[]{:S(2)}, u32[]{:S(2)}) %collective-permute-start.5) | collective-permute-done | bytes 32800 | tf_op jit(solution)/shard_map/ppermute | solution.py:22
  56.5 1.2 %collective-permute-start.6 = (f32[4,1,128]{2,1,0:T(1,128)S(1)}, f32[4,1,128]{2,1,0:T(1,128)S(1)}, u32[]{:S(2)}, u32[]{:S(2)}) collective-permute-start(f32[4,1,128]{2,1,0:T(1,128)S(1)} %broadcast_select_fusion.4), channel_id=1, source_target_pairs={{0,1},{1,0},{2,3},{3,2},{4,5},{5,4},{6,7},{7,6},{8,9},{9,8},{10,11... | collective-permute-start | bytes 6152 | tf_op jit(solution)/shard_map/ppermute | solution.py:16
  57.7 0.6 broadcast_multiply_fusion
  58.3 0.6 %collective-permute-done.6 = f32[4,1,128]{2,1,0:T(1,128)S(1)} collective-permute-done((f32[4,1,128]{2,1,0:T(1,128)S(1)}, f32[4,1,128]{2,1,0:T(1,128)S(1)}, u32[]{:S(2)}, u32[]{:S(2)}) %collective-permute-start.6) | collective-permute-done | bytes 2080 | tf_op jit(solution)/shard_map/ppermute | solution.py:16
  59.1 0.7 %fusion.35 = f32[2,64,128]{2,1,0:T(8,128)} fusion(f32[4,66,128]{2,1,0:T(8,128)S(1)} %pad_maximum_fusion.1, f32[2,64,128]{2,1,0:T(8,128)S(1)} %copy-done.1, f32[128]{0:T(128)S(1)} %copy-done.7, f32[128]{0:T(128)S(1)} %copy-done.8, f32[128]{0:T(128)S(1)} %copy-done.9, f32[128]{0:T(128)S(1)} %copy-done.10, f32[128]{0:T(128)S(1)} %copy-done.11, ...), kind=kLoop, calls=%fused_computation.46 | loop fusion | flops 311296 | bytes 725504 | tf_op jit(solution)/shard_map/add | solution.py:132
  (59 shorter events, 2.0 us)
Async XLA Ops:
  0.6 20.3 %copy-start = (bf16[96,128,128]{2,1,0:T(8,128)(2,1)S(1)}, bf16[96,128,128]{2,1,0:T(8,128)(2,1)}, u32[]{:S(2)}) copy-start(bf16[96,128,128]{2,1,0:T(8,128)(2,1)} %param.16) | copy-start | bytes 9437188
  3.1 7.9 %collective-permute-start = (f32[4,1,64,128]{3,2,1,0:T(8,128)}, f32[4,1,64,128]{3,2,1,0:T(8,128)S(1)}, u32[]{:S(2)}, u32[]{:S(2)}) collective-permute-start(f32[4,1,64,128]{3,2,1,0:T(8,128)} %get-tuple-element.6), channel_id=1, source_target_pairs={{0,2},{2,4},{4,6},{6,8},{8,10},{10,12},{12,14},{14,16},{16,18},{18... | collective-permute-start | bytes 393224 | tf_op jit(solution)/shard_map/ppermute | solution.py:21
  7.7 6.6 %collective-permute-start.1 = (f32[4,1,64,128]{3,2,1,0:T(8,128)}, f32[4,1,64,128]{3,2,1,0:T(8,128)}, u32[]{:S(2)}, u32[]{:S(2)}) collective-permute-start(f32[4,1,64,128]{3,2,1,0:T(8,128)} %get-tuple-element.7), channel_id=1, source_target_pairs={{2,0},{4,2},{6,4},{8,6},{10,8},{12,10},{14,12},{16,14},{18,16},{20... | collective-permute-start | bytes 393224 | tf_op jit(solution)/shard_map/ppermute | solution.py:22
  15.0 2.6 %collective-permute-start.2 = (f32[4,4,1,128]{3,2,1,0:T(1,128)S(1)}, f32[4,4,1,128]{3,2,1,0:T(1,128)S(1)}, u32[]{:S(2)}, u32[]{:S(2)}) collective-permute-start(f32[4,4,1,128]{3,2,1,0:T(1,128)S(1)} %broadcast_select_fusion.1), channel_id=1, source_target_pairs={{0,1},{1,0},{2,3},{3,2},{4,5},{5,4},{6,7},{7,6},{8,9},{9,8},{10,11... | collective-permute-start | bytes 24584 | tf_op jit(solution)/shard_map/ppermute | solution.py:16
  18.6 4.1 %copy-start.17 = (s32[96]{0:T(128)S(1)}, s32[96]{0:T(128)}, u32[]{:S(2)}) copy-start(s32[96]{0:T(128)} %bitcast_add_fusion.1) | copy-start | bytes 1156
  20.7 15.4 %copy-start.4 = (f32[8,128]{1,0:T(8,128)S(1)}, f32[8,128]{1,0:T(8,128)}, u32[]{:S(2)}) copy-start(f32[8,128]{1,0:T(8,128)} %param.20) | copy-start | bytes 12292
  20.7 15.4 %copy-start.5 = (f32[8,128]{1,0:T(8,128)S(1)}, f32[8,128]{1,0:T(8,128)}, u32[]{:S(2)}) copy-start(f32[8,128]{1,0:T(8,128)} %param.21) | copy-start | bytes 12292
  22.7 25.8 %copy-start.16 = (s32[96]{0:T(128)S(1)}, s32[96]{0:T(128)}, u32[]{:S(2)}) copy-start(s32[96]{0:T(128)} %param.17) | copy-start | bytes 1156
  23.1 25.8 %copy-start.3 = (f32[128,128]{1,0:T(8,128)S(1)}, f32[128,128]{1,0:T(8,128)}, u32[]{:S(2)}) copy-start(f32[128,128]{1,0:T(8,128)} %param.14) | copy-start | bytes 196612
  23.1 1.4 %collective-permute-start.3 = (f32[8,8,4,128]{3,1,2,0:T(8,128)S(1)}, f32[8,8,4,128]{3,1,2,0:T(8,128)S(1)}, u32[]{:S(2)}, u32[]{:S(2)}) collective-permute-start(f32[8,8,4,128]{3,1,2,0:T(8,128)S(1)} %bitcast.60), channel_id=1, source_target_pairs={{0,2},{2,0},{1,3},{3,1},{4,6},{6,4},{5,7},{7,5},{8,10},{10,8},{9,1... | collective-permute-start | bytes 393224 | tf_op jit(solution)/shard_map/ppermute | solution.py:102
  24.6 34.4 %copy-start.1 = (f32[2,64,128]{2,1,0:T(8,128)S(1)}, f32[2,64,128]{2,1,0:T(8,128)}, u32[]{:S(2)}) copy-start(f32[2,64,128]{2,1,0:T(8,128)} %get-tuple-element.2) | copy-start | bytes 196612
  24.6 34.4 %copy-start.6 = (f32[128]{0:T(128)S(1)}, f32[128]{0:T(128)}, u32[]{:S(2)}) copy-start(f32[128]{0:T(128)} %get-tuple-element.12) | copy-start | bytes 1540
  24.6 34.4 %copy-start.7 = (f32[128]{0:T(128)S(1)}, f32[128]{0:T(128)}, u32[]{:S(2)}) copy-start(f32[128]{0:T(128)} %get-tuple-element.13) | copy-start | bytes 1540
  24.6 34.4 %copy-start.8 = (f32[128]{0:T(128)S(1)}, f32[128]{0:T(128)}, u32[]{:S(2)}) copy-start(f32[128]{0:T(128)} %get-tuple-element.14) | copy-start | bytes 1540
  24.6 34.4 %copy-start.9 = (f32[128]{0:T(128)S(1)}, f32[128]{0:T(128)}, u32[]{:S(2)}) copy-start(f32[128]{0:T(128)} %get-tuple-element.15) | copy-start | bytes 1540
  24.6 34.4 %copy-start.10 = (f32[128]{0:T(128)S(1)}, f32[128]{0:T(128)}, u32[]{:S(2)}) copy-start(f32[128]{0:T(128)} %get-tuple-element.16) | copy-start | bytes 1540
  24.6 34.4 %copy-start.11 = (f32[128]{0:T(128)S(1)}, f32[128]{0:T(128)}, u32[]{:S(2)}) copy-start(f32[128]{0:T(128)} %get-tuple-element.17) | copy-start | bytes 1540
  24.6 34.4 %copy-start.12 = (f32[128]{0:T(128)S(1)}, f32[128]{0:T(128)}, u32[]{:S(2)}) copy-start(f32[128]{0:T(128)} %get-tuple-element.18) | copy-start | bytes 1540
  24.7 34.4 %copy-start.13 = (f32[128]{0:T(128)S(1)}, f32[128]{0:T(128)}, u32[]{:S(2)}) copy-start(f32[128]{0:T(128)} %get-tuple-element.19) | copy-start | bytes 1540
  24.7 34.4 %copy-start.14 = (f32[128]{0:T(128)S(1)}, f32[128]{0:T(128)}, u32[]{:S(2)}) copy-start(f32[128]{0:T(128)} %get-tuple-element.20) | copy-start | bytes 1540
  36.1 12.8 %copy-start.2 = (f32[4,2,64,128]{3,2,1,0:T(8,128)S(1)}, f32[4,2,64,128]{3,2,1,0:T(8,128)}, u32[]{:S(2)}) copy-start(f32[4,2,64,128]{3,2,1,0:T(8,128)} %get-tuple-element.26) | copy-start | bytes 786436
  49.2 4.4 %collective-permute-start.4 = (f32[1,64,128]{2,1,0:T(8,128)S(1)}, f32[1,64,128]{2,1,0:T(8,128)S(1)}, u32[]{:S(2)}, u32[]{:S(2)}) collective-permute-start(f32[1,64,128]{2,1,0:T(8,128)S(1)} %get-tuple-element.8), channel_id=1, source_target_pairs={{0,2},{2,4},{4,6},{6,8},{8,10},{10,12},{12,14},{14,16},{16,18},{18... | collective-permute-start | bytes 98312 | tf_op jit(solution)/shard_map/ppermute | solution.py:21
  51.3 5.2 %collective-permute-start.5 = (f32[1,64,128]{2,1,0:T(8,128)S(1)}, f32[1,64,128]{2,1,0:T(8,128)S(1)}, u32[]{:S(2)}, u32[]{:S(2)}) collective-permute-start(f32[1,64,128]{2,1,0:T(8,128)S(1)} %get-tuple-element.9), channel_id=1, source_target_pairs={{2,0},{4,2},{6,4},{8,6},{10,8},{12,10},{14,12},{16,14},{18,16},{20... | collective-permute-start | bytes 98312 | tf_op jit(solution)/shard_map/ppermute | solution.py:22
  56.5 2.4 %collective-permute-start.6 = (f32[4,1,128]{2,1,0:T(1,128)S(1)}, f32[4,1,128]{2,1,0:T(1,128)S(1)}, u32[]{:S(2)}, u32[]{:S(2)}) collective-permute-start(f32[4,1,128]{2,1,0:T(1,128)S(1)} %broadcast_select_fusion.4), channel_id=1, source_target_pairs={{0,1},{1,0},{2,3},{3,2},{4,5},{5,4},{6,7},{7,6},{8,9},{9,8},{10,11... | collective-permute-start | bytes 6152 | tf_op jit(solution)/shard_map/ppermute | solution.py:16
  (1 other events, 3.2 us)

commit v17 on v16

--- a/solution.py
+++ b/solution.py
@@ -27,7 +27,7 @@
 
 
 def with_halo(cells, dim):
-    return lax.optimization_barrier(exchange(exchange(cells, VOX, dim), "star", dim + 1))
+    return exchange(exchange(cells, VOX, dim), "star", dim + 1)
 
 
 def rows(table, index, axis):

time: 60.3 us -> 60.4 us (level)
  no operation moved by 1% of the time
where the time goes in v17:
time: 60.4 us; the launch traced here: 60 us
  blocking collectives  22.6 us (37%)
  starting transfers between devices  13.4 us (22%)
  waiting for transfers between devices  8.21 us (14%)
  matrix products  6.27 us (10%)
  other arithmetic  6.18 us (10%)
  local copies, waits for them, and re-layouts  2.35 us (4%)
  between operations  1.01 us (2%)
    all_to_all x1, blocking collectives, per_device(): lax.all_to_all(merged, 'vh', split_axis=0, concat_axis=0, tiled=True)  11.4 us
    all_to_all x1, blocking collectives, per_device(): lax.all_to_all(spread, VOX, split_axis=0, concat_axis=0, tiled=True)  11.1 us
    ppermute x2, starting transfers between devices, exchange(): below = lax.ppermute(tail, axis, [(i, i + 1) for i in range(count - 1)])  6.59 us
    ppermute x2, waiting for transfers between devices, exchange(): above = lax.ppermute(head, axis, [(i + 1, i) for i in range(count - 1)])  6.13 us
    ppermute x2, starting transfers between devices, exchange(): above = lax.ppermute(head, axis, [(i + 1, i) for i in range(count - 1)])  4.22 us
    ppermute x2, starting transfers between devices, exchange(): lax.ppermute(jnp.where(index == 0, tail, head), axis, [(0, 1), (1, 0)])  2.49 us
    dot_general x1, matrix products, per_device(): jnp.einsum('sxyw,zw->sxyz', smoothed, vertical_mix, precision=HIGH)  2.21 us
    reduce_sum x1, other arithmetic, per_device(): gradient = grad_latent + jnp.mean(latent, axis=0)  1.76 us
  transfers between devices with their start and end apart: 7, of which 5 were waited for; matrix products, arithmetic and copies ran while one was open for 5% of the time, Pallas kernels for 0%

profile of v17, /device:TPU:1, one launch (start us, length us, event | category | flops | bytes accessed | tf_op | source)
XLA Modules:
  0.0 60.0 jit_solution(8528349513318074152)
XLA Ops:
  0.6 1.8 %fusion.71 = (f32[2,64,128]{2,1,0:T(8,128)}, f32[4,2,64,128]{3,2,1,0:T(8,128)S(1)}) fusion(f32[4,2,64,128]{3,2,1,0:T(8,128)} %param.12, f32[2,64,128]{2,1,0:T(8,128)} %param.11), kind=kLoop, calls=%fused_computation.115 | loop fusion | flops 114688 | bytes 655360 | tf_op jit(solution)/shard_map/reduce_sum | solution.py:132
  2.4 0.7 %fusion.72 = (f32[4,1,64,128]{3,2,1,0:T(8,128)}, f32[4,1,64,128]{3,2,1,0:T(8,128)}) fusion(f32[4,2,64,128]{3,2,1,0:T(8,128)S(1)} %get-tuple-element.3), kind=kLoop, calls=%fused_computation.116 | loop fusion | bytes 524288 | tf_op jit(solution)/shard_map/slice | solution.py:13
  3.1 4.5 %collective-permute-start = (f32[4,1,64,128]{3,2,1,0:T(8,128)}, f32[4,1,64,128]{3,2,1,0:T(8,128)S(1)}, u32[]{:S(2)}, u32[]{:S(2)}) collective-permute-start(f32[4,1,64,128]{3,2,1,0:T(8,128)} %get-tuple-element.8), channel_id=1, source_target_pairs={{0,2},{2,4},{4,6},{6,8},{8,10},{10,12},{12,14},{14,16},{16,18},{18... | collective-permute-start | bytes 393224 | tf_op jit(solution)/shard_map/ppermute | solution.py:21
  7.7 1.9 %collective-permute-start.1 = (f32[4,1,64,128]{3,2,1,0:T(8,128)}, f32[4,1,64,128]{3,2,1,0:T(8,128)}, u32[]{:S(2)}, u32[]{:S(2)}) collective-permute-start(f32[4,1,64,128]{3,2,1,0:T(8,128)} %get-tuple-element.9), channel_id=1, source_target_pairs={{2,0},{4,2},{6,4},{8,6},{10,8},{12,10},{14,12},{16,14},{18,16},{20... | collective-permute-start | bytes 393224 | tf_op jit(solution)/shard_map/ppermute | solution.py:22
  9.6 0.8 %broadcast_in_dim.10 = f32[9]{0:T(128)S(1)} reshape(f32[3,3]{1,0:T(4,128)} %param.13) | data formatting | bytes 72 | tf_op jit(solution)/shard_map/broadcast_in_dim | solution.py:71
  10.4 0.6 %slice_bitcast_fusion.8 = (f32[128]{0:T(128)}, f32[128]{0:T(128)}, f32[128]{0:T(128)}, f32[128]{0:T(128)}, f32[128]{0:T(128)}, /*index=5*/f32[128]{0:T(128)}, f32[128]{0:T(128)}, f32[128]{0:T(128)}, f32[128]{0:T(128)}) fusion(f32[9,128]{1,0:T(8,128)S(1)} %broadcast_in_dim.11), kind=kLoop, calls=%fused_computation.109 | loop fusion | bytes 9216 | tf_op jit(solution)/shard_map/mul | solution.py:129
  11.1 3.2 %collective-permute-done.1 = f32[4,1,64,128]{3,2,1,0:T(8,128)} collective-permute-done((f32[4,1,64,128]{3,2,1,0:T(8,128)}, f32[4,1,64,128]{3,2,1,0:T(8,128)}, u32[]{:S(2)}, u32[]{:S(2)}) %collective-permute-start.1) | collective-permute-done | bytes 131104 | tf_op jit(solution)/shard_map/ppermute | solution.py:22
  14.3 0.7 %broadcast_select_fusion.1 = f32[4,4,1,128]{3,2,1,0:T(1,128)S(1)} fusion(pred[]{:T(512)S(6)} %eq.17, f32[4,1,64,128]{3,2,1,0:T(8,128)} %collective-permute-done.1, f32[4,2,64,128]{3,2,1,0:T(8,128)S(1)} %get-tuple-element.3, f32[4,1,64,128]{3,2,1,0:T(8,128)S(1)} %collective-permute-done), kind=kLoop, calls=%fused_computation.89 | loop fusion | flops 10240 | bytes 532481 | tf_op jit(solution)/shard_map/jit(_where)/select_n | solution.py:16
  15.0 1.3 %collective-permute-start.2 = (f32[4,4,1,128]{3,2,1,0:T(1,128)S(1)}, f32[4,4,1,128]{3,2,1,0:T(1,128)S(1)}, u32[]{:S(2)}, u32[]{:S(2)}) collective-permute-start(f32[4,4,1,128]{3,2,1,0:T(1,128)S(1)} %broadcast_select_fusion.1), channel_id=1, source_target_pairs={{0,1},{1,0},{2,3},{3,2},{4,5},{5,4},{6,7},{7,6},{8,9},{9,8},{10,11... | collective-permute-start | bytes 24584 | tf_op jit(solution)/shard_map/ppermute | solution.py:16
  16.3 1.2 %bitcast_add_fusion.1 = s32[96]{0:T(128)} fusion(s32[96]{0:T(128)} %param.19, s32[96,1]{0,1:T(1,128)} %param.18), kind=kLoop, calls=%fused_computation.110 | loop fusion | flops 192 | bytes 1152 | tf_op jit(solution)/shard_map/add | solution.py:92
  17.6 1.1 %maximum_maximum_fusion = (f32[4,4,65,128]{3,2,1,0:T(8,128)S(1)}, f32[4,4,65,128]{3,2,1,0:T(8,128)S(1)}) fusion(f32[4,1,64,128]{3,2,1,0:T(8,128)} %collective-permute-done.1, f32[4,2,64,128]{3,2,1,0:T(8,128)S(1)} %get-tuple-element.3, f32[4,1,64,128]{3,2,1,0:T(8,128)S(1)} %collective-permute-done, f32[4,4,1,128]{3,2,1,0:T(1,128)S(1)} %get-tuple-element.25, ...), kind=kLoop, calls=%fused_computation.2 | loop fusion | flops 798720 | bytes 1605632 | tf_op jit(solution)/shard_map/concatenate | solution.py:23
  18.7 2.2 %fusion.74 = (bf16[4,2,64,128]{3,2,1,0:T(8,128)(2,1)S(1)}, f32[4,2,64,128]{3,2,1,0:T(8,128)}) fusion(f32[128]{0:T(128)} %param.15, f32[128,128]{1,0:T(8,128)} %param.14, f32[4,4,65,128]{3,2,1,0:T(8,128)S(1)} %get-tuple-element.5, f32[4,1,64,128]{3,2,1,0:T(8,128)} %collective-permute-done.1, f32[4,2,64,128]{3,2,1,0:T(8,128)S(1)} %get-tuple-element.3, ...), kind=kOutput, calls=%fused_computation.118 | convolution fusion | flops 102039552 | bytes 2561024 | tf_op jit(solution)/shard_map/sxyw,zw->sxyz/dot_general | solution.py:82
  21.2 1.7 %fusion.36 = f32[96,4,128]{2,1,0:T(4,128)S(1)} fusion(bf16[96,128,128]{2,1,0:T(8,128)(2,1)S(1)} %copy-done, bf16[96,4,128]{2,0,1:T(8,128)(2,1)S(1)} %fusion.61), kind=kOutput, calls=%fused_computation.48 | convolution fusion | flops 12582912 | bytes 3440640 | tf_op jit(solution)/shard_map/pij,psj->psi/dot_general | solution.py:91
  23.4 1.3 %collective-permute-done.3 = f32[8,8,4,128]{3,1,2,0:T(8,128)S(1)} collective-permute-done((f32[8,8,4,128]{3,1,2,0:T(8,128)S(1)}, f32[8,8,4,128]{3,1,2,0:T(8,128)S(1)}, u32[]{:S(2)}, u32[]{:S(2)}) %collective-permute-start.3) | collective-permute-done | bytes 131104 | tf_op jit(solution)/shard_map/ppermute | solution.py:102
  24.8 11.4 %all_to_all.10 = f32[8,8,4,128]{3,1,2,0:T(8,128)S(1)} all-to-all(f32[8,8,4,128]{3,1,2,0:T(8,128)S(1)} %bitcast_add_fusion), channel_id=1, replica_groups=mesh['vh'=8,'vc'=2,'star'=2] {'vh'}, dimensions={0} | all-to-all | bytes 262144 | tf_op jit(solution)/shard_map/all_to_all | solution.py:103
  36.4 11.1 %all_to_all.11 = bf16[16,8,4,128]{3,2,1,0:T(4,128)(2,1)S(1)} all-to-all(bf16[16,8,4,128]{3,2,1,0:T(4,128)(2,1)S(1)} %broadcast_in_dim.13), channel_id=1, replica_groups=mesh['vh'=8,'vc'=2,'star'=2] {'vh','vc'}, dimensions={0} | all-to-all | bytes 262144 | tf_op jit(solution)/shard_map/all_to_all | solution.py:109
  47.8 0.9 %fusion.37 = f32[96,4,128]{2,1,0:T(4,128)S(1)} fusion(bf16[96,128,128]{2,1,0:T(8,128)(2,1)S(1)} %copy-done, bf16[96,4,128]{2,0,1:T(8,128)(2,1)S(1)} %fusion.25), kind=kOutput, calls=%fused_computation.49 | convolution fusion | flops 12582912 | bytes 3440640 | tf_op jit(solution)/shard_map/pij,psi->psj/dot_general | solution.py:115
  49.4 2.1 %collective-permute-start.4 = (f32[1,64,128]{2,1,0:T(8,128)S(1)}, f32[1,64,128]{2,1,0:T(8,128)S(1)}, u32[]{:S(2)}, u32[]{:S(2)}) collective-permute-start(f32[1,64,128]{2,1,0:T(8,128)S(1)} %get-tuple-element.12), channel_id=1, source_target_pairs={{0,2},{2,4},{4,6},{6,8},{8,10},{10,12},{12,14},{14,16},{16,18},{18... | collective-permute-start | bytes 98312 | tf_op jit(solution)/shard_map/ppermute | solution.py:21
  51.4 2.3 %collective-permute-start.5 = (f32[1,64,128]{2,1,0:T(8,128)S(1)}, f32[1,64,128]{2,1,0:T(8,128)S(1)}, u32[]{:S(2)}, u32[]{:S(2)}) collective-permute-start(f32[1,64,128]{2,1,0:T(8,128)S(1)} %get-tuple-element.13), channel_id=1, source_target_pairs={{2,0},{4,2},{6,4},{8,6},{10,8},{12,10},{14,12},{16,14},{18,16},{20... | collective-permute-start | bytes 98312 | tf_op jit(solution)/shard_map/ppermute | solution.py:22
  53.8 2.9 %collective-permute-done.5 = f32[1,64,128]{2,1,0:T(8,128)S(1)} collective-permute-done((f32[1,64,128]{2,1,0:T(8,128)S(1)}, f32[1,64,128]{2,1,0:T(8,128)S(1)}, u32[]{:S(2)}, u32[]{:S(2)}) %collective-permute-start.5) | collective-permute-done | bytes 32800 | tf_op jit(solution)/shard_map/ppermute | solution.py:22
  56.7 1.2 %collective-permute-start.6 = (f32[4,1,128]{2,1,0:T(1,128)S(1)}, f32[4,1,128]{2,1,0:T(1,128)S(1)}, u32[]{:S(2)}, u32[]{:S(2)}) collective-permute-start(f32[4,1,128]{2,1,0:T(1,128)S(1)} %broadcast_select_fusion.5), channel_id=1, source_target_pairs={{0,1},{1,0},{2,3},{3,2},{4,5},{5,4},{6,7},{7,6},{8,9},{9,8},{10,11... | collective-permute-start | bytes 6152 | tf_op jit(solution)/shard_map/ppermute | solution.py:16
  57.9 0.6 broadcast_multiply_fusion
  58.5 0.6 %collective-permute-done.6 = f32[4,1,128]{2,1,0:T(1,128)S(1)} collective-permute-done((f32[4,1,128]{2,1,0:T(1,128)S(1)}, f32[4,1,128]{2,1,0:T(1,128)S(1)}, u32[]{:S(2)}, u32[]{:S(2)}) %collective-permute-start.6) | collective-permute-done | bytes 2080 | tf_op jit(solution)/shard_map/ppermute | solution.py:16
  59.3 0.7 %fusion.39 = f32[2,64,128]{2,1,0:T(8,128)} fusion(f32[4,65,128]{2,1,0:T(8,128)S(1)} %get-tuple-element.11, f32[2,64,128]{2,1,0:T(8,128)S(1)} %fusion.50, f32[1,64,128]{2,1,0:T(8,128)S(1)} %collective-permute-done.4, f32[4,65,128]{2,1,0:T(8,128)S(1)} %get-tuple-element.10, f32[1,64,128]{2,1,0:T(8,128)S(1)} %collective-permute-done.5, ...), kind=kLoop, calls=%fused_computation.52 | loop fusion | flops 344064 | bytes 659968 | tf_op jit(solution)/shard_map/add | solution.py:132
  (59 shorter events, 2.0 us)
Async XLA Ops:
  0.6 20.5 %copy-start = (bf16[96,128,128]{2,1,0:T(8,128)(2,1)S(1)}, bf16[96,128,128]{2,1,0:T(8,128)(2,1)}, u32[]{:S(2)}) copy-start(bf16[96,128,128]{2,1,0:T(8,128)(2,1)} %param.16) | copy-start | bytes 9437188
  3.1 7.9 %collective-permute-start = (f32[4,1,64,128]{3,2,1,0:T(8,128)}, f32[4,1,64,128]{3,2,1,0:T(8,128)S(1)}, u32[]{:S(2)}, u32[]{:S(2)}) collective-permute-start(f32[4,1,64,128]{3,2,1,0:T(8,128)} %get-tuple-element.8), channel_id=1, source_target_pairs={{0,2},{2,4},{4,6},{6,8},{8,10},{10,12},{12,14},{14,16},{16,18},{18... | collective-permute-start | bytes 393224 | tf_op jit(solution)/shard_map/ppermute | solution.py:21
  7.7 6.6 %collective-permute-start.1 = (f32[4,1,64,128]{3,2,1,0:T(8,128)}, f32[4,1,64,128]{3,2,1,0:T(8,128)}, u32[]{:S(2)}, u32[]{:S(2)}) collective-permute-start(f32[4,1,64,128]{3,2,1,0:T(8,128)} %get-tuple-element.9), channel_id=1, source_target_pairs={{2,0},{4,2},{6,4},{8,6},{10,8},{12,10},{14,12},{16,14},{18,16},{20... | collective-permute-start | bytes 393224 | tf_op jit(solution)/shard_map/ppermute | solution.py:22
  15.0 2.6 %collective-permute-start.2 = (f32[4,4,1,128]{3,2,1,0:T(1,128)S(1)}, f32[4,4,1,128]{3,2,1,0:T(1,128)S(1)}, u32[]{:S(2)}, u32[]{:S(2)}) collective-permute-start(f32[4,4,1,128]{3,2,1,0:T(1,128)S(1)} %broadcast_select_fusion.1), channel_id=1, source_target_pairs={{0,1},{1,0},{2,3},{3,2},{4,5},{5,4},{6,7},{7,6},{8,9},{9,8},{10,11... | collective-permute-start | bytes 24584 | tf_op jit(solution)/shard_map/ppermute | solution.py:16
  18.7 4.2 %copy-start.8 = (s32[96]{0:T(128)S(1)}, s32[96]{0:T(128)}, u32[]{:S(2)}) copy-start(s32[96]{0:T(128)} %bitcast_add_fusion.1) | copy-start | bytes 1156
  20.9 15.4 %copy-start.4 = (f32[8,128]{1,0:T(8,128)S(1)}, f32[8,128]{1,0:T(8,128)}, u32[]{:S(2)}) copy-start(f32[8,128]{1,0:T(8,128)} %param.20) | copy-start | bytes 12292
  20.9 15.4 %copy-start.5 = (f32[8,128]{1,0:T(8,128)S(1)}, f32[8,128]{1,0:T(8,128)}, u32[]{:S(2)}) copy-start(f32[8,128]{1,0:T(8,128)} %param.21) | copy-start | bytes 12292
  22.9 25.8 %copy-start.7 = (s32[96]{0:T(128)S(1)}, s32[96]{0:T(128)}, u32[]{:S(2)}) copy-start(s32[96]{0:T(128)} %param.17) | copy-start | bytes 1156
  23.3 25.8 %copy-start.3 = (f32[128,128]{1,0:T(8,128)S(1)}, f32[128,128]{1,0:T(8,128)}, u32[]{:S(2)}) copy-start(f32[128,128]{1,0:T(8,128)} %param.14) | copy-start | bytes 196612
  23.4 1.4 %collective-permute-start.3 = (f32[8,8,4,128]{3,1,2,0:T(8,128)S(1)}, f32[8,8,4,128]{3,1,2,0:T(8,128)S(1)}, u32[]{:S(2)}, u32[]{:S(2)}) collective-permute-start(f32[8,8,4,128]{3,1,2,0:T(8,128)S(1)} %bitcast.60), channel_id=1, source_target_pairs={{0,2},{2,0},{1,3},{3,1},{4,6},{6,4},{5,7},{7,5},{8,10},{10,8},{9,1... | collective-permute-start | bytes 393224 | tf_op jit(solution)/shard_map/ppermute | solution.py:102
  36.2 22.9 %copy-start.1 = (f32[2,64,128]{2,1,0:T(8,128)S(1)}, f32[2,64,128]{2,1,0:T(8,128)}, u32[]{:S(2)}) copy-start(f32[2,64,128]{2,1,0:T(8,128)} %get-tuple-element.2) | copy-start | bytes 196612
  36.2 22.9 %copy-start.9 = (f32[128]{0:T(128)S(1)}, f32[128]{0:T(128)}, u32[]{:S(2)}) copy-start(f32[128]{0:T(128)} %get-tuple-element.16) | copy-start | bytes 1540
  36.2 23.0 %copy-start.10 = (f32[128]{0:T(128)S(1)}, f32[128]{0:T(128)}, u32[]{:S(2)}) copy-start(f32[128]{0:T(128)} %get-tuple-element.17) | copy-start | bytes 1540
  36.2 23.0 %copy-start.11 = (f32[128]{0:T(128)S(1)}, f32[128]{0:T(128)}, u32[]{:S(2)}) copy-start(f32[128]{0:T(128)} %get-tuple-element.18) | copy-start | bytes 1540
  36.2 23.0 %copy-start.12 = (f32[128]{0:T(128)S(1)}, f32[128]{0:T(128)}, u32[]{:S(2)}) copy-start(f32[128]{0:T(128)} %get-tuple-element.19) | copy-start | bytes 1540
  36.2 23.0 %copy-start.13 = (f32[128]{0:T(128)S(1)}, f32[128]{0:T(128)}, u32[]{:S(2)}) copy-start(f32[128]{0:T(128)} %get-tuple-element.20) | copy-start | bytes 1540
  36.3 23.0 %copy-start.14 = (f32[128]{0:T(128)S(1)}, f32[128]{0:T(128)}, u32[]{:S(2)}) copy-start(f32[128]{0:T(128)} %get-tuple-element.21) | copy-start | bytes 1540
  36.3 23.0 %copy-start.15 = (f32[128]{0:T(128)S(1)}, f32[128]{0:T(128)}, u32[]{:S(2)}) copy-start(f32[128]{0:T(128)} %get-tuple-element.22) | copy-start | bytes 1540
  36.3 23.0 %copy-start.16 = (f32[128]{0:T(128)S(1)}, f32[128]{0:T(128)}, u32[]{:S(2)}) copy-start(f32[128]{0:T(128)} %get-tuple-element.23) | copy-start | bytes 1540
  36.3 23.0 %copy-start.17 = (f32[128]{0:T(128)S(1)}, f32[128]{0:T(128)}, u32[]{:S(2)}) copy-start(f32[128]{0:T(128)} %get-tuple-element.24) | copy-start | bytes 1540
  36.3 12.8 %copy-start.2 = (f32[4,2,64,128]{3,2,1,0:T(8,128)S(1)}, f32[4,2,64,128]{3,2,1,0:T(8,128)}, u32[]{:S(2)}) copy-start(f32[4,2,64,128]{3,2,1,0:T(8,128)} %get-tuple-element.30) | copy-start | bytes 786436
  49.4 4.4 %collective-permute-start.4 = (f32[1,64,128]{2,1,0:T(8,128)S(1)}, f32[1,64,128]{2,1,0:T(8,128)S(1)}, u32[]{:S(2)}, u32[]{:S(2)}) collective-permute-start(f32[1,64,128]{2,1,0:T(8,128)S(1)} %get-tuple-element.12), channel_id=1, source_target_pairs={{0,2},{2,4},{4,6},{6,8},{8,10},{10,12},{12,14},{14,16},{16,18},{18... | collective-permute-start | bytes 98312 | tf_op jit(solution)/shard_map/ppermute | solution.py:21
  51.4 5.2 %collective-permute-start.5 = (f32[1,64,128]{2,1,0:T(8,128)S(1)}, f32[1,64,128]{2,1,0:T(8,128)S(1)}, u32[]{:S(2)}, u32[]{:S(2)}) collective-permute-start(f32[1,64,128]{2,1,0:T(8,128)S(1)} %get-tuple-element.13), channel_id=1, source_target_pairs={{2,0},{4,2},{6,4},{8,6},{10,8},{12,10},{14,12},{16,14},{18,16},{20... | collective-permute-start | bytes 98312 | tf_op jit(solution)/shard_map/ppermute | solution.py:22
  56.7 2.4 %collective-permute-start.6 = (f32[4,1,128]{2,1,0:T(1,128)S(1)}, f32[4,1,128]{2,1,0:T(1,128)S(1)}, u32[]{:S(2)}, u32[]{:S(2)}) collective-permute-start(f32[4,1,128]{2,1,0:T(1,128)S(1)} %broadcast_select_fusion.5), channel_id=1, source_target_pairs={{0,1},{1,0},{2,3},{3,2},{4,5},{5,4},{6,7},{7,6},{8,9},{9,8},{10,11... | collective-permute-start | bytes 6152 | tf_op jit(solution)/shard_map/ppermute | solution.py:16
  (1 other events, 3.4 us)

commit v18 on v17

--- a/solution.py
+++ b/solution.py
@@ -6,11 +6,14 @@
 HIGH = lax.Precision.HIGHEST
 
 
-def exchange(cells, axis, dim):
+def exchange(cells, axis, dim, ends=None):
     count = lax.psum(1, axis)
     size = cells.shape[dim]
-    head = lax.slice_in_dim(cells, 0, 1, axis=dim)
-    tail = lax.slice_in_dim(cells, size - 1, size, axis=dim)
+    if ends is None:
+        head = lax.slice_in_dim(cells, 0, 1, axis=dim)
+        tail = lax.slice_in_dim(cells, size - 1, size, axis=dim)
+    else:
+        head, tail = ends
     if count == 2:
         index = lax.axis_index(axis)
         incoming = lax.ppermute(jnp.where(index == 0, tail, head), axis, [(0, 1), (1, 0)])
@@ -26,8 +29,8 @@
 VOX = ("vh", "vc")
 
 
-def with_halo(cells, dim):
-    return exchange(exchange(cells, VOX, dim), "star", dim + 1)
+def with_halo(cells, dim, ends=None):
+    return lax.optimization_barrier(exchange(exchange(cells, VOX, dim, ends), "star", dim + 1))
 
 
 def rows(table, index, axis):
@@ -70,7 +73,8 @@
     weights = lax.optimization_barrier(
         jnp.broadcast_to(stencil.reshape(9, 1), (9, length))
     )
-    padded = with_halo(latent, 1)
+    ends = [mean_field[None, at : at + 1] + deviations[:, at : at + 1] for at in (0, width_x - 1)]
+    padded = with_halo(latent, 1, ends)
     smoothed = jnp.zeros(latent.shape, jnp.float32)
     for offset_x in range(3):
         for offset_y in range(3):

time: 60.4 us -> 60.4 us (level)
  waiting for transfers between devices: 8.21 us -> 6.59 us
  other arithmetic: 6.18 us -> 7.64 us
    add x0 -> x1, other arithmetic: none -> 1.72 us  [per_device(): mean_field[None, at:at + 1] + deviations[:, at:at + 1]]
    ppermute x2, waiting for transfers between devices: 6.13 us -> 4.53 us  [exchange(): above = lax.ppermute(head, axis, [(i + 1, i) for i in range(count - 1)])]
    add x0 -> x1, local copies, waits for them, and re-layouts: none -> 0.93 us  [per_device(): mean_field[None, at:at + 1] + deviations[:, at:at + 1]]
    slice x2 -> x1, local copies, waits for them, and re-layouts: 0.74 us -> 0.01 us  [exchange(): tail = lax.slice_in_dim(cells, size - 1, size, axis=dim)]
  transfers between devices with their start and end apart: 7 -> 7, of which waited for: 5 -> 5; matrix products, arithmetic and copies ran while one was open for 5% -> 8% of each run, Pallas kernels for 0% -> 0%
where the time goes in v18:
time: 60.4 us; the launch traced here: 59.9 us
  blocking collectives  22.6 us (37%)
  starting transfers between devices  13.4 us (22%)
  other arithmetic  7.64 us (13%)
  waiting for transfers between devices  6.59 us (11%)
  matrix products  6.2 us (10%)
  local copies, waits for them, and re-layouts  2.54 us (4%)
  between operations  1.04 us (2%)
    all_to_all x1, blocking collectives, per_device(): lax.all_to_all(merged, 'vh', split_axis=0, concat_axis=0, tiled=True)  11.4 us
    all_to_all x1, blocking collectives, per_device(): lax.all_to_all(spread, VOX, split_axis=0, concat_axis=0, tiled=True)  11.1 us
    ppermute x2, starting transfers between devices, exchange(): below = lax.ppermute(tail, axis, [(i, i + 1) for i in range(count - 1)])  6.59 us
    ppermute x2, waiting for transfers between devices, exchange(): above = lax.ppermute(head, axis, [(i + 1, i) for i in range(count - 1)])  4.53 us
    ppermute x2, starting transfers between devices, exchange(): above = lax.ppermute(head, axis, [(i + 1, i) for i in range(count - 1)])  4.22 us
    ppermute x2, starting transfers between devices, exchange(): lax.ppermute(jnp.where(index == 0, tail, head), axis, [(0, 1), (1, 0)])  2.49 us
    dot_general x1, matrix products, per_device(): jnp.einsum('sxyw,zw->sxyz', smoothed, vertical_mix, precision=HIGH)  2.13 us
    add x1, other arithmetic, per_device(): mean_field[None, at:at + 1] + deviations[:, at:at + 1]  1.72 us
  transfers between devices with their start and end apart: 7, of which 5 were waited for; matrix products, arithmetic and copies ran while one was open for 8% of the time, Pallas kernels for 0%

profile of v18, /device:TPU:1, one launch (start us, length us, event | category | flops | bytes accessed | tf_op | source)
XLA Modules:
  0.0 59.9 jit_solution(8456168644475895873)
XLA Ops:
  0.6 0.9 %slice_bitcast_fusion.1 = (f32[64,128]{1,0:T(8,128)S(1)}, f32[64,128]{1,0:T(8,128)S(1)}) fusion(f32[2,64,128]{2,1,0:T(8,128)} %param.11), kind=kLoop, calls=%fused_computation.76 | loop fusion | bytes 131072 | tf_op jit(solution)/shard_map/add | solution.py:76
  1.6 1.7 %slice_add_fusion.1 = (f32[4,1,64,128]{3,2,1,0:T(8,128)}, f32[4,1,64,128]{3,2,1,0:T(8,128)}) fusion(f32[4,2,64,128]{3,2,1,0:T(8,128)} %param.12, f32[64,128]{1,0:T(8,128)S(1)} %get-tuple-element.10, f32[64,128]{1,0:T(8,128)S(1)} %get-tuple-element.11), kind=kLoop, calls=%fused_computation.42 | loop fusion | flops 65536 | bytes 589824 | tf_op jit(solution)/shard_map/add | solution.py:76
  3.3 4.5 %collective-permute-start = (f32[4,1,64,128]{3,2,1,0:T(8,128)}, f32[4,1,64,128]{3,2,1,0:T(8,128)S(1)}, u32[]{:S(2)}, u32[]{:S(2)}) collective-permute-start(f32[4,1,64,128]{3,2,1,0:T(8,128)} %get-tuple-element.6), channel_id=1, source_target_pairs={{0,2},{2,4},{4,6},{6,8},{8,10},{10,12},{12,14},{14,16},{16,18},{18... | collective-permute-start | bytes 393224 | tf_op jit(solution)/shard_map/ppermute | solution.py:24
  7.8 1.9 %collective-permute-start.1 = (f32[4,1,64,128]{3,2,1,0:T(8,128)}, f32[4,1,64,128]{3,2,1,0:T(8,128)}, u32[]{:S(2)}, u32[]{:S(2)}) collective-permute-start(f32[4,1,64,128]{3,2,1,0:T(8,128)} %get-tuple-element.7), channel_id=1, source_target_pairs={{2,0},{4,2},{6,4},{8,6},{10,8},{12,10},{14,12},{16,14},{18,16},{20... | collective-permute-start | bytes 393224 | tf_op jit(solution)/shard_map/ppermute | solution.py:25
  9.8 1.6 %fusion.64 = (f32[2,64,128]{2,1,0:T(8,128)}, f32[4,2,64,128]{3,2,1,0:T(8,128)S(1)}) fusion(f32[4,2,64,128]{3,2,1,0:T(8,128)} %param.12, f32[2,64,128]{2,1,0:T(8,128)} %param.11), kind=kLoop, calls=%fused_computation.111 | loop fusion | flops 114688 | bytes 655360 | tf_op jit(solution)/shard_map/reduce_sum | solution.py:136
  11.4 0.8 %broadcast_in_dim.10 = f32[9]{0:T(128)S(1)} reshape(f32[3,3]{1,0:T(4,128)} %param.13) | data formatting | bytes 72 | tf_op jit(solution)/shard_map/broadcast_in_dim | solution.py:74
  12.2 0.6 %slice_bitcast_fusion.10 = (f32[128]{0:T(128)}, f32[128]{0:T(128)}, f32[128]{0:T(128)}, f32[128]{0:T(128)}, f32[128]{0:T(128)}, /*index=5*/f32[128]{0:T(128)}, f32[128]{0:T(128)}, f32[128]{0:T(128)}, f32[128]{0:T(128)}) fusion(f32[9,128]{1,0:T(8,128)S(1)} %broadcast_in_dim.11), kind=kLoop, calls=%fused_computation.106 | loop fusion | bytes 9216 | tf_op jit(solution)/shard_map/mul | solution.py:133
  12.8 1.6 %collective-permute-done.1 = f32[4,1,64,128]{3,2,1,0:T(8,128)} collective-permute-done((f32[4,1,64,128]{3,2,1,0:T(8,128)}, f32[4,1,64,128]{3,2,1,0:T(8,128)}, u32[]{:S(2)}, u32[]{:S(2)}) %collective-permute-start.1) | collective-permute-done | bytes 131104 | tf_op jit(solution)/shard_map/ppermute | solution.py:25
  14.4 0.7 %broadcast_select_fusion.1 = f32[4,4,1,128]{3,2,1,0:T(1,128)S(1)} fusion(pred[]{:T(512)S(6)} %eq.17, f32[4,1,64,128]{3,2,1,0:T(8,128)} %collective-permute-done.1, f32[4,2,64,128]{3,2,1,0:T(8,128)S(1)} %get-tuple-element.3, f32[4,1,64,128]{3,2,1,0:T(8,128)S(1)} %collective-permute-done), kind=kLoop, calls=%fused_computation.86 | loop fusion | flops 10240 | bytes 532481 | tf_op jit(solution)/shard_map/jit(_where)/select_n | solution.py:19
  15.2 1.3 %collective-permute-start.2 = (f32[4,4,1,128]{3,2,1,0:T(1,128)S(1)}, f32[4,4,1,128]{3,2,1,0:T(1,128)S(1)}, u32[]{:S(2)}, u32[]{:S(2)}) collective-permute-start(f32[4,4,1,128]{3,2,1,0:T(1,128)S(1)} %broadcast_select_fusion.1), channel_id=1, source_target_pairs={{0,1},{1,0},{2,3},{3,2},{4,5},{5,4},{6,7},{7,6},{8,9},{9,8},{10,11... | collective-permute-start | bytes 24584 | tf_op jit(solution)/shard_map/ppermute | solution.py:19
  16.5 1.2 %bitcast_add_fusion.1 = s32[96]{0:T(128)} fusion(s32[96]{0:T(128)} %param.19, s32[96,1]{0,1:T(1,128)} %param.18), kind=kLoop, calls=%fused_computation.107 | loop fusion | flops 192 | bytes 1152 | tf_op jit(solution)/shard_map/add | solution.py:96
  17.8 1.0 %pad_maximum_fusion = f32[4,4,66,128]{3,2,1,0:T(8,128)S(1)} fusion(f32[4,4,1,128]{3,2,1,0:T(1,128)S(1)} %get-tuple-element.24, f32[4,1,64,128]{3,2,1,0:T(8,128)} %collective-permute-done.1, f32[4,2,64,128]{3,2,1,0:T(8,128)S(1)} %get-tuple-element.3, f32[4,1,64,128]{3,2,1,0:T(8,128)S(1)} %collective-permute-done, f32[4,4,1,128]{3,2,1,0:T(1,128)S(1)} %get-tuple-element.23), kind=kLoop, calls=%fused_computation.2 | loop fusion | flops 540672 | bytes 1081344 | tf_op jit(solution)/shard_map/concatenate | solution.py:26
  18.8 2.1 %fusion.66 = (bf16[4,2,64,128]{3,2,1,0:T(8,128)(2,1)S(1)}, f32[4,2,64,128]{3,2,1,0:T(8,128)}) fusion(f32[128]{0:T(128)} %param.15, f32[128,128]{1,0:T(8,128)} %param.14, f32[4,4,66,128]{3,2,1,0:T(8,128)S(1)} %pad_maximum_fusion, f32[128]{0:T(128)} %get-tuple-element.15, f32[128]{0:T(128)} %get-tuple-element.16, f32[128]{0:T(128)} %get-tuple-element.17, ...), kind=kOutput, calls=%fused_computation.113 | convolution fusion | flops 101908480 | bytes 2823168 | tf_op jit(solution)/shard_map/sxyw,zw->sxyz/dot_general | solution.py:86
  21.1 1.7 %fusion.32 = f32[96,4,128]{2,1,0:T(4,128)S(1)} fusion(bf16[96,128,128]{2,1,0:T(8,128)(2,1)S(1)} %copy-done, bf16[96,4,128]{2,0,1:T(8,128)(2,1)S(1)} %fusion.55), kind=kOutput, calls=%fused_computation.44 | convolution fusion | flops 12582912 | bytes 3440640 | tf_op jit(solution)/shard_map/pij,psj->psi/dot_general | solution.py:95
  23.4 1.3 %collective-permute-done.3 = f32[8,8,4,128]{3,1,2,0:T(8,128)S(1)} collective-permute-done((f32[8,8,4,128]{3,1,2,0:T(8,128)S(1)}, f32[8,8,4,128]{3,1,2,0:T(8,128)S(1)}, u32[]{:S(2)}, u32[]{:S(2)}) %collective-permute-start.3) | collective-permute-done | bytes 131104 | tf_op jit(solution)/shard_map/ppermute | solution.py:106
  24.9 11.4 %all_to_all.10 = f32[8,8,4,128]{3,1,2,0:T(8,128)S(1)} all-to-all(f32[8,8,4,128]{3,1,2,0:T(8,128)S(1)} %bitcast_add_fusion), channel_id=1, replica_groups=mesh['vh'=8,'vc'=2,'star'=2] {'vh'}, dimensions={0} | all-to-all | bytes 262144 | tf_op jit(solution)/shard_map/all_to_all | solution.py:107
  36.4 11.1 %all_to_all.11 = bf16[16,8,4,128]{3,2,1,0:T(4,128)(2,1)S(1)} all-to-all(bf16[16,8,4,128]{3,2,1,0:T(4,128)(2,1)S(1)} %broadcast_in_dim.13), channel_id=1, replica_groups=mesh['vh'=8,'vc'=2,'star'=2] {'vh','vc'}, dimensions={0} | all-to-all | bytes 262144 | tf_op jit(solution)/shard_map/all_to_all | solution.py:113
  47.8 0.9 %fusion.33 = f32[96,4,128]{2,1,0:T(4,128)S(1)} fusion(bf16[96,128,128]{2,1,0:T(8,128)(2,1)S(1)} %copy-done, bf16[96,4,128]{2,0,1:T(8,128)(2,1)S(1)} %fusion.21), kind=kOutput, calls=%fused_computation.45 | convolution fusion | flops 12582912 | bytes 3440640 | tf_op jit(solution)/shard_map/pij,psi->psj/dot_general | solution.py:119
  49.4 2.1 %collective-permute-start.4 = (f32[1,64,128]{2,1,0:T(8,128)S(1)}, f32[1,64,128]{2,1,0:T(8,128)S(1)}, u32[]{:S(2)}, u32[]{:S(2)}) collective-permute-start(f32[1,64,128]{2,1,0:T(8,128)S(1)} %get-tuple-element.8), channel_id=1, source_target_pairs={{0,2},{2,4},{4,6},{6,8},{8,10},{10,12},{12,14},{14,16},{16,18},{18... | collective-permute-start | bytes 98312 | tf_op jit(solution)/shard_map/ppermute | solution.py:24
  51.4 2.3 %collective-permute-start.5 = (f32[1,64,128]{2,1,0:T(8,128)S(1)}, f32[1,64,128]{2,1,0:T(8,128)S(1)}, u32[]{:S(2)}, u32[]{:S(2)}) collective-permute-start(f32[1,64,128]{2,1,0:T(8,128)S(1)} %get-tuple-element.9), channel_id=1, source_target_pairs={{2,0},{4,2},{6,4},{8,6},{10,8},{12,10},{14,12},{16,14},{18,16},{20... | collective-permute-start | bytes 98312 | tf_op jit(solution)/shard_map/ppermute | solution.py:25
  53.8 2.9 %collective-permute-done.5 = f32[1,64,128]{2,1,0:T(8,128)S(1)} collective-permute-done((f32[1,64,128]{2,1,0:T(8,128)S(1)}, f32[1,64,128]{2,1,0:T(8,128)S(1)}, u32[]{:S(2)}, u32[]{:S(2)}) %collective-permute-start.5) | collective-permute-done | bytes 32800 | tf_op jit(solution)/shard_map/ppermute | solution.py:25
  56.7 1.2 %collective-permute-start.6 = (f32[4,1,128]{2,1,0:T(1,128)S(1)}, f32[4,1,128]{2,1,0:T(1,128)S(1)}, u32[]{:S(2)}, u32[]{:S(2)}) collective-permute-start(f32[4,1,128]{2,1,0:T(1,128)S(1)} %broadcast_select_fusion.4), channel_id=1, source_target_pairs={{0,1},{1,0},{2,3},{3,2},{4,5},{5,4},{6,7},{7,6},{8,9},{9,8},{10,11... | collective-permute-start | bytes 6152 | tf_op jit(solution)/shard_map/ppermute | solution.py:19
  58.5 0.6 %collective-permute-done.6 = f32[4,1,128]{2,1,0:T(1,128)S(1)} collective-permute-done((f32[4,1,128]{2,1,0:T(1,128)S(1)}, f32[4,1,128]{2,1,0:T(1,128)S(1)}, u32[]{:S(2)}, u32[]{:S(2)}) %collective-permute-start.6) | collective-permute-done | bytes 2080 | tf_op jit(solution)/shard_map/ppermute | solution.py:19
  59.2 0.7 %fusion.35 = f32[2,64,128]{2,1,0:T(8,128)} fusion(f32[4,66,128]{2,1,0:T(8,128)S(1)} %pad_maximum_fusion.1, f32[2,64,128]{2,1,0:T(8,128)S(1)} %copy-done.1, f32[128]{0:T(128)S(1)} %copy-done.7, f32[128]{0:T(128)S(1)} %copy-done.8, f32[128]{0:T(128)S(1)} %copy-done.9, f32[128]{0:T(128)S(1)} %copy-done.10, f32[128]{0:T(128)S(1)} %copy-done.11, ...), kind=kLoop, calls=%fused_computation.48 | loop fusion | flops 311296 | bytes 725504 | tf_op jit(solution)/shard_map/add | solution.py:136
  (60 shorter events, 2.6 us)
Async XLA Ops:
  0.6 20.5 %copy-start = (bf16[96,128,128]{2,1,0:T(8,128)(2,1)S(1)}, bf16[96,128,128]{2,1,0:T(8,128)(2,1)}, u32[]{:S(2)}) copy-start(bf16[96,128,128]{2,1,0:T(8,128)(2,1)} %param.16) | copy-start | bytes 9437188
  3.3 9.5 %collective-permute-start = (f32[4,1,64,128]{3,2,1,0:T(8,128)}, f32[4,1,64,128]{3,2,1,0:T(8,128)S(1)}, u32[]{:S(2)}, u32[]{:S(2)}) collective-permute-start(f32[4,1,64,128]{3,2,1,0:T(8,128)} %get-tuple-element.6), channel_id=1, source_target_pairs={{0,2},{2,4},{4,6},{6,8},{8,10},{10,12},{12,14},{14,16},{16,18},{18... | collective-permute-start | bytes 393224 | tf_op jit(solution)/shard_map/ppermute | solution.py:24
  7.8 6.6 %collective-permute-start.1 = (f32[4,1,64,128]{3,2,1,0:T(8,128)}, f32[4,1,64,128]{3,2,1,0:T(8,128)}, u32[]{:S(2)}, u32[]{:S(2)}) collective-permute-start(f32[4,1,64,128]{3,2,1,0:T(8,128)} %get-tuple-element.7), channel_id=1, source_target_pairs={{2,0},{4,2},{6,4},{8,6},{10,8},{12,10},{14,12},{16,14},{18,16},{20... | collective-permute-start | bytes 393224 | tf_op jit(solution)/shard_map/ppermute | solution.py:25
  15.2 2.6 %collective-permute-start.2 = (f32[4,4,1,128]{3,2,1,0:T(1,128)S(1)}, f32[4,4,1,128]{3,2,1,0:T(1,128)S(1)}, u32[]{:S(2)}, u32[]{:S(2)}) collective-permute-start(f32[4,4,1,128]{3,2,1,0:T(1,128)S(1)} %broadcast_select_fusion.1), channel_id=1, source_target_pairs={{0,1},{1,0},{2,3},{3,2},{4,5},{5,4},{6,7},{7,6},{8,9},{9,8},{10,11... | collective-permute-start | bytes 24584 | tf_op jit(solution)/shard_map/ppermute | solution.py:19
  18.7 4.1 %copy-start.17 = (s32[96]{0:T(128)S(1)}, s32[96]{0:T(128)}, u32[]{:S(2)}) copy-start(s32[96]{0:T(128)} %bitcast_add_fusion.1) | copy-start | bytes 1156
  20.9 15.4 %copy-start.4 = (f32[8,128]{1,0:T(8,128)S(1)}, f32[8,128]{1,0:T(8,128)}, u32[]{:S(2)}) copy-start(f32[8,128]{1,0:T(8,128)} %param.20) | copy-start | bytes 12292
  20.9 15.4 %copy-start.5 = (f32[8,128]{1,0:T(8,128)S(1)}, f32[8,128]{1,0:T(8,128)}, u32[]{:S(2)}) copy-start(f32[8,128]{1,0:T(8,128)} %param.21) | copy-start | bytes 12292
  22.8 25.8 %copy-start.16 = (s32[96]{0:T(128)S(1)}, s32[96]{0:T(128)}, u32[]{:S(2)}) copy-start(s32[96]{0:T(128)} %param.17) | copy-start | bytes 1156
  23.3 25.8 %copy-start.3 = (f32[128,128]{1,0:T(8,128)S(1)}, f32[128,128]{1,0:T(8,128)}, u32[]{:S(2)}) copy-start(f32[128,128]{1,0:T(8,128)} %param.14) | copy-start | bytes 196612
  23.3 1.4 %collective-permute-start.3 = (f32[8,8,4,128]{3,1,2,0:T(8,128)S(1)}, f32[8,8,4,128]{3,1,2,0:T(8,128)S(1)}, u32[]{:S(2)}, u32[]{:S(2)}) collective-permute-start(f32[8,8,4,128]{3,1,2,0:T(8,128)S(1)} %bitcast.64), channel_id=1, source_target_pairs={{0,2},{2,0},{1,3},{3,1},{4,6},{6,4},{5,7},{7,5},{8,10},{10,8},{9,1... | collective-permute-start | bytes 393224 | tf_op jit(solution)/shard_map/ppermute | solution.py:106
  24.8 34.4 %copy-start.1 = (f32[2,64,128]{2,1,0:T(8,128)S(1)}, f32[2,64,128]{2,1,0:T(8,128)}, u32[]{:S(2)}) copy-start(f32[2,64,128]{2,1,0:T(8,128)} %get-tuple-element.2) | copy-start | bytes 196612
  24.8 34.4 %copy-start.6 = (f32[128]{0:T(128)S(1)}, f32[128]{0:T(128)}, u32[]{:S(2)}) copy-start(f32[128]{0:T(128)} %get-tuple-element.14) | copy-start | bytes 1540
  24.8 34.4 %copy-start.7 = (f32[128]{0:T(128)S(1)}, f32[128]{0:T(128)}, u32[]{:S(2)}) copy-start(f32[128]{0:T(128)} %get-tuple-element.15) | copy-start | bytes 1540
  24.8 34.4 %copy-start.8 = (f32[128]{0:T(128)S(1)}, f32[128]{0:T(128)}, u32[]{:S(2)}) copy-start(f32[128]{0:T(128)} %get-tuple-element.16) | copy-start | bytes 1540
  24.8 34.4 %copy-start.9 = (f32[128]{0:T(128)S(1)}, f32[128]{0:T(128)}, u32[]{:S(2)}) copy-start(f32[128]{0:T(128)} %get-tuple-element.17) | copy-start | bytes 1540
  24.8 34.4 %copy-start.10 = (f32[128]{0:T(128)S(1)}, f32[128]{0:T(128)}, u32[]{:S(2)}) copy-start(f32[128]{0:T(128)} %get-tuple-element.18) | copy-start | bytes 1540
  24.8 34.4 %copy-start.11 = (f32[128]{0:T(128)S(1)}, f32[128]{0:T(128)}, u32[]{:S(2)}) copy-start(f32[128]{0:T(128)} %get-tuple-element.19) | copy-start | bytes 1540
  24.8 34.4 %copy-start.12 = (f32[128]{0:T(128)S(1)}, f32[128]{0:T(128)}, u32[]{:S(2)}) copy-start(f32[128]{0:T(128)} %get-tuple-element.20) | copy-start | bytes 1540
  24.8 34.4 %copy-start.13 = (f32[128]{0:T(128)S(1)}, f32[128]{0:T(128)}, u32[]{:S(2)}) copy-start(f32[128]{0:T(128)} %get-tuple-element.21) | copy-start | bytes 1540
  24.8 34.4 %copy-start.14 = (f32[128]{0:T(128)S(1)}, f32[128]{0:T(128)}, u32[]{:S(2)}) copy-start(f32[128]{0:T(128)} %get-tuple-element.22) | copy-start | bytes 1540
  36.3 12.8 %copy-start.2 = (f32[4,2,64,128]{3,2,1,0:T(8,128)S(1)}, f32[4,2,64,128]{3,2,1,0:T(8,128)}, u32[]{:S(2)}) copy-start(f32[4,2,64,128]{3,2,1,0:T(8,128)} %get-tuple-element.28) | copy-start | bytes 786436
  49.4 4.4 %collective-permute-start.4 = (f32[1,64,128]{2,1,0:T(8,128)S(1)}, f32[1,64,128]{2,1,0:T(8,128)S(1)}, u32[]{:S(2)}, u32[]{:S(2)}) collective-permute-start(f32[1,64,128]{2,1,0:T(8,128)S(1)} %get-tuple-element.8), channel_id=1, source_target_pairs={{0,2},{2,4},{4,6},{6,8},{8,10},{10,12},{12,14},{14,16},{16,18},{18... | collective-permute-start | bytes 98312 | tf_op jit(solution)/shard_map/ppermute | solution.py:24
  51.4 5.2 %collective-permute-start.5 = (f32[1,64,128]{2,1,0:T(8,128)S(1)}, f32[1,64,128]{2,1,0:T(8,128)S(1)}, u32[]{:S(2)}, u32[]{:S(2)}) collective-permute-start(f32[1,64,128]{2,1,0:T(8,128)S(1)} %get-tuple-element.9), channel_id=1, source_target_pairs={{2,0},{4,2},{6,4},{8,6},{10,8},{12,10},{14,12},{16,14},{18,16},{20... | collective-permute-start | bytes 98312 | tf_op jit(solution)/shard_map/ppermute | solution.py:25
  56.7 2.4 %collective-permute-start.6 = (f32[4,1,128]{2,1,0:T(1,128)S(1)}, f32[4,1,128]{2,1,0:T(1,128)S(1)}, u32[]{:S(2)}, u32[]{:S(2)}) collective-permute-start(f32[4,1,128]{2,1,0:T(1,128)S(1)} %broadcast_select_fusion.4), channel_id=1, source_target_pairs={{0,1},{1,0},{2,3},{3,2},{4,5},{5,4},{6,7},{7,6},{8,9},{9,8},{10,11... | collective-permute-start | bytes 6152 | tf_op jit(solution)/shard_map/ppermute | solution.py:19
  (1 other events, 3.2 us)

commit v19 on v16

--- a/solution.py
+++ b/solution.py
@@ -23,7 +23,7 @@
     return jnp.concatenate([below, cells, above], axis=dim)
 
 
-VOX = ("vh", "vc")
+VOX = ("va", "vb", "vc")
 
 
 def with_halo(cells, dim):
@@ -94,13 +94,13 @@
         target[:, None] == jnp.arange(group_blocks, dtype=jnp.int32)[None, :]
     ).astype(jnp.float32)
     partial = jnp.einsum("pb,psi->bsi", target_onehot, contribution, precision=HIGH)
-    pair_size = lax.psum(1, "vc")
-    core = lax.axis_index("vc")
-    halves = partial.reshape(group_size // pair_size, pair_size, star_count, samples, length)
-    keep = lax.dynamic_index_in_dim(halves, core, axis=1, keepdims=False)
-    send = lax.dynamic_index_in_dim(halves, 1 - core, axis=1, keepdims=False)
-    merged = keep + lax.ppermute(send, "vc", [(0, 1), (1, 0)])
-    arrived = lax.all_to_all(merged, "vh", split_axis=0, concat_axis=0, tiled=True)
+    merged = partial.reshape(group_size // 4, 2, 2, star_count, samples, length)
+    for axis, place in (("vc", 2), ("vb", 1)):
+        bit = lax.axis_index(axis)
+        keep = lax.dynamic_index_in_dim(merged, bit, axis=place, keepdims=False)
+        send = lax.dynamic_index_in_dim(merged, 1 - bit, axis=place, keepdims=False)
+        merged = keep + lax.ppermute(send, axis, [(0, 1), (1, 0)])
+    arrived = lax.all_to_all(merged, "va", split_axis=0, concat_axis=0, tiled=True)
     extinction = jnp.sum(arrived, axis=0)
     misfit = inv_var[:, None, :] * (extinction - observed[:, None, :])
     residual_mean = jnp.mean(misfit, axis=1)
@@ -136,7 +136,7 @@
 def solution(mesh):
     shape = mesh.devices.shape
     view = jax.sharding.Mesh(
-        mesh.devices.reshape(shape[0] // 2, 2, shape[1]), ("vh", "vc", "star")
+        mesh.devices.reshape(shape[0] // 4, 2, 2, shape[1]), ("va", "vb", "vc", "star")
     )
     placed = (
         P(VOX, "star", None),

time: 60.3 us -> 65.4 us (1.085)
  waiting for transfers between devices: 8.2 us -> 10.5 us
  blocking collectives: 22.6 us -> 20.4 us
  starting transfers between devices: 13.4 us -> 15.6 us
  other arithmetic: 6.06 us -> 7.72 us
  matrix products: 6.19 us -> 7.51 us
    all_to_all x1, blocking collectives: 11.4 us -> 8.07 us  [per_device(): lax.all_to_all(merged, 'va', split_axis=0, concat_axis=0, tiled=True)]
    ppermute x1 -> x2, waiting for transfers between devices: 1.33 us -> 3.65 us  [per_device(): merged = keep + lax.ppermute(send, axis, [(0, 1), (1, 0)])]
    ppermute x1 -> x2, starting transfers between devices: 0.07 us -> 2.28 us  [per_device(): merged = keep + lax.ppermute(send, axis, [(0, 1), (1, 0)])]
    all_to_all x1, blocking collectives: 11.1 us -> 12.3 us  [per_device(): lax.all_to_all(spread, VOX, split_axis=0, concat_axis=0, tiled=True)]
    reduce_sum x1, other arithmetic: 0.03 us -> 1 us  [per_device(): grad_log = jnp.mean(density * adjoint, axis=0)]
    add x1, other arithmetic: 0.7 us -> 1.38 us  [per_device(): gradient = grad_latent + jnp.mean(latent, axis=0)]
    dot_general x1, matrix products: 0.21 us -> 0.87 us  [per_device(): jnp.einsum('pb,bsi->psi', target_onehot.astype(jnp.bfloat16), misfit_b, p...]
  transfers between devices with their start and end apart: 7 -> 8, of which waited for: 5 -> 6; matrix products, arithmetic and copies ran while one was open for 5% -> 5% of each run, Pallas kernels for 0% -> 0%
where the time goes in v19:
time: 65.4 us; the launch traced here: 64.9 us
  blocking collectives  20.4 us (31%)
  starting transfers between devices  15.6 us (24%)
  waiting for transfers between devices  10.5 us (16%)
  other arithmetic  7.72 us (12%)
  matrix products  7.51 us (11%)
  local copies, waits for them, and re-layouts  2.28 us (3%)
  between operations  0.89 us (1%)
    all_to_all x1, blocking collectives, per_device(): lax.all_to_all(spread, VOX, split_axis=0, concat_axis=0, tiled=True)  12.3 us
    all_to_all x1, blocking collectives, per_device(): lax.all_to_all(merged, 'va', split_axis=0, concat_axis=0, tiled=True)  8.07 us
    ppermute x2, starting transfers between devices, exchange(): below = lax.ppermute(tail, axis, [(i, i + 1) for i in range(count - 1)])  6.58 us
    ppermute x2, waiting for transfers between devices, exchange(): above = lax.ppermute(head, axis, [(i + 1, i) for i in range(count - 1)])  6.13 us
    ppermute x2, starting transfers between devices, exchange(): above = lax.ppermute(head, axis, [(i + 1, i) for i in range(count - 1)])  4.23 us
    ppermute x2, waiting for transfers between devices, per_device(): merged = keep + lax.ppermute(send, axis, [(0, 1), (1, 0)])  3.65 us
    ppermute x2, starting transfers between devices, exchange(): lax.ppermute(jnp.where(index == 0, tail, head), axis, [(0, 1), (1, 0)])  2.49 us
    ppermute x2, starting transfers between devices, per_device(): merged = keep + lax.ppermute(send, axis, [(0, 1), (1, 0)])  2.28 us
  transfers between devices with their start and end apart: 8, of which 6 were waited for; matrix products, arithmetic and copies ran while one was open for 5% of the time, Pallas kernels for 0%

profile of v19, /device:TPU:1, one launch (start us, length us, event | category | flops | bytes accessed | tf_op | source)
XLA Modules:
  0.0 64.9 jit_solution(7259180308089456248)
XLA Ops:
  0.6 1.8 %fusion.66 = (f32[2,64,128]{2,1,0:T(8,128)}, f32[4,2,64,128]{3,2,1,0:T(8,128)S(1)}) fusion(f32[4,2,64,128]{3,2,1,0:T(8,128)} %param.12, f32[2,64,128]{2,1,0:T(8,128)} %param.11), kind=kLoop, calls=%fused_computation.111 | loop fusion | flops 114688 | bytes 655360 | tf_op jit(solution)/shard_map/reduce_sum | solution.py:132
  3.1 4.5 %collective-permute-start = (f32[4,1,64,128]{3,2,1,0:T(8,128)}, f32[4,1,64,128]{3,2,1,0:T(8,128)S(1)}, u32[]{:S(2)}, u32[]{:S(2)}) collective-permute-start(f32[4,1,64,128]{3,2,1,0:T(8,128)} %get-tuple-element.6), channel_id=1, source_target_pairs={{0,2},{2,4},{4,6},{6,8},{8,10},{10,12},{12,14},{14,16},{16,18},{18... | collective-permute-start | bytes 393224 | tf_op jit(solution)/shard_map/ppermute | solution.py:21
  7.7 1.9 %collective-permute-start.1 = (f32[4,1,64,128]{3,2,1,0:T(8,128)}, f32[4,1,64,128]{3,2,1,0:T(8,128)}, u32[]{:S(2)}, u32[]{:S(2)}) collective-permute-start(f32[4,1,64,128]{3,2,1,0:T(8,128)} %get-tuple-element.7), channel_id=1, source_target_pairs={{2,0},{4,2},{6,4},{8,6},{10,8},{12,10},{14,12},{16,14},{18,16},{20... | collective-permute-start | bytes 393224 | tf_op jit(solution)/shard_map/ppermute | solution.py:22
  9.6 0.8 %broadcast_in_dim.10 = f32[9]{0:T(128)S(1)} reshape(f32[3,3]{1,0:T(4,128)} %param.13) | data formatting | bytes 72 | tf_op jit(solution)/shard_map/broadcast_in_dim | solution.py:71
  11.0 3.2 %collective-permute-done.1 = f32[4,1,64,128]{3,2,1,0:T(8,128)} collective-permute-done((f32[4,1,64,128]{3,2,1,0:T(8,128)}, f32[4,1,64,128]{3,2,1,0:T(8,128)}, u32[]{:S(2)}, u32[]{:S(2)}) %collective-permute-start.1) | collective-permute-done | bytes 131104 | tf_op jit(solution)/shard_map/ppermute | solution.py:22
  15.0 1.3 %collective-permute-start.2 = (f32[4,4,1,128]{3,2,1,0:T(1,128)S(1)}, f32[4,4,1,128]{3,2,1,0:T(1,128)S(1)}, u32[]{:S(2)}, u32[]{:S(2)}) collective-permute-start(f32[4,4,1,128]{3,2,1,0:T(1,128)S(1)} %broadcast_select_fusion.1), channel_id=1, source_target_pairs={{0,1},{1,0},{2,3},{3,2},{4,5},{5,4},{6,7},{7,6},{8,9},{9,8},{10,11... | collective-permute-start | bytes 24584 | tf_op jit(solution)/shard_map/ppermute | solution.py:16
  16.3 1.2 %bitcast_add_fusion.1 = s32[96]{0:T(128)} fusion(s32[96]{0:T(128)} %param.19, s32[96,1]{0,1:T(1,128)} %param.18), kind=kLoop, calls=%fused_computation.109 | loop fusion | flops 192 | bytes 1152 | tf_op jit(solution)/shard_map/add | solution.py:92
  17.6 1.0 %pad_maximum_fusion = f32[4,4,66,128]{3,2,1,0:T(8,128)S(1)} fusion(f32[4,4,1,128]{3,2,1,0:T(1,128)S(1)} %get-tuple-element.22, f32[4,1,64,128]{3,2,1,0:T(8,128)} %collective-permute-done.1, f32[4,2,64,128]{3,2,1,0:T(8,128)S(1)} %get-tuple-element.3, f32[4,1,64,128]{3,2,1,0:T(8,128)S(1)} %collective-permute-done, f32[4,4,1,128]{3,2,1,0:T(1,128)S(1)} %get-tuple-element.21), kind=kLoop, calls=%fused_computation.4 | loop fusion | flops 540672 | bytes 1081344 | tf_op jit(solution)/shard_map/concatenate | solution.py:23
  18.6 2.1 %fusion.69 = (bf16[4,2,64,128]{3,2,1,0:T(8,128)(2,1)S(1)}, f32[4,2,64,128]{3,2,1,0:T(8,128)}) fusion(f32[128]{0:T(128)} %param.15, f32[128,128]{1,0:T(8,128)} %param.14, f32[4,4,66,128]{3,2,1,0:T(8,128)S(1)} %pad_maximum_fusion, f32[128]{0:T(128)} %get-tuple-element.13, f32[128]{0:T(128)} %get-tuple-element.14, f32[128]{0:T(128)} %get-tuple-element.15, ...), kind=kOutput, calls=%fused_computation.114 | convolution fusion | flops 101908480 | bytes 2823168 | tf_op jit(solution)/shard_map/sxyw,zw->sxyz/dot_general | solution.py:82
  21.0 1.7 %fusion.35 = f32[96,4,128]{2,1,0:T(4,128)S(1)} fusion(bf16[96,128,128]{2,1,0:T(8,128)(2,1)S(1)} %copy-done, bf16[96,4,128]{2,0,1:T(8,128)(2,1)S(1)} %convolution_convert_fusion.1), kind=kOutput, calls=%fused_computation.45 | convolution fusion | flops 12582912 | bytes 3440640 | tf_op jit(solution)/shard_map/pij,psj->psi/dot_general | solution.py:91
  23.2 1.3 %collective-permute-done.3 = f32[4,2,8,4,128]{4,2,3,1,0:T(8,128)S(1)} collective-permute-done((f32[4,2,8,4,128]{4,2,3,1,0:T(8,128)S(1)}, f32[4,2,8,4,128]{4,2,3,1,0:T(8,128)S(1)}, u32[]{:S(2)}, u32[]{:S(2)}) %collective-permute-start.3) | collective-permute-done | bytes 131104 | tf_op jit(solution)/shard_map/ppermute | solution.py:102
  24.6 2.2 %collective-permute-start.4 = (f32[4,8,4,128]{3,1,2,0:T(8,128)S(1)}, f32[4,8,4,128]{3,1,2,0:T(8,128)S(1)}, u32[]{:S(2)}, u32[]{:S(2)}) collective-permute-start(f32[4,8,4,128]{3,1,2,0:T(8,128)S(1)} %dynamic-slice_bitcast_fusion), channel_id=1, source_target_pairs={{0,4},{4,0},{1,5},{5,1},{2,6},{6,2},{3,7},{7,3},{8,12},{12,8},{9,1... | collective-permute-start | bytes 196616 | tf_op jit(solution)/shard_map/ppermute | solution.py:102
  26.8 2.3 %collective-permute-done.4 = f32[4,8,4,128]{3,1,2,0:T(8,128)S(1)} collective-permute-done((f32[4,8,4,128]{3,1,2,0:T(8,128)S(1)}, f32[4,8,4,128]{3,1,2,0:T(8,128)S(1)}, u32[]{:S(2)}, u32[]{:S(2)}) %collective-permute-start.4) | collective-permute-done | bytes 65568 | tf_op jit(solution)/shard_map/ppermute | solution.py:102
  29.2 8.1 %all_to_all.10 = f32[4,8,4,128]{3,1,2,0:T(8,128)S(1)} all-to-all(f32[4,8,4,128]{3,1,2,0:T(8,128)S(1)} %bitcast_add_fusion), channel_id=1, replica_groups=mesh['va'=4,'vb'=2,'vc'=2,'star'=2] {'va'}, dimensions={0} | all-to-all | bytes 131072 | tf_op jit(solution)/shard_map/all_to_all | solution.py:103
  37.3 12.3 %all_to_all.11 = bf16[16,8,4,128]{3,1,2,0:T(8,128)(2,1)S(1)} all-to-all(bf16[16,8,4,128]{3,1,2,0:T(8,128)(2,1)S(1)} %broadcast_in_dim.13), channel_id=1, replica_groups=mesh['va'=4,'vb'=2,'vc'=2,'star'=2] {'va','vb','vc'}, dimensions={0} | all-to-all | bytes 262144 | tf_op jit(solution)/shard_map/all_to_all | solution.py:109
  49.6 0.9 %convolution_convert_fusion = bf16[96,4,128]{2,0,1:T(8,128)(2,1)S(1)} fusion(bf16[16,8,4,128]{3,1,2,0:T(8,128)(2,1)S(1)} %all_to_all.11, s32[96]{0:T(128)} %bitcast_add_fusion.1), kind=kOutput, calls=%fused_computation.2 | convolution fusion | flops 12668928 | bytes 229760 | tf_op jit(solution)/shard_map/pb,bsi->psi/dot_general | solution.py:112
  50.5 0.9 %fusion.33 = f32[96,4,128]{2,1,0:T(4,128)S(1)} fusion(bf16[96,128,128]{2,1,0:T(8,128)(2,1)S(1)} %copy-done, bf16[96,4,128]{2,0,1:T(8,128)(2,1)S(1)} %convolution_convert_fusion), kind=kOutput, calls=%fused_computation.43 | convolution fusion | flops 12582912 | bytes 3440640 | tf_op jit(solution)/shard_map/pij,psi->psj/dot_general | solution.py:115
  51.4 1.0 %fusion.17 = f32[4,128,128]{1,2,0:T(8,128)S(1)} fusion(f32[96,4,128]{2,1,0:T(4,128)S(1)} %fusion.33, s32[96]{0:T(128)} %param.17), kind=kOutput, calls=%fused_computation.23 | convolution fusion | flops 75509760 | bytes 459136 | tf_op jit(solution)/shard_map/pb,psj->sbj/dot_general | solution.py:118
  52.4 1.0 %multiply_reduce_fusion = f32[2,64,128]{2,1,0:T(8,128)S(1)} fusion(f32[4,2,64,128]{3,2,1,0:T(8,128)} %get-tuple-element.26, f32[4,2,64,128]{3,2,1,0:T(8,128)S(1)} %bitcast.65), kind=kLoop, calls=%fused_computation.22 | loop fusion | flops 114688 | bytes 589824 | tf_op jit(solution)/shard_map/reduce_sum | solution.py:121
  53.7 2.1 %collective-permute-start.5 = (f32[1,64,128]{2,1,0:T(8,128)S(1)}, f32[1,64,128]{2,1,0:T(8,128)S(1)}, u32[]{:S(2)}, u32[]{:S(2)}) collective-permute-start(f32[1,64,128]{2,1,0:T(8,128)S(1)} %get-tuple-element.8), channel_id=1, source_target_pairs={{0,2},{2,4},{4,6},{6,8},{8,10},{10,12},{12,14},{14,16},{16,18},{18... | collective-permute-start | bytes 98312 | tf_op jit(solution)/shard_map/ppermute | solution.py:21
  55.7 2.3 %collective-permute-start.6 = (f32[1,64,128]{2,1,0:T(8,128)S(1)}, f32[1,64,128]{2,1,0:T(8,128)S(1)}, u32[]{:S(2)}, u32[]{:S(2)}) collective-permute-start(f32[1,64,128]{2,1,0:T(8,128)S(1)} %get-tuple-element.9), channel_id=1, source_target_pairs={{2,0},{4,2},{6,4},{8,6},{10,8},{12,10},{14,12},{16,14},{18,16},{20... | collective-permute-start | bytes 98312 | tf_op jit(solution)/shard_map/ppermute | solution.py:22
  58.1 2.9 %collective-permute-done.6 = f32[1,64,128]{2,1,0:T(8,128)S(1)} collective-permute-done((f32[1,64,128]{2,1,0:T(8,128)S(1)}, f32[1,64,128]{2,1,0:T(8,128)S(1)}, u32[]{:S(2)}, u32[]{:S(2)}) %collective-permute-start.6) | collective-permute-done | bytes 32800 | tf_op jit(solution)/shard_map/ppermute | solution.py:22
  61.0 1.2 %collective-permute-start.7 = (f32[4,1,128]{2,1,0:T(1,128)S(1)}, f32[4,1,128]{2,1,0:T(1,128)S(1)}, u32[]{:S(2)}, u32[]{:S(2)}) collective-permute-start(f32[4,1,128]{2,1,0:T(1,128)S(1)} %broadcast_select_fusion.4), channel_id=1, source_target_pairs={{0,1},{1,0},{2,3},{3,2},{4,5},{5,4},{6,7},{7,6},{8,9},{9,8},{10,11... | collective-permute-start | bytes 6152 | tf_op jit(solution)/shard_map/ppermute | solution.py:16
  63.5 1.4 %fusion.38 = f32[2,64,128]{2,1,0:T(8,128)} fusion(f32[4,66,128]{2,1,0:T(8,128)S(1)} %pad_maximum_fusion.1, f32[2,64,128]{2,1,0:T(8,128)S(1)} %copy-done.1, f32[128]{0:T(128)S(1)} %copy-done.6, f32[128]{0:T(128)} %get-tuple-element.14, f32[128]{0:T(128)} %get-tuple-element.15, f32[128]{0:T(128)} %get-tuple-element.16, f32[128]{0:T(128)} %get-tuple-element.17, ...), kind=kLoop, calls=%fused_computation.49 | loop fusion | flops 311296 | bytes 725504 | tf_op jit(solution)/shard_map/add | solution.py:132
  (44 shorter events, 4.6 us)
Async XLA Ops:
  0.6 20.3 %copy-start = (bf16[96,128,128]{2,1,0:T(8,128)(2,1)S(1)}, bf16[96,128,128]{2,1,0:T(8,128)(2,1)}, u32[]{:S(2)}) copy-start(bf16[96,128,128]{2,1,0:T(8,128)(2,1)} %param.16) | copy-start | bytes 9437188
  3.1 7.9 %collective-permute-start = (f32[4,1,64,128]{3,2,1,0:T(8,128)}, f32[4,1,64,128]{3,2,1,0:T(8,128)S(1)}, u32[]{:S(2)}, u32[]{:S(2)}) collective-permute-start(f32[4,1,64,128]{3,2,1,0:T(8,128)} %get-tuple-element.6), channel_id=1, source_target_pairs={{0,2},{2,4},{4,6},{6,8},{8,10},{10,12},{12,14},{14,16},{16,18},{18... | collective-permute-start | bytes 393224 | tf_op jit(solution)/shard_map/ppermute | solution.py:21
  7.7 6.6 %collective-permute-start.1 = (f32[4,1,64,128]{3,2,1,0:T(8,128)}, f32[4,1,64,128]{3,2,1,0:T(8,128)}, u32[]{:S(2)}, u32[]{:S(2)}) collective-permute-start(f32[4,1,64,128]{3,2,1,0:T(8,128)} %get-tuple-element.7), channel_id=1, source_target_pairs={{2,0},{4,2},{6,4},{8,6},{10,8},{12,10},{14,12},{16,14},{18,16},{20... | collective-permute-start | bytes 393224 | tf_op jit(solution)/shard_map/ppermute | solution.py:22
  15.0 2.6 %collective-permute-start.2 = (f32[4,4,1,128]{3,2,1,0:T(1,128)S(1)}, f32[4,4,1,128]{3,2,1,0:T(1,128)S(1)}, u32[]{:S(2)}, u32[]{:S(2)}) collective-permute-start(f32[4,4,1,128]{3,2,1,0:T(1,128)S(1)} %broadcast_select_fusion.1), channel_id=1, source_target_pairs={{0,1},{1,0},{2,3},{3,2},{4,5},{5,4},{6,7},{7,6},{8,9},{9,8},{10,11... | collective-permute-start | bytes 24584 | tf_op jit(solution)/shard_map/ppermute | solution.py:16
  17.5 3.3 %copy-start.7 = (s32[96]{0:T(128)S(1)}, s32[96]{0:T(128)}, u32[]{:S(2)}) copy-start(s32[96]{0:T(128)} %param.17) | copy-start | bytes 1156
  18.6 4.1 %copy-start.8 = (s32[96]{0:T(128)S(1)}, s32[96]{0:T(128)}, u32[]{:S(2)}) copy-start(s32[96]{0:T(128)} %bitcast_add_fusion.1) | copy-start | bytes 1156
  20.7 16.5 %copy-start.3 = (f32[8,128]{1,0:T(8,128)S(1)}, f32[8,128]{1,0:T(8,128)}, u32[]{:S(2)}) copy-start(f32[8,128]{1,0:T(8,128)} %param.20) | copy-start | bytes 12292
  20.7 16.5 %copy-start.4 = (f32[8,128]{1,0:T(8,128)S(1)}, f32[8,128]{1,0:T(8,128)}, u32[]{:S(2)}) copy-start(f32[8,128]{1,0:T(8,128)} %param.21) | copy-start | bytes 12292
  23.1 1.4 %collective-permute-start.3 = (f32[4,2,8,4,128]{4,2,3,1,0:T(8,128)S(1)}, f32[4,2,8,4,128]{4,2,3,1,0:T(8,128)S(1)}, u32[]{:S(2)}, u32[]{:S(2)}) collective-permute-start(f32[4,2,8,4,128]{4,2,3,1,0:T(8,128)S(1)} %bitcast.67), channel_id=1, source_target_pairs={{0,2},{2,0},{1,3},{3,1},{4,6},{6,4},{5,7},{7,5},{8,10},{10,8},{9,1... | collective-permute-start | bytes 393224 | tf_op jit(solution)/shard_map/ppermute | solution.py:102
  24.6 28.9 %copy-start.2 = (f32[128,128]{1,0:T(8,128)S(1)}, f32[128,128]{1,0:T(8,128)}, u32[]{:S(2)}) copy-start(f32[128,128]{1,0:T(8,128)} %param.14) | copy-start | bytes 196612
  24.6 4.5 %collective-permute-start.4 = (f32[4,8,4,128]{3,1,2,0:T(8,128)S(1)}, f32[4,8,4,128]{3,1,2,0:T(8,128)S(1)}, u32[]{:S(2)}, u32[]{:S(2)}) collective-permute-start(f32[4,8,4,128]{3,1,2,0:T(8,128)S(1)} %dynamic-slice_bitcast_fusion), channel_id=1, source_target_pairs={{0,4},{4,0},{1,5},{5,1},{2,6},{6,2},{3,7},{7,3},{8,12},{12,8},{9,1... | collective-permute-start | bytes 196616 | tf_op jit(solution)/shard_map/ppermute | solution.py:102
  26.8 36.6 %copy-start.1 = (f32[2,64,128]{2,1,0:T(8,128)S(1)}, f32[2,64,128]{2,1,0:T(8,128)}, u32[]{:S(2)}) copy-start(f32[2,64,128]{2,1,0:T(8,128)} %get-tuple-element.2) | copy-start | bytes 196612
  26.8 36.6 %copy-start.5 = (f32[128]{0:T(128)S(1)}, f32[128]{0:T(128)}, u32[]{:S(2)}) copy-start(f32[128]{0:T(128)} %get-tuple-element.12) | copy-start | bytes 1540
  26.8 36.6 %copy-start.6 = (f32[128]{0:T(128)S(1)}, f32[128]{0:T(128)}, u32[]{:S(2)}) copy-start(f32[128]{0:T(128)} %get-tuple-element.13) | copy-start | bytes 1540
  53.7 4.4 %collective-permute-start.5 = (f32[1,64,128]{2,1,0:T(8,128)S(1)}, f32[1,64,128]{2,1,0:T(8,128)S(1)}, u32[]{:S(2)}, u32[]{:S(2)}) collective-permute-start(f32[1,64,128]{2,1,0:T(8,128)S(1)} %get-tuple-element.8), channel_id=1, source_target_pairs={{0,2},{2,4},{4,6},{6,8},{8,10},{10,12},{12,14},{14,16},{16,18},{18... | collective-permute-start | bytes 98312 | tf_op jit(solution)/shard_map/ppermute | solution.py:21
  55.7 5.2 %collective-permute-start.6 = (f32[1,64,128]{2,1,0:T(8,128)S(1)}, f32[1,64,128]{2,1,0:T(8,128)S(1)}, u32[]{:S(2)}, u32[]{:S(2)}) collective-permute-start(f32[1,64,128]{2,1,0:T(8,128)S(1)} %get-tuple-element.9), channel_id=1, source_target_pairs={{2,0},{4,2},{6,4},{8,6},{10,8},{12,10},{14,12},{16,14},{18,16},{20... | collective-permute-start | bytes 98312 | tf_op jit(solution)/shard_map/ppermute | solution.py:22
  61.0 2.4 %collective-permute-start.7 = (f32[4,1,128]{2,1,0:T(1,128)S(1)}, f32[4,1,128]{2,1,0:T(1,128)S(1)}, u32[]{:S(2)}, u32[]{:S(2)}) collective-permute-start(f32[4,1,128]{2,1,0:T(1,128)S(1)} %broadcast_select_fusion.4), channel_id=1, source_target_pairs={{0,1},{1,0},{2,3},{3,2},{4,5},{5,4},{6,7},{7,6},{8,9},{9,8},{10,11... | collective-permute-start | bytes 6152 | tf_op jit(solution)/shard_map/ppermute | solution.py:16

commit v20 on v16

--- a/solution.py
+++ b/solution.py
@@ -105,10 +105,7 @@
     misfit = inv_var[:, None, :] * (extinction - observed[:, None, :])
     residual_mean = jnp.mean(misfit, axis=1)
     misfit_b = misfit.astype(jnp.bfloat16)
-    spread = jnp.broadcast_to(misfit_b[None], (group_size,) + misfit_b.shape)
-    misfit_b = lax.all_to_all(spread, VOX, split_axis=0, concat_axis=0, tiled=True).reshape(
-        group_blocks, samples, length
-    )
+    misfit_b = lax.all_gather(misfit_b, VOX, axis=0, tiled=True)
     pair_misfit = jnp.einsum(
         "pb,bsi->psi", target_onehot.astype(jnp.bfloat16), misfit_b, preferred_element_type=jnp.float32
     ).astype(jnp.bfloat16)

time: 60.3 us -> 69.8 us (1.16)
  blocking collectives: 22.6 us -> 32 us
    all_gather x0 -> x1, blocking collectives: none -> 20.6 us  [per_device(): misfit_b = lax.all_gather(misfit_b, VOX, axis=0, tiled=True)]
    all_to_all x1 -> x0, blocking collectives: 11.1 us -> none  [per_device(): lax.all_to_all(spread, VOX, split_axis=0, concat_axis=0, tiled=True)]
where the time goes in v20:
time: 69.8 us; the launch traced here: 69.4 us
  blocking collectives  32 us (46%)
  starting transfers between devices  13.3 us (19%)
  waiting for transfers between devices  8.45 us (12%)
  matrix products  6.2 us (9%)
  other arithmetic  6.06 us (9%)
  local copies, waits for them, and re-layouts  2.3 us (3%)
  between operations  1.02 us (1%)
    all_gather x1, blocking collectives, per_device(): misfit_b = lax.all_gather(misfit_b, VOX, axis=0, tiled=True)  20.6 us
    all_to_all x1, blocking collectives, per_device(): lax.all_to_all(merged, 'vh', split_axis=0, concat_axis=0, tiled=True)  11.4 us
    ppermute x2, starting transfers between devices, exchange(): below = lax.ppermute(tail, axis, [(i, i + 1) for i in range(count - 1)])  6.79 us
    ppermute x2, waiting for transfers between devices, exchange(): above = lax.ppermute(head, axis, [(i + 1, i) for i in range(count - 1)])  6.37 us
    ppermute x2, starting transfers between devices, exchange(): above = lax.ppermute(head, axis, [(i + 1, i) for i in range(count - 1)])  3.98 us
    ppermute x2, starting transfers between devices, exchange(): lax.ppermute(jnp.where(index == 0, tail, head), axis, [(0, 1), (1, 0)])  2.49 us
    dot_general x1, matrix products, per_device(): jnp.einsum('sxyw,zw->sxyz', smoothed, vertical_mix, precision=HIGH)  2.13 us
    reduce_sum x1, other arithmetic, per_device(): gradient = grad_latent + jnp.mean(latent, axis=0)  1.76 us
  transfers between devices with their start and end apart: 7, of which 5 were waited for; matrix products, arithmetic and copies ran while one was open for 5% of the time, Pallas kernels for 0%

profile of v20, /device:TPU:1, one launch (start us, length us, event | category | flops | bytes accessed | tf_op | source)
XLA Modules:
  0.0 69.4 jit_solution(3027833255120211826)
XLA Ops:
  0.6 1.8 %fusion.64 = (f32[2,64,128]{2,1,0:T(8,128)}, f32[4,2,64,128]{3,2,1,0:T(8,128)S(1)}) fusion(f32[4,2,64,128]{3,2,1,0:T(8,128)} %param.12, f32[2,64,128]{2,1,0:T(8,128)} %param.11), kind=kLoop, calls=%fused_computation.107 | loop fusion | flops 114688 | bytes 655360 | tf_op jit(solution)/shard_map/reduce_sum | solution.py:129
  2.4 0.7 %fusion.65 = (f32[4,1,64,128]{3,2,1,0:T(8,128)}, f32[4,1,64,128]{3,2,1,0:T(8,128)}) fusion(f32[4,2,64,128]{3,2,1,0:T(8,128)S(1)} %get-tuple-element.3), kind=kLoop, calls=%fused_computation.108 | loop fusion | bytes 524288 | tf_op jit(solution)/shard_map/slice | solution.py:13
  3.1 4.5 %collective-permute-start = (f32[4,1,64,128]{3,2,1,0:T(8,128)}, f32[4,1,64,128]{3,2,1,0:T(8,128)S(1)}, u32[]{:S(2)}, u32[]{:S(2)}) collective-permute-start(f32[4,1,64,128]{3,2,1,0:T(8,128)} %get-tuple-element.6), channel_id=1, source_target_pairs={{0,2},{2,4},{4,6},{6,8},{8,10},{10,12},{12,14},{14,16},{16,18},{18... | collective-permute-start | bytes 393224 | tf_op jit(solution)/shard_map/ppermute | solution.py:21
  7.7 1.9 %collective-permute-start.1 = (f32[4,1,64,128]{3,2,1,0:T(8,128)}, f32[4,1,64,128]{3,2,1,0:T(8,128)}, u32[]{:S(2)}, u32[]{:S(2)}) collective-permute-start(f32[4,1,64,128]{3,2,1,0:T(8,128)} %get-tuple-element.7), channel_id=1, source_target_pairs={{2,0},{4,2},{6,4},{8,6},{10,8},{12,10},{14,12},{16,14},{18,16},{20... | collective-permute-start | bytes 393224 | tf_op jit(solution)/shard_map/ppermute | solution.py:22
  9.6 0.8 %broadcast_in_dim.8 = f32[9]{0:T(128)S(1)} reshape(f32[3,3]{1,0:T(4,128)} %param.13) | data formatting | bytes 72 | tf_op jit(solution)/shard_map/broadcast_in_dim | solution.py:71
  10.4 0.6 slice_bitcast_fusion.8
  11.0 3.2 %collective-permute-done.1 = f32[4,1,64,128]{3,2,1,0:T(8,128)} collective-permute-done((f32[4,1,64,128]{3,2,1,0:T(8,128)}, f32[4,1,64,128]{3,2,1,0:T(8,128)}, u32[]{:S(2)}, u32[]{:S(2)}) %collective-permute-start.1) | collective-permute-done | bytes 131104 | tf_op jit(solution)/shard_map/ppermute | solution.py:22
  14.3 0.7 %broadcast_select_fusion.1 = f32[4,4,1,128]{3,2,1,0:T(1,128)S(1)} fusion(pred[]{:T(512)S(6)} %eq.17, f32[4,1,64,128]{3,2,1,0:T(8,128)} %collective-permute-done.1, f32[4,2,64,128]{3,2,1,0:T(8,128)S(1)} %get-tuple-element.3, f32[4,1,64,128]{3,2,1,0:T(8,128)S(1)} %collective-permute-done), kind=kLoop, calls=%fused_computation.82 | loop fusion | flops 10240 | bytes 532481 | tf_op jit(solution)/shard_map/jit(_where)/select_n | solution.py:16
  15.0 1.3 %collective-permute-start.2 = (f32[4,4,1,128]{3,2,1,0:T(1,128)S(1)}, f32[4,4,1,128]{3,2,1,0:T(1,128)S(1)}, u32[]{:S(2)}, u32[]{:S(2)}) collective-permute-start(f32[4,4,1,128]{3,2,1,0:T(1,128)S(1)} %broadcast_select_fusion.1), channel_id=1, source_target_pairs={{0,1},{1,0},{2,3},{3,2},{4,5},{5,4},{6,7},{7,6},{8,9},{9,8},{10,11... | collective-permute-start | bytes 24584 | tf_op jit(solution)/shard_map/ppermute | solution.py:16
  16.3 1.2 %bitcast_add_fusion.1 = s32[96]{0:T(128)} fusion(s32[96]{0:T(128)} %param.19, s32[96,1]{0,1:T(1,128)} %param.18), kind=kLoop, calls=%fused_computation.103 | loop fusion | flops 192 | bytes 1152 | tf_op jit(solution)/shard_map/add | solution.py:92
  17.6 1.0 %pad_maximum_fusion = f32[4,4,66,128]{3,2,1,0:T(8,128)S(1)} fusion(f32[4,4,1,128]{3,2,1,0:T(1,128)S(1)} %get-tuple-element.22, f32[4,1,64,128]{3,2,1,0:T(8,128)} %collective-permute-done.1, f32[4,2,64,128]{3,2,1,0:T(8,128)S(1)} %get-tuple-element.3, f32[4,1,64,128]{3,2,1,0:T(8,128)S(1)} %collective-permute-done, f32[4,4,1,128]{3,2,1,0:T(1,128)S(1)} %get-tuple-element.21), kind=kLoop, calls=%fused_computation.2 | loop fusion | flops 540672 | bytes 1081344 | tf_op jit(solution)/shard_map/concatenate | solution.py:23
  18.6 2.1 %fusion.67 = (bf16[4,2,64,128]{3,2,1,0:T(8,128)(2,1)S(1)}, f32[4,2,64,128]{3,2,1,0:T(8,128)}) fusion(f32[128]{0:T(128)} %param.15, f32[128,128]{1,0:T(8,128)} %param.14, f32[4,4,66,128]{3,2,1,0:T(8,128)S(1)} %pad_maximum_fusion, f32[128]{0:T(128)} %get-tuple-element.13, f32[128]{0:T(128)} %get-tuple-element.14, f32[128]{0:T(128)} %get-tuple-element.15, ...), kind=kOutput, calls=%fused_computation.110 | convolution fusion | flops 101908480 | bytes 2823168 | tf_op jit(solution)/shard_map/sxyw,zw->sxyz/dot_general | solution.py:82
  20.9 1.7 %fusion.32 = f32[96,4,128]{2,1,0:T(4,128)S(1)} fusion(bf16[96,128,128]{2,1,0:T(8,128)(2,1)S(1)} %copy-done, bf16[96,4,128]{2,0,1:T(8,128)(2,1)S(1)} %fusion.55), kind=kOutput, calls=%fused_computation.42 | convolution fusion | flops 12582912 | bytes 3440640 | tf_op jit(solution)/shard_map/pij,psj->psi/dot_general | solution.py:91
  23.2 1.3 %collective-permute-done.3 = f32[8,8,4,128]{3,1,2,0:T(8,128)S(1)} collective-permute-done((f32[8,8,4,128]{3,1,2,0:T(8,128)S(1)}, f32[8,8,4,128]{3,1,2,0:T(8,128)S(1)}, u32[]{:S(2)}, u32[]{:S(2)}) %collective-permute-start.3) | collective-permute-done | bytes 131104 | tf_op jit(solution)/shard_map/ppermute | solution.py:102
  24.7 11.4 %all_to_all.5 = f32[8,8,4,128]{3,1,2,0:T(8,128)S(1)} all-to-all(f32[8,8,4,128]{3,1,2,0:T(8,128)S(1)} %bitcast_add_fusion), channel_id=1, replica_groups=mesh['vh'=8,'vc'=2,'star'=2] {'vh'}, dimensions={0} | all-to-all | bytes 262144 | tf_op jit(solution)/shard_map/all_to_all | solution.py:103
  36.2 20.6 %all_gather.3 = bf16[128,4,128]{2,1,0:T(4,128)(2,1)S(1)} all-gather(bf16[8,4,128]{2,1,0:T(4,128)(2,1)S(1)} %copy.16), channel_id=1, replica_groups=mesh['vh'=8,'vc'=2,'star'=2] {'vh','vc'}, dimensions={0}, use_global_device_ids=true | all-gather | bytes 139264 | tf_op jit(solution)/shard_map/all_gather | solution.py:108
  57.0 0.9 %fusion.33 = f32[96,4,128]{2,1,0:T(4,128)S(1)} fusion(bf16[96,128,128]{2,1,0:T(8,128)(2,1)S(1)} %copy-done, bf16[96,4,128]{2,0,1:T(8,128)(2,1)S(1)} %fusion.21), kind=kOutput, calls=%fused_computation.43 | convolution fusion | flops 12582912 | bytes 3440640 | tf_op jit(solution)/shard_map/pij,psi->psj/dot_general | solution.py:112
  58.6 2.3 %collective-permute-start.4 = (f32[1,64,128]{2,1,0:T(8,128)S(1)}, f32[1,64,128]{2,1,0:T(8,128)S(1)}, u32[]{:S(2)}, u32[]{:S(2)}) collective-permute-start(f32[1,64,128]{2,1,0:T(8,128)S(1)} %get-tuple-element.8), channel_id=1, source_target_pairs={{0,2},{2,4},{4,6},{6,8},{8,10},{10,12},{12,14},{14,16},{16,18},{18... | collective-permute-start | bytes 98312 | tf_op jit(solution)/shard_map/ppermute | solution.py:21
  60.9 2.1 %collective-permute-start.5 = (f32[1,64,128]{2,1,0:T(8,128)S(1)}, f32[1,64,128]{2,1,0:T(8,128)S(1)}, u32[]{:S(2)}, u32[]{:S(2)}) collective-permute-start(f32[1,64,128]{2,1,0:T(8,128)S(1)} %get-tuple-element.9), channel_id=1, source_target_pairs={{2,0},{4,2},{6,4},{8,6},{10,8},{12,10},{14,12},{16,14},{18,16},{20... | collective-permute-start | bytes 98312 | tf_op jit(solution)/shard_map/ppermute | solution.py:22
  63.0 3.2 %collective-permute-done.5 = f32[1,64,128]{2,1,0:T(8,128)S(1)} collective-permute-done((f32[1,64,128]{2,1,0:T(8,128)S(1)}, f32[1,64,128]{2,1,0:T(8,128)S(1)}, u32[]{:S(2)}, u32[]{:S(2)}) %collective-permute-start.5) | collective-permute-done | bytes 32800 | tf_op jit(solution)/shard_map/ppermute | solution.py:22
  66.1 1.2 %collective-permute-start.6 = (f32[4,1,128]{2,1,0:T(1,128)S(1)}, f32[4,1,128]{2,1,0:T(1,128)S(1)}, u32[]{:S(2)}, u32[]{:S(2)}) collective-permute-start(f32[4,1,128]{2,1,0:T(1,128)S(1)} %broadcast_select_fusion.4), channel_id=1, source_target_pairs={{0,1},{1,0},{2,3},{3,2},{4,5},{5,4},{6,7},{7,6},{8,9},{9,8},{10,11... | collective-permute-start | bytes 6152 | tf_op jit(solution)/shard_map/ppermute | solution.py:16
  67.3 0.6 broadcast_multiply_fusion
  67.9 0.6 collective-permute-done.6
  68.7 0.7 %fusion.35 = f32[2,64,128]{2,1,0:T(8,128)} fusion(f32[4,66,128]{2,1,0:T(8,128)S(1)} %pad_maximum_fusion.1, f32[2,64,128]{2,1,0:T(8,128)S(1)} %copy-done.1, f32[128]{0:T(128)S(1)} %copy-done.7, f32[128]{0:T(128)S(1)} %copy-done.8, f32[128]{0:T(128)S(1)} %copy-done.9, f32[128]{0:T(128)S(1)} %copy-done.10, f32[128]{0:T(128)S(1)} %copy-done.11, ...), kind=kLoop, calls=%fused_computation.46 | loop fusion | flops 311296 | bytes 725504 | tf_op jit(solution)/shard_map/add | solution.py:129
  (58 shorter events, 1.9 us)
Async XLA Ops:
  0.6 20.3 %copy-start = (bf16[96,128,128]{2,1,0:T(8,128)(2,1)S(1)}, bf16[96,128,128]{2,1,0:T(8,128)(2,1)}, u32[]{:S(2)}) copy-start(bf16[96,128,128]{2,1,0:T(8,128)(2,1)} %param.16) | copy-start | bytes 9437188
  3.1 7.9 %collective-permute-start = (f32[4,1,64,128]{3,2,1,0:T(8,128)}, f32[4,1,64,128]{3,2,1,0:T(8,128)S(1)}, u32[]{:S(2)}, u32[]{:S(2)}) collective-permute-start(f32[4,1,64,128]{3,2,1,0:T(8,128)} %get-tuple-element.6), channel_id=1, source_target_pairs={{0,2},{2,4},{4,6},{6,8},{8,10},{10,12},{12,14},{14,16},{16,18},{18... | collective-permute-start | bytes 393224 | tf_op jit(solution)/shard_map/ppermute | solution.py:21
  7.7 6.6 %collective-permute-start.1 = (f32[4,1,64,128]{3,2,1,0:T(8,128)}, f32[4,1,64,128]{3,2,1,0:T(8,128)}, u32[]{:S(2)}, u32[]{:S(2)}) collective-permute-start(f32[4,1,64,128]{3,2,1,0:T(8,128)} %get-tuple-element.7), channel_id=1, source_target_pairs={{2,0},{4,2},{6,4},{8,6},{10,8},{12,10},{14,12},{16,14},{18,16},{20... | collective-permute-start | bytes 393224 | tf_op jit(solution)/shard_map/ppermute | solution.py:22
  15.0 2.6 %collective-permute-start.2 = (f32[4,4,1,128]{3,2,1,0:T(1,128)S(1)}, f32[4,4,1,128]{3,2,1,0:T(1,128)S(1)}, u32[]{:S(2)}, u32[]{:S(2)}) collective-permute-start(f32[4,4,1,128]{3,2,1,0:T(1,128)S(1)} %broadcast_select_fusion.1), channel_id=1, source_target_pairs={{0,1},{1,0},{2,3},{3,2},{4,5},{5,4},{6,7},{7,6},{8,9},{9,8},{10,11... | collective-permute-start | bytes 24584 | tf_op jit(solution)/shard_map/ppermute | solution.py:16
  18.6 4.1 %copy-start.17 = (s32[96]{0:T(128)S(1)}, s32[96]{0:T(128)}, u32[]{:S(2)}) copy-start(s32[96]{0:T(128)} %bitcast_add_fusion.1) | copy-start | bytes 1156
  20.7 15.4 %copy-start.4 = (f32[8,128]{1,0:T(8,128)S(1)}, f32[8,128]{1,0:T(8,128)}, u32[]{:S(2)}) copy-start(f32[8,128]{1,0:T(8,128)} %param.20) | copy-start | bytes 12292
  20.7 15.4 %copy-start.5 = (f32[8,128]{1,0:T(8,128)S(1)}, f32[8,128]{1,0:T(8,128)}, u32[]{:S(2)}) copy-start(f32[8,128]{1,0:T(8,128)} %param.21) | copy-start | bytes 12292
  22.7 35.3 %copy-start.16 = (s32[96]{0:T(128)S(1)}, s32[96]{0:T(128)}, u32[]{:S(2)}) copy-start(s32[96]{0:T(128)} %param.17) | copy-start | bytes 1156
  23.1 35.3 %copy-start.3 = (f32[128,128]{1,0:T(8,128)S(1)}, f32[128,128]{1,0:T(8,128)}, u32[]{:S(2)}) copy-start(f32[128,128]{1,0:T(8,128)} %param.14) | copy-start | bytes 196612
  23.1 1.4 %collective-permute-start.3 = (f32[8,8,4,128]{3,1,2,0:T(8,128)S(1)}, f32[8,8,4,128]{3,1,2,0:T(8,128)S(1)}, u32[]{:S(2)}, u32[]{:S(2)}) collective-permute-start(f32[8,8,4,128]{3,1,2,0:T(8,128)S(1)} %bitcast.58), channel_id=1, source_target_pairs={{0,2},{2,0},{1,3},{3,1},{4,6},{6,4},{5,7},{7,5},{8,10},{10,8},{9,1... | collective-permute-start | bytes 393224 | tf_op jit(solution)/shard_map/ppermute | solution.py:102
  24.6 44.0 %copy-start.1 = (f32[2,64,128]{2,1,0:T(8,128)S(1)}, f32[2,64,128]{2,1,0:T(8,128)}, u32[]{:S(2)}) copy-start(f32[2,64,128]{2,1,0:T(8,128)} %get-tuple-element.2) | copy-start | bytes 196612
  24.6 44.0 %copy-start.6 = (f32[128]{0:T(128)S(1)}, f32[128]{0:T(128)}, u32[]{:S(2)}) copy-start(f32[128]{0:T(128)} %get-tuple-element.12) | copy-start | bytes 1540
  24.6 44.0 %copy-start.7 = (f32[128]{0:T(128)S(1)}, f32[128]{0:T(128)}, u32[]{:S(2)}) copy-start(f32[128]{0:T(128)} %get-tuple-element.13) | copy-start | bytes 1540
  24.6 44.0 %copy-start.8 = (f32[128]{0:T(128)S(1)}, f32[128]{0:T(128)}, u32[]{:S(2)}) copy-start(f32[128]{0:T(128)} %get-tuple-element.14) | copy-start | bytes 1540
  24.6 44.0 %copy-start.9 = (f32[128]{0:T(128)S(1)}, f32[128]{0:T(128)}, u32[]{:S(2)}) copy-start(f32[128]{0:T(128)} %get-tuple-element.15) | copy-start | bytes 1540
  24.6 44.0 %copy-start.10 = (f32[128]{0:T(128)S(1)}, f32[128]{0:T(128)}, u32[]{:S(2)}) copy-start(f32[128]{0:T(128)} %get-tuple-element.16) | copy-start | bytes 1540
  24.6 44.0 %copy-start.11 = (f32[128]{0:T(128)S(1)}, f32[128]{0:T(128)}, u32[]{:S(2)}) copy-start(f32[128]{0:T(128)} %get-tuple-element.17) | copy-start | bytes 1540
  24.6 44.0 %copy-start.12 = (f32[128]{0:T(128)S(1)}, f32[128]{0:T(128)}, u32[]{:S(2)}) copy-start(f32[128]{0:T(128)} %get-tuple-element.18) | copy-start | bytes 1540
  24.7 44.0 %copy-start.13 = (f32[128]{0:T(128)S(1)}, f32[128]{0:T(128)}, u32[]{:S(2)}) copy-start(f32[128]{0:T(128)} %get-tuple-element.19) | copy-start | bytes 1540
  24.7 44.0 %copy-start.14 = (f32[128]{0:T(128)S(1)}, f32[128]{0:T(128)}, u32[]{:S(2)}) copy-start(f32[128]{0:T(128)} %get-tuple-element.20) | copy-start | bytes 1540
  36.1 22.2 %copy-start.2 = (f32[4,2,64,128]{3,2,1,0:T(8,128)S(1)}, f32[4,2,64,128]{3,2,1,0:T(8,128)}, u32[]{:S(2)}) copy-start(f32[4,2,64,128]{3,2,1,0:T(8,128)} %get-tuple-element.26) | copy-start | bytes 786436
  58.6 4.3 %collective-permute-start.4 = (f32[1,64,128]{2,1,0:T(8,128)S(1)}, f32[1,64,128]{2,1,0:T(8,128)S(1)}, u32[]{:S(2)}, u32[]{:S(2)}) collective-permute-start(f32[1,64,128]{2,1,0:T(8,128)S(1)} %get-tuple-element.8), channel_id=1, source_target_pairs={{0,2},{2,4},{4,6},{6,8},{8,10},{10,12},{12,14},{14,16},{16,18},{18... | collective-permute-start | bytes 98312 | tf_op jit(solution)/shard_map/ppermute | solution.py:21
  60.9 5.2 %collective-permute-start.5 = (f32[1,64,128]{2,1,0:T(8,128)S(1)}, f32[1,64,128]{2,1,0:T(8,128)S(1)}, u32[]{:S(2)}, u32[]{:S(2)}) collective-permute-start(f32[1,64,128]{2,1,0:T(8,128)S(1)} %get-tuple-element.9), channel_id=1, source_target_pairs={{2,0},{4,2},{6,4},{8,6},{10,8},{12,10},{14,12},{16,14},{18,16},{20... | collective-permute-start | bytes 98312 | tf_op jit(solution)/shard_map/ppermute | solution.py:22
  66.1 2.4 %collective-permute-start.6 = (f32[4,1,128]{2,1,0:T(1,128)S(1)}, f32[4,1,128]{2,1,0:T(1,128)S(1)}, u32[]{:S(2)}, u32[]{:S(2)}) collective-permute-start(f32[4,1,128]{2,1,0:T(1,128)S(1)} %broadcast_select_fusion.4), channel_id=1, source_target_pairs={{0,1},{1,0},{2,3},{3,2},{4,5},{5,4},{6,7},{7,6},{8,9},{9,8},{10,11... | collective-permute-start | bytes 6152 | tf_op jit(solution)/shard_map/ppermute | solution.py:16
  (1 other events, 3.2 us)

commit v21 on v18

--- a/solution.py
+++ b/solution.py
@@ -73,8 +73,17 @@
     weights = lax.optimization_barrier(
         jnp.broadcast_to(stencil.reshape(9, 1), (9, length))
     )
-    ends = [mean_field[None, at : at + 1] + deviations[:, at : at + 1] for at in (0, width_x - 1)]
-    padded = with_halo(latent, 1, ends)
+    ends = [
+        jnp.einsum(
+            "sxyw,zw->sxyz",
+            mean_field[None, at : at + 1] + deviations[:, at : at + 1],
+            vertical_mix,
+            precision=HIGH,
+        )
+        for at in (0, width_x - 1)
+    ]
+    mixed = jnp.einsum("sxyw,zw->sxyz", latent, vertical_mix, precision=HIGH)
+    padded = with_halo(mixed, 1, ends)
     smoothed = jnp.zeros(latent.shape, jnp.float32)
     for offset_x in range(3):
         for offset_y in range(3):
@@ -83,7 +92,7 @@
                 + weights[offset_x * 3 + offset_y]
                 * padded[:, offset_x : offset_x + width_x, offset_y : offset_y + width_y]
             )
-    log_density = jnp.einsum("sxyw,zw->sxyz", smoothed, vertical_mix, precision=HIGH) + log_mean
+    log_density = smoothed + log_mean
     density = jnp.exp(log_density)
     density_b = density.astype(jnp.bfloat16).reshape(samples, width_x * width_y, length)
     line_onehot = (

time: 60.4 us -> 64.5 us (1.068)
  matrix products: 6.2 us -> 9.79 us
    dot_general x1 -> x3, matrix products: 2.13 us -> 5.07 us  [the longest x2 3.7 us: per_device(): jnp.einsum('sxyw,zw->sxyz', mean_field[None, at:at + 1] + deviations[:, a...]
    add x1 -> x0, other arithmetic: 1.72 us -> none  [per_device(): mean_field[None, at:at + 1] + deviations[:, at:at + 1]]
    convert_element_type x0 -> x1, other arithmetic: none -> 1.68 us  [per_device(): density.astype(jnp.bfloat16).reshape(samples, width_x * width_y, length)]
    reduce_sum x1, other arithmetic: 1.61 us -> 0.02 us  [per_device(): gradient = grad_latent + jnp.mean(latent, axis=0)]
    reduce_sum x1, other arithmetic: 0.01 us -> 0.92 us  [per_device(): extinction = jnp.sum(arrived, axis=0)]
    reduce_sum x1, other arithmetic: 0.01 us -> 0.76 us  [per_device(): residual_mean = jnp.mean(misfit, axis=1)]
    dot_general x1, matrix products: 0.21 us -> 0.87 us  [per_device(): jnp.einsum('pb,bsi->psi', target_onehot.astype(jnp.bfloat16), misfit_b, p...]
  transfers between devices with their start and end apart: 7 -> 7, of which waited for: 5 -> 5; matrix products, arithmetic and copies ran while one was open for 8% -> 10% of each run, Pallas kernels for 0% -> 0%
where the time goes in v21:
time: 64.5 us; the launch traced here: 64 us
  blocking collectives  22.8 us (35%)
  starting transfers between devices  13.4 us (21%)
  matrix products  9.79 us (15%)
  other arithmetic  7.66 us (12%)
  waiting for transfers between devices  6.78 us (11%)
  local copies, waits for them, and re-layouts  2.55 us (4%)
  between operations  1.03 us (2%)
    all_to_all x1, blocking collectives, per_device(): lax.all_to_all(merged, 'vh', split_axis=0, concat_axis=0, tiled=True)  11.7 us
    all_to_all x1, blocking collectives, per_device(): lax.all_to_all(spread, VOX, split_axis=0, concat_axis=0, tiled=True)  11.1 us
    ppermute x2, starting transfers between devices, exchange(): below = lax.ppermute(tail, axis, [(i, i + 1) for i in range(count - 1)])  6.59 us
    ppermute x2, waiting for transfers between devices, exchange(): above = lax.ppermute(head, axis, [(i + 1, i) for i in range(count - 1)])  4.71 us
    ppermute x2, starting transfers between devices, exchange(): above = lax.ppermute(head, axis, [(i + 1, i) for i in range(count - 1)])  4.21 us
    dot_general x2, matrix products, per_device(): jnp.einsum('sxyw,zw->sxyz', mean_field[None, at:at + 1] + deviations[:, a...  3.7 us
    ppermute x2, starting transfers between devices, exchange(): lax.ppermute(jnp.where(index == 0, tail, head), axis, [(0, 1), (1, 0)])  2.49 us
    dot_general x1, matrix products, per_device(): jnp.einsum('pij,psj->psi', responses, picked, preferred_element_type=jnp....  1.71 us
  transfers between devices with their start and end apart: 7, of which 5 were waited for; matrix products, arithmetic and copies ran while one was open for 10% of the time, Pallas kernels for 0%

profile of v21, /device:TPU:1, one launch (start us, length us, event | category | flops | bytes accessed | tf_op | source)
XLA Modules:
  0.0 64.0 jit_solution(10290010307567852894)
XLA Ops:
  0.6 0.9 %slice_bitcast_fusion.1 = (f32[64,128]{1,0:T(8,128)S(1)}, f32[64,128]{1,0:T(8,128)S(1)}) fusion(f32[2,64,128]{2,1,0:T(8,128)} %param.11), kind=kLoop, calls=%fused_computation.80 | loop fusion | bytes 131072 | tf_op jit(solution)/shard_map/add | solution.py:79
  1.6 1.9 %convolution_bitcast_fusion.1 = f32[4,1,64,128]{3,2,0,1:T(8,128)} fusion(f32[4,2,64,128]{3,2,1,0:T(8,128)} %param.12, f32[128,128]{1,0:T(8,128)} %param.14, f32[64,128]{1,0:T(8,128)S(1)} %get-tuple-element.8), kind=kOutput, calls=%fused_computation.1 | convolution fusion | flops 50364416 | bytes 360448 | tf_op jit(solution)/shard_map/sxyw,zw->sxyz/dot_general | solution.py:77
  3.4 4.5 %collective-permute-start = (f32[4,1,64,128]{3,2,0,1:T(8,128)}, f32[4,1,64,128]{3,2,0,1:T(8,128)S(1)}, u32[]{:S(2)}, u32[]{:S(2)}) collective-permute-start(f32[4,1,64,128]{3,2,0,1:T(8,128)} %convolution_bitcast_fusion.1), channel_id=1, source_target_pairs={{0,2},{2,4},{4,6},{6,8},{8,10},{10,12},{12,14},{14,16},{16,18},{18... | collective-permute-start | bytes 393224 | tf_op jit(solution)/shard_map/ppermute | solution.py:24
  8.0 1.8 %convolution_bitcast_fusion = f32[4,1,64,128]{3,2,1,0:T(8,128)} fusion(f32[4,2,64,128]{3,2,1,0:T(8,128)} %param.12, f32[128,128]{1,0:T(8,128)} %param.14, f32[64,128]{1,0:T(8,128)S(1)} %get-tuple-element.9), kind=kOutput, calls=%fused_computation | convolution fusion | flops 50364416 | bytes 360448 | tf_op jit(solution)/shard_map/sxyw,zw->sxyz/dot_general | solution.py:77
  9.8 1.9 %collective-permute-start.1 = (f32[4,1,64,128]{3,2,1,0:T(8,128)}, f32[4,1,64,128]{3,2,1,0:T(8,128)}, u32[]{:S(2)}, u32[]{:S(2)}) collective-permute-start(f32[4,1,64,128]{3,2,1,0:T(8,128)} %convolution_bitcast_fusion), channel_id=1, source_target_pairs={{2,0},{4,2},{6,4},{8,6},{10,8},{12,10},{14,12},{16,14},{18,16},{20... | collective-permute-start | bytes 393224 | tf_op jit(solution)/shard_map/ppermute | solution.py:25
  11.7 1.4 %fusion.10 = f32[4,2,64,128]{3,2,1,0:T(8,128)S(1)} fusion(f32[4,2,64,128]{3,2,1,0:T(8,128)} %param.12, f32[2,64,128]{2,1,0:T(8,128)} %param.11, f32[128,128]{1,0:T(8,128)} %param.14), kind=kOutput, calls=%fused_computation.24 | convolution fusion | flops 100728832 | bytes 655360 | tf_op jit(solution)/shard_map/sxyw,zw->sxyz/dot_general | solution.py:85
  13.1 0.8 %broadcast_in_dim.10 = f32[9]{0:T(128)S(1)} reshape(f32[3,3]{1,0:T(4,128)} %param.13) | data formatting | bytes 72 | tf_op jit(solution)/shard_map/broadcast_in_dim | solution.py:74
  14.6 1.8 %collective-permute-done.1 = f32[4,1,64,128]{3,2,1,0:T(8,128)} collective-permute-done((f32[4,1,64,128]{3,2,1,0:T(8,128)}, f32[4,1,64,128]{3,2,1,0:T(8,128)}, u32[]{:S(2)}, u32[]{:S(2)}) %collective-permute-start.1) | collective-permute-done | bytes 131104 | tf_op jit(solution)/shard_map/ppermute | solution.py:25
  17.2 1.3 %collective-permute-start.2 = (f32[4,4,1,128]{3,2,1,0:T(1,128)S(1)}, f32[4,4,1,128]{3,2,1,0:T(1,128)S(1)}, u32[]{:S(2)}, u32[]{:S(2)}) collective-permute-start(f32[4,4,1,128]{3,2,1,0:T(1,128)S(1)} %broadcast_select_fusion.1), channel_id=1, source_target_pairs={{0,1},{1,0},{2,3},{3,2},{4,5},{5,4},{6,7},{7,6},{8,9},{9,8},{10,11... | collective-permute-start | bytes 24584 | tf_op jit(solution)/shard_map/ppermute | solution.py:19
  18.4 1.2 %bitcast_add_fusion.1 = s32[96]{0:T(128)} fusion(s32[96]{0:T(128)} %param.19, s32[96,1]{0,1:T(1,128)} %param.18), kind=kLoop, calls=%fused_computation.111 | loop fusion | flops 192 | bytes 1152 | tf_op jit(solution)/shard_map/add | solution.py:105
  19.7 1.0 %pad_maximum_fusion = f32[4,4,66,128]{3,2,1,0:T(8,128)S(1)} fusion(f32[4,4,1,128]{3,2,1,0:T(1,128)S(1)} %get-tuple-element.22, f32[4,1,64,128]{3,2,1,0:T(8,128)} %collective-permute-done.1, f32[4,2,64,128]{3,2,1,0:T(8,128)S(1)} %fusion.10, f32[4,1,64,128]{3,2,1,0:T(8,128)S(1)} %bitcast.76, f32[4,4,1,128]{3,2,1,0:T(1,128)S(1)} %get-tuple-element.21), kind=kLoop, calls=%fused_computation.2 | loop fusion | flops 540672 | bytes 1081344 | tf_op jit(solution)/shard_map/concatenate | solution.py:26
  20.7 1.7 %fusion.61 = (bf16[4,2,64,128]{3,2,1,0:T(8,128)(2,1)S(1)}, f32[4,2,64,128]{3,2,1,0:T(8,128)}) fusion(f32[128]{0:T(128)} %param.15, f32[4,4,66,128]{3,2,1,0:T(8,128)S(1)} %pad_maximum_fusion, f32[128]{0:T(128)} %get-tuple-element.13, f32[128]{0:T(128)} %get-tuple-element.14, f32[128]{0:T(128)} %get-tuple-element.15, f32[128]{0:T(128)} %get-tuple-element.16, ...), kind=kLoop, calls=%fused_computation.115 | loop fusion | flops 1245184 | bytes 2757632 | tf_op jit(solution)/shard_map/convert_element_type | solution.py:97
  22.6 1.7 %fusion.25 = f32[96,4,128]{2,1,0:T(4,128)S(1)} fusion(bf16[96,128,128]{2,1,0:T(8,128)(2,1)S(1)} %copy-done, bf16[96,4,128]{2,0,1:T(8,128)(2,1)S(1)} %fusion.52), kind=kOutput, calls=%fused_computation.44 | convolution fusion | flops 12582912 | bytes 3440640 | tf_op jit(solution)/shard_map/pij,psj->psi/dot_general | solution.py:104
  24.9 1.3 %collective-permute-done.3 = f32[8,8,4,128]{3,1,2,0:T(8,128)S(1)} collective-permute-done((f32[8,8,4,128]{3,1,2,0:T(8,128)S(1)}, f32[8,8,4,128]{3,1,2,0:T(8,128)S(1)}, u32[]{:S(2)}, u32[]{:S(2)}) %collective-permute-start.3) | collective-permute-done | bytes 131104 | tf_op jit(solution)/shard_map/ppermute | solution.py:115
  26.3 11.7 %all_to_all.10 = f32[8,8,4,128]{3,1,2,0:T(8,128)} all-to-all(f32[8,8,4,128]{3,1,2,0:T(8,128)S(1)} %bitcast_add_fusion), channel_id=1, replica_groups=mesh['vh'=8,'vc'=2,'star'=2] {'vh'}, dimensions={0} | all-to-all | bytes 262144 | tf_op jit(solution)/shard_map/all_to_all | solution.py:116
  37.9 0.9 %reduce_sum.36 = f32[8,4,128]{2,0,1:T(8,128)S(1)} reduce(f32[8,8,4,128]{3,1,2,0:T(8,128)} %all_to_all.10, f32[]{:T(128)} %constant.26.clone.1), dimensions={0}, to_apply=%region_0.1 | reduce | flops 28672 | bytes 147460 | tf_op jit(solution)/shard_map/reduce_sum | solution.py:117
  38.9 0.8 %fusion.58 = (f32[8,128]{1,0:T(8,128)S(1)}, bf16[8,4,128]{2,0,1:T(8,128)(2,1)S(1)}) fusion(f32[8,4,128]{2,0,1:T(8,128)S(1)} %reduce_sum.36, f32[8,128]{1,0:T(8,128)} %param.20, f32[8,128]{1,0:T(8,128)} %param.21), kind=kLoop, calls=%fused_computation.92 | loop fusion | flops 15360 | bytes 36864 | tf_op jit(solution)/shard_map/reduce_sum | solution.py:119
  39.8 11.1 %all_to_all.11 = bf16[16,8,4,128]{3,2,1,0:T(4,128)(2,1)S(1)} all-to-all(bf16[16,8,4,128]{3,2,1,0:T(4,128)(2,1)S(1)} %broadcast_in_dim.13), channel_id=1, replica_groups=mesh['vh'=8,'vc'=2,'star'=2] {'vh','vc'}, dimensions={0} | all-to-all | bytes 262144 | tf_op jit(solution)/shard_map/all_to_all | solution.py:122
  50.9 0.9 %fusion.18 = bf16[96,4,128]{2,0,1:T(8,128)(2,1)S(1)} fusion(bf16[128,4,128]{2,1,0:T(4,128)(2,1)S(1)} %bitcast.78, s32[96]{0:T(128)} %bitcast_add_fusion.1), kind=kOutput, calls=%fused_computation.36 | convolution fusion | flops 12619776 | bytes 229760 | tf_op jit(solution)/shard_map/pb,bsi->psi/dot_general | solution.py:125
  51.8 0.9 %fusion.26 = f32[96,4,128]{2,1,0:T(4,128)S(1)} fusion(bf16[96,128,128]{2,1,0:T(8,128)(2,1)S(1)} %copy-done, bf16[96,4,128]{2,0,1:T(8,128)(2,1)S(1)} %fusion.18), kind=kOutput, calls=%fused_computation.45 | convolution fusion | flops 12582912 | bytes 3440640 | tf_op jit(solution)/shard_map/pij,psi->psj/dot_general | solution.py:128
  53.4 2.1 %collective-permute-start.4 = (f32[1,64,128]{2,1,0:T(8,128)S(1)}, f32[1,64,128]{2,1,0:T(8,128)S(1)}, u32[]{:S(2)}, u32[]{:S(2)}) collective-permute-start(f32[1,64,128]{2,1,0:T(8,128)S(1)} %get-tuple-element.6), channel_id=1, source_target_pairs={{0,2},{2,4},{4,6},{6,8},{8,10},{10,12},{12,14},{14,16},{16,18},{18... | collective-permute-start | bytes 98312 | tf_op jit(solution)/shard_map/ppermute | solution.py:24
  55.5 2.3 %collective-permute-start.5 = (f32[1,64,128]{2,1,0:T(8,128)S(1)}, f32[1,64,128]{2,1,0:T(8,128)S(1)}, u32[]{:S(2)}, u32[]{:S(2)}) collective-permute-start(f32[1,64,128]{2,1,0:T(8,128)S(1)} %get-tuple-element.7), channel_id=1, source_target_pairs={{2,0},{4,2},{6,4},{8,6},{10,8},{12,10},{14,12},{16,14},{18,16},{20... | collective-permute-start | bytes 98312 | tf_op jit(solution)/shard_map/ppermute | solution.py:25
  57.8 2.9 %collective-permute-done.5 = f32[1,64,128]{2,1,0:T(8,128)S(1)} collective-permute-done((f32[1,64,128]{2,1,0:T(8,128)S(1)}, f32[1,64,128]{2,1,0:T(8,128)S(1)}, u32[]{:S(2)}, u32[]{:S(2)}) %collective-permute-start.5) | collective-permute-done | bytes 32800 | tf_op jit(solution)/shard_map/ppermute | solution.py:25
  60.7 1.2 %collective-permute-start.6 = (f32[4,1,128]{2,1,0:T(1,128)S(1)}, f32[4,1,128]{2,1,0:T(1,128)S(1)}, u32[]{:S(2)}, u32[]{:S(2)}) collective-permute-start(f32[4,1,128]{2,1,0:T(1,128)S(1)} %broadcast_select_fusion.4), channel_id=1, source_target_pairs={{0,1},{1,0},{2,3},{3,2},{4,5},{5,4},{6,7},{7,6},{8,9},{9,8},{10,11... | collective-permute-start | bytes 6152 | tf_op jit(solution)/shard_map/ppermute | solution.py:19
  (60 shorter events, 5.0 us)
Async XLA Ops:
  0.6 22.0 %copy-start = (bf16[96,128,128]{2,1,0:T(8,128)(2,1)S(1)}, bf16[96,128,128]{2,1,0:T(8,128)(2,1)}, u32[]{:S(2)}) copy-start(bf16[96,128,128]{2,1,0:T(8,128)(2,1)} %param.16) | copy-start | bytes 9437188
  3.4 11.1 %collective-permute-start = (f32[4,1,64,128]{3,2,0,1:T(8,128)}, f32[4,1,64,128]{3,2,0,1:T(8,128)S(1)}, u32[]{:S(2)}, u32[]{:S(2)}) collective-permute-start(f32[4,1,64,128]{3,2,0,1:T(8,128)} %convolution_bitcast_fusion.1), channel_id=1, source_target_pairs={{0,2},{2,4},{4,6},{6,8},{8,10},{10,12},{12,14},{14,16},{16,18},{18... | collective-permute-start | bytes 393224 | tf_op jit(solution)/shard_map/ppermute | solution.py:24
  9.8 6.6 %collective-permute-start.1 = (f32[4,1,64,128]{3,2,1,0:T(8,128)}, f32[4,1,64,128]{3,2,1,0:T(8,128)}, u32[]{:S(2)}, u32[]{:S(2)}) collective-permute-start(f32[4,1,64,128]{3,2,1,0:T(8,128)} %convolution_bitcast_fusion), channel_id=1, source_target_pairs={{2,0},{4,2},{6,4},{8,6},{10,8},{12,10},{14,12},{16,14},{18,16},{20... | collective-permute-start | bytes 393224 | tf_op jit(solution)/shard_map/ppermute | solution.py:25
  17.2 2.6 %collective-permute-start.2 = (f32[4,4,1,128]{3,2,1,0:T(1,128)S(1)}, f32[4,4,1,128]{3,2,1,0:T(1,128)S(1)}, u32[]{:S(2)}, u32[]{:S(2)}) collective-permute-start(f32[4,4,1,128]{3,2,1,0:T(1,128)S(1)} %broadcast_select_fusion.1), channel_id=1, source_target_pairs={{0,1},{1,0},{2,3},{3,2},{4,5},{5,4},{6,7},{7,6},{8,9},{9,8},{10,11... | collective-permute-start | bytes 24584 | tf_op jit(solution)/shard_map/ppermute | solution.py:19
  19.6 2.8 %copy-start.14 = (s32[96]{0:T(128)S(1)}, s32[96]{0:T(128)}, u32[]{:S(2)}) copy-start(s32[96]{0:T(128)} %param.17) | copy-start | bytes 1156
  20.7 3.6 %copy-start.16 = (s32[96]{0:T(128)S(1)}, s32[96]{0:T(128)}, u32[]{:S(2)}) copy-start(s32[96]{0:T(128)} %bitcast_add_fusion.1) | copy-start | bytes 1156
  24.8 28.4 %copy-start.3 = (f32[128,128]{1,0:T(8,128)S(1)}, f32[128,128]{1,0:T(8,128)}, u32[]{:S(2)}) copy-start(f32[128,128]{1,0:T(8,128)} %param.14) | copy-start | bytes 196612
  24.8 1.4 %collective-permute-start.3 = (f32[8,8,4,128]{3,1,2,0:T(8,128)S(1)}, f32[8,8,4,128]{3,1,2,0:T(8,128)S(1)}, u32[]{:S(2)}, u32[]{:S(2)}) collective-permute-start(f32[8,8,4,128]{3,1,2,0:T(8,128)S(1)} %bitcast.79), channel_id=1, source_target_pairs={{0,2},{2,0},{1,3},{3,1},{4,6},{6,4},{5,7},{7,5},{8,10},{10,8},{9,1... | collective-permute-start | bytes 393224 | tf_op jit(solution)/shard_map/ppermute | solution.py:115
  26.2 31.5 %copy-start.1 = (f32[4,2,64,128]{3,2,1,0:T(8,128)S(1)}, f32[4,2,64,128]{3,2,1,0:T(8,128)}, u32[]{:S(2)}) copy-start(f32[4,2,64,128]{3,2,1,0:T(8,128)} %param.12) | copy-start | bytes 786436
  26.2 31.5 %copy-start.4 = (f32[2,64,128]{2,1,0:T(8,128)S(1)}, f32[2,64,128]{2,1,0:T(8,128)}, u32[]{:S(2)}) copy-start(f32[2,64,128]{2,1,0:T(8,128)} %param.11) | copy-start | bytes 196612
  38.9 13.9 %copy-start.15 = (s32[96]{0:T(128)S(1)}, s32[96]{0:T(128)}, u32[]{:S(2)}) copy-start(s32[96]{0:T(128)} %param.17) | copy-start | bytes 1156
  38.9 14.2 %copy-start.2 = (f32[4,2,64,128]{3,2,1,0:T(8,128)S(1)}, f32[4,2,64,128]{3,2,1,0:T(8,128)}, u32[]{:S(2)}) copy-start(f32[4,2,64,128]{3,2,1,0:T(8,128)} %get-tuple-element.3) | copy-start | bytes 786436
  39.6 23.5 %copy-start.5 = (f32[128]{0:T(128)S(1)}, f32[128]{0:T(128)}, u32[]{:S(2)}) copy-start(f32[128]{0:T(128)} %get-tuple-element.12) | copy-start | bytes 1540
  39.7 23.5 %copy-start.6 = (f32[128]{0:T(128)S(1)}, f32[128]{0:T(128)}, u32[]{:S(2)}) copy-start(f32[128]{0:T(128)} %get-tuple-element.13) | copy-start | bytes 1540
  39.7 23.5 %copy-start.7 = (f32[128]{0:T(128)S(1)}, f32[128]{0:T(128)}, u32[]{:S(2)}) copy-start(f32[128]{0:T(128)} %get-tuple-element.14) | copy-start | bytes 1540
  39.7 23.5 %copy-start.8 = (f32[128]{0:T(128)S(1)}, f32[128]{0:T(128)}, u32[]{:S(2)}) copy-start(f32[128]{0:T(128)} %get-tuple-element.15) | copy-start | bytes 1540
  39.7 23.5 %copy-start.9 = (f32[128]{0:T(128)S(1)}, f32[128]{0:T(128)}, u32[]{:S(2)}) copy-start(f32[128]{0:T(128)} %get-tuple-element.16) | copy-start | bytes 1540
  39.7 23.5 %copy-start.10 = (f32[128]{0:T(128)S(1)}, f32[128]{0:T(128)}, u32[]{:S(2)}) copy-start(f32[128]{0:T(128)} %get-tuple-element.17) | copy-start | bytes 1540
  39.7 23.5 %copy-start.11 = (f32[128]{0:T(128)S(1)}, f32[128]{0:T(128)}, u32[]{:S(2)}) copy-start(f32[128]{0:T(128)} %get-tuple-element.18) | copy-start | bytes 1540
  39.7 23.5 %copy-start.12 = (f32[128]{0:T(128)S(1)}, f32[128]{0:T(128)}, u32[]{:S(2)}) copy-start(f32[128]{0:T(128)} %get-tuple-element.19) | copy-start | bytes 1540
  39.7 23.5 %copy-start.13 = (f32[128]{0:T(128)S(1)}, f32[128]{0:T(128)}, u32[]{:S(2)}) copy-start(f32[128]{0:T(128)} %get-tuple-element.20) | copy-start | bytes 1540
  53.4 4.4 %collective-permute-start.4 = (f32[1,64,128]{2,1,0:T(8,128)S(1)}, f32[1,64,128]{2,1,0:T(8,128)S(1)}, u32[]{:S(2)}, u32[]{:S(2)}) collective-permute-start(f32[1,64,128]{2,1,0:T(8,128)S(1)} %get-tuple-element.6), channel_id=1, source_target_pairs={{0,2},{2,4},{4,6},{6,8},{8,10},{10,12},{12,14},{14,16},{16,18},{18... | collective-permute-start | bytes 98312 | tf_op jit(solution)/shard_map/ppermute | solution.py:24
  55.5 5.2 %collective-permute-start.5 = (f32[1,64,128]{2,1,0:T(8,128)S(1)}, f32[1,64,128]{2,1,0:T(8,128)S(1)}, u32[]{:S(2)}, u32[]{:S(2)}) collective-permute-start(f32[1,64,128]{2,1,0:T(8,128)S(1)} %get-tuple-element.7), channel_id=1, source_target_pairs={{2,0},{4,2},{6,4},{8,6},{10,8},{12,10},{14,12},{16,14},{18,16},{20... | collective-permute-start | bytes 98312 | tf_op jit(solution)/shard_map/ppermute | solution.py:25
  60.7 2.4 %collective-permute-start.6 = (f32[4,1,128]{2,1,0:T(1,128)S(1)}, f32[4,1,128]{2,1,0:T(1,128)S(1)}, u32[]{:S(2)}, u32[]{:S(2)}) collective-permute-start(f32[4,1,128]{2,1,0:T(1,128)S(1)} %broadcast_select_fusion.4), channel_id=1, source_target_pairs={{0,1},{1,0},{2,3},{3,2},{4,5},{5,4},{6,7},{7,6},{8,9},{9,8},{10,11... | collective-permute-start | bytes 6152 | tf_op jit(solution)/shard_map/ppermute | solution.py:19

commit v22 on v18

--- a/solution.py
+++ b/solution.py
@@ -73,8 +73,8 @@
     weights = lax.optimization_barrier(
         jnp.broadcast_to(stencil.reshape(9, 1), (9, length))
     )
-    ends = [mean_field[None, at : at + 1] + deviations[:, at : at + 1] for at in (0, width_x - 1)]
-    padded = with_halo(latent, 1, ends)
+    mixed = jnp.einsum("sxyw,zw->sxyz", latent, vertical_mix, precision=HIGH)
+    padded = with_halo(mixed, 1)
     smoothed = jnp.zeros(latent.shape, jnp.float32)
     for offset_x in range(3):
         for offset_y in range(3):
@@ -83,7 +83,7 @@
                 + weights[offset_x * 3 + offset_y]
                 * padded[:, offset_x : offset_x + width_x, offset_y : offset_y + width_y]
             )
-    log_density = jnp.einsum("sxyw,zw->sxyz", smoothed, vertical_mix, precision=HIGH) + log_mean
+    log_density = smoothed + log_mean
     density = jnp.exp(log_density)
     density_b = density.astype(jnp.bfloat16).reshape(samples, width_x * width_y, length)
     line_onehot = (

time: 60.4 us -> 60.2 us (level)
  other arithmetic: 7.64 us -> 6.06 us
  waiting for transfers between devices: 6.59 us -> 8.15 us
    add x1 -> x0, other arithmetic: 1.72 us -> none  [per_device(): mean_field[None, at:at + 1] + deviations[:, at:at + 1]]
    reduce_sum x1, other arithmetic: 1.61 us -> 0.02 us  [per_device(): gradient = grad_latent + jnp.mean(latent, axis=0)]
    ppermute x2, waiting for transfers between devices: 4.53 us -> 6.08 us  [exchange(): above = lax.ppermute(head, axis, [(i + 1, i) for i in range(count - 1)])]
    convert_element_type x0 -> x1, other arithmetic: none -> 0.98 us  [per_device(): density.astype(jnp.bfloat16).reshape(samples, width_x * width_y, length)]
    add x1 -> x0, local copies, waits for them, and re-layouts: 0.93 us -> none  [per_device(): mean_field[None, at:at + 1] + deviations[:, at:at + 1]]
    reduce_sum x1, other arithmetic: 0.01 us -> 0.76 us  [per_device(): residual_mean = jnp.mean(misfit, axis=1)]
    slice x1 -> x2, local copies, waits for them, and re-layouts: 0.01 us -> 0.72 us  [exchange(): tail = lax.slice_in_dim(cells, size - 1, size, axis=dim)]
    dot_general x1, matrix products: 0.21 us -> 0.87 us  [per_device(): jnp.einsum('pb,bsi->psi', target_onehot.astype(jnp.bfloat16), misfit_b, p...]
  transfers between devices with their start and end apart: 7 -> 7, of which waited for: 5 -> 5; matrix products, arithmetic and copies ran while one was open for 8% -> 5% of each run, Pallas kernels for 0% -> 0%
where the time goes in v22:
time: 60.2 us; the launch traced here: 59.7 us
  blocking collectives  22.6 us (38%)
  starting transfers between devices  13.4 us (22%)
  waiting for transfers between devices  8.15 us (14%)
  matrix products  6.22 us (10%)
  other arithmetic  6.06 us (10%)
  local copies, waits for them, and re-layouts  2.33 us (4%)
  between operations  1.03 us (2%)
    all_to_all x1, blocking collectives, per_device(): lax.all_to_all(merged, 'vh', split_axis=0, concat_axis=0, tiled=True)  11.4 us
    all_to_all x1, blocking collectives, per_device(): lax.all_to_all(spread, VOX, split_axis=0, concat_axis=0, tiled=True)  11.1 us
    ppermute x2, starting transfers between devices, exchange(): below = lax.ppermute(tail, axis, [(i, i + 1) for i in range(count - 1)])  6.59 us
    ppermute x2, waiting for transfers between devices, exchange(): above = lax.ppermute(head, axis, [(i + 1, i) for i in range(count - 1)])  6.08 us
    ppermute x2, starting transfers between devices, exchange(): above = lax.ppermute(head, axis, [(i + 1, i) for i in range(count - 1)])  4.22 us
    ppermute x2, starting transfers between devices, exchange(): lax.ppermute(jnp.where(index == 0, tail, head), axis, [(0, 1), (1, 0)])  2.49 us
    dot_general x1, matrix products, per_device(): jnp.einsum('pij,psj->psi', responses, picked, preferred_element_type=jnp....  1.71 us
    dot_general x1, matrix products, per_device(): mixed = jnp.einsum('sxyw,zw->sxyz', latent, vertical_mix, precision=HIGH)  1.51 us
  transfers between devices with their start and end apart: 7, of which 5 were waited for; matrix products, arithmetic and copies ran while one was open for 5% of the time, Pallas kernels for 0%

profile of v22, /device:TPU:1, one launch (start us, length us, event | category | flops | bytes accessed | tf_op | source)
XLA Modules:
  0.0 59.7 jit_solution(10547663822181290411)
XLA Ops:
  0.6 1.5 %fusion.10 = f32[4,2,64,128]{3,2,1,0:T(8,128)S(1)} fusion(f32[4,2,64,128]{3,2,1,0:T(8,128)} %param.12, f32[2,64,128]{2,1,0:T(8,128)} %param.11, f32[128,128]{1,0:T(8,128)} %param.14), kind=kOutput, calls=%fused_computation.22 | convolution fusion | flops 100728832 | bytes 655360 | tf_op jit(solution)/shard_map/sxyw,zw->sxyz/dot_general | solution.py:76
  2.2 0.7 %fusion.53 = (f32[4,1,64,128]{3,2,1,0:T(8,128)}, f32[4,1,64,128]{3,2,1,0:T(8,128)}) fusion(f32[4,2,64,128]{3,2,1,0:T(8,128)S(1)} %fusion.10), kind=kLoop, calls=%fused_computation.102 | loop fusion | bytes 524288 | tf_op jit(solution)/shard_map/slice | solution.py:14
  2.9 4.5 %collective-permute-start = (f32[4,1,64,128]{3,2,1,0:T(8,128)}, f32[4,1,64,128]{3,2,1,0:T(8,128)S(1)}, u32[]{:S(2)}, u32[]{:S(2)}) collective-permute-start(f32[4,1,64,128]{3,2,1,0:T(8,128)} %get-tuple-element.6), channel_id=1, source_target_pairs={{0,2},{2,4},{4,6},{6,8},{8,10},{10,12},{12,14},{14,16},{16,18},{18... | collective-permute-start | bytes 393224 | tf_op jit(solution)/shard_map/ppermute | solution.py:24
  7.4 1.9 %collective-permute-start.1 = (f32[4,1,64,128]{3,2,1,0:T(8,128)}, f32[4,1,64,128]{3,2,1,0:T(8,128)}, u32[]{:S(2)}, u32[]{:S(2)}) collective-permute-start(f32[4,1,64,128]{3,2,1,0:T(8,128)} %get-tuple-element.7), channel_id=1, source_target_pairs={{2,0},{4,2},{6,4},{8,6},{10,8},{12,10},{14,12},{16,14},{18,16},{20... | collective-permute-start | bytes 393224 | tf_op jit(solution)/shard_map/ppermute | solution.py:25
  9.3 0.8 %broadcast_in_dim.10 = f32[9]{0:T(128)S(1)} reshape(f32[3,3]{1,0:T(4,128)} %param.13) | data formatting | bytes 72 | tf_op jit(solution)/shard_map/broadcast_in_dim | solution.py:74
  10.8 3.2 %collective-permute-done.1 = f32[4,1,64,128]{3,2,1,0:T(8,128)} collective-permute-done((f32[4,1,64,128]{3,2,1,0:T(8,128)}, f32[4,1,64,128]{3,2,1,0:T(8,128)}, u32[]{:S(2)}, u32[]{:S(2)}) %collective-permute-start.1) | collective-permute-done | bytes 131104 | tf_op jit(solution)/shard_map/ppermute | solution.py:25
  14.0 0.7 %broadcast_select_fusion.1 = f32[4,4,1,128]{3,2,1,0:T(1,128)S(1)} fusion(pred[]{:T(512)S(6)} %eq.17, f32[4,1,64,128]{3,2,1,0:T(8,128)} %collective-permute-done.1, f32[4,2,64,128]{3,2,1,0:T(8,128)S(1)} %fusion.10, f32[4,1,64,128]{3,2,1,0:T(8,128)S(1)} %collective-permute-done), kind=kLoop, calls=%fused_computation.76 | loop fusion | flops 10240 | bytes 532481 | tf_op jit(solution)/shard_map/jit(_where)/select_n | solution.py:19
  14.8 1.3 %collective-permute-start.2 = (f32[4,4,1,128]{3,2,1,0:T(1,128)S(1)}, f32[4,4,1,128]{3,2,1,0:T(1,128)S(1)}, u32[]{:S(2)}, u32[]{:S(2)}) collective-permute-start(f32[4,4,1,128]{3,2,1,0:T(1,128)S(1)} %broadcast_select_fusion.1), channel_id=1, source_target_pairs={{0,1},{1,0},{2,3},{3,2},{4,5},{5,4},{6,7},{7,6},{8,9},{9,8},{10,11... | collective-permute-start | bytes 24584 | tf_op jit(solution)/shard_map/ppermute | solution.py:19
  16.0 1.2 %bitcast_add_fusion.1 = s32[96]{0:T(128)} fusion(s32[96]{0:T(128)} %param.19, s32[96,1]{0,1:T(1,128)} %param.18), kind=kLoop, calls=%fused_computation.97 | loop fusion | flops 192 | bytes 1152 | tf_op jit(solution)/shard_map/add | solution.py:96
  17.3 1.0 %pad_maximum_fusion = f32[4,4,66,128]{3,2,1,0:T(8,128)S(1)} fusion(f32[4,4,1,128]{3,2,1,0:T(1,128)S(1)} %get-tuple-element.22, f32[4,1,64,128]{3,2,1,0:T(8,128)} %collective-permute-done.1, f32[4,2,64,128]{3,2,1,0:T(8,128)S(1)} %fusion.10, f32[4,1,64,128]{3,2,1,0:T(8,128)S(1)} %collective-permute-done, f32[4,4,1,128]{3,2,1,0:T(1,128)S(1)} %get-tuple-element.21), kind=kLoop, calls=%fused_computation | loop fusion | flops 540672 | bytes 1081344 | tf_op jit(solution)/shard_map/concatenate | solution.py:26
  18.3 1.0 %fusion.51 = (bf16[4,2,64,128]{3,2,1,0:T(8,128)(2,1)S(1)}, f32[4,2,64,128]{3,2,1,0:T(8,128)S(1)}) fusion(f32[128]{0:T(128)} %param.15, f32[4,4,66,128]{3,2,1,0:T(8,128)S(1)} %pad_maximum_fusion, f32[128]{0:T(128)} %get-tuple-element.13, f32[128]{0:T(128)} %get-tuple-element.14, f32[128]{0:T(128)} %get-tuple-element.15, f32[128]{0:T(128)} %get-tuple-element.16, ...), kind=kLoop, calls=%fused_computation.101 | loop fusion | flops 1245184 | bytes 2757632 | tf_op jit(solution)/shard_map/convert_element_type | solution.py:88
  19.5 1.7 %fusion.19 = f32[96,4,128]{2,1,0:T(4,128)S(1)} fusion(bf16[96,128,128]{2,1,0:T(8,128)(2,1)S(1)} %copy-done, bf16[96,4,128]{2,0,1:T(8,128)(2,1)S(1)} %fusion.42), kind=kOutput, calls=%fused_computation.36 | convolution fusion | flops 12582912 | bytes 3440640 | tf_op jit(solution)/shard_map/pij,psj->psi/dot_general | solution.py:95
  21.8 1.3 %collective-permute-done.3 = f32[8,8,4,128]{3,1,2,0:T(8,128)S(1)} collective-permute-done((f32[8,8,4,128]{3,1,2,0:T(8,128)S(1)}, f32[8,8,4,128]{3,1,2,0:T(8,128)S(1)}, u32[]{:S(2)}, u32[]{:S(2)}) %collective-permute-start.3) | collective-permute-done | bytes 131104 | tf_op jit(solution)/shard_map/ppermute | solution.py:106
  23.2 11.4 %all_to_all.10 = f32[8,8,4,128]{3,1,2,0:T(8,128)S(1)} all-to-all(f32[8,8,4,128]{3,1,2,0:T(8,128)S(1)} %bitcast_add_fusion), channel_id=1, replica_groups=mesh['vh'=8,'vc'=2,'star'=2] {'vh'}, dimensions={0} | all-to-all | bytes 262144 | tf_op jit(solution)/shard_map/all_to_all | solution.py:107
  34.7 0.8 %fusion.48 = (f32[8,128]{1,0:T(8,128)S(1)}, bf16[8,4,128]{2,0,1:T(8,128)(2,1)S(1)}) fusion(f32[8,4,128]{2,0,1:T(8,128)S(1)} %reduce_sum.36, f32[8,128]{1,0:T(8,128)} %param.20, f32[8,128]{1,0:T(8,128)} %param.21), kind=kLoop, calls=%fused_computation.78 | loop fusion | flops 15360 | bytes 36864 | tf_op jit(solution)/shard_map/reduce_sum | solution.py:110
  35.6 11.1 %all_to_all.11 = bf16[16,8,4,128]{3,2,1,0:T(4,128)(2,1)S(1)} all-to-all(bf16[16,8,4,128]{3,2,1,0:T(4,128)(2,1)S(1)} %broadcast_in_dim.13), channel_id=1, replica_groups=mesh['vh'=8,'vc'=2,'star'=2] {'vh','vc'}, dimensions={0} | all-to-all | bytes 262144 | tf_op jit(solution)/shard_map/all_to_all | solution.py:113
  46.7 0.9 %fusion.16 = bf16[96,4,128]{2,0,1:T(8,128)(2,1)S(1)} fusion(bf16[128,4,128]{2,1,0:T(4,128)(2,1)S(1)} %bitcast.57, s32[96]{0:T(128)} %bitcast_add_fusion.1), kind=kOutput, calls=%fused_computation.32 | convolution fusion | flops 12619776 | bytes 229760 | tf_op jit(solution)/shard_map/pb,bsi->psi/dot_general | solution.py:116
  47.6 0.9 %fusion.20 = f32[96,4,128]{2,1,0:T(4,128)S(1)} fusion(bf16[96,128,128]{2,1,0:T(8,128)(2,1)S(1)} %copy-done, bf16[96,4,128]{2,0,1:T(8,128)(2,1)S(1)} %fusion.16), kind=kOutput, calls=%fused_computation.37 | convolution fusion | flops 12582912 | bytes 3440640 | tf_op jit(solution)/shard_map/pij,psi->psj/dot_general | solution.py:119
  49.2 2.1 %collective-permute-start.4 = (f32[1,64,128]{2,1,0:T(8,128)S(1)}, f32[1,64,128]{2,1,0:T(8,128)S(1)}, u32[]{:S(2)}, u32[]{:S(2)}) collective-permute-start(f32[1,64,128]{2,1,0:T(8,128)S(1)} %get-tuple-element.8), channel_id=1, source_target_pairs={{0,2},{2,4},{4,6},{6,8},{8,10},{10,12},{12,14},{14,16},{16,18},{18... | collective-permute-start | bytes 98312 | tf_op jit(solution)/shard_map/ppermute | solution.py:24
  51.2 2.3 %collective-permute-start.5 = (f32[1,64,128]{2,1,0:T(8,128)S(1)}, f32[1,64,128]{2,1,0:T(8,128)S(1)}, u32[]{:S(2)}, u32[]{:S(2)}) collective-permute-start(f32[1,64,128]{2,1,0:T(8,128)S(1)} %get-tuple-element.9), channel_id=1, source_target_pairs={{2,0},{4,2},{6,4},{8,6},{10,8},{12,10},{14,12},{16,14},{18,16},{20... | collective-permute-start | bytes 98312 | tf_op jit(solution)/shard_map/ppermute | solution.py:25
  53.6 2.9 %collective-permute-done.5 = f32[1,64,128]{2,1,0:T(8,128)S(1)} collective-permute-done((f32[1,64,128]{2,1,0:T(8,128)S(1)}, f32[1,64,128]{2,1,0:T(8,128)S(1)}, u32[]{:S(2)}, u32[]{:S(2)}) %collective-permute-start.5) | collective-permute-done | bytes 32800 | tf_op jit(solution)/shard_map/ppermute | solution.py:25
  56.5 1.2 %collective-permute-start.6 = (f32[4,1,128]{2,1,0:T(1,128)S(1)}, f32[4,1,128]{2,1,0:T(1,128)S(1)}, u32[]{:S(2)}, u32[]{:S(2)}) collective-permute-start(f32[4,1,128]{2,1,0:T(1,128)S(1)} %broadcast_select_fusion.4), channel_id=1, source_target_pairs={{0,1},{1,0},{2,3},{3,2},{4,5},{5,4},{6,7},{7,6},{8,9},{9,8},{10,11... | collective-permute-start | bytes 6152 | tf_op jit(solution)/shard_map/ppermute | solution.py:19
  58.3 0.6 %collective-permute-done.6 = f32[4,1,128]{2,1,0:T(1,128)S(1)} collective-permute-done((f32[4,1,128]{2,1,0:T(1,128)S(1)}, f32[4,1,128]{2,1,0:T(1,128)S(1)}, u32[]{:S(2)}, u32[]{:S(2)}) %collective-permute-start.6) | collective-permute-done | bytes 2080 | tf_op jit(solution)/shard_map/ppermute | solution.py:19
  59.0 0.7 %fusion.22 = f32[2,64,128]{2,1,0:T(8,128)} fusion(f32[4,66,128]{2,1,0:T(8,128)S(1)} %pad_maximum_fusion.1, f32[2,64,128]{2,1,0:T(8,128)S(1)} %add_reduce_fusion, f32[128]{0:T(128)S(1)} %copy-done.5, f32[128]{0:T(128)S(1)} %copy-done.6, f32[128]{0:T(128)S(1)} %copy-done.7, f32[128]{0:T(128)S(1)} %copy-done.8, f32[128]{0:T(128)S(1)} %copy-done.9, ...), kind=kLoop, calls=%fused_computation.40 | loop fusion | flops 311296 | bytes 725504 | tf_op jit(solution)/shard_map/add | solution.py:136
  (56 shorter events, 3.0 us)
Async XLA Ops:
  0.6 18.9 %copy-start = (bf16[96,128,128]{2,1,0:T(8,128)(2,1)S(1)}, bf16[96,128,128]{2,1,0:T(8,128)(2,1)}, u32[]{:S(2)}) copy-start(bf16[96,128,128]{2,1,0:T(8,128)(2,1)} %param.16) | copy-start | bytes 9437188
  2.9 7.9 %collective-permute-start = (f32[4,1,64,128]{3,2,1,0:T(8,128)}, f32[4,1,64,128]{3,2,1,0:T(8,128)S(1)}, u32[]{:S(2)}, u32[]{:S(2)}) collective-permute-start(f32[4,1,64,128]{3,2,1,0:T(8,128)} %get-tuple-element.6), channel_id=1, source_target_pairs={{0,2},{2,4},{4,6},{6,8},{8,10},{10,12},{12,14},{14,16},{16,18},{18... | collective-permute-start | bytes 393224 | tf_op jit(solution)/shard_map/ppermute | solution.py:24
  7.4 6.6 %collective-permute-start.1 = (f32[4,1,64,128]{3,2,1,0:T(8,128)}, f32[4,1,64,128]{3,2,1,0:T(8,128)}, u32[]{:S(2)}, u32[]{:S(2)}) collective-permute-start(f32[4,1,64,128]{3,2,1,0:T(8,128)} %get-tuple-element.7), channel_id=1, source_target_pairs={{2,0},{4,2},{6,4},{8,6},{10,8},{12,10},{14,12},{16,14},{18,16},{20... | collective-permute-start | bytes 393224 | tf_op jit(solution)/shard_map/ppermute | solution.py:25
  14.8 2.6 %collective-permute-start.2 = (f32[4,4,1,128]{3,2,1,0:T(1,128)S(1)}, f32[4,4,1,128]{3,2,1,0:T(1,128)S(1)}, u32[]{:S(2)}, u32[]{:S(2)}) collective-permute-start(f32[4,4,1,128]{3,2,1,0:T(1,128)S(1)} %broadcast_select_fusion.1), channel_id=1, source_target_pairs={{0,1},{1,0},{2,3},{3,2},{4,5},{5,4},{6,7},{7,6},{8,9},{9,8},{10,11... | collective-permute-start | bytes 24584 | tf_op jit(solution)/shard_map/ppermute | solution.py:19
  17.2 2.1 %copy-start.13 = (s32[96]{0:T(128)S(1)}, s32[96]{0:T(128)}, u32[]{:S(2)}) copy-start(s32[96]{0:T(128)} %param.17) | copy-start | bytes 1156
  18.3 2.9 %copy-start.15 = (s32[96]{0:T(128)S(1)}, s32[96]{0:T(128)}, u32[]{:S(2)}) copy-start(s32[96]{0:T(128)} %bitcast_add_fusion.1) | copy-start | bytes 1156
  21.7 1.4 %collective-permute-start.3 = (f32[8,8,4,128]{3,1,2,0:T(8,128)S(1)}, f32[8,8,4,128]{3,1,2,0:T(8,128)S(1)}, u32[]{:S(2)}, u32[]{:S(2)}) collective-permute-start(f32[8,8,4,128]{3,1,2,0:T(8,128)S(1)} %bitcast.58), channel_id=1, source_target_pairs={{0,2},{2,0},{1,3},{3,1},{4,6},{6,4},{5,7},{7,5},{8,10},{10,8},{9,1... | collective-permute-start | bytes 393224 | tf_op jit(solution)/shard_map/ppermute | solution.py:106
  34.6 13.9 %copy-start.14 = (s32[96]{0:T(128)S(1)}, s32[96]{0:T(128)}, u32[]{:S(2)}) copy-start(s32[96]{0:T(128)} %param.17) | copy-start | bytes 1156
  34.6 14.3 %copy-start.2 = (f32[128,128]{1,0:T(8,128)S(1)}, f32[128,128]{1,0:T(8,128)}, u32[]{:S(2)}) copy-start(f32[128,128]{1,0:T(8,128)} %param.14) | copy-start | bytes 196612
  34.6 18.9 %copy-start.1 = (f32[4,2,64,128]{3,2,1,0:T(8,128)S(1)}, f32[4,2,64,128]{3,2,1,0:T(8,128)}, u32[]{:S(2)}) copy-start(f32[4,2,64,128]{3,2,1,0:T(8,128)} %param.12) | copy-start | bytes 786436
  34.6 18.9 %copy-start.3 = (f32[2,64,128]{2,1,0:T(8,128)S(1)}, f32[2,64,128]{2,1,0:T(8,128)}, u32[]{:S(2)}) copy-start(f32[2,64,128]{2,1,0:T(8,128)} %param.11) | copy-start | bytes 196612
  35.4 23.5 %copy-start.4 = (f32[128]{0:T(128)S(1)}, f32[128]{0:T(128)}, u32[]{:S(2)}) copy-start(f32[128]{0:T(128)} %get-tuple-element.12) | copy-start | bytes 1540
  35.4 23.5 %copy-start.5 = (f32[128]{0:T(128)S(1)}, f32[128]{0:T(128)}, u32[]{:S(2)}) copy-start(f32[128]{0:T(128)} %get-tuple-element.13) | copy-start | bytes 1540
  35.5 23.5 %copy-start.6 = (f32[128]{0:T(128)S(1)}, f32[128]{0:T(128)}, u32[]{:S(2)}) copy-start(f32[128]{0:T(128)} %get-tuple-element.14) | copy-start | bytes 1540
  35.5 23.5 %copy-start.7 = (f32[128]{0:T(128)S(1)}, f32[128]{0:T(128)}, u32[]{:S(2)}) copy-start(f32[128]{0:T(128)} %get-tuple-element.15) | copy-start | bytes 1540
  35.5 23.5 %copy-start.8 = (f32[128]{0:T(128)S(1)}, f32[128]{0:T(128)}, u32[]{:S(2)}) copy-start(f32[128]{0:T(128)} %get-tuple-element.16) | copy-start | bytes 1540
  35.5 23.5 %copy-start.9 = (f32[128]{0:T(128)S(1)}, f32[128]{0:T(128)}, u32[]{:S(2)}) copy-start(f32[128]{0:T(128)} %get-tuple-element.17) | copy-start | bytes 1540
  35.5 23.5 %copy-start.10 = (f32[128]{0:T(128)S(1)}, f32[128]{0:T(128)}, u32[]{:S(2)}) copy-start(f32[128]{0:T(128)} %get-tuple-element.18) | copy-start | bytes 1540
  35.5 23.5 %copy-start.11 = (f32[128]{0:T(128)S(1)}, f32[128]{0:T(128)}, u32[]{:S(2)}) copy-start(f32[128]{0:T(128)} %get-tuple-element.19) | copy-start | bytes 1540
  35.5 23.5 %copy-start.12 = (f32[128]{0:T(128)S(1)}, f32[128]{0:T(128)}, u32[]{:S(2)}) copy-start(f32[128]{0:T(128)} %get-tuple-element.20) | copy-start | bytes 1540
  49.2 4.4 %collective-permute-start.4 = (f32[1,64,128]{2,1,0:T(8,128)S(1)}, f32[1,64,128]{2,1,0:T(8,128)S(1)}, u32[]{:S(2)}, u32[]{:S(2)}) collective-permute-start(f32[1,64,128]{2,1,0:T(8,128)S(1)} %get-tuple-element.8), channel_id=1, source_target_pairs={{0,2},{2,4},{4,6},{6,8},{8,10},{10,12},{12,14},{14,16},{16,18},{18... | collective-permute-start | bytes 98312 | tf_op jit(solution)/shard_map/ppermute | solution.py:24
  51.2 5.2 %collective-permute-start.5 = (f32[1,64,128]{2,1,0:T(8,128)S(1)}, f32[1,64,128]{2,1,0:T(8,128)S(1)}, u32[]{:S(2)}, u32[]{:S(2)}) collective-permute-start(f32[1,64,128]{2,1,0:T(8,128)S(1)} %get-tuple-element.9), channel_id=1, source_target_pairs={{2,0},{4,2},{6,4},{8,6},{10,8},{12,10},{14,12},{16,14},{18,16},{20... | collective-permute-start | bytes 98312 | tf_op jit(solution)/shard_map/ppermute | solution.py:25
  56.5 2.4 %collective-permute-start.6 = (f32[4,1,128]{2,1,0:T(1,128)S(1)}, f32[4,1,128]{2,1,0:T(1,128)S(1)}, u32[]{:S(2)}, u32[]{:S(2)}) collective-permute-start(f32[4,1,128]{2,1,0:T(1,128)S(1)} %broadcast_select_fusion.4), channel_id=1, source_target_pairs={{0,1},{1,0},{2,3},{3,2},{4,5},{5,4},{6,7},{7,6},{8,9},{9,8},{10,11... | collective-permute-start | bytes 6152 | tf_op jit(solution)/shard_map/ppermute | solution.py:19

commit v23 on v16

--- a/solution.py
+++ b/solution.py
@@ -13,10 +13,10 @@
     tail = lax.slice_in_dim(cells, size - 1, size, axis=dim)
     if count == 2:
         index = lax.axis_index(axis)
-        incoming = lax.ppermute(jnp.where(index == 0, tail, head), axis, [(0, 1), (1, 0)])
-        zero = jnp.zeros_like(incoming)
-        below = jnp.where(index == 1, incoming, zero)
-        above = jnp.where(index == 0, incoming, zero)
+        both = lax.ppermute(jnp.concatenate([head, tail], axis=dim), axis, [(0, 1), (1, 0)])
+        zero = jnp.zeros_like(head)
+        below = jnp.where(index == 1, lax.slice_in_dim(both, 1, 2, axis=dim), zero)
+        above = jnp.where(index == 0, lax.slice_in_dim(both, 0, 1, axis=dim), zero)
     else:
         below = lax.ppermute(tail, axis, [(i, i + 1) for i in range(count - 1)])
         above = lax.ppermute(head, axis, [(i + 1, i) for i in range(count - 1)])

time: 60.3 us -> 61.4 us (1.018)
  other arithmetic: 6.06 us -> 6.87 us
    concatenate x0 -> x2, other arithmetic: none -> 0.76 us  [exchange(): jnp.concatenate([head, tail], axis=dim)]
where the time goes in v23:
time: 61.4 us; the launch traced here: 60.9 us
  blocking collectives  22.6 us (37%)
  starting transfers between devices  13.4 us (22%)
  waiting for transfers between devices  8.43 us (14%)
  other arithmetic  6.87 us (11%)
  matrix products  6.19 us (10%)
  local copies, waits for them, and re-layouts  2.35 us (4%)
  between operations  1.03 us (2%)
    all_to_all x1, blocking collectives, per_device(): lax.all_to_all(merged, 'vh', split_axis=0, concat_axis=0, tiled=True)  11.4 us
    all_to_all x1, blocking collectives, per_device(): lax.all_to_all(spread, VOX, split_axis=0, concat_axis=0, tiled=True)  11.1 us
    ppermute x2, starting transfers between devices, exchange(): below = lax.ppermute(tail, axis, [(i, i + 1) for i in range(count - 1)])  6.6 us
    ppermute x2, waiting for transfers between devices, exchange(): above = lax.ppermute(head, axis, [(i + 1, i) for i in range(count - 1)])  6.14 us
    ppermute x2, starting transfers between devices, exchange(): above = lax.ppermute(head, axis, [(i + 1, i) for i in range(count - 1)])  4.22 us
    ppermute x2, starting transfers between devices, exchange(): lax.ppermute(jnp.concatenate([head, tail], axis=dim), axis, [(0, 1), (1,...  2.55 us
    dot_general x1, matrix products, per_device(): jnp.einsum('sxyw,zw->sxyz', smoothed, vertical_mix, precision=HIGH)  2.13 us
    reduce_sum x1, other arithmetic, per_device(): gradient = grad_latent + jnp.mean(latent, axis=0)  1.76 us
  transfers between devices with their start and end apart: 7, of which 5 were waited for; matrix products, arithmetic and copies ran while one was open for 5% of the time, Pallas kernels for 0%

profile of v23, /device:TPU:1, one launch (start us, length us, event | category | flops | bytes accessed | tf_op | source)
XLA Modules:
  0.0 60.9 jit_solution(10902278493655598054)
XLA Ops:
  0.6 1.8 %fusion.66 = (f32[2,64,128]{2,1,0:T(8,128)}, f32[4,2,64,128]{3,2,1,0:T(8,128)S(1)}) fusion(f32[4,2,64,128]{3,2,1,0:T(8,128)} %param.12, f32[2,64,128]{2,1,0:T(8,128)} %param.11), kind=kLoop, calls=%fused_computation.111 | loop fusion | flops 114688 | bytes 655360 | tf_op jit(solution)/shard_map/reduce_sum | solution.py:132
  2.4 0.7 %fusion.67 = (f32[4,1,64,128]{3,2,1,0:T(8,128)}, f32[4,1,64,128]{3,2,1,0:T(8,128)}) fusion(f32[4,2,64,128]{3,2,1,0:T(8,128)S(1)} %get-tuple-element.3), kind=kLoop, calls=%fused_computation.112 | loop fusion | bytes 524288 | tf_op jit(solution)/shard_map/slice | solution.py:13
  3.1 4.5 %collective-permute-start = (f32[4,1,64,128]{3,2,1,0:T(8,128)}, f32[4,1,64,128]{3,2,1,0:T(8,128)S(1)}, u32[]{:S(2)}, u32[]{:S(2)}) collective-permute-start(f32[4,1,64,128]{3,2,1,0:T(8,128)} %get-tuple-element.6), channel_id=1, source_target_pairs={{0,2},{2,4},{4,6},{6,8},{8,10},{10,12},{12,14},{14,16},{16,18},{18... | collective-permute-start | bytes 393224 | tf_op jit(solution)/shard_map/ppermute | solution.py:21
  7.7 1.9 %collective-permute-start.1 = (f32[4,1,64,128]{3,2,1,0:T(8,128)}, f32[4,1,64,128]{3,2,1,0:T(8,128)}, u32[]{:S(2)}, u32[]{:S(2)}) collective-permute-start(f32[4,1,64,128]{3,2,1,0:T(8,128)} %get-tuple-element.7), channel_id=1, source_target_pairs={{2,0},{4,2},{6,4},{8,6},{10,8},{12,10},{14,12},{16,14},{18,16},{20... | collective-permute-start | bytes 393224 | tf_op jit(solution)/shard_map/ppermute | solution.py:22
  9.6 0.8 %broadcast_in_dim.10 = f32[9]{0:T(128)S(1)} reshape(f32[3,3]{1,0:T(4,128)} %param.13) | data formatting | bytes 72 | tf_op jit(solution)/shard_map/broadcast_in_dim | solution.py:71
  10.4 0.6 %slice_bitcast_fusion.8 = (f32[128]{0:T(128)}, f32[128]{0:T(128)}, f32[128]{0:T(128)}, f32[128]{0:T(128)}, f32[128]{0:T(128)}, /*index=5*/f32[128]{0:T(128)}, f32[128]{0:T(128)}, f32[128]{0:T(128)}, f32[128]{0:T(128)}) fusion(f32[9,128]{1,0:T(8,128)S(1)} %broadcast_in_dim.11), kind=kLoop, calls=%fused_computation.106 | loop fusion | bytes 9216 | tf_op jit(solution)/shard_map/mul | solution.py:129
  11.1 3.2 %collective-permute-done.1 = f32[4,1,64,128]{3,2,1,0:T(8,128)} collective-permute-done((f32[4,1,64,128]{3,2,1,0:T(8,128)}, f32[4,1,64,128]{3,2,1,0:T(8,128)}, u32[]{:S(2)}, u32[]{:S(2)}) %collective-permute-start.1) | collective-permute-done | bytes 131104 | tf_op jit(solution)/shard_map/ppermute | solution.py:22
  14.3 0.8 %fusion.61 = f32[4,4,2,128]{3,2,1,0:T(2,128)S(1)} fusion(f32[4,1,64,128]{3,2,1,0:T(8,128)} %collective-permute-done.1, f32[4,2,64,128]{3,2,1,0:T(8,128)S(1)} %get-tuple-element.3, f32[4,1,64,128]{3,2,1,0:T(8,128)S(1)} %collective-permute-done), kind=kLoop, calls=%fused_computation.81 | loop fusion | flops 53248 | bytes 540672 | tf_op jit(solution)/shard_map/concatenate | solution.py:16
  15.0 1.3 %collective-permute-start.2 = (f32[4,4,2,128]{3,2,1,0:T(2,128)S(1)}, f32[4,4,2,128]{3,2,1,0:T(2,128)}, u32[]{:S(2)}, u32[]{:S(2)}) collective-permute-start(f32[4,4,2,128]{3,2,1,0:T(2,128)S(1)} %fusion.61), channel_id=1, source_target_pairs={{0,1},{1,0},{2,3},{3,2},{4,5},{5,4},{6,7},{7,6},{8,9},{9,8},{10,11... | collective-permute-start | bytes 49160 | tf_op jit(solution)/shard_map/ppermute | solution.py:16
  16.3 1.2 %bitcast_add_fusion.1 = s32[96]{0:T(128)} fusion(s32[96]{0:T(128)} %param.19, s32[96,1]{0,1:T(1,128)} %param.18), kind=kLoop, calls=%fused_computation.107 | loop fusion | flops 192 | bytes 1152 | tf_op jit(solution)/shard_map/add | solution.py:92
  17.8 0.8 %broadcast_select_fusion.1 = (f32[4,4,1,128]{3,2,1,0:T(1,128)S(1)}, f32[4,4,1,128]{3,2,1,0:T(1,128)S(1)}) fusion(pred[]{:T(512)S(6)} %eq.16, f32[4,4,2,128]{3,2,1,0:T(2,128)} %collective-permute-done.2, pred[]{:T(512)S(6)} %eq.17), kind=kLoop, calls=%fused_computation.87 | loop fusion | flops 4096 | bytes 32770 | tf_op jit(solution)/shard_map/jit(_where)/select_n | solution.py:18
  18.6 1.0 %pad_maximum_fusion = f32[4,4,66,128]{3,2,1,0:T(8,128)S(1)} fusion(f32[4,4,1,128]{3,2,1,0:T(1,128)S(1)} %get-tuple-element.13, f32[4,1,64,128]{3,2,1,0:T(8,128)} %collective-permute-done.1, f32[4,2,64,128]{3,2,1,0:T(8,128)S(1)} %get-tuple-element.3, f32[4,1,64,128]{3,2,1,0:T(8,128)S(1)} %collective-permute-done, f32[4,4,1,128]{3,2,1,0:T(1,128)S(1)} %get-tuple-element.12), kind=kLoop, calls=%fused_computation.2 | loop fusion | flops 540672 | bytes 1081344 | tf_op jit(solution)/shard_map/concatenate | solution.py:23
  19.6 2.1 %fusion.69 = (bf16[4,2,64,128]{3,2,1,0:T(8,128)(2,1)S(1)}, f32[4,2,64,128]{3,2,1,0:T(8,128)}) fusion(f32[128]{0:T(128)} %param.15, f32[128,128]{1,0:T(8,128)} %param.14, f32[4,4,66,128]{3,2,1,0:T(8,128)S(1)} %pad_maximum_fusion, f32[128]{0:T(128)} %get-tuple-element.15, f32[128]{0:T(128)} %get-tuple-element.16, f32[128]{0:T(128)} %get-tuple-element.17, ...), kind=kOutput, calls=%fused_computation.114 | convolution fusion | flops 101908480 | bytes 2823168 | tf_op jit(solution)/shard_map/sxyw,zw->sxyz/dot_general | solution.py:82
  22.0 1.7 %fusion.32 = f32[96,4,128]{2,1,0:T(4,128)S(1)} fusion(bf16[96,128,128]{2,1,0:T(8,128)(2,1)S(1)} %copy-done, bf16[96,4,128]{2,0,1:T(8,128)(2,1)S(1)} %fusion.55), kind=kOutput, calls=%fused_computation.42 | convolution fusion | flops 12582912 | bytes 3440640 | tf_op jit(solution)/shard_map/pij,psj->psi/dot_general | solution.py:91
  24.2 1.3 %collective-permute-done.3 = f32[8,8,4,128]{3,1,2,0:T(8,128)S(1)} collective-permute-done((f32[8,8,4,128]{3,1,2,0:T(8,128)S(1)}, f32[8,8,4,128]{3,1,2,0:T(8,128)S(1)}, u32[]{:S(2)}, u32[]{:S(2)}) %collective-permute-start.3) | collective-permute-done | bytes 131104 | tf_op jit(solution)/shard_map/ppermute | solution.py:102
  25.7 11.4 %all_to_all.10 = f32[8,8,4,128]{3,1,2,0:T(8,128)S(1)} all-to-all(f32[8,8,4,128]{3,1,2,0:T(8,128)S(1)} %bitcast_add_fusion), channel_id=1, replica_groups=mesh['vh'=8,'vc'=2,'star'=2] {'vh'}, dimensions={0} | all-to-all | bytes 262144 | tf_op jit(solution)/shard_map/all_to_all | solution.py:103
  37.2 11.1 %all_to_all.11 = bf16[16,8,4,128]{3,2,1,0:T(4,128)(2,1)S(1)} all-to-all(bf16[16,8,4,128]{3,2,1,0:T(4,128)(2,1)S(1)} %broadcast_in_dim.13), channel_id=1, replica_groups=mesh['vh'=8,'vc'=2,'star'=2] {'vh','vc'}, dimensions={0} | all-to-all | bytes 262144 | tf_op jit(solution)/shard_map/all_to_all | solution.py:109
  48.6 0.9 %fusion.33 = f32[96,4,128]{2,1,0:T(4,128)S(1)} fusion(bf16[96,128,128]{2,1,0:T(8,128)(2,1)S(1)} %copy-done, bf16[96,4,128]{2,0,1:T(8,128)(2,1)S(1)} %fusion.21), kind=kOutput, calls=%fused_computation.43 | convolution fusion | flops 12582912 | bytes 3440640 | tf_op jit(solution)/shard_map/pij,psi->psj/dot_general | solution.py:115
  50.2 2.1 %collective-permute-start.4 = (f32[1,64,128]{2,1,0:T(8,128)S(1)}, f32[1,64,128]{2,1,0:T(8,128)S(1)}, u32[]{:S(2)}, u32[]{:S(2)}) collective-permute-start(f32[1,64,128]{2,1,0:T(8,128)S(1)} %get-tuple-element.8), channel_id=1, source_target_pairs={{0,2},{2,4},{4,6},{6,8},{8,10},{10,12},{12,14},{14,16},{16,18},{18... | collective-permute-start | bytes 98312 | tf_op jit(solution)/shard_map/ppermute | solution.py:21
  52.3 2.3 %collective-permute-start.5 = (f32[1,64,128]{2,1,0:T(8,128)S(1)}, f32[1,64,128]{2,1,0:T(8,128)S(1)}, u32[]{:S(2)}, u32[]{:S(2)}) collective-permute-start(f32[1,64,128]{2,1,0:T(8,128)S(1)} %get-tuple-element.9), channel_id=1, source_target_pairs={{2,0},{4,2},{6,4},{8,6},{10,8},{12,10},{14,12},{16,14},{18,16},{20... | collective-permute-start | bytes 98312 | tf_op jit(solution)/shard_map/ppermute | solution.py:22
  54.6 2.9 %collective-permute-done.5 = f32[1,64,128]{2,1,0:T(8,128)S(1)} collective-permute-done((f32[1,64,128]{2,1,0:T(8,128)S(1)}, f32[1,64,128]{2,1,0:T(8,128)S(1)}, u32[]{:S(2)}, u32[]{:S(2)}) %collective-permute-start.5) | collective-permute-done | bytes 32800 | tf_op jit(solution)/shard_map/ppermute | solution.py:22
  57.5 1.3 %collective-permute-start.6 = (f32[4,2,128]{2,1,0:T(2,128)S(1)}, f32[4,2,128]{2,1,0:T(2,128)S(1)}, u32[]{:S(2)}, u32[]{:S(2)}) collective-permute-start(f32[4,2,128]{2,1,0:T(2,128)S(1)} %fusion.64), channel_id=1, source_target_pairs={{0,1},{1,0},{2,3},{3,2},{4,5},{5,4},{6,7},{7,6},{8,9},{9,8},{10,11... | collective-permute-start | bytes 12296 | tf_op jit(solution)/shard_map/ppermute | solution.py:16
  59.4 0.7 %collective-permute-done.6 = f32[4,2,128]{2,1,0:T(2,128)S(1)} collective-permute-done((f32[4,2,128]{2,1,0:T(2,128)S(1)}, f32[4,2,128]{2,1,0:T(2,128)S(1)}, u32[]{:S(2)}, u32[]{:S(2)}) %collective-permute-start.6) | collective-permute-done | bytes 4128 | tf_op jit(solution)/shard_map/ppermute | solution.py:16
  60.2 0.7 %fusion.35 = f32[2,64,128]{2,1,0:T(8,128)} fusion(f32[4,66,128]{2,1,0:T(8,128)S(1)} %pad_maximum_fusion.1, f32[2,64,128]{2,1,0:T(8,128)S(1)} %copy-done.1, f32[128]{0:T(128)S(1)} %copy-done.7, f32[128]{0:T(128)S(1)} %copy-done.8, f32[128]{0:T(128)S(1)} %copy-done.9, f32[128]{0:T(128)S(1)} %copy-done.10, f32[128]{0:T(128)S(1)} %copy-done.11, ...), kind=kLoop, calls=%fused_computation.46 | loop fusion | flops 311296 | bytes 725504 | tf_op jit(solution)/shard_map/add | solution.py:132
  (59 shorter events, 2.7 us)
Async XLA Ops:
  0.6 21.3 %copy-start = (bf16[96,128,128]{2,1,0:T(8,128)(2,1)S(1)}, bf16[96,128,128]{2,1,0:T(8,128)(2,1)}, u32[]{:S(2)}) copy-start(bf16[96,128,128]{2,1,0:T(8,128)(2,1)} %param.16) | copy-start | bytes 9437188
  3.1 7.9 %collective-permute-start = (f32[4,1,64,128]{3,2,1,0:T(8,128)}, f32[4,1,64,128]{3,2,1,0:T(8,128)S(1)}, u32[]{:S(2)}, u32[]{:S(2)}) collective-permute-start(f32[4,1,64,128]{3,2,1,0:T(8,128)} %get-tuple-element.6), channel_id=1, source_target_pairs={{0,2},{2,4},{4,6},{6,8},{8,10},{10,12},{12,14},{14,16},{16,18},{18... | collective-permute-start | bytes 393224 | tf_op jit(solution)/shard_map/ppermute | solution.py:21
  7.7 6.6 %collective-permute-start.1 = (f32[4,1,64,128]{3,2,1,0:T(8,128)}, f32[4,1,64,128]{3,2,1,0:T(8,128)}, u32[]{:S(2)}, u32[]{:S(2)}) collective-permute-start(f32[4,1,64,128]{3,2,1,0:T(8,128)} %get-tuple-element.7), channel_id=1, source_target_pairs={{2,0},{4,2},{6,4},{8,6},{10,8},{12,10},{14,12},{16,14},{18,16},{20... | collective-permute-start | bytes 393224 | tf_op jit(solution)/shard_map/ppermute | solution.py:22
  15.0 2.8 %collective-permute-start.2 = (f32[4,4,2,128]{3,2,1,0:T(2,128)S(1)}, f32[4,4,2,128]{3,2,1,0:T(2,128)}, u32[]{:S(2)}, u32[]{:S(2)}) collective-permute-start(f32[4,4,2,128]{3,2,1,0:T(2,128)S(1)} %fusion.61), channel_id=1, source_target_pairs={{0,1},{1,0},{2,3},{3,2},{4,5},{5,4},{6,7},{7,6},{8,9},{9,8},{10,11... | collective-permute-start | bytes 49160 | tf_op jit(solution)/shard_map/ppermute | solution.py:16
  17.5 4.2 %copy-start.15 = (s32[96]{0:T(128)S(1)}, s32[96]{0:T(128)}, u32[]{:S(2)}) copy-start(s32[96]{0:T(128)} %param.17) | copy-start | bytes 1156
  21.7 15.4 %copy-start.4 = (f32[8,128]{1,0:T(8,128)S(1)}, f32[8,128]{1,0:T(8,128)}, u32[]{:S(2)}) copy-start(f32[8,128]{1,0:T(8,128)} %param.20) | copy-start | bytes 12292
  21.7 15.4 %copy-start.5 = (f32[8,128]{1,0:T(8,128)S(1)}, f32[8,128]{1,0:T(8,128)}, u32[]{:S(2)}) copy-start(f32[8,128]{1,0:T(8,128)} %param.21) | copy-start | bytes 12292
  23.7 25.8 %copy-start.16 = (s32[96]{0:T(128)S(1)}, s32[96]{0:T(128)}, u32[]{:S(2)}) copy-start(s32[96]{0:T(128)} %param.17) | copy-start | bytes 1156
  24.1 25.8 %copy-start.3 = (f32[128,128]{1,0:T(8,128)S(1)}, f32[128,128]{1,0:T(8,128)}, u32[]{:S(2)}) copy-start(f32[128,128]{1,0:T(8,128)} %param.14) | copy-start | bytes 196612
  24.1 1.4 %collective-permute-start.3 = (f32[8,8,4,128]{3,1,2,0:T(8,128)S(1)}, f32[8,8,4,128]{3,1,2,0:T(8,128)S(1)}, u32[]{:S(2)}, u32[]{:S(2)}) collective-permute-start(f32[8,8,4,128]{3,1,2,0:T(8,128)S(1)} %bitcast.60), channel_id=1, source_target_pairs={{0,2},{2,0},{1,3},{3,1},{4,6},{6,4},{5,7},{7,5},{8,10},{10,8},{9,1... | collective-permute-start | bytes 393224 | tf_op jit(solution)/shard_map/ppermute | solution.py:102
  25.6 34.5 %copy-start.1 = (f32[2,64,128]{2,1,0:T(8,128)S(1)}, f32[2,64,128]{2,1,0:T(8,128)}, u32[]{:S(2)}) copy-start(f32[2,64,128]{2,1,0:T(8,128)} %get-tuple-element.2) | copy-start | bytes 196612
  25.6 34.5 %copy-start.6 = (f32[128]{0:T(128)S(1)}, f32[128]{0:T(128)}, u32[]{:S(2)}) copy-start(f32[128]{0:T(128)} %get-tuple-element.14) | copy-start | bytes 1540
  25.6 34.5 %copy-start.7 = (f32[128]{0:T(128)S(1)}, f32[128]{0:T(128)}, u32[]{:S(2)}) copy-start(f32[128]{0:T(128)} %get-tuple-element.15) | copy-start | bytes 1540
  25.6 34.5 %copy-start.8 = (f32[128]{0:T(128)S(1)}, f32[128]{0:T(128)}, u32[]{:S(2)}) copy-start(f32[128]{0:T(128)} %get-tuple-element.16) | copy-start | bytes 1540
  25.6 34.5 %copy-start.9 = (f32[128]{0:T(128)S(1)}, f32[128]{0:T(128)}, u32[]{:S(2)}) copy-start(f32[128]{0:T(128)} %get-tuple-element.17) | copy-start | bytes 1540
  25.6 34.5 %copy-start.10 = (f32[128]{0:T(128)S(1)}, f32[128]{0:T(128)}, u32[]{:S(2)}) copy-start(f32[128]{0:T(128)} %get-tuple-element.18) | copy-start | bytes 1540
  25.6 34.5 %copy-start.11 = (f32[128]{0:T(128)S(1)}, f32[128]{0:T(128)}, u32[]{:S(2)}) copy-start(f32[128]{0:T(128)} %get-tuple-element.19) | copy-start | bytes 1540
  25.7 34.5 %copy-start.12 = (f32[128]{0:T(128)S(1)}, f32[128]{0:T(128)}, u32[]{:S(2)}) copy-start(f32[128]{0:T(128)} %get-tuple-element.20) | copy-start | bytes 1540
  25.7 34.5 %copy-start.13 = (f32[128]{0:T(128)S(1)}, f32[128]{0:T(128)}, u32[]{:S(2)}) copy-start(f32[128]{0:T(128)} %get-tuple-element.21) | copy-start | bytes 1540
  25.7 34.5 %copy-start.14 = (f32[128]{0:T(128)S(1)}, f32[128]{0:T(128)}, u32[]{:S(2)}) copy-start(f32[128]{0:T(128)} %get-tuple-element.22) | copy-start | bytes 1540
  37.1 12.8 %copy-start.2 = (f32[4,2,64,128]{3,2,1,0:T(8,128)S(1)}, f32[4,2,64,128]{3,2,1,0:T(8,128)}, u32[]{:S(2)}) copy-start(f32[4,2,64,128]{3,2,1,0:T(8,128)} %get-tuple-element.26) | copy-start | bytes 786436
  50.2 4.4 %collective-permute-start.4 = (f32[1,64,128]{2,1,0:T(8,128)S(1)}, f32[1,64,128]{2,1,0:T(8,128)S(1)}, u32[]{:S(2)}, u32[]{:S(2)}) collective-permute-start(f32[1,64,128]{2,1,0:T(8,128)S(1)} %get-tuple-element.8), channel_id=1, source_target_pairs={{0,2},{2,4},{4,6},{6,8},{8,10},{10,12},{12,14},{14,16},{16,18},{18... | collective-permute-start | bytes 98312 | tf_op jit(solution)/shard_map/ppermute | solution.py:21
  52.3 5.2 %collective-permute-start.5 = (f32[1,64,128]{2,1,0:T(8,128)S(1)}, f32[1,64,128]{2,1,0:T(8,128)S(1)}, u32[]{:S(2)}, u32[]{:S(2)}) collective-permute-start(f32[1,64,128]{2,1,0:T(8,128)S(1)} %get-tuple-element.9), channel_id=1, source_target_pairs={{2,0},{4,2},{6,4},{8,6},{10,8},{12,10},{14,12},{16,14},{18,16},{20... | collective-permute-start | bytes 98312 | tf_op jit(solution)/shard_map/ppermute | solution.py:22
  57.5 2.5 %collective-permute-start.6 = (f32[4,2,128]{2,1,0:T(2,128)S(1)}, f32[4,2,128]{2,1,0:T(2,128)S(1)}, u32[]{:S(2)}, u32[]{:S(2)}) collective-permute-start(f32[4,2,128]{2,1,0:T(2,128)S(1)} %fusion.64), channel_id=1, source_target_pairs={{0,1},{1,0},{2,3},{3,2},{4,5},{5,4},{6,7},{7,6},{8,9},{9,8},{10,11... | collective-permute-start | bytes 12296 | tf_op jit(solution)/shard_map/ppermute | solution.py:16
  (1 other events, 4.1 us)

commit v24 on v16

--- a/solution.py
+++ b/solution.py
@@ -115,8 +115,12 @@
     pair_adjoint = jnp.einsum(
         "pij,psi->psj", responses, pair_misfit, preferred_element_type=jnp.float32
     )
-    adjoint = jnp.einsum("pb,psj->sbj", line_onehot, pair_adjoint, precision=HIGH).reshape(
-        samples, width_x, width_y, length
+    adjoint = (
+        jnp.zeros((width_x * width_y, samples, length), jnp.float32)
+        .at[pair_line]
+        .add(pair_adjoint, mode="promise_in_bounds")
+        .transpose(1, 0, 2)
+        .reshape(samples, width_x, width_y, length)
     )
     grad_log = jnp.mean(density * adjoint, axis=0)
     grad_smooth = jnp.einsum("xyz,zw->xyw", grad_log, vertical_mix, precision=HIGH)

time: 60.3 us -> 71 us (1.18)
  blocking collectives: 22.6 us -> 11.4 us
  other arithmetic: 6.06 us -> 15.2 us
  waiting for transfers between devices: 8.2 us -> 14.6 us
  starting transfers between devices: 13.4 us -> 18.4 us
    all_to_all x1 -> x0, blocking collectives: 11.1 us -> none  [per_device(): lax.all_to_all(spread, VOX, split_axis=0, concat_axis=0, tiled=True)]
    scatter-add x0 -> x1, other arithmetic: none -> 6.93 us  [per_device(): adjoint = jnp.zeros((width_x * width_y, samples, length), jnp.float32).at...]
    all_to_all x0 -> x1, waiting for transfers between devices: none -> 6.43 us  [per_device(): lax.all_to_all(spread, VOX, split_axis=0, concat_axis=0, tiled=True)]
    all_to_all x0 -> x1, starting transfers between devices: none -> 5.04 us  [per_device(): lax.all_to_all(spread, VOX, split_axis=0, concat_axis=0, tiled=True)]
    reduce_sum x1, other arithmetic: 0.03 us -> 1 us  [per_device(): grad_log = jnp.mean(density * adjoint, axis=0)]
  transfers between devices with their start and end apart: 7 -> 8, of which waited for: 5 -> 6; matrix products, arithmetic and copies ran while one was open for 5% -> 5% of each run, Pallas kernels for 0% -> 0%
where the time goes in v24:
time: 71 us; the launch traced here: 70 us
  starting transfers between devices  18.4 us (26%)
  other arithmetic  15.2 us (21%)
  waiting for transfers between devices  14.6 us (21%)
  blocking collectives  11.4 us (16%)
  matrix products  6.49 us (9%)
  local copies, waits for them, and re-layouts  2.99 us (4%)
  between operations  0.92 us (1%)
    all_to_all x1, blocking collectives, per_device(): lax.all_to_all(merged, 'vh', split_axis=0, concat_axis=0, tiled=True)  11.4 us
    scatter-add x1, other arithmetic, per_device(): adjoint = jnp.zeros((width_x * width_y, samples, length), jnp.float32).at...  6.93 us
    ppermute x2, starting transfers between devices, exchange(): below = lax.ppermute(tail, axis, [(i, i + 1) for i in range(count - 1)])  6.57 us
    all_to_all x1, waiting for transfers between devices, per_device(): lax.all_to_all(spread, VOX, split_axis=0, concat_axis=0, tiled=True)  6.43 us
    ppermute x2, waiting for transfers between devices, exchange(): above = lax.ppermute(head, axis, [(i + 1, i) for i in range(count - 1)])  6.11 us
    all_to_all x1, starting transfers between devices, per_device(): lax.all_to_all(spread, VOX, split_axis=0, concat_axis=0, tiled=True)  5.04 us
    ppermute x2, starting transfers between devices, exchange(): above = lax.ppermute(head, axis, [(i + 1, i) for i in range(count - 1)])  4.24 us
    ppermute x2, starting transfers between devices, exchange(): lax.ppermute(jnp.where(index == 0, tail, head), axis, [(0, 1), (1, 0)])  2.48 us
  transfers between devices with their start and end apart: 8, of which 6 were waited for; matrix products, arithmetic and copies ran while one was open for 5% of the time, Pallas kernels for 0%

profile of v24, /device:TPU:1, one launch (start us, length us, event | category | flops | bytes accessed | tf_op | source)
XLA Modules:
  0.0 70.0 jit_solution(14967794333243219066)
XLA Ops:
  0.6 1.8 %fusion.60 = (f32[2,64,128]{2,1,0:T(8,128)}, f32[4,2,64,128]{3,2,1,0:T(8,128)S(1)}) fusion(f32[4,2,64,128]{3,2,1,0:T(8,128)} %param.12, f32[2,64,128]{2,1,0:T(8,128)} %param.11), kind=kLoop, calls=%fused_computation.106 | loop fusion | flops 114688 | bytes 655360 | tf_op jit(solution)/shard_map/reduce_sum | solution.py:136
  2.4 0.7 %fusion.61 = (f32[4,1,64,128]{3,2,1,0:T(8,128)}, f32[4,1,64,128]{3,2,1,0:T(8,128)}) fusion(f32[4,2,64,128]{3,2,1,0:T(8,128)S(1)} %get-tuple-element.3), kind=kLoop, calls=%fused_computation.107 | loop fusion | bytes 524288 | tf_op jit(solution)/shard_map/slice | solution.py:13
  3.1 4.5 %collective-permute-start = (f32[4,1,64,128]{3,2,1,0:T(8,128)}, f32[4,1,64,128]{3,2,1,0:T(8,128)S(1)}, u32[]{:S(2)}, u32[]{:S(2)}) collective-permute-start(f32[4,1,64,128]{3,2,1,0:T(8,128)} %get-tuple-element.6), channel_id=1, source_target_pairs={{0,2},{2,4},{4,6},{6,8},{8,10},{10,12},{12,14},{14,16},{16,18},{18... | collective-permute-start | bytes 393224 | tf_op jit(solution)/shard_map/ppermute | solution.py:21
  7.7 1.9 %collective-permute-start.1 = (f32[4,1,64,128]{3,2,1,0:T(8,128)}, f32[4,1,64,128]{3,2,1,0:T(8,128)}, u32[]{:S(2)}, u32[]{:S(2)}) collective-permute-start(f32[4,1,64,128]{3,2,1,0:T(8,128)} %get-tuple-element.7), channel_id=1, source_target_pairs={{2,0},{4,2},{6,4},{8,6},{10,8},{12,10},{14,12},{16,14},{18,16},{20... | collective-permute-start | bytes 393224 | tf_op jit(solution)/shard_map/ppermute | solution.py:22
  9.6 0.8 %broadcast_in_dim.14 = f32[9]{0:T(128)S(1)} reshape(f32[3,3]{1,0:T(4,128)} %param.13) | data formatting | bytes 72 | tf_op jit(solution)/shard_map/broadcast_in_dim | solution.py:71
  11.1 3.2 %collective-permute-done.1 = f32[4,1,64,128]{3,2,1,0:T(8,128)} collective-permute-done((f32[4,1,64,128]{3,2,1,0:T(8,128)}, f32[4,1,64,128]{3,2,1,0:T(8,128)}, u32[]{:S(2)}, u32[]{:S(2)}) %collective-permute-start.1) | collective-permute-done | bytes 131104 | tf_op jit(solution)/shard_map/ppermute | solution.py:22
  14.3 0.7 %broadcast_select_fusion.1 = f32[4,4,1,128]{3,2,1,0:T(1,128)S(1)} fusion(pred[]{:T(512)S(6)} %eq.17, f32[4,1,64,128]{3,2,1,0:T(8,128)} %collective-permute-done.1, f32[4,2,64,128]{3,2,1,0:T(8,128)S(1)} %get-tuple-element.3, f32[4,1,64,128]{3,2,1,0:T(8,128)S(1)} %collective-permute-done), kind=kLoop, calls=%fused_computation.80 | loop fusion | flops 10240 | bytes 532481 | tf_op jit(solution)/shard_map/jit(_where)/select_n | solution.py:16
  15.0 1.3 %collective-permute-start.2 = (f32[4,4,1,128]{3,2,1,0:T(1,128)S(1)}, f32[4,4,1,128]{3,2,1,0:T(1,128)S(1)}, u32[]{:S(2)}, u32[]{:S(2)}) collective-permute-start(f32[4,4,1,128]{3,2,1,0:T(1,128)S(1)} %broadcast_select_fusion.1), channel_id=1, source_target_pairs={{0,1},{1,0},{2,3},{3,2},{4,5},{5,4},{6,7},{7,6},{8,9},{9,8},{10,11... | collective-permute-start | bytes 24584 | tf_op jit(solution)/shard_map/ppermute | solution.py:16
  16.3 1.2 %bitcast_add_fusion.1 = s32[96]{0:T(128)} fusion(s32[96]{0:T(128)} %param.19, s32[96,1]{0,1:T(1,128)} %param.18), kind=kLoop, calls=%fused_computation.102 | loop fusion | flops 192 | bytes 1152 | tf_op jit(solution)/shard_map/add | solution.py:92
  17.6 1.0 %pad_maximum_fusion = f32[4,4,66,128]{3,2,1,0:T(8,128)S(1)} fusion(f32[4,4,1,128]{3,2,1,0:T(1,128)S(1)} %get-tuple-element.22, f32[4,1,64,128]{3,2,1,0:T(8,128)} %collective-permute-done.1, f32[4,2,64,128]{3,2,1,0:T(8,128)S(1)} %get-tuple-element.3, f32[4,1,64,128]{3,2,1,0:T(8,128)S(1)} %collective-permute-done, f32[4,4,1,128]{3,2,1,0:T(1,128)S(1)} %get-tuple-element.21), kind=kLoop, calls=%fused_computation.5 | loop fusion | flops 540672 | bytes 1081344 | tf_op jit(solution)/shard_map/concatenate | solution.py:23
  18.6 2.1 %fusion.63 = (bf16[4,2,64,128]{3,2,1,0:T(8,128)(2,1)S(1)}, f32[4,2,64,128]{3,2,1,0:T(8,128)}) fusion(f32[128]{0:T(128)} %param.15, f32[128,128]{1,0:T(8,128)} %param.14, f32[4,4,66,128]{3,2,1,0:T(8,128)S(1)} %pad_maximum_fusion, f32[128]{0:T(128)} %get-tuple-element.13, f32[128]{0:T(128)} %get-tuple-element.14, f32[128]{0:T(128)} %get-tuple-element.15, ...), kind=kOutput, calls=%fused_computation.109 | convolution fusion | flops 101908480 | bytes 2823168 | tf_op jit(solution)/shard_map/sxyw,zw->sxyz/dot_general | solution.py:82
  21.0 1.7 %fusion.32 = f32[96,4,128]{2,1,0:T(4,128)S(1)} fusion(bf16[96,128,128]{2,1,0:T(8,128)(2,1)S(1)} %copy-done, bf16[96,4,128]{2,0,1:T(8,128)(2,1)S(1)} %convolution_convert_fusion.1), kind=kOutput, calls=%fused_computation.43 | convolution fusion | flops 12582912 | bytes 3440640 | tf_op jit(solution)/shard_map/pij,psj->psi/dot_general | solution.py:91
  23.2 1.3 %collective-permute-done.3 = f32[8,8,4,128]{3,1,2,0:T(8,128)S(1)} collective-permute-done((f32[8,8,4,128]{3,1,2,0:T(8,128)S(1)}, f32[8,8,4,128]{3,1,2,0:T(8,128)S(1)}, u32[]{:S(2)}, u32[]{:S(2)}) %collective-permute-start.3) | collective-permute-done | bytes 131104 | tf_op jit(solution)/shard_map/ppermute | solution.py:102
  24.6 11.4 %all_to_all.10 = f32[8,8,4,128]{3,1,2,0:T(8,128)S(1)} all-to-all(f32[8,8,4,128]{3,1,2,0:T(8,128)S(1)} %bitcast_add_fusion), channel_id=1, replica_groups=mesh['vh'=8,'vc'=2,'star'=2] {'vh'}, dimensions={0} | all-to-all | bytes 262144 | tf_op jit(solution)/shard_map/all_to_all | solution.py:103
  36.7 5.0 %all-to-all-start.1 = ((bf16[16,8,4,128]{3,1,2,0:T(8,128)(2,1)}), bf16[16,8,4,128]{3,1,2,0:T(8,128)(2,1)S(1)}, u32[]{:S(2)}, u32[]{:S(2)}) async-start(bf16[16,8,4,128]{3,1,2,0:T(8,128)(2,1)} %broadcast_in_dim.38), calls=%async_computation.1 | async-start | bytes 262144 | tf_op jit(solution)/shard_map/all_to_all | solution.py:109
  42.3 6.4 %all-to-all-done.1 = bf16[16,8,4,128]{3,1,2,0:T(8,128)(2,1)S(1)} async-done(((bf16[16,8,4,128]{3,1,2,0:T(8,128)(2,1)}), bf16[16,8,4,128]{3,1,2,0:T(8,128)(2,1)S(1)}, u32[]{:S(2)}, u32[]{:S(2)}) %all-to-all-start.1) | async-done | bytes 131104 | tf_op jit(solution)/shard_map/all_to_all | solution.py:109
  49.0 1.6 %fusion.30 = f32[96,4,128]{2,1,0:T(4,128)} fusion(bf16[96,128,128]{2,1,0:T(8,128)(2,1)S(1)} %copy-done, bf16[96,4,128]{2,0,1:T(8,128)(2,1)S(1)} %convolution_convert_fusion), kind=kOutput, calls=%fused_computation.41 | convolution fusion | flops 12582912 | bytes 3440640 | tf_op jit(solution)/shard_map/pij,psi->psj/dot_general | solution.py:115
  50.6 6.9 %scatter_fusion = f32[128,4,128]{2,1,0:T(4,128)S(1)} fusion(f32[128,4,128]{2,1,0:T(4,128)S(1)} %broadcast_in_dim.17, s32[96]{0:T(128)} %compare_select_fusion, f32[96,4,128]{2,1,0:T(4,128)} %fusion.30), kind=kCustom, calls=%fused_computation | custom fusion | flops 49152 | bytes 590208 | tf_op jit(solution)/shard_map/scatter-add | solution.py:121
  57.6 1.0 %multiply_reduce_fusion = f32[2,64,128]{2,1,0:T(8,128)S(1)} fusion(f32[4,2,64,128]{3,2,1,0:T(8,128)} %get-tuple-element.26, f32[4,2,64,128]{3,2,1,0:T(8,128)S(1)} %bitcast.56), kind=kLoop, calls=%fused_computation.23 | loop fusion | flops 114688 | bytes 589824 | tf_op jit(solution)/shard_map/reduce_sum | solution.py:125
  58.8 2.0 %collective-permute-start.4 = (f32[1,64,128]{2,1,0:T(8,128)S(1)}, f32[1,64,128]{2,1,0:T(8,128)S(1)}, u32[]{:S(2)}, u32[]{:S(2)}) collective-permute-start(f32[1,64,128]{2,1,0:T(8,128)S(1)} %get-tuple-element.8), channel_id=1, source_target_pairs={{0,2},{2,4},{4,6},{6,8},{8,10},{10,12},{12,14},{14,16},{16,18},{18... | collective-permute-start | bytes 98312 | tf_op jit(solution)/shard_map/ppermute | solution.py:21
  60.9 2.3 %collective-permute-start.5 = (f32[1,64,128]{2,1,0:T(8,128)S(1)}, f32[1,64,128]{2,1,0:T(8,128)S(1)}, u32[]{:S(2)}, u32[]{:S(2)}) collective-permute-start(f32[1,64,128]{2,1,0:T(8,128)S(1)} %get-tuple-element.9), channel_id=1, source_target_pairs={{2,0},{4,2},{6,4},{8,6},{10,8},{12,10},{14,12},{16,14},{18,16},{20... | collective-permute-start | bytes 98312 | tf_op jit(solution)/shard_map/ppermute | solution.py:22
  63.2 2.9 %collective-permute-done.5 = f32[1,64,128]{2,1,0:T(8,128)S(1)} collective-permute-done((f32[1,64,128]{2,1,0:T(8,128)S(1)}, f32[1,64,128]{2,1,0:T(8,128)S(1)}, u32[]{:S(2)}, u32[]{:S(2)}) %collective-permute-start.5) | collective-permute-done | bytes 32800 | tf_op jit(solution)/shard_map/ppermute | solution.py:22
  66.1 1.2 %collective-permute-start.6 = (f32[4,1,128]{2,1,0:T(1,128)S(1)}, f32[4,1,128]{2,1,0:T(1,128)S(1)}, u32[]{:S(2)}, u32[]{:S(2)}) collective-permute-start(f32[4,1,128]{2,1,0:T(1,128)S(1)} %broadcast_select_fusion.4), channel_id=1, source_target_pairs={{0,1},{1,0},{2,3},{3,2},{4,5},{5,4},{6,7},{7,6},{8,9},{9,8},{10,11... | collective-permute-start | bytes 6152 | tf_op jit(solution)/shard_map/ppermute | solution.py:16
  68.6 1.4 %fusion.35 = f32[2,64,128]{2,1,0:T(8,128)} fusion(f32[4,66,128]{2,1,0:T(8,128)S(1)} %pad_maximum_fusion.1, f32[2,64,128]{2,1,0:T(8,128)S(1)} %copy-done.1, f32[128]{0:T(128)S(1)} %copy-done.6, f32[128]{0:T(128)S(1)} %copy-done.7, f32[128]{0:T(128)} %get-tuple-element.15, f32[128]{0:T(128)} %get-tuple-element.16, f32[128]{0:T(128)} %get-tuple-element.17, ...), kind=kLoop, calls=%fused_computation.47 | loop fusion | flops 311296 | bytes 725504 | tf_op jit(solution)/shard_map/add | solution.py:136
  (48 shorter events, 4.5 us)
Async XLA Ops:
  0.6 20.3 %copy-start = (bf16[96,128,128]{2,1,0:T(8,128)(2,1)S(1)}, bf16[96,128,128]{2,1,0:T(8,128)(2,1)}, u32[]{:S(2)}) copy-start(bf16[96,128,128]{2,1,0:T(8,128)(2,1)} %param.16) | copy-start | bytes 9437188
  3.1 7.9 %collective-permute-start = (f32[4,1,64,128]{3,2,1,0:T(8,128)}, f32[4,1,64,128]{3,2,1,0:T(8,128)S(1)}, u32[]{:S(2)}, u32[]{:S(2)}) collective-permute-start(f32[4,1,64,128]{3,2,1,0:T(8,128)} %get-tuple-element.6), channel_id=1, source_target_pairs={{0,2},{2,4},{4,6},{6,8},{8,10},{10,12},{12,14},{14,16},{16,18},{18... | collective-permute-start | bytes 393224 | tf_op jit(solution)/shard_map/ppermute | solution.py:21
  7.7 6.6 %collective-permute-start.1 = (f32[4,1,64,128]{3,2,1,0:T(8,128)}, f32[4,1,64,128]{3,2,1,0:T(8,128)}, u32[]{:S(2)}, u32[]{:S(2)}) collective-permute-start(f32[4,1,64,128]{3,2,1,0:T(8,128)} %get-tuple-element.7), channel_id=1, source_target_pairs={{2,0},{4,2},{6,4},{8,6},{10,8},{12,10},{14,12},{16,14},{18,16},{20... | collective-permute-start | bytes 393224 | tf_op jit(solution)/shard_map/ppermute | solution.py:22
  15.0 2.6 %collective-permute-start.2 = (f32[4,4,1,128]{3,2,1,0:T(1,128)S(1)}, f32[4,4,1,128]{3,2,1,0:T(1,128)S(1)}, u32[]{:S(2)}, u32[]{:S(2)}) collective-permute-start(f32[4,4,1,128]{3,2,1,0:T(1,128)S(1)} %broadcast_select_fusion.1), channel_id=1, source_target_pairs={{0,1},{1,0},{2,3},{3,2},{4,5},{5,4},{6,7},{7,6},{8,9},{9,8},{10,11... | collective-permute-start | bytes 24584 | tf_op jit(solution)/shard_map/ppermute | solution.py:16
  17.5 3.3 %copy-start.9 = (s32[96]{0:T(128)S(1)}, s32[96]{0:T(128)}, u32[]{:S(2)}) copy-start(s32[96]{0:T(128)} %param.17) | copy-start | bytes 1156
  18.6 4.1 %copy-start.8 = (s32[96]{0:T(128)S(1)}, s32[96]{0:T(128)}, u32[]{:S(2)}) copy-start(s32[96]{0:T(128)} %bitcast_add_fusion.1) | copy-start | bytes 1156
  20.7 15.3 %copy-start.3 = (f32[8,128]{1,0:T(8,128)S(1)}, f32[8,128]{1,0:T(8,128)}, u32[]{:S(2)}) copy-start(f32[8,128]{1,0:T(8,128)} %param.20) | copy-start | bytes 12292
  20.7 15.3 %copy-start.4 = (f32[8,128]{1,0:T(8,128)S(1)}, f32[8,128]{1,0:T(8,128)}, u32[]{:S(2)}) copy-start(f32[8,128]{1,0:T(8,128)} %param.21) | copy-start | bytes 12292
  20.7 21.1 %copy-start.10 = (s32[96]{0:T(128)S(1)}, s32[96]{0:T(128)}, u32[]{:S(2)}) copy-start(s32[96]{0:T(128)} %param.17) | copy-start | bytes 1156
  23.2 1.4 %collective-permute-start.3 = (f32[8,8,4,128]{3,1,2,0:T(8,128)S(1)}, f32[8,8,4,128]{3,1,2,0:T(8,128)S(1)}, u32[]{:S(2)}, u32[]{:S(2)}) collective-permute-start(f32[8,8,4,128]{3,1,2,0:T(8,128)S(1)} %bitcast.58), channel_id=1, source_target_pairs={{0,2},{2,0},{1,3},{3,1},{4,6},{6,4},{5,7},{7,5},{8,10},{10,8},{9,1... | collective-permute-start | bytes 393224 | tf_op jit(solution)/shard_map/ppermute | solution.py:102
  36.0 22.6 %copy-start.2 = (f32[128,128]{1,0:T(8,128)S(1)}, f32[128,128]{1,0:T(8,128)}, u32[]{:S(2)}) copy-start(f32[128,128]{1,0:T(8,128)} %param.14) | copy-start | bytes 196612
  36.7 12.0 %all-to-all-start.1 = ((bf16[16,8,4,128]{3,1,2,0:T(8,128)(2,1)}), bf16[16,8,4,128]{3,1,2,0:T(8,128)(2,1)S(1)}, u32[]{:S(2)}, u32[]{:S(2)}) async-start(bf16[16,8,4,128]{3,1,2,0:T(8,128)(2,1)} %broadcast_in_dim.38), calls=%async_computation.1 | async-start | bytes 262144 | tf_op jit(solution)/shard_map/all_to_all | solution.py:109
  49.0 19.6 %copy-start.1 = (f32[2,64,128]{2,1,0:T(8,128)S(1)}, f32[2,64,128]{2,1,0:T(8,128)}, u32[]{:S(2)}) copy-start(f32[2,64,128]{2,1,0:T(8,128)} %get-tuple-element.2) | copy-start | bytes 196612
  49.0 19.6 %copy-start.5 = (f32[128]{0:T(128)S(1)}, f32[128]{0:T(128)}, u32[]{:S(2)}) copy-start(f32[128]{0:T(128)} %get-tuple-element.12) | copy-start | bytes 1540
  49.0 19.6 %copy-start.6 = (f32[128]{0:T(128)S(1)}, f32[128]{0:T(128)}, u32[]{:S(2)}) copy-start(f32[128]{0:T(128)} %get-tuple-element.13) | copy-start | bytes 1540
  49.0 19.6 %copy-start.7 = (f32[128]{0:T(128)S(1)}, f32[128]{0:T(128)}, u32[]{:S(2)}) copy-start(f32[128]{0:T(128)} %get-tuple-element.14) | copy-start | bytes 1540
  58.8 4.4 %collective-permute-start.4 = (f32[1,64,128]{2,1,0:T(8,128)S(1)}, f32[1,64,128]{2,1,0:T(8,128)S(1)}, u32[]{:S(2)}, u32[]{:S(2)}) collective-permute-start(f32[1,64,128]{2,1,0:T(8,128)S(1)} %get-tuple-element.8), channel_id=1, source_target_pairs={{0,2},{2,4},{4,6},{6,8},{8,10},{10,12},{12,14},{14,16},{16,18},{18... | collective-permute-start | bytes 98312 | tf_op jit(solution)/shard_map/ppermute | solution.py:21
  60.9 5.2 %collective-permute-start.5 = (f32[1,64,128]{2,1,0:T(8,128)S(1)}, f32[1,64,128]{2,1,0:T(8,128)S(1)}, u32[]{:S(2)}, u32[]{:S(2)}) collective-permute-start(f32[1,64,128]{2,1,0:T(8,128)S(1)} %get-tuple-element.9), channel_id=1, source_target_pairs={{2,0},{4,2},{6,4},{8,6},{10,8},{12,10},{14,12},{16,14},{18,16},{20... | collective-permute-start | bytes 98312 | tf_op jit(solution)/shard_map/ppermute | solution.py:22
  66.1 2.4 %collective-permute-start.6 = (f32[4,1,128]{2,1,0:T(1,128)S(1)}, f32[4,1,128]{2,1,0:T(1,128)S(1)}, u32[]{:S(2)}, u32[]{:S(2)}) collective-permute-start(f32[4,1,128]{2,1,0:T(1,128)S(1)} %broadcast_select_fusion.4), channel_id=1, source_target_pairs={{0,1},{1,0},{2,3},{3,2},{4,5},{5,4},{6,7},{7,6},{8,9},{9,8},{10,11... | collective-permute-start | bytes 6152 | tf_op jit(solution)/shard_map/ppermute | solution.py:16
